TPU v7x, 32 devices: a whole 2x2x4 slice. The times are simulated.
32 devices in a mesh: seq: 8 (over y, x, core), head: 4 (over z).
Axes of the slice: x: 2, y: 2, z: 4, core: 2. Of those that a mesh axis runs over, the one named last changes fastest.
Arguments:
- queries: bfloat16 [2048, 4096], P('seq', 'head'), may hold values from -24 to 24
- keys: bfloat16 [2048, 4096], P('seq', 'head'), may hold values from -24 to 24
- values: bfloat16 [2048, 4096], P('seq', 'head'), may hold values from -6 to 6
- out_weight: bfloat16 [4096, 4096], P('head'), may hold values from -0.75 to 0.75
- global_blocks: int32 [2], replicated, may hold values from 0 to 31, as said below
- random_blocks: int32 [32, 3], replicated, may hold values from 0 to 31, as said below
- window_blocks: int32 [32], P('head'), may hold values from 1 to 2, as said below
- yarn_scale: int32 [1], replicated, may hold values from 2 to 64
- yarn_context: int32 [1], replicated, may hold values from 1024 to 4096
Outputs:
- mixed: bfloat16 [2048, 4096], P('seq', 'head')
Inputs may be any that keep to these rules, and one draw needn't show every extreme that they name: `global_blocks`: 2 different block numbers. `random_blocks`: of the 12 random blocks named by the query blocks of one index of seq, at most 2 lie among the blocks of any one index of seq, and some index of seq holds exactly 2 of them. `window_blocks`: some head has reach 2.
All inputs are finite; a program needn't handle non-finite values.
Results may differ from a plain program's by a relative error of at most 0.013.
Values may be sent and summed in bfloat16 or wider, within the bound.
No kernel may reach another device: no remote copies, remote signals or barrier semaphores. Data moves between devices by JAX's collectives and lax.ppermute only.
A program may use at most 128 MiB of HBM per device.

v0:
```python
import math

import jax
import jax.numpy as jnp
from jax import lax
from jax.sharding import PartitionSpec as P

HEAD_DIM = 128
BLOCK = 64
GLOB = 2
RAND = 3
WMAX = 2


masked_score = -1e30


def padded_2(cells, sides, width):
    for axis, dim in sides:
        count = lax.axis_size(axis)
        ends = count - 1
        head = lax.slice_in_dim(cells, 0, width, axis=dim)
        tail = lax.slice_in_dim(cells, cells.shape[dim] - width, cells.shape[dim], axis=dim)
        cells = jnp.concatenate(
            [
                lax.ppermute(tail, axis, [(i, (i + 1) % count) for i in range(ends)]),
                cells,
                lax.ppermute(head, axis, [((i + 1) % count, i) for i in range(ends)]),
            ],
            axis=dim,
        )
    return cells


def yarn_tables(yarn_scale, yarn_context):
    half_dim = HEAD_DIM // 2
    pair_index = jnp.arange(half_dim).astype(jnp.float32)
    base_rate = 10000.0 ** (-2.0 * pair_index / HEAD_DIM)
    factor = yarn_scale[0].astype(jnp.float32)
    context = yarn_context[0].astype(jnp.float32)
    turn_ratio = context * base_rate / (2.0 * math.pi)
    ramp_weight = jnp.clip((turn_ratio - 1.0) / 31.0, 0.0, 1.0)
    frequency = base_rate * ((1.0 - ramp_weight) / factor + ramp_weight)
    mscale = 0.1 * jnp.log(factor) + 1.0
    return (frequency, mscale)


def rotate(source, first_row, frequency, mscale):
    row_count, row_width = source.shape
    half_dim = HEAD_DIM // 2
    position = (first_row + jnp.arange(row_count)).astype(jnp.float32)
    angle_table = position[:, None] * frequency[None, :]
    cosine = jnp.cos(angle_table)[:, None, :] * mscale
    sine_part = jnp.sin(angle_table)[:, None, :] * mscale
    halves_view = source.astype(jnp.float32).reshape(row_count, row_width // HEAD_DIM, 2, half_dim)
    lower_half = halves_view[:, :, 0]
    upper_half = halves_view[:, :, 1]
    turned = jnp.stack(
        [
            lower_half * cosine - upper_half * sine_part,
            upper_half * cosine + lower_half * sine_part,
        ],
        axis=2,
    )
    return turned.reshape(row_count, row_width).astype(jnp.bfloat16)


def block_attend(query_blocks, key_blocks, value_blocks, valid_slots):
    count_q, slot_count = (key_blocks.shape[0], key_blocks.shape[1])
    heads_here = query_blocks.shape[-1] // HEAD_DIM
    query_grid = query_blocks.reshape(count_q, BLOCK, heads_here, HEAD_DIM)
    key_grid = key_blocks.reshape(count_q, slot_count * BLOCK, heads_here, HEAD_DIM)
    value_grid = value_blocks.reshape(count_q, slot_count * BLOCK, heads_here, HEAD_DIM)
    scores = jnp.einsum(
        "bqhd,bshd->bhqs", query_grid, key_grid, preferred_element_type=jnp.float32
    ) * (1.0 / math.sqrt(HEAD_DIM))
    present = jnp.repeat(jnp.transpose(valid_slots, (0, 2, 1)), BLOCK, axis=2)[:, :, None, :]
    scores = jnp.where(present, scores, masked_score)
    peak = jnp.max(scores, axis=3, keepdims=True)
    expo = jnp.exp(scores - peak)
    total = jnp.sum(expo, axis=3)
    weights = expo.astype(jnp.bfloat16)
    mixture = jnp.einsum("bhqs,bshd->bqhd", weights, value_grid, preferred_element_type=jnp.float32)
    mixture = mixture / jnp.transpose(total, (0, 2, 1))[..., None]
    return mixture.reshape(count_q, BLOCK, heads_here * HEAD_DIM).astype(jnp.bfloat16)


def on_device(
    queries,
    keys,
    values,
    out_weight,
    global_blocks,
    random_blocks,
    window_blocks,
    yarn_scale,
    yarn_context,
):
    tok_here, width_here = queries.shape
    heads_here = width_here // HEAD_DIM
    blocks_here = tok_here // BLOCK
    seq_count = lax.axis_size("seq")
    seq_place = lax.axis_index("seq")
    block_total = seq_count * blocks_here
    frequency, mscale = yarn_tables(yarn_scale, yarn_context)
    first_row = seq_place * tok_here
    query_rot = rotate(queries, first_row, frequency, mscale)
    key_rot = rotate(keys, first_row, frequency, mscale)
    pair_kv = jnp.stack([key_rot, values])
    padded = padded_2(pair_kv, (("seq", 1),), WMAX * BLOCK)
    padded_blocks = padded.reshape(2, blocks_here + 2 * WMAX, BLOCK, width_here)
    offsets = jnp.arange(-WMAX, WMAX + 1)
    window_ids = seq_place * blocks_here + jnp.arange(blocks_here)[:, None] + offsets[None, :]
    inside = (window_ids >= 0) & (window_ids < block_total)
    reach = jnp.abs(offsets)[None, :, None] <= window_blocks[None, None, :]
    window_valid = inside[:, :, None] & reach
    owner_global = global_blocks // blocks_here
    local_global = jnp.clip(global_blocks - seq_place * blocks_here, 0, blocks_here - 1)
    mine_global = owner_global == seq_place
    query_view = query_rot.reshape(blocks_here, BLOCK, width_here)
    key_view = key_rot.reshape(blocks_here, BLOCK, width_here)
    value_view = values.reshape(blocks_here, BLOCK, width_here)
    picked = jnp.stack([query_view[local_global], key_view[local_global], value_view[local_global]])
    masked = jnp.where(mine_global[None, :, None, None], picked.astype(jnp.float32), 0.0)
    shared = lax.psum(masked.astype(jnp.bfloat16), "seq")
    slot_total = blocks_here * RAND
    capacity = (slot_total + seq_count - 1) // seq_count
    flat_ids = random_blocks.reshape(seq_count, slot_total)
    owners = flat_ids // blocks_here
    slot_order = jnp.arange(slot_total)
    same_owner = (owners[:, :, None] == owners[:, None, :]) & (
        slot_order[None, None, :] < slot_order[None, :, None]
    )
    ranks = jnp.sum(same_owner.astype(jnp.int32), axis=2)
    local_ids = flat_ids - owners * blocks_here
    wanted = (owners[:, None, :] == seq_place) & (
        ranks[:, None, :] == jnp.arange(capacity)[None, :, None]
    )
    send_local = jnp.sum(jnp.where(wanted, local_ids[:, None, :], 0), axis=2)
    kv_blocks = pair_kv.reshape(2, blocks_here, BLOCK, width_here)
    outgoing = kv_blocks[:, send_local]
    incoming = lax.all_to_all(outgoing, "seq", split_axis=1, concat_axis=1, tiled=True)
    my_owners = owners[seq_place]
    my_ranks = ranks[seq_place]
    random_kv = incoming[:, my_owners, my_ranks].reshape(2, blocks_here, RAND, BLOCK, width_here)
    slot_parts = [
        padded_blocks[:, offset_slot : offset_slot + blocks_here][:, :, None]
        for offset_slot in range(2 * WMAX + 1)
    ]
    slot_parts.append(
        jnp.broadcast_to(shared[1:3][:, None], (2, blocks_here, GLOB, BLOCK, width_here))
    )
    slot_parts.append(random_kv)
    all_kv = jnp.concatenate(slot_parts, axis=2)
    all_valid = jnp.concatenate(
        [window_valid, jnp.ones((blocks_here, GLOB + RAND, heads_here), dtype=bool)], axis=1
    )
    attended = block_attend(query_view, all_kv[0], all_kv[1], all_valid)
    global_query = shared[0].reshape(GLOB, BLOCK, heads_here, HEAD_DIM)
    key_grid = key_rot.reshape(tok_here, heads_here, HEAD_DIM)
    value_grid = values.reshape(tok_here, heads_here, HEAD_DIM)
    global_scores = jnp.einsum(
        "gqhd,khd->ghqk", global_query, key_grid, preferred_element_type=jnp.float32
    ) * (1.0 / math.sqrt(HEAD_DIM))
    local_peak = jnp.max(global_scores, axis=3)
    peak = lax.pmax(local_peak, "seq")
    expo = jnp.exp(global_scores - peak[..., None])
    partial_total = jnp.sum(expo, axis=3)
    partial_mix = jnp.einsum(
        "ghqk,khd->gqhd", expo.astype(jnp.bfloat16), value_grid, preferred_element_type=jnp.float32
    )
    mix_sum, total_sum = (
        lax.psum(partial_mix.astype(jnp.bfloat16), "seq").astype(jnp.float32),
        lax.psum(partial_total.astype(jnp.bfloat16), "seq").astype(jnp.float32),
    )
    global_out = (
        (mix_sum / jnp.transpose(total_sum, (0, 2, 1))[..., None])
        .reshape(GLOB, BLOCK, width_here)
        .astype(jnp.bfloat16)
    )
    block_index = jnp.arange(blocks_here)
    for global_slot in range(GLOB):
        hit = mine_global[global_slot] & (block_index == local_global[global_slot])
        attended = jnp.where(hit[:, None, None], global_out[global_slot][None], attended)
    attention_out = attended.reshape(tok_here, width_here)
    share = lax.psum_scatter(
        lax.dot_general(
            out_weight, attention_out, (((0,), (1,)), ((), ())), preferred_element_type=jnp.float32
        ).astype(jnp.bfloat16),
        "head",
        scatter_dimension=0,
        tiled=True,
    ).astype(jnp.float32)
    return share.T.astype(jnp.bfloat16)


def solution(mesh):
    in_specs = (
        P("seq", "head"),
        P("seq", "head"),
        P("seq", "head"),
        P("head", None),
        P(),
        P(),
        P("head"),
        P(),
        P(),
    )
    out_specs = P("seq", "head")
    return jax.shard_map(
        on_device, mesh=mesh, in_specs=in_specs, out_specs=out_specs, check_vma=False
    )
```

profile of v0, /device:TPU:2, one launch (start us, length us, event | category | flops | bytes accessed | tf_op | source)
XLA Modules:
  0.0 287.3 jit_solution(7155592734332625758)
XLA Ops:
  8.0 1.2 copy.100
  9.3 1.2 copy.101
  10.6 1.1 convert.4
  11.7 0.2 copy.109
  11.9 0.3 fusion.42
  12.2 1.5 multiply_subtract_fusion
  13.8 1.2 fusion.33
  15.0 1.9 collective-permute-start
  16.9 3.6 %collective-permute-start.1 = (bf16[2,128,1024]{1,2,0:T(8,128)(2,1)}, bf16[2,128,1024]{1,2,0:T(8,128)(2,1)}, u32[]{:S(2)}, u32[]{:S(2)}) collective-permute-start(bf16[2,128,1024]{1,2,0:T(8,128)(2,1)} %get-tuple-element.14), channel_id=1, source_target_pairs={{4,0},{8,4},{12,8},{16,12},{20,16},{24,20},{28,24},{5,1},{9,5},{13... | collective-permute-start | bytes 1572872 | tf_op jit(solution)/shard_map/ppermute | solution.py:28
  20.5 0.4 reshape.472
  21.2 1.3 copy.130
  22.6 0.3 convert_reduce_fusion
  23.0 0.2 select_reduce_fusion
  23.4 0.4 reshape.471
  23.8 1.4 copy.129
  25.2 1.6 gather_fusion.1
  26.8 1.6 gather_fusion
  28.4 0.6 gather_fusion.2
  29.0 1.1 select_convert_fusion
  30.1 0.4 reshape.473
  30.6 1.3 copy.133
  31.9 1.1 pad_maximum_fusion.1
  33.0 2.8 gather_fusion.3
  35.8 4.6 %all-to-all-start = ((bf16[2,8,2,64,1024]{4,3,0,2,1:T(8,128)(2,1)}), bf16[2,8,2,64,1024]{4,3,0,2,1:T(8,128)(2,1)}, u32[]{:S(2)}, u32[]{:S(2)}) async-start(bf16[2,8,2,64,1024]{4,3,0,2,1:T(8,128)(2,1)} %bitcast.165), calls=%async_computation | async-start | bytes 8388608 | tf_op jit(solution)/shard_map/all_to_all | solution.py:142
  40.5 0.7 fusion.63
  41.2 0.7 fusion.62
  42.0 1.4 reshape.474
  43.4 0.1 broadcast_in_dim.164
  43.5 0.1 broadcast_in_dim.165
  43.7 0.9 copy.137
  44.6 1.3 compare_and_fusion.1
  46.1 1.2 compare_and_fusion
  47.4 0.2 dynamic-slice_reduce_fusion
  47.6 63.1 %all-reduce.4.cloned.1.call-done = bf16[3,2,64,1024]{3,2,1,0:T(8,128)(2,1)} async-done(((bf16[3,2,64,1024]{3,2,1,0:T(8,128)(2,1)}), bf16[3,2,64,1024]{3,2,1,0:T(8,128)(2,1)}) %all-reduce.4.cloned.1.call-update) | async-done | bytes 786448 | tf_op jit(solution)/shard_map/psum | solution.py:125
  110.7 1.0 slice.100
  111.8 0.3 fusion.64
  112.1 0.2 bitcast_reduce_fusion
  112.3 10.3 %pmax.7 = f32[2,8,64]{2,0,1:T(2,128)S(1)} all-reduce(f32[2,8,64]{2,0,1:T(2,128)S(1)} %bitcast_reduce_fusion), channel_id=1, replica_groups=mesh['seq'=8,'head'=4] {'seq'}, use_global_device_ids=true, to_apply=%region_2.3 | all-reduce | flops 1024 | bytes 8192 | tf_op jit(solution)/shard_map/pmax | solution.py:166
  122.6 0.5 fusion.30
  123.1 12.5 %psum.23 = bf16[2,64,8]{1,0,2:T(2,128)(2,1)S(1)} all-reduce(bf16[2,64,8]{1,0,2:T(2,128)(2,1)S(1)} %bitcast.194), channel_id=1, replica_groups=mesh['seq'=8,'head'=4] {'seq'}, use_global_device_ids=true, to_apply=%region_5.6 | all-reduce | flops 1024 | bytes 4096 | tf_op jit(solution)/shard_map/psum | solution.py:174
  135.6 2.1 fusion.18
  137.8 0.2 reduce-scatter.2.cloned.1.call-start
  138.0 2.8 pad_maximum_fusion
  140.8 3.0 %copy.110 = bf16[2,512,1024]{2,1,0:T(8,128)(2,1)S(1)} copy(bf16[2,512,1024]{1,2,0:T(8,128)(2,1)} %pad_maximum_fusion) | data formatting | bytes 4194304 | tf_op jit(solution)/shard_map/concatenate | solution.py:24
  143.8 48.1 %all-reduce.6.cloned.1.call-done = bf16[2,64,8,128]{3,1,0,2:T(8,128)(2,1)} async-done(((bf16[2,64,8,128]{3,1,0,2:T(8,128)(2,1)}), bf16[2,64,8,128]{3,1,0,2:T(8,128)(2,1)}) %all-reduce.6.cloned.1.call-update) | async-done | bytes 262160 | tf_op jit(solution)/shard_map/psum | solution.py:173
  191.9 1.2 divide_convert_fusion.1
  193.3 1.2 fusion.23
  194.5 1.1 fusion.22
  195.5 1.2 fusion.21
  196.7 1.1 fusion.20
  197.8 1.1 fusion.19
  199.0 1.6 broadcast_dynamic-update-slice_fusion
  200.6 4.6 %gather_fusion.4 = bf16[12,2,64,1024]{3,2,1,0:T(8,128)(2,1)} fusion(bf16[2,8,2,64,1024]{4,3,0,2,1:T(8,128)(2,1)} %all-to-all-done, s32[12]{0:T(128)S(1)} %fusion.55), kind=kCustom, calls=%fused_computation.4 | custom fusion | bytes 6291552 | tf_op jit(solution)/shard_map/gather | solution.py:145
  205.2 2.4 copy.116
  207.6 2.2 constant_dynamic-update-slice_fusion
  209.8 10.2 %fusion.60 = (bf16[1,4,10,64,1024]{4,3,2,1,0:T(8,128)(2,1)}, bf16[1,4,10,64,1024]{4,3,2,1,0:T(8,128)(2,1)}) fusion(bf16[2,4,10,64,1024]{4,3,2,1,0:T(8,128)(2,1)} %constant_dynamic-update-slice_fusion), kind=kLoop, calls=%fused_computation.121 | loop fusion | bytes 20971520 | tf_op jit(solution)/shard_map/slice | solution.py:158
  220.0 4.0 %copy.140 = bf16[320,8,8,128]{3,2,1,0:T(8,128)(2,1)S(1)} copy(bf16[320,8,8,128]{3,1,2,0:T(8,128)(2,1)} %bitcast.160) | data formatting | bytes 10485760
  224.0 1.4 copy.141
  225.4 2.5 fusion.5
  227.9 1.6 fusion.6
  229.6 2.8 divide_convert_fusion
  232.4 0.3 copy.126
  232.9 3.8 %fusion.4 = bf16[4096,256]{0,1:T(8,128)(2,1)} fusion(bf16[1024,4096]{1,0:T(8,128)(2,1)S(1)} %bitcast.196, bf16[256,1024]{1,0:T(8,128)(2,1)S(1)} %bitcast.185, bf16[256,1024]{1,0:T(8,128)(2,1)S(1)} %bitcast.186, bf16[32,8,8,128]{3,2,1,0:T(8,128)(2,1)S(1)} %bitcast.190, pred[256]{0:T(512)(128)(4,1)S(1)} %broadcast_in_dim.151, ...), kind=kOutput, calls=%fused_computation.12 | convolution fusion | flops 2149056512 | bytes 12059136 | tf_op jit(solution)/shard_map/dot_general | solution.py:187
  236.7 44.0 %reduce-scatter.2.cloned.1.call-done = bf16[1024,256]{0,1:T(8,128)(2,1)} async-done(((bf16[4096,256]{0,1:T(8,128)(2,1)}), bf16[1024,256]{0,1:T(8,128)(2,1)}) %reduce-scatter.2.cloned.1.call-update) | async-done | bytes 524304 | tf_op jit(solution)/shard_map/reduce_scatter | solution.py:186
  (66 shorter events, 1.9 us)
Async XLA Ops:
  6.5 5.1 %copy-start.1 = (bf16[256,1024]{1,0:T(8,128)(2,1)S(1)}, bf16[256,1024]{1,0:T(8,128)(2,1)}, u32[]{:S(2)}) copy-start(bf16[256,1024]{1,0:T(8,128)(2,1)} %param.11) | copy-start | bytes 1572868
  6.5 104.2 %all-reduce.4.cloned.1.call-start = ((), (), s32[]{:S(2)}) async-start(), calls=%async_computation.2 | async-start | bytes 1572864 | tf_op jit(solution)/shard_map/psum | solution.py:125
  11.7 9.3 %copy-start.3 = (s32[32,3]{0,1:T(4,128)S(1)}, s32[32,3]{0,1:T(4,128)}, u32[]{:S(2)}) copy-start(s32[32,3]{0,1:T(4,128)} %param.14) | copy-start | bytes 1156
  12.2 11.2 %copy-start.4 = (s32[2]{0:T(128)S(1)}, s32[2]{0:T(128)}, u32[]{:S(2)}) copy-start(s32[2]{0:T(128)} %param.13) | copy-start | bytes 28
  15.0 123.0 %collective-permute-start = (bf16[2,128,1024]{1,2,0:T(8,128)(2,1)}, bf16[2,128,1024]{1,2,0:T(8,128)(2,1)}, u32[]{:S(2)}, u32[]{:S(2)}) collective-permute-start(bf16[2,128,1024]{1,2,0:T(8,128)(2,1)} %get-tuple-element.13), channel_id=1, source_target_pairs={{0,4},{4,8},{8,12},{12,16},{16,20},{20,24},{24,28},{1,5},{5,9},{9,... | collective-permute-start | bytes 1572872 | tf_op jit(solution)/shard_map/ppermute | solution.py:26
  16.9 121.1 %collective-permute-start.1 = (bf16[2,128,1024]{1,2,0:T(8,128)(2,1)}, bf16[2,128,1024]{1,2,0:T(8,128)(2,1)}, u32[]{:S(2)}, u32[]{:S(2)}) collective-permute-start(bf16[2,128,1024]{1,2,0:T(8,128)(2,1)} %get-tuple-element.14), channel_id=1, source_target_pairs={{4,0},{8,4},{12,8},{16,12},{20,16},{24,20},{28,24},{5,1},{9,5},{13... | collective-permute-start | bytes 1572872 | tf_op jit(solution)/shard_map/ppermute | solution.py:28
  35.8 6.1 %copy-start.5 = (s32[8]{0:T(128)S(1)}, s32[8]{0:T(128)}, u32[]{:S(2)}) copy-start(s32[8]{0:T(128)} %param.15) | copy-start | bytes 100
  35.8 164.8 %all-to-all-start = ((bf16[2,8,2,64,1024]{4,3,0,2,1:T(8,128)(2,1)}), bf16[2,8,2,64,1024]{4,3,0,2,1:T(8,128)(2,1)}, u32[]{:S(2)}, u32[]{:S(2)}) async-start(bf16[2,8,2,64,1024]{4,3,0,2,1:T(8,128)(2,1)} %bitcast.165), calls=%async_computation | async-start | bytes 8388608 | tf_op jit(solution)/shard_map/all_to_all | solution.py:142
  40.4 151.4 %all-reduce.6.cloned.1.call-start = ((), (), s32[]{:S(2)}) async-start(), calls=%async_computation.3 | async-start | bytes 524288 | tf_op jit(solution)/shard_map/psum | solution.py:173
  137.8 143.0 %reduce-scatter.2.cloned.1.call-start = ((), (), s32[]{:S(2)}) async-start(), calls=%async_computation.4 | async-start | bytes 2621440 | tf_op jit(solution)/shard_map/reduce_scatter | solution.py:186
  193.3 5.7 %slice-start = ((bf16[3,2,64,1024]{3,2,1,0:T(8,128)(2,1)}), bf16[2,2,64,1024]{3,2,1,0:T(8,128)(2,1)S(1)}, s32[]{:S(2)}) async-start(bf16[3,2,64,1024]{3,2,1,0:T(8,128)(2,1)} %all-reduce.4.cloned.1.call-done), calls=%async_computation.5 | async-start | bytes 1048576 | tf_op jit(solution)/shard_map/slice | solution.py:151
  220.0 4.1 %copy-start = (bf16[1,4,10,64,1024]{4,3,2,1,0:T(8,128)(2,1)S(1)}, bf16[1,4,10,64,1024]{4,3,2,1,0:T(8,128)(2,1)}, u32[]{:S(2)}) copy-start(bf16[1,4,10,64,1024]{4,3,2,1,0:T(8,128)(2,1)} %get-tuple-element.8) | copy-start | bytes 15728644
  224.0 1.4 copy-start.2
  227.9 4.9 %slice-start.1 = ((s8[8388608]{0:T(1024)(128)(4,1)}), s8[4194304]{0:T(1024)(128)(4,1)S(1)}, s32[]{:S(2)}) async-start(s8[8388608]{0:T(1024)(128)(4,1)} %bitcast.195), calls=%async_computation.6 | async-start | bytes 8388608
  229.6 3.3 %slice-start.2 = ((s8[8388608]{0:T(1024)(128)(4,1)}), s8[4194304]{0:T(1024)(128)(4,1)S(1)}, s32[]{:S(2)}) async-start(s8[8388608]{0:T(1024)(128)(4,1)} %bitcast.195), calls=%async_computation.7 | async-start | bytes 8388608
Sparse Core Ops, SparseCore 0:
  30.3 80.4 all-reduce.3
  137.9 53.9 all-reduce.5
  236.9 43.8 reduce-scatter.1
where the time goes:
time: 290 us; the launch traced here: 287 us
  waiting for transfers between devices  155 us (53%)
  local copies, waits for them, and re-layouts  56.2 us (19%)
  blocking collectives  22.8 us (8%)
  other arithmetic  16.1 us (6%)
  between operations  15 us (5%)
  matrix products  11.5 us (4%)
  starting transfers between devices  10.4 us (4%)
    psum x1, waiting for transfers between devices, on_device(): shared = lax.psum(masked.astype(jnp.bfloat16), 'seq')  63.1 us
    psum x1, waiting for transfers between devices, on_device(): lax.psum(partial_mix.astype(jnp.bfloat16), 'seq').astype(jnp.float32)  48.1 us
    reduce_scatter x1, waiting for transfers between devices, on_device(): lax.psum_scatter(lax.dot_general(out_weight, attention_out, (((0,), (1,))...  44 us
    unnamed x32, local copies, waits for them, and re-layouts  16.5 us
    psum x1, blocking collectives, on_device(): lax.psum(partial_total.astype(jnp.bfloat16), 'seq').astype(jnp.float32)  12.5 us
    pmax x1, blocking collectives, on_device(): peak = lax.pmax(local_peak, 'seq')  10.3 us
    slice x1, local copies, waits for them, and re-layouts, on_device(): attended = block_attend(query_view, all_kv[0], all_kv[1], all_valid)  10.2 us
    gather x2, local copies, waits for them, and re-layouts, on_device(): incoming[:, my_owners, my_ranks]  6.98 us
  transfers between devices with their start and end apart: 6, of which 3 were waited for; matrix products, arithmetic and copies ran while one was open for 14% of the time, Pallas kernels for 0%

commit v1 on v0

--- a/solution.py
+++ b/solution.py
@@ -83,6 +83,63 @@
     mixture = jnp.einsum("bhqs,bshd->bqhd", weights, value_grid, preferred_element_type=jnp.float32)
     mixture = mixture / jnp.transpose(total, (0, 2, 1))[..., None]
     return mixture.reshape(count_q, BLOCK, heads_here * HEAD_DIM).astype(jnp.bfloat16)
+
+
+def xor_perm(count, bit):
+    return [(i, i ^ bit) for i in range(count)]
+
+
+def tree_reduce(parts, merge, axis):
+    count = lax.axis_size(axis)
+    place = lax.axis_index(axis)
+    bits = []
+    bit = 1
+    while bit < count:
+        bits.append(bit)
+        bit *= 2
+    for bit in bits:
+        upper = (place // bit) % 2
+        halves = jax.tree.map(lambda x: x.reshape((2, x.shape[0] // 2) + x.shape[1:]), parts)
+        keep = jax.tree.map(lambda h: lax.dynamic_index_in_dim(h, upper, 0, keepdims=False), halves)
+        send = jax.tree.map(lambda h: lax.dynamic_index_in_dim(h, 1 - upper, 0, keepdims=False), halves)
+        got = lax.ppermute(send, axis, xor_perm(count, bit))
+        parts = merge(keep, got)
+    for bit in reversed(bits):
+        upper = (place // bit) % 2
+        got = lax.ppermute(parts, axis, xor_perm(count, bit))
+
+        def join(mine, theirs):
+            pair = jnp.stack([mine, theirs])
+            first = lax.dynamic_index_in_dim(pair, upper, 0, keepdims=False)
+            second = lax.dynamic_index_in_dim(pair, 1 - upper, 0, keepdims=False)
+            return jnp.concatenate([first, second], axis=0)
+
+        parts = jax.tree.map(join, parts, got)
+    return parts
+
+
+def add_merge(a, b):
+    return jax.tree.map(jnp.add, a, b)
+
+
+def softmax_merge(a, b):
+    mix_a, total_a, peak_a = a
+    mix_b, total_b, peak_b = b
+    peak = jnp.maximum(peak_a, peak_b)
+    scale_a = jnp.exp(peak_a - peak)
+    scale_b = jnp.exp(peak_b - peak)
+    mix = mix_a * scale_a[..., None] + mix_b * scale_b[..., None]
+    total = total_a * scale_a + total_b * scale_b
+    return (mix, total, peak)
+
+
+def project_over_head(rows, out_weight):
+    head_count = lax.axis_size("head")
+    row_count, width_here = rows.shape
+    weight_view = out_weight.reshape(width_here, head_count, out_weight.shape[1] // head_count)
+    partial = jnp.einsum("td,dhc->htc", rows, weight_view, preferred_element_type=jnp.float32)
+    gathered = lax.all_to_all(partial.astype(jnp.bfloat16), "head", 0, 0, tiled=True)
+    return jnp.sum(gathered.astype(jnp.float32), axis=0)
 
 
 def on_device(
@@ -121,8 +178,9 @@
     key_view = key_rot.reshape(blocks_here, BLOCK, width_here)
     value_view = values.reshape(blocks_here, BLOCK, width_here)
     picked = jnp.stack([query_view[local_global], key_view[local_global], value_view[local_global]])
-    masked = jnp.where(mine_global[None, :, None, None], picked.astype(jnp.float32), 0.0)
-    shared = lax.psum(masked.astype(jnp.bfloat16), "seq")
+    masked = jnp.where(mine_global[None, :, None, None], picked, jnp.zeros_like(picked))
+    shared = tree_reduce(masked.reshape(3 * GLOB * BLOCK, width_here), add_merge, "seq")
+    shared = shared.reshape(3, GLOB, BLOCK, width_here)
     slot_total = blocks_here * RAND
     capacity = (slot_total + seq_count - 1) // seq_count
     flat_ids = random_blocks.reshape(seq_count, slot_total)
@@ -156,42 +214,37 @@
         [window_valid, jnp.ones((blocks_here, GLOB + RAND, heads_here), dtype=bool)], axis=1
     )
     attended = block_attend(query_view, all_kv[0], all_kv[1], all_valid)
+    mixed = project_over_head(attended.reshape(tok_here, width_here), out_weight)
     global_query = shared[0].reshape(GLOB, BLOCK, heads_here, HEAD_DIM)
     key_grid = key_rot.reshape(tok_here, heads_here, HEAD_DIM)
     value_grid = values.reshape(tok_here, heads_here, HEAD_DIM)
     global_scores = jnp.einsum(
-        "gqhd,khd->ghqk", global_query, key_grid, preferred_element_type=jnp.float32
+        "gqhd,khd->gqhk", global_query, key_grid, preferred_element_type=jnp.float32
     ) * (1.0 / math.sqrt(HEAD_DIM))
     local_peak = jnp.max(global_scores, axis=3)
-    peak = lax.pmax(local_peak, "seq")
-    expo = jnp.exp(global_scores - peak[..., None])
+    expo = jnp.exp(global_scores - local_peak[..., None])
     partial_total = jnp.sum(expo, axis=3)
     partial_mix = jnp.einsum(
-        "ghqk,khd->gqhd", expo.astype(jnp.bfloat16), value_grid, preferred_element_type=jnp.float32
-    )
-    mix_sum, total_sum = (
-        lax.psum(partial_mix.astype(jnp.bfloat16), "seq").astype(jnp.float32),
-        lax.psum(partial_total.astype(jnp.bfloat16), "seq").astype(jnp.float32),
-    )
-    global_out = (
-        (mix_sum / jnp.transpose(total_sum, (0, 2, 1))[..., None])
-        .reshape(GLOB, BLOCK, width_here)
-        .astype(jnp.bfloat16)
-    )
+        "gqhk,khd->gqhd", expo.astype(jnp.bfloat16), value_grid, preferred_element_type=jnp.float32
+    )
+    row_total = GLOB * BLOCK
+    mix_sum, total_sum, _ = tree_reduce(
+        (
+            partial_mix.reshape(row_total, heads_here, HEAD_DIM),
+            partial_total.reshape(row_total, heads_here),
+            local_peak.reshape(row_total, heads_here),
+        ),
+        softmax_merge,
+        "seq",
+    )
+    global_out = (mix_sum / total_sum[..., None]).reshape(row_total, width_here).astype(jnp.bfloat16)
+    global_mixed = project_over_head(global_out, out_weight).reshape(GLOB, BLOCK, -1)
+    mixed = mixed.reshape(blocks_here, BLOCK, -1)
     block_index = jnp.arange(blocks_here)
     for global_slot in range(GLOB):
         hit = mine_global[global_slot] & (block_index == local_global[global_slot])
-        attended = jnp.where(hit[:, None, None], global_out[global_slot][None], attended)
-    attention_out = attended.reshape(tok_here, width_here)
-    share = lax.psum_scatter(
-        lax.dot_general(
-            out_weight, attention_out, (((0,), (1,)), ((), ())), preferred_element_type=jnp.float32
-        ).astype(jnp.bfloat16),
-        "head",
-        scatter_dimension=0,
-        tiled=True,
-    ).astype(jnp.float32)
-    return share.T.astype(jnp.bfloat16)
+        mixed = jnp.where(hit[:, None, None], global_mixed[global_slot][None], mixed)
+    return mixed.reshape(tok_here, -1).astype(jnp.bfloat16)
 
 
 def solution(mesh):

time: 290 us -> 246 us (0.85)
  waiting for transfers between devices: 155 us -> 113 us
  starting transfers between devices: 10.4 us -> 36 us
  blocking collectives: 22.8 us -> 0 us
  between operations: 15 us -> 2.2 us
  other arithmetic: 16.1 us -> 24.5 us
  matrix products: 11.5 us -> 18.4 us
  local copies, waits for them, and re-layouts: 56.2 us -> 49.5 us
    psum x2 -> x0, waiting for transfers between devices: 111 us -> none  [the longest x1 63.1 us: on_device(): shared = lax.psum(masked.astype(jnp.bfloat16), 'seq')]
    ppermute x0 -> x21, waiting for transfers between devices: none -> 70.1 us  [the longest x12 53 us: tree_reduce(): got = lax.ppermute(send, axis, xor_perm(count, bit))]
    reduce_scatter x1 -> x0, waiting for transfers between devices: 44 us -> none  [on_device(): lax.psum_scatter(lax.dot_general(out_weight, attention_out, (((0,), (1,))...]
    all_to_all x0 -> x2, waiting for transfers between devices: none -> 42.5 us  [project_over_head(): lax.all_to_all(partial.astype(jnp.bfloat16), 'head', 0, 0, tiled=True)]
    ppermute x0 -> x21, starting transfers between devices: none -> 15.7 us  [the longest x12 9.16 us: tree_reduce(): got = lax.ppermute(send, axis, xor_perm(count, bit))]
    psum x1 -> x0, blocking collectives: 12.5 us -> none  [on_device(): lax.psum(partial_total.astype(jnp.bfloat16), 'seq').astype(jnp.float32)]
    pmax x1 -> x0, blocking collectives: 10.3 us -> none  [on_device(): peak = lax.pmax(local_peak, 'seq')]
    all_to_all x0 -> x2, starting transfers between devices: none -> 9.97 us  [project_over_head(): lax.all_to_all(partial.astype(jnp.bfloat16), 'head', 0, 0, tiled=True)]
  transfers between devices with their start and end apart: 6 -> 26, of which waited for: 3 -> 18; matrix products, arithmetic and copies ran while one was open for 14% -> 32% of each run, Pallas kernels for 0% -> 0%
where the time goes in v1:
time: 246 us; the launch traced here: 243 us
  waiting for transfers between devices  113 us (46%)
  local copies, waits for them, and re-layouts  49.5 us (20%)
  starting transfers between devices  36 us (15%)
  other arithmetic  24.5 us (10%)
  matrix products  18.4 us (7%)
    ppermute x12, waiting for transfers between devices, tree_reduce(): got = lax.ppermute(send, axis, xor_perm(count, bit))  53 us
    all_to_all x2, waiting for transfers between devices, project_over_head(): lax.all_to_all(partial.astype(jnp.bfloat16), 'head', 0, 0, tiled=True)  42.5 us
    ppermute x9, waiting for transfers between devices, tree_reduce(): got = lax.ppermute(parts, axis, xor_perm(count, bit))  17 us
    unnamed x44, local copies, waits for them, and re-layouts  12.8 us
    dot_general x2, matrix products, project_over_head(): jnp.einsum('td,dhc->htc', rows, weight_view, preferred_element_type=jnp.f...  12.7 us
    slice x1, local copies, waits for them, and re-layouts, on_device(): attended = block_attend(query_view, all_kv[0], all_kv[1], all_valid)  10.2 us
    all_to_all x2, starting transfers between devices, project_over_head(): lax.all_to_all(partial.astype(jnp.bfloat16), 'head', 0, 0, tiled=True)  9.97 us
    ppermute x12, starting transfers between devices, tree_reduce(): got = lax.ppermute(send, axis, xor_perm(count, bit))  9.16 us
  transfers between devices with their start and end apart: 26, of which 18 were waited for; matrix products, arithmetic and copies ran while one was open for 32% of the time, Pallas kernels for 0%

profile of v1, /device:TPU:2, one launch (start us, length us, event | category | flops | bytes accessed | tf_op | source)
XLA Modules:
  0.0 243.2 jit_solution(16437196699560398077)
XLA Ops:
  1.4 1.2 copy.173
  2.7 1.2 copy.174
  4.4 1.0 multiply_subtract_fusion
  7.1 1.0 maximum_convert_fusion
  8.5 1.3 copy.214
  10.4 1.6 gather_fusion
  13.1 0.8 copy-done.3
  14.1 1.1 fusion.48
  15.3 2.4 collective-permute-start.21
  17.7 3.1 %collective-permute-start.22 = (bf16[2,128,1024]{1,2,0:T(8,128)(2,1)}, bf16[2,128,1024]{1,2,0:T(8,128)(2,1)}, u32[]{:S(2)}, u32[]{:S(2)}) collective-permute-start(bf16[2,128,1024]{1,2,0:T(8,128)(2,1)} %get-tuple-element.25), channel_id=1, source_target_pairs={{4,0},{8,4},{12,8},{16,12},{20,16},{24,20},{28,24},{5,1},{9,5},{13... | collective-permute-start | bytes 1572872 | tf_op jit(solution)/shard_map/ppermute | solution.py:28
  21.8 0.8 copy.196
  24.0 1.3 broadcast_compare_fusion.1
  25.9 1.3 copy.218
  27.2 1.1 convert_reduce_fusion.2
  28.4 0.8 select_reduce_fusion
  29.4 1.1 pad_maximum_fusion.1
  30.5 2.8 %gather_fusion.3 = bf16[16,2,64,1024]{3,2,1,0:T(8,128)(2,1)} fusion(bf16[2,4,64,1024]{3,2,1,0:T(8,128)(2,1)S(1)} %pad_maximum_fusion.1, s32[1024]{0:T(1024)S(1)} %pad_clamp_fusion), kind=kCustom, calls=%fused_computation.3 | custom fusion | bytes 8388672 | tf_op jit(solution)/shard_map/gather | solution.py:199
  33.3 4.8 %all-to-all-start.1 = ((bf16[2,8,2,64,1024]{4,3,0,2,1:T(8,128)(2,1)}), bf16[2,8,2,64,1024]{4,3,0,2,1:T(8,128)(2,1)}, u32[]{:S(2)}, u32[]{:S(2)}) async-start(bf16[2,8,2,64,1024]{4,3,0,2,1:T(8,128)(2,1)} %bitcast.302), calls=%async_computation.1 | async-start | bytes 8388608 | tf_op jit(solution)/shard_map/all_to_all | solution.py:200
  38.6 1.0 bitcast_add_fusion
  40.4 1.4 reshape.571
  41.9 0.9 copy.229
  42.9 0.7 broadcast_in_dim.173
  43.6 2.8 %pad_maximum_fusion = bf16[2,512,1024]{1,2,0:T(8,128)(2,1)} fusion(bf16[2,128,1024]{1,2,0:T(8,128)(2,1)} %collective-permute-done.22, bf16[1,256,1024]{1,2,0:T(8,128)(2,1)S(1)} %bitcast.310, bf16[1,256,1024]{1,2,0:T(8,128)(2,1)S(1)} %bitcast.297, bf16[2,128,1024]{1,2,0:T(8,128)(2,1)} %collective-permute-done.21), kind=kLoop, calls=%fused_computation.25 | loop fusion | flops 8388608 | bytes 4194304 | tf_op jit(solution)/shard_map/concatenate | solution.py:24
  46.4 3.0 %copy.194 = bf16[2,512,1024]{2,1,0:T(8,128)(2,1)S(1)} copy(bf16[2,512,1024]{1,2,0:T(8,128)(2,1)} %pad_maximum_fusion) | data formatting | bytes 4194304 | tf_op jit(solution)/shard_map/concatenate | solution.py:24
  49.4 39.3 %collective-permute-done.1 = bf16[96,1024]{1,0:T(8,128)(2,1)} collective-permute-done((bf16[96,1024]{1,0:T(8,128)(2,1)}, bf16[96,1024]{1,0:T(8,128)(2,1)}, u32[]{:S(2)}, u32[]{:S(2)}) %collective-permute-start.1) | collective-permute-done | bytes 196640 | tf_op jit(solution)/shard_map/ppermute | solution.py:105
  88.7 0.9 bitcast_add_fusion.1
  89.7 1.8 collective-permute-start.2
  91.6 3.0 %collective-permute-done.2 = bf16[48,1024]{1,0:T(8,128)(2,1)S(1)} collective-permute-done((bf16[48,1024]{1,0:T(8,128)(2,1)S(1)}, bf16[48,1024]{1,0:T(8,128)(2,1)S(1)}, u32[]{:S(2)}, u32[]{:S(2)}) %collective-permute-start.2) | collective-permute-done | bytes 98336 | tf_op jit(solution)/shard_map/ppermute | solution.py:105
  94.6 1.6 collective-permute-start.3
  96.3 3.0 %collective-permute-done.3 = bf16[48,1024]{1,0:T(8,128)(2,1)S(1)} collective-permute-done((bf16[48,1024]{1,0:T(8,128)(2,1)S(1)}, bf16[48,1024]{1,0:T(8,128)(2,1)S(1)}, u32[]{:S(2)}, u32[]{:S(2)}) %collective-permute-start.3) | collective-permute-done | bytes 98336 | tf_op jit(solution)/shard_map/ppermute | solution.py:109
  99.4 1.5 collective-permute-start.4
  101.0 4.1 %collective-permute-done.4 = bf16[96,1024]{1,0:T(8,128)(2,1)S(1)} collective-permute-done((bf16[96,1024]{1,0:T(8,128)(2,1)S(1)}, bf16[96,1024]{1,0:T(8,128)(2,1)S(1)}, u32[]{:S(2)}, u32[]{:S(2)}) %collective-permute-start.4) | collective-permute-done | bytes 196640 | tf_op jit(solution)/shard_map/ppermute | solution.py:109
  105.6 1.5 collective-permute-done.5
  110.1 1.5 collective-permute-start.8
  112.5 1.3 collective-permute-done.8
  113.8 1.6 collective-permute-done.16
  115.5 1.7 collective-permute-start.10
  117.8 1.4 collective-permute-done.10
  119.2 1.8 collective-permute-done.17
  122.4 1.7 broadcast_dynamic-update-slice_fusion
  124.8 2.1 collective-permute-done.9
  127.0 1.8 collective-permute-start.11
  129.3 2.1 collective-permute-done.11
  131.4 1.8 collective-permute-start.12
  133.3 2.5 %collective-permute-done.12 = f32[16,8,128]{2,1,0:T(8,128)S(1)} collective-permute-done((f32[16,8,128]{2,1,0:T(8,128)S(1)}, f32[16,8,128]{2,1,0:T(8,128)S(1)}, u32[]{:S(2)}, u32[]{:S(2)}) %collective-permute-start.12) | collective-permute-done | bytes 65568 | tf_op jit(solution)/shard_map/ppermute | solution.py:109
  136.6 4.3 %collective-permute-done.13 = f32[32,8,128]{2,1,0:T(8,128)S(1)} collective-permute-done((f32[32,8,128]{2,1,0:T(8,128)S(1)}, f32[32,8,128]{2,1,0:T(8,128)S(1)}, u32[]{:S(2)}, u32[]{:S(2)}) %collective-permute-start.13) | collective-permute-done | bytes 131104 | tf_op jit(solution)/shard_map/ppermute | solution.py:109
  141.3 1.2 collective-permute-done.14
  143.0 5.6 %fusion.23 = bf16[4,128,1024]{2,1,0:T(8,128)(2,1)} fusion(bf16[128,1024,1]{1,0,2:T(8,128)(2,1)S(1)} %reshape.565, bf16[128,4,8,1024]{3,2,1,0:T(8,128)(2,1)} %bitcast.355), kind=kOutput, calls=%fused_computation.29 | convolution fusion | flops 1074266112 | bytes 9699328 | tf_op jit(solution)/shard_map/td,dhc->htc/dot_general | solution.py:140
  148.7 4.9 %all-to-all-start = ((bf16[4,128,1024]{2,1,0:T(8,128)(2,1)}), bf16[4,128,1024]{2,1,0:T(8,128)(2,1)}, u32[]{:S(2)}, u32[]{:S(2)}) async-start(bf16[4,128,1024]{2,1,0:T(8,128)(2,1)} %fusion.23), calls=%async_computation | async-start | bytes 2097152 | tf_op jit(solution)/shard_map/all_to_all | solution.py:141
  153.5 2.9 %gather_fusion.4 = bf16[12,2,64,1024]{3,2,1,0:T(8,128)(2,1)S(1)} fusion(bf16[2,8,2,64,1024]{4,3,0,2,1:T(8,128)(2,1)} %all-to-all-done.1, s32[12]{0:T(128)S(1)} %fusion.108), kind=kCustom, calls=%fused_computation.4 | custom fusion | bytes 6291552 | tf_op jit(solution)/shard_map/gather | solution.py:203
  156.9 2.1 constant_dynamic-update-slice_fusion
  159.0 10.2 %fusion.119 = (bf16[1,4,10,64,1024]{4,3,2,1,0:T(8,128)(2,1)}, bf16[1,4,10,64,1024]{4,3,2,1,0:T(8,128)(2,1)}) fusion(bf16[2,4,10,64,1024]{4,3,2,1,0:T(8,128)(2,1)} %constant_dynamic-update-slice_fusion), kind=kLoop, calls=%fused_computation.253 | loop fusion | bytes 20971520 | tf_op jit(solution)/shard_map/slice | solution.py:216
  169.2 3.9 %copy.230 = bf16[320,8,8,128]{3,2,1,0:T(8,128)(2,1)S(1)} copy(bf16[320,8,8,128]{3,1,2,0:T(8,128)(2,1)} %bitcast.294) | data formatting | bytes 10485760
  173.2 2.5 %fusion.10 = (f32[4,8,64]{2,1,0:T(8,128)S(1)}, f32[4,8,64,640]{3,2,1,0:T(8,128)S(1)}) fusion(pred[4,8,640]{2,1,0:T(8,128)(4,1)S(1)} %copy-done.6, bf16[4,640,8,128]{3,2,1,0:T(8,128)(2,1)S(1)} %bitcast.295, bf16[4,64,8,128]{1,0,3,2:T(4,128)(2,1)S(1)} %copy-done.2), kind=kOutput, calls=%fused_computation.17 | convolution fusion | flops 339474432 | bytes 11038720 | tf_op jit(solution)/shard_map/bqhd,bshd->bhqs/dot_general | solution.py:74
  175.7 1.6 fusion.11
  177.2 1.4 copy.231
  178.6 2.5 %divide_convert_fusion = bf16[4,64,8,128]{3,1,2,0:T(8,128)(2,1)S(1)} fusion(bf16[4,640,8,128]{3,2,1,0:T(8,128)(2,1)S(1)} %bitcast.308, f32[4,8,64,640]{3,2,1,0:T(8,128)S(1)} %get-tuple-element.79, f32[4,8,64]{2,1,0:T(8,128)S(1)} %get-tuple-element.78, pred[4,8,640]{2,1,0:T(8,128)(4,1)S(1)} %copy-done.6, f32[4,64,8]{1,2,0:T(8,128)S(1)} %bitcast.338), kind=kOutput, calls=%fused_computation.53 | convolution fusion | flops 341311488 | bytes 11046912 | tf_op jit(solution)/shard_map/bhqs,bshd->bqhd/dot_general | solution.py:83
  181.8 7.1 %convert_bitcast_fusion = bf16[4,256,1024]{2,1,0:T(8,128)(2,1)} fusion(bf16[256,1024,1]{1,0,2:T(8,128)(2,1)S(1)} %reshape.566, bf16[128,4,8,1024]{3,2,1,0:T(8,128)(2,1)} %bitcast.356), kind=kOutput, calls=%fused_computation.26 | convolution fusion | flops 2148532224 | bytes 11010048 | tf_op jit(solution)/shard_map/td,dhc->htc/dot_general | solution.py:140
  188.8 5.1 %all-to-all-start.2 = ((bf16[4,256,1024]{2,1,0:T(8,128)(2,1)}), bf16[4,256,1024]{2,1,0:T(8,128)(2,1)S(1)}, u32[]{:S(2)}, u32[]{:S(2)}) async-start(bf16[4,256,1024]{2,1,0:T(8,128)(2,1)} %convert_bitcast_fusion), calls=%async_computation.2 | async-start | bytes 4194304 | tf_op jit(solution)/shard_map/all_to_all | solution.py:141
  195.1 1.2 compare_and_fusion.1
  196.5 1.3 compare_and_fusion
  198.0 1.4 convert_reduce_fusion.1
  199.4 42.5 %all-to-all-done.2 = bf16[4,256,1024]{2,1,0:T(8,128)(2,1)S(1)} async-done(((bf16[4,256,1024]{2,1,0:T(8,128)(2,1)}), bf16[4,256,1024]{2,1,0:T(8,128)(2,1)S(1)}, u32[]{:S(2)}, u32[]{:S(2)}) %all-to-all-start.2) | async-done | bytes 2097184 | tf_op jit(solution)/shard_map/all_to_all | solution.py:141
  242.2 0.9 fusion.38
  (164 shorter events, 21.3 us)
Async XLA Ops:
  2.7 3.8 %copy-start.10 = (s32[2]{0:T(128)S(1)}, s32[2]{0:T(128)}, u32[]{:S(2)}) copy-start(s32[2]{0:T(128)} %param.13) | copy-start | bytes 28
  5.5 6.6 %copy-start.1 = (bf16[256,1024]{1,0:T(8,128)(2,1)S(1)}, bf16[256,1024]{1,0:T(8,128)(2,1)}, u32[]{:S(2)}) copy-start(bf16[256,1024]{1,0:T(8,128)(2,1)} %param.11) | copy-start | bytes 1572868
  6.6 6.3 %copy-start.7 = (pred[2]{0:T(512)(128)(4,1)}, pred[2]{0:T(512)(128)(4,1)S(1)}, u32[]{:S(2)}) copy-start(pred[2]{0:T(512)(128)(4,1)S(1)} %fusion.107) | copy-start | bytes 10
  13.0 0.9 copy-start.3
  13.9 24.7 %collective-permute-start = (bf16[192,1024]{1,0:T(8,128)(2,1)S(1)}, bf16[192,1024]{1,0:T(8,128)(2,1)}, u32[]{:S(2)}, u32[]{:S(2)}) collective-permute-start(bf16[192,1024]{1,0:T(8,128)(2,1)S(1)} %dynamic-slice_bitcast_fusion), channel_id=1, source_target_pairs={{0,4},{4,0},{8,12},{12,8},{16,20},{20,16},{24,28},{28,24},{1,5},{5... | collective-permute-start | bytes 1179656 | tf_op jit(solution)/shard_map/ppermute | solution.py:105
  15.3 28.4 %collective-permute-start.21 = (bf16[2,128,1024]{1,2,0:T(8,128)(2,1)}, bf16[2,128,1024]{1,2,0:T(8,128)(2,1)}, u32[]{:S(2)}, u32[]{:S(2)}) collective-permute-start(bf16[2,128,1024]{1,2,0:T(8,128)(2,1)} %get-tuple-element.24), channel_id=1, source_target_pairs={{0,4},{4,8},{8,12},{12,16},{16,20},{20,24},{24,28},{1,5},{5,9},{9,... | collective-permute-start | bytes 1572872 | tf_op jit(solution)/shard_map/ppermute | solution.py:26
  17.7 26.0 %collective-permute-start.22 = (bf16[2,128,1024]{1,2,0:T(8,128)(2,1)}, bf16[2,128,1024]{1,2,0:T(8,128)(2,1)}, u32[]{:S(2)}, u32[]{:S(2)}) collective-permute-start(bf16[2,128,1024]{1,2,0:T(8,128)(2,1)} %get-tuple-element.25), channel_id=1, source_target_pairs={{4,0},{8,4},{12,8},{16,12},{20,16},{24,20},{28,24},{5,1},{9,5},{13... | collective-permute-start | bytes 1572872 | tf_op jit(solution)/shard_map/ppermute | solution.py:28
  33.3 5.1 %copy-start.11 = (s32[8]{0:T(128)S(1)}, s32[8]{0:T(128)}, u32[]{:S(2)}) copy-start(s32[8]{0:T(128)} %param.15) | copy-start | bytes 100
  33.3 5.3 %copy-start.4 = (bf16[2,192,1024]{2,1,0:T(8,128)(2,1)S(1)}, bf16[2,192,1024]{2,1,0:T(8,128)(2,1)}, u32[]{:S(2)}) copy-start(bf16[2,192,1024]{2,1,0:T(8,128)(2,1)} %copy-done.3) | copy-start | bytes 2359300
  33.3 115.3 %all-to-all-start.1 = ((bf16[2,8,2,64,1024]{4,3,0,2,1:T(8,128)(2,1)}), bf16[2,8,2,64,1024]{4,3,0,2,1:T(8,128)(2,1)}, u32[]{:S(2)}, u32[]{:S(2)}) async-start(bf16[2,8,2,64,1024]{4,3,0,2,1:T(8,128)(2,1)} %bitcast.302), calls=%async_computation.1 | async-start | bytes 8388608 | tf_op jit(solution)/shard_map/all_to_all | solution.py:200
  40.4 48.3 %collective-permute-start.1 = (bf16[96,1024]{1,0:T(8,128)(2,1)}, bf16[96,1024]{1,0:T(8,128)(2,1)}, u32[]{:S(2)}, u32[]{:S(2)}) collective-permute-start(bf16[96,1024]{1,0:T(8,128)(2,1)} %dynamic-slice_bitcast_fusion.2), channel_id=1, source_target_pairs={{0,8},{4,12},{8,0},{12,4},{16,24},{20,28},{24,16},{28,20},{1,9},{5... | collective-permute-start | bytes 589832 | tf_op jit(solution)/shard_map/ppermute | solution.py:105
  89.7 4.9 %collective-permute-start.2 = (bf16[48,1024]{1,0:T(8,128)(2,1)S(1)}, bf16[48,1024]{1,0:T(8,128)(2,1)S(1)}, u32[]{:S(2)}, u32[]{:S(2)}) collective-permute-start(bf16[48,1024]{1,0:T(8,128)(2,1)S(1)} %dynamic-slice_bitcast_fusion.3), channel_id=1, source_target_pairs={{0,16},{4,20},{8,24},{12,28},{16,0},{20,4},{24,8},{28,12},{1,17},{... | collective-permute-start | bytes 294920 | tf_op jit(solution)/shard_map/ppermute | solution.py:105
  94.6 4.7 %collective-permute-start.3 = (bf16[48,1024]{1,0:T(8,128)(2,1)S(1)}, bf16[48,1024]{1,0:T(8,128)(2,1)S(1)}, u32[]{:S(2)}, u32[]{:S(2)}) collective-permute-start(bf16[48,1024]{1,0:T(8,128)(2,1)S(1)} %bitcast_add_fusion.2), channel_id=1, source_target_pairs={{0,16},{4,20},{8,24},{12,28},{16,0},{20,4},{24,8},{28,12},{1,17},{... | collective-permute-start | bytes 294920 | tf_op jit(solution)/shard_map/ppermute | solution.py:109
  99.4 5.7 %collective-permute-start.4 = (bf16[96,1024]{1,0:T(8,128)(2,1)S(1)}, bf16[96,1024]{1,0:T(8,128)(2,1)S(1)}, u32[]{:S(2)}, u32[]{:S(2)}) collective-permute-start(bf16[96,1024]{1,0:T(8,128)(2,1)S(1)} %get-tuple-element.42), channel_id=1, source_target_pairs={{0,8},{4,12},{8,0},{12,4},{16,24},{20,28},{24,16},{28,20},{1,9},{5... | collective-permute-start | bytes 589832 | tf_op jit(solution)/shard_map/ppermute | solution.py:109
  105.4 3.8 %copy-start.5 = (bf16[32,8,8,128]{3,2,1,0:T(8,128)(2,1)S(1)}, bf16[32,8,8,128]{3,2,1,0:T(8,128)(2,1)}, u32[]{:S(2)}) copy-start(bf16[32,8,8,128]{3,2,1,0:T(8,128)(2,1)} %copy.229) | copy-start | bytes 1572868
  105.4 1.8 collective-permute-start.5
  105.6 4.0 %copy-start = (bf16[2,4,10,64,1024]{4,3,2,1,0:T(8,128)(2,1)}, bf16[2,4,10,64,1024]{4,3,2,1,0:T(8,128)(2,1)S(1)}, u32[]{:S(2)}) copy-start(bf16[2,4,10,64,1024]{4,3,2,1,0:T(8,128)(2,1)S(1)} %fusion.31) | copy-start | bytes 31457284
  108.6 1.2 collective-permute-start.15
  108.8 1.2 collective-permute-start.6
  110.1 3.7 %collective-permute-start.8 = (f32[32,8]{0,1:T(8,128)S(1)}, f32[32,8]{0,1:T(8,128)S(1)}, u32[]{:S(2)}, u32[]{:S(2)}) collective-permute-start(f32[32,8]{0,1:T(8,128)S(1)} %bitcast.349), channel_id=1, source_target_pairs={{0,8},{4,12},{8,0},{12,4},{16,24},{20,28},{24,16},{28,20},{1,9},{5... | collective-permute-start | bytes 3080 | tf_op jit(solution)/shard_map/ppermute | solution.py:105
  111.8 3.7 %collective-permute-start.16 = (f32[32,8]{0,1:T(8,128)S(1)}, f32[32,8]{0,1:T(8,128)S(1)}, u32[]{:S(2)}, u32[]{:S(2)}) collective-permute-start(f32[32,8]{0,1:T(8,128)S(1)} %bitcast.353), channel_id=1, source_target_pairs={{0,8},{4,12},{8,0},{12,4},{16,24},{20,28},{24,16},{28,20},{1,9},{5... | collective-permute-start | bytes 3080 | tf_op jit(solution)/shard_map/ppermute | solution.py:105
  112.4 9.1 %collective-permute-start.7 = (f32[64,8,128]{2,0,1:T(8,128)S(1)}, f32[64,8,128]{2,0,1:T(8,128)S(1)}, u32[]{:S(2)}, u32[]{:S(2)}) collective-permute-start(f32[64,8,128]{2,0,1:T(8,128)S(1)} %dynamic-slice_bitcast_fusion.1), channel_id=1, source_target_pairs={{0,4},{4,0},{8,12},{12,8},{16,20},{20,16},{24,28},{28,24},{1,5},{5... | collective-permute-start | bytes 786440 | tf_op jit(solution)/shard_map/ppermute | solution.py:105
  115.5 3.7 %collective-permute-start.10 = (f32[16,8]{0,1:T(8,128)S(1)}, f32[16,8]{0,1:T(8,128)S(1)}, u32[]{:S(2)}, u32[]{:S(2)}) collective-permute-start(f32[16,8]{0,1:T(8,128)S(1)} %bitcast.350), channel_id=1, source_target_pairs={{0,16},{4,20},{8,24},{12,28},{16,0},{20,4},{24,8},{28,12},{1,17},{... | collective-permute-start | bytes 1544 | tf_op jit(solution)/shard_map/ppermute | solution.py:105
  117.4 3.7 %collective-permute-start.17 = (f32[16,8]{0,1:T(8,128)S(1)}, f32[16,8]{0,1:T(8,128)S(1)}, u32[]{:S(2)}, u32[]{:S(2)}) collective-permute-start(f32[16,8]{0,1:T(8,128)S(1)} %bitcast.354), channel_id=1, source_target_pairs={{0,16},{4,20},{8,24},{12,28},{16,0},{20,4},{24,8},{28,12},{1,17},{... | collective-permute-start | bytes 1544 | tf_op jit(solution)/shard_map/ppermute | solution.py:105
  121.1 3.7 %collective-permute-start.18 = (f32[16,8]{0,1:T(8,128)S(1)}, f32[16,8]{0,1:T(8,128)S(1)}, u32[]{:S(2)}, u32[]{:S(2)}) collective-permute-start(f32[16,8]{0,1:T(8,128)S(1)} %get-tuple-element.5), channel_id=1, source_target_pairs={{0,16},{4,20},{8,24},{12,28},{16,0},{20,4},{24,8},{28,12},{1,17},{... | collective-permute-start | bytes 1544 | tf_op jit(solution)/shard_map/ppermute | solution.py:109
  121.8 5.0 %collective-permute-start.9 = (f32[32,8,128]{2,1,0:T(8,128)S(1)}, f32[32,8,128]{2,1,0:T(8,128)S(1)}, u32[]{:S(2)}, u32[]{:S(2)}) collective-permute-start(f32[32,8,128]{2,1,0:T(8,128)S(1)} %bitcast.334), channel_id=1, source_target_pairs={{0,8},{4,12},{8,0},{12,4},{16,24},{20,28},{24,16},{28,20},{1,9},{5... | collective-permute-start | bytes 393224 | tf_op jit(solution)/shard_map/ppermute | solution.py:105
  127.0 4.3 %collective-permute-start.11 = (f32[16,8,128]{2,1,0:T(8,128)S(1)}, f32[16,8,128]{2,1,0:T(8,128)S(1)}, u32[]{:S(2)}, u32[]{:S(2)}) collective-permute-start(f32[16,8,128]{2,1,0:T(8,128)S(1)} %dynamic-slice_bitcast_fusion.4), channel_id=1, source_target_pairs={{0,16},{4,20},{8,24},{12,28},{16,0},{20,4},{24,8},{28,12},{1,17},{... | collective-permute-start | bytes 196616 | tf_op jit(solution)/shard_map/ppermute | solution.py:105
  128.9 7.6 %collective-permute-start.19 = (f32[32,8]{0,1:T(8,128)S(1)}, f32[32,8]{0,1:T(8,128)S(1)}, u32[]{:S(2)}, u32[]{:S(2)}) collective-permute-start(f32[32,8]{0,1:T(8,128)S(1)} %pad_maximum_fusion.9), channel_id=1, source_target_pairs={{0,8},{4,12},{8,0},{12,4},{16,24},{20,28},{24,16},{28,20},{1,9},{5... | collective-permute-start | bytes 3080 | tf_op jit(solution)/shard_map/ppermute | solution.py:109
  131.4 4.3 %collective-permute-start.12 = (f32[16,8,128]{2,1,0:T(8,128)S(1)}, f32[16,8,128]{2,1,0:T(8,128)S(1)}, u32[]{:S(2)}, u32[]{:S(2)}) collective-permute-start(f32[16,8,128]{2,1,0:T(8,128)S(1)} %fusion.80), channel_id=1, source_target_pairs={{0,16},{4,20},{8,24},{12,28},{16,0},{20,4},{24,8},{28,12},{1,17},{... | collective-permute-start | bytes 196616 | tf_op jit(solution)/shard_map/ppermute | solution.py:109
  135.8 5.0 %collective-permute-start.13 = (f32[32,8,128]{2,1,0:T(8,128)S(1)}, f32[32,8,128]{2,1,0:T(8,128)S(1)}, u32[]{:S(2)}, u32[]{:S(2)}) collective-permute-start(f32[32,8,128]{2,1,0:T(8,128)S(1)} %get-tuple-element.46), channel_id=1, source_target_pairs={{0,8},{4,12},{8,0},{12,4},{16,24},{20,28},{24,16},{28,20},{1,9},{5... | collective-permute-start | bytes 393224 | tf_op jit(solution)/shard_map/ppermute | solution.py:109
  136.5 4.6 %collective-permute-start.20 = (f32[64,8]{0,1:T(8,128)S(1)}, f32[64,8]{0,1:T(8,128)S(1)}, u32[]{:S(2)}, u32[]{:S(2)}) collective-permute-start(f32[64,8]{0,1:T(8,128)S(1)} %pad_maximum_fusion.10), channel_id=1, source_target_pairs={{0,4},{4,0},{8,12},{12,8},{16,20},{20,16},{24,28},{28,24},{1,5},{5... | collective-permute-start | bytes 6152 | tf_op jit(solution)/shard_map/ppermute | solution.py:109
  141.0 1.6 collective-permute-start.14
  148.7 40.2 %all-to-all-start = ((bf16[4,128,1024]{2,1,0:T(8,128)(2,1)}), bf16[4,128,1024]{2,1,0:T(8,128)(2,1)}, u32[]{:S(2)}, u32[]{:S(2)}) async-start(bf16[4,128,1024]{2,1,0:T(8,128)(2,1)} %fusion.23), calls=%async_computation | async-start | bytes 2097152 | tf_op jit(solution)/shard_map/all_to_all | solution.py:141
  169.2 4.0 %copy-start.2 = (bf16[4,64,8,128]{1,0,3,2:T(4,128)(2,1)S(1)}, bf16[4,64,8,128]{1,0,3,2:T(4,128)(2,1)}, u32[]{:S(2)}) copy-start(bf16[4,64,8,128]{1,0,3,2:T(4,128)(2,1)} %reshape.571) | copy-start | bytes 1572868
  169.2 4.0 %copy-start.6 = (pred[4,8,640]{2,1,0:T(8,128)(4,1)S(1)}, pred[4,8,640]{2,1,0:T(8,128)(4,1)}, u32[]{:S(2)}) copy-start(pred[4,8,640]{2,1,0:T(8,128)(4,1)} %broadcast_in_dim.173) | copy-start | bytes 61444
  173.2 4.1 %slice-start = ((s8[5242880]{0:T(1024)(128)(4,1)}), s8[4194304]{0:T(1024)(128)(4,1)S(1)}, s32[]{:S(2)}) async-start(s8[5242880]{0:T(1024)(128)(4,1)} %bitcast.291), calls=%async_computation.3 | async-start | bytes 8388608
  173.2 4.0 %slice-start.1 = ((s8[5242880]{0:T(1024)(128)(4,1)}), s8[1048576]{0:T(1024)(128)(4,1)S(1)}, s32[]{:S(2)}) async-start(s8[5242880]{0:T(1024)(128)(4,1)} %bitcast.291), calls=%async_computation.4 | async-start | bytes 2097152
  181.7 12.2 %copy-start.9 = (s32[2]{0:T(128)S(1)}, s32[2]{0:T(128)}, u32[]{:S(2)}) copy-start(s32[2]{0:T(128)} %get-tuple-element.17) | copy-start | bytes 28
  181.7 12.8 %copy-start.8 = (pred[2]{0:T(512)(128)(4,1)S(1)}, pred[2]{0:T(512)(128)(4,1)}, u32[]{:S(2)}) copy-start(pred[2]{0:T(512)(128)(4,1)} %copy-done.7) | copy-start | bytes 10
  188.8 53.0 %all-to-all-start.2 = ((bf16[4,256,1024]{2,1,0:T(8,128)(2,1)}), bf16[4,256,1024]{2,1,0:T(8,128)(2,1)S(1)}, u32[]{:S(2)}, u32[]{:S(2)}) async-start(bf16[4,256,1024]{2,1,0:T(8,128)(2,1)} %convert_bitcast_fusion), calls=%async_computation.2 | async-start | bytes 4194304 | tf_op jit(solution)/shard_map/all_to_all | solution.py:141

commit v2 on v1

--- a/solution.py
+++ b/solution.py
@@ -123,23 +123,60 @@
 
 
 def softmax_merge(a, b):
-    mix_a, total_a, peak_a = a
-    mix_b, total_b, peak_b = b
-    peak = jnp.maximum(peak_a, peak_b)
-    scale_a = jnp.exp(peak_a - peak)
-    scale_b = jnp.exp(peak_b - peak)
-    mix = mix_a * scale_a[..., None] + mix_b * scale_b[..., None]
-    total = total_a * scale_a + total_b * scale_b
-    return (mix, total, peak)
+    peak = jnp.maximum(a[..., -1], b[..., -1])
+    scale_a = jnp.exp(a[..., -1] - peak)
+    scale_b = jnp.exp(b[..., -1] - peak)
+    merged = a[..., :-1] * scale_a[..., None] + b[..., :-1] * scale_b[..., None]
+    return jnp.concatenate([merged, peak[..., None]], axis=-1)
 
 
 def project_over_head(rows, out_weight):
     head_count = lax.axis_size("head")
-    row_count, width_here = rows.shape
-    weight_view = out_weight.reshape(width_here, head_count, out_weight.shape[1] // head_count)
-    partial = jnp.einsum("td,dhc->htc", rows, weight_view, preferred_element_type=jnp.float32)
-    gathered = lax.all_to_all(partial.astype(jnp.bfloat16), "head", 0, 0, tiled=True)
-    return jnp.sum(gathered.astype(jnp.float32), axis=0)
+    row_count = rows.shape[0]
+    partial = lax.dot_general(
+        out_weight, rows, (((0,), (1,)), ((), ())), preferred_element_type=jnp.float32
+    ).astype(jnp.bfloat16)
+    partial = partial.reshape(head_count, out_weight.shape[1] // head_count, row_count)
+    gathered = lax.all_to_all(partial, "head", 0, 0, tiled=True)
+    return jnp.sum(gathered.astype(jnp.float32), axis=0).T
+
+
+def sparse_attend(query_view, window_kv, global_kv, random_kv, window_valid):
+    blocks_here, _, width_here = query_view.shape
+    heads_here = width_here // HEAD_DIM
+    q = query_view.reshape(blocks_here, BLOCK, heads_here, HEAD_DIM)
+    win = window_kv.reshape(2, blocks_here + 2 * WMAX, BLOCK, heads_here, HEAD_DIM)
+    glo = global_kv.reshape(2, GLOB, BLOCK, heads_here, HEAD_DIM)
+    ran = random_kv.reshape(blocks_here, RAND, 2, BLOCK, heads_here, HEAD_DIM)
+    scale = 1.0 / math.sqrt(HEAD_DIM)
+    parts = []
+    for offset_slot in range(2 * WMAX + 1):
+        keys_o = win[0, offset_slot : offset_slot + blocks_here]
+        s = jnp.einsum("bqhd,bkhd->bhqk", q, keys_o, preferred_element_type=jnp.float32) * scale
+        valid = window_valid[:, offset_slot, :]
+        parts.append(jnp.where(valid[:, :, None, None], s, masked_score))
+    s = jnp.einsum("bqhd,gkhd->bhqgk", q, glo[0], preferred_element_type=jnp.float32) * scale
+    parts.append(s.reshape(blocks_here, heads_here, BLOCK, GLOB * BLOCK))
+    s = jnp.einsum("bqhd,brkhd->bhqrk", q, ran[:, :, 0], preferred_element_type=jnp.float32) * scale
+    parts.append(s.reshape(blocks_here, heads_here, BLOCK, RAND * BLOCK))
+    scores = jnp.concatenate(parts, axis=3)
+    peak = jnp.max(scores, axis=3, keepdims=True)
+    expo = jnp.exp(scores - peak)
+    total = jnp.sum(expo, axis=3)
+    weights = expo.astype(jnp.bfloat16)
+    window_count = (2 * WMAX + 1) * BLOCK
+    mixture = None
+    for offset_slot in range(2 * WMAX + 1):
+        w = weights[..., offset_slot * BLOCK : (offset_slot + 1) * BLOCK]
+        vals_o = win[1, offset_slot : offset_slot + blocks_here]
+        m = jnp.einsum("bhqk,bkhd->bqhd", w, vals_o, preferred_element_type=jnp.float32)
+        mixture = m if mixture is None else mixture + m
+    w = weights[..., window_count : window_count + GLOB * BLOCK].reshape(blocks_here, heads_here, BLOCK, GLOB, BLOCK)
+    mixture = mixture + jnp.einsum("bhqgk,gkhd->bqhd", w, glo[1], preferred_element_type=jnp.float32)
+    w = weights[..., window_count + GLOB * BLOCK :].reshape(blocks_here, heads_here, BLOCK, RAND, BLOCK)
+    mixture = mixture + jnp.einsum("bhqrk,brkhd->bqhd", w, ran[:, :, 1], preferred_element_type=jnp.float32)
+    mixture = mixture / jnp.transpose(total, (0, 2, 1))[..., None]
+    return mixture.reshape(blocks_here, BLOCK, width_here).astype(jnp.bfloat16)
 
 
 def on_device(
@@ -195,25 +232,15 @@
         ranks[:, None, :] == jnp.arange(capacity)[None, :, None]
     )
     send_local = jnp.sum(jnp.where(wanted, local_ids[:, None, :], 0), axis=2)
-    kv_blocks = pair_kv.reshape(2, blocks_here, BLOCK, width_here)
-    outgoing = kv_blocks[:, send_local]
-    incoming = lax.all_to_all(outgoing, "seq", split_axis=1, concat_axis=1, tiled=True)
+    kv_blocks = jnp.stack(
+        [key_rot.reshape(blocks_here, BLOCK, width_here), value_view], axis=1
+    )
+    outgoing = kv_blocks[send_local]
+    incoming = lax.all_to_all(outgoing, "seq", split_axis=0, concat_axis=0, tiled=True)
     my_owners = owners[seq_place]
     my_ranks = ranks[seq_place]
-    random_kv = incoming[:, my_owners, my_ranks].reshape(2, blocks_here, RAND, BLOCK, width_here)
-    slot_parts = [
-        padded_blocks[:, offset_slot : offset_slot + blocks_here][:, :, None]
-        for offset_slot in range(2 * WMAX + 1)
-    ]
-    slot_parts.append(
-        jnp.broadcast_to(shared[1:3][:, None], (2, blocks_here, GLOB, BLOCK, width_here))
-    )
-    slot_parts.append(random_kv)
-    all_kv = jnp.concatenate(slot_parts, axis=2)
-    all_valid = jnp.concatenate(
-        [window_valid, jnp.ones((blocks_here, GLOB + RAND, heads_here), dtype=bool)], axis=1
-    )
-    attended = block_attend(query_view, all_kv[0], all_kv[1], all_valid)
+    random_kv = incoming[my_owners, my_ranks].reshape(blocks_here, RAND, 2, BLOCK, width_here)
+    attended = sparse_attend(query_view, padded_blocks, shared[1:3], random_kv, window_valid)
     mixed = project_over_head(attended.reshape(tok_here, width_here), out_weight)
     global_query = shared[0].reshape(GLOB, BLOCK, heads_here, HEAD_DIM)
     key_grid = key_rot.reshape(tok_here, heads_here, HEAD_DIM)
@@ -228,16 +255,20 @@
         "gqhk,khd->gqhd", expo.astype(jnp.bfloat16), value_grid, preferred_element_type=jnp.float32
     )
     row_total = GLOB * BLOCK
-    mix_sum, total_sum, _ = tree_reduce(
-        (
+    packed = jnp.concatenate(
+        [
             partial_mix.reshape(row_total, heads_here, HEAD_DIM),
-            partial_total.reshape(row_total, heads_here),
-            local_peak.reshape(row_total, heads_here),
-        ),
-        softmax_merge,
-        "seq",
-    )
-    global_out = (mix_sum / total_sum[..., None]).reshape(row_total, width_here).astype(jnp.bfloat16)
+            partial_total.reshape(row_total, heads_here, 1),
+            local_peak.reshape(row_total, heads_here, 1),
+        ],
+        axis=2,
+    )
+    reduced = tree_reduce(packed, softmax_merge, "seq")
+    global_out = (
+        (reduced[..., :HEAD_DIM] / reduced[..., HEAD_DIM : HEAD_DIM + 1])
+        .reshape(row_total, width_here)
+        .astype(jnp.bfloat16)
+    )
     global_mixed = project_over_head(global_out, out_weight).reshape(GLOB, BLOCK, -1)
     mixed = mixed.reshape(blocks_here, BLOCK, -1)
     block_index = jnp.arange(blocks_here)

time: 246 us -> 314 us (1.28)
  local copies, waits for them, and re-layouts: 49.5 us -> 108 us
  matrix products: 18.4 us -> 36 us
  waiting for transfers between devices: 113 us -> 99.7 us
  other arithmetic: 24.5 us -> 34.3 us
  starting transfers between devices: 36 us -> 29.4 us
    unnamed x44 -> x90, local copies, waits for them, and re-layouts: 12.8 us -> 31.8 us
    dot_general x4 -> x15, matrix products: 17.7 us -> 33.9 us  [the longest x5 13.1 us: sparse_attend(): jnp.einsum('bqhd,bkhd->bhqk', q, keys_o, preferred_element_type=jnp.float32)]
    slice x1 -> x11, local copies, waits for them, and re-layouts: 10.2 us -> 23.2 us  [the longest x1 15.2 us: sparse_attend(): vals_o = win[1, offset_slot:offset_slot + blocks_here]]
    reshape x4 -> x5, local copies, waits for them, and re-layouts: 0.31 us -> 8.7 us  [the longest x2 2.67 us: project_over_head(): partial.reshape(head_count, out_weight.shape[1] // head_count, row_count)]
    ppermute x12 -> x6, waiting for transfers between devices: 53 us -> 46.2 us  [tree_reduce(): got = lax.ppermute(send, axis, xor_perm(count, bit))]
    ppermute x9 -> x6, waiting for transfers between devices: 17 us -> 10.5 us  [tree_reduce(): got = lax.ppermute(parts, axis, xor_perm(count, bit))]
    another operation x0 -> x1, local copies, waits for them, and re-layouts: none -> 6.23 us  [sparse_attend(): window_kv.reshape(2, blocks_here + 2 * WMAX, BLOCK, heads_here, HEAD_DIM)]
    concatenate x3 -> x7, local copies, waits for them, and re-layouts: 5.2 us -> 10.6 us  [the longest x1 8.9 us: sparse_attend(): scores = jnp.concatenate(parts, axis=3)]
  transfers between devices with their start and end apart: 26 -> 17, of which waited for: 18 -> 7; matrix products, arithmetic and copies ran while one was open for 32% -> 53% of each run, Pallas kernels for 0% -> 0%
where the time goes in v2:
time: 314 us; the launch traced here: 310 us
  local copies, waits for them, and re-layouts  108 us (34%)
  waiting for transfers between devices  99.7 us (32%)
  matrix products  36 us (11%)
  other arithmetic  34.3 us (11%)
  starting transfers between devices  29.4 us (9%)
    ppermute x6, waiting for transfers between devices, tree_reduce(): got = lax.ppermute(send, axis, xor_perm(count, bit))  46.2 us
    all_to_all x2, waiting for transfers between devices, project_over_head(): gathered = lax.all_to_all(partial, 'head', 0, 0, tiled=True)  42.9 us
    unnamed x90, local copies, waits for them, and re-layouts  31.8 us
    slice x1, local copies, waits for them, and re-layouts, sparse_attend(): vals_o = win[1, offset_slot:offset_slot + blocks_here]  15.2 us
    dot_general x5, matrix products, sparse_attend(): jnp.einsum('bqhd,bkhd->bhqk', q, keys_o, preferred_element_type=jnp.float32)  13.1 us
    ppermute x6, waiting for transfers between devices, tree_reduce(): got = lax.ppermute(parts, axis, xor_perm(count, bit))  10.5 us
    dot_general x2, matrix products, project_over_head(): lax.dot_general(out_weight, rows, (((0,), (1,)), ((), ())), preferred_ele...  10.4 us
    all_to_all x2, starting transfers between devices, project_over_head(): gathered = lax.all_to_all(partial, 'head', 0, 0, tiled=True)  9.84 us
  transfers between devices with their start and end apart: 17, of which 7 were waited for; matrix products, arithmetic and copies ran while one was open for 53% of the time, Pallas kernels for 0%

profile of v2, /device:TPU:2, one launch (start us, length us, event | category | flops | bytes accessed | tf_op | source)
XLA Modules:
  0.0 309.7 jit_solution(363394588606167429)
XLA Ops:
  3.4 1.2 copy.666
  7.5 1.3 gather_fusion
  14.0 2.4 collective-permute-start.12
  16.4 3.1 %collective-permute-start.13 = (bf16[2,128,1024]{1,2,0:T(8,128)(2,1)}, bf16[2,128,1024]{1,2,0:T(8,128)(2,1)}, u32[]{:S(2)}, u32[]{:S(2)}) collective-permute-start(bf16[2,128,1024]{1,2,0:T(8,128)(2,1)} %get-tuple-element.38), channel_id=1, source_target_pairs={{4,0},{8,4},{12,8},{16,12},{20,16},{24,20},{28,24},{5,1},{9,5},{13... | collective-permute-start | bytes 1572872 | tf_op jit(solution)/shard_map/ppermute | solution.py:28
  27.0 1.3 copy.763
  29.5 2.9 gather_fusion.3
  32.4 4.8 %all-to-all-start.1 = ((bf16[8,2,2,64,1024]{4,3,2,1,0:T(8,128)(2,1)}), bf16[8,2,2,64,1024]{4,3,2,1,0:T(8,128)(2,1)}, u32[]{:S(2)}, u32[]{:S(2)}) async-start(bf16[8,2,2,64,1024]{4,3,2,1,0:T(8,128)(2,1)} %bitcast.325), calls=%async_computation.1 | async-start | bytes 8388608 | tf_op jit(solution)/shard_map/all_to_all | solution.py:239
  42.2 2.7 pad_maximum_fusion
  44.9 6.2 %reshape.558 = bf16[2,8,64,8,128]{2,1,4,3,0:T(8,128)(2,1)} reshape(bf16[2,512,1024]{1,2,0:T(8,128)(2,1)} %pad_maximum_fusion) | data formatting | bytes 4194304 | tf_op jit(solution)/shard_map/reshape;reshape | solution.py:148
  51.1 36.6 %collective-permute-done.1 = bf16[96,1024]{1,0:T(8,128)(2,1)} collective-permute-done((bf16[96,1024]{1,0:T(8,128)(2,1)}, bf16[96,1024]{1,0:T(8,128)(2,1)}, u32[]{:S(2)}, u32[]{:S(2)}) %collective-permute-start.1) | collective-permute-done | bytes 196640 | tf_op jit(solution)/shard_map/ppermute | solution.py:105
  89.3 1.8 collective-permute-start.2
  91.1 15.2 %fusion.108 = (bf16[1,4,64,8,128]{2,1,4,3,0:T(4,128)(2,1)}, bf16[1,4,64,8,128]{2,1,4,3,0:T(4,128)(2,1)}, bf16[1,4,64,8,128]{2,1,4,3,0:T(4,128)(2,1)}, bf16[1,4,6...) fusion(bf16[2,8,64,8,128]{2,1,4,3,0:T(8,128)(2,1)} %reshape.558), kind=kLoop, calls=%fused_computation.258 | loop fusion | bytes 10485760 | tf_op jit(solution)/shard_map/slice | solution.py:171
  106.3 2.3 copy.772
  108.9 3.0 fusion.117
  111.9 2.3 copy.774
  114.2 2.3 copy.773
  116.6 1.8 collective-permute-start.4
  118.4 3.1 fusion.118
  121.4 1.6 collective-permute-done.4
  124.1 2.0 fusion.116
  126.1 2.3 copy.782
  128.3 2.3 copy.781
  130.6 2.3 copy.780
  133.0 2.3 copy.779
  135.2 2.3 copy.778
  137.5 2.3 copy.776
  139.8 1.3 copy.775
  141.1 3.0 fusion.115
  144.2 1.3 fusion.53
  148.3 1.3 pad_maximum_fusion.1
  151.3 2.0 fusion.114
  158.0 1.2 fusion.37
  160.3 1.2 collective-permute-start.7
  162.5 6.1 %collective-permute-done.7 = f32[32,8,130]{2,1,0:T(8,128)S(1)} collective-permute-done((f32[32,8,130]{2,1,0:T(8,128)S(1)}, f32[32,8,130]{2,1,0:T(8,128)S(1)}, u32[]{:S(2)}, u32[]{:S(2)}) %collective-permute-start.7) | collective-permute-done | bytes 133152 | tf_op jit(solution)/shard_map/ppermute | solution.py:105
  171.1 3.5 %collective-permute-done.8 = f32[16,8,130]{2,1,0:T(8,128)S(1)} collective-permute-done((f32[16,8,130]{2,1,0:T(8,128)S(1)}, f32[16,8,130]{2,1,0:T(8,128)S(1)}, u32[]{:S(2)}, u32[]{:S(2)}) %collective-permute-start.8) | collective-permute-done | bytes 66592 | tf_op jit(solution)/shard_map/ppermute | solution.py:105
  175.3 1.2 collective-permute-start.9
  176.6 3.7 %collective-permute-done.9 = f32[16,8,130]{2,1,0:T(8,128)S(1)} collective-permute-done((f32[16,8,130]{2,1,0:T(8,128)S(1)}, f32[16,8,130]{2,1,0:T(8,128)S(1)}, u32[]{:S(2)}, u32[]{:S(2)}) %collective-permute-start.9) | collective-permute-done | bytes 66592 | tf_op jit(solution)/shard_map/ppermute | solution.py:109
  180.4 1.2 collective-permute-start.10
  181.7 5.2 %collective-permute-done.10 = f32[32,8,130]{2,1,0:T(8,128)S(1)} collective-permute-done((f32[32,8,130]{2,1,0:T(8,128)S(1)}, f32[32,8,130]{2,1,0:T(8,128)S(1)}, u32[]{:S(2)}, u32[]{:S(2)}) %collective-permute-start.10) | collective-permute-done | bytes 133152 | tf_op jit(solution)/shard_map/ppermute | solution.py:109
  187.9 1.8 fusion.113
  189.7 2.9 copy.713
  192.6 2.2 reshape.492
  197.3 4.7 %convolution_convert_fusion.1 = bf16[128,4096]{1,0:T(8,128)(2,1)S(1)} fusion(bf16[128,1024]{0,1:T(8,128)(2,1)S(1)} %bitcast.350, bf16[1024,4096]{1,0:T(8,128)(2,1)} %param.12), kind=kOutput, calls=%fused_computation.7 | convolution fusion | flops 1074266112 | bytes 9699328 | tf_op jit(solution)/shard_map/dot_general | solution.py:136
  203.0 4.7 %all-to-all-start = ((bf16[4,1024,128]{1,2,0:T(8,128)(2,1)}), bf16[4,1024,128]{1,2,0:T(8,128)(2,1)}, u32[]{:S(2)}, u32[]{:S(2)}) async-start(bf16[4,1024,128]{1,2,0:T(8,128)(2,1)} %bitcast.315), calls=%async_computation | async-start | bytes 2097152 | tf_op jit(solution)/shard_map/all_to_all | solution.py:140
  207.8 4.7 %gather_fusion.4 = bf16[12,2,64,1024]{3,2,1,0:T(8,128)(2,1)} fusion(bf16[8,2,2,64,1024]{4,3,2,1,0:T(8,128)(2,1)} %all-to-all-done.1, s32[12]{0:T(128)S(1)} %fusion.100), kind=kCustom, calls=%fused_computation.4 | custom fusion | bytes 6291552 | tf_op jit(solution)/shard_map/gather | solution.py:242
  212.4 2.7 copy.789
  215.2 1.6 fusion.109
  218.2 2.4 copy.721
  220.6 8.9 %concatenate.72 = f32[4,8,64,640]{3,2,1,0:T(8,128)} concatenate(f32[4,8,64,64]{3,2,1,0:T(8,128)} %get-tuple-element.87, f32[4,8,64,64]{3,2,1,0:T(8,128)} %get-tuple-element.89, f32[4,8,64,64]{3,2,1,0:T(8,128)} %get-tuple-element.85, f32[4,8,64,64]{3,2,1,0:T(8,128)} %get-tuple-element.83, f32[4,8,64,64]{3,2,1,0:T(8,128)} %get-tuple-element.81, f32[4,8,64,128]{3,2,1,0:T(8,128)} %reshape.492, ...), dimensions={3} | concatenate | bytes 10485760 | tf_op jit(solution)/shard_map/concatenate | solution.py:162
  229.6 3.2 %fusion = (f32[4,8,64]{2,1,0:T(8,128)S(1)}, bf16[4,8,64,640]{3,2,1,0:T(8,128)(2,1)S(1)}) fusion(f32[4,8,64,640]{3,2,1,0:T(8,128)} %concatenate.72, f32[4,8,64]{2,1,0:T(8,128)S(1)} %fusion.86), kind=kLoop, calls=%fused_computation.8 | loop fusion | flops 3930112 | bytes 7880704 | tf_op jit(solution)/shard_map/reduce_sum | solution.py:165
  232.8 1.4 slice.288
  234.3 1.3 fusion.35
  235.5 2.6 copy.730
  238.1 1.9 convolution_add_fusion.3
  240.0 1.3 convolution_add_fusion.2
  241.3 1.7 fusion.3
  243.2 1.5 reshape.495
  244.7 1.7 convolution_bitcast_fusion
  247.6 5.7 %convolution_convert_fusion = bf16[256,4096]{1,0:T(8,128)(2,1)S(1)} fusion(bf16[1024,4096]{1,0:T(8,128)(2,1)} %param.12, bf16[32,8,8,128]{3,2,1,0:T(8,128)(2,1)S(1)} %bitcast.364), kind=kOutput, calls=%fused_computation.6 | convolution fusion | flops 2148532224 | bytes 11010048 | tf_op jit(solution)/shard_map/dot_general | solution.py:136
  253.4 1.6 copy.823
  255.0 5.1 %all-to-all-start.2 = ((bf16[4,1024,256]{1,2,0:T(8,128)(2,1)}), bf16[4,1024,256]{1,2,0:T(8,128)(2,1)S(1)}, u32[]{:S(2)}, u32[]{:S(2)}) async-start(bf16[4,1024,256]{1,2,0:T(8,128)(2,1)} %bitcast.331), calls=%async_computation.2 | async-start | bytes 4194304 | tf_op jit(solution)/shard_map/all_to_all | solution.py:140
  261.2 1.2 compare_and_fusion.1
  264.0 1.4 convert_reduce_fusion.1
  265.4 42.9 %all-to-all-done.2 = bf16[4,1024,256]{1,2,0:T(8,128)(2,1)S(1)} async-done(((bf16[4,1024,256]{1,2,0:T(8,128)(2,1)}), bf16[4,1024,256]{1,2,0:T(8,128)(2,1)S(1)}, u32[]{:S(2)}, u32[]{:S(2)}) %all-to-all-start.2) | async-done | bytes 2097184 | tf_op jit(solution)/shard_map/all_to_all | solution.py:140
  (219 shorter events, 52.3 us)
Async XLA Ops:
  0.0 4.8 %copy-start.17 = (bf16[256,1024]{1,0:T(8,128)(2,1)S(1)}, bf16[256,1024]{1,0:T(8,128)(2,1)}, u32[]{:S(2)}) copy-start(bf16[256,1024]{1,0:T(8,128)(2,1)} %param.10) | copy-start | bytes 1572868
  2.1 2.6 copy-start.23
  5.8 1.2 copy-start
  11.5 8.6 %copy-start.29 = (s32[32,3]{0,1:T(4,128)S(1)}, s32[32,3]{0,1:T(4,128)}, u32[]{:S(2)}) copy-start(s32[32,3]{0,1:T(4,128)} %param.14) | copy-start | bytes 1156
  11.6 0.9 copy-start.4
  12.6 25.7 %collective-permute-start = (bf16[192,1024]{1,0:T(8,128)(2,1)S(1)}, bf16[192,1024]{1,0:T(8,128)(2,1)}, u32[]{:S(2)}, u32[]{:S(2)}) collective-permute-start(bf16[192,1024]{1,0:T(8,128)(2,1)S(1)} %dynamic-slice_bitcast_fusion), channel_id=1, source_target_pairs={{0,4},{4,0},{8,12},{12,8},{16,20},{20,16},{24,28},{28,24},{1,5},{5... | collective-permute-start | bytes 1179656 | tf_op jit(solution)/shard_map/ppermute | solution.py:105
  14.0 28.2 %collective-permute-start.12 = (bf16[2,128,1024]{1,2,0:T(8,128)(2,1)}, bf16[2,128,1024]{1,2,0:T(8,128)(2,1)}, u32[]{:S(2)}, u32[]{:S(2)}) collective-permute-start(bf16[2,128,1024]{1,2,0:T(8,128)(2,1)} %get-tuple-element.37), channel_id=1, source_target_pairs={{0,4},{4,8},{8,12},{12,16},{16,20},{20,24},{24,28},{1,5},{5,9},{9,... | collective-permute-start | bytes 1572872 | tf_op jit(solution)/shard_map/ppermute | solution.py:26
  16.4 25.8 %collective-permute-start.13 = (bf16[2,128,1024]{1,2,0:T(8,128)(2,1)}, bf16[2,128,1024]{1,2,0:T(8,128)(2,1)}, u32[]{:S(2)}, u32[]{:S(2)}) collective-permute-start(bf16[2,128,1024]{1,2,0:T(8,128)(2,1)} %get-tuple-element.38), channel_id=1, source_target_pairs={{4,0},{8,4},{12,8},{16,12},{20,16},{24,20},{28,24},{5,1},{9,5},{13... | collective-permute-start | bytes 1572872 | tf_op jit(solution)/shard_map/ppermute | solution.py:28
  32.4 5.1 %copy-start.30 = (s32[8]{0:T(128)S(1)}, s32[8]{0:T(128)}, u32[]{:S(2)}) copy-start(s32[8]{0:T(128)} %param.15) | copy-start | bytes 100
  32.4 5.9 %copy-start.5 = (bf16[2,192,1024]{2,1,0:T(8,128)(2,1)S(1)}, bf16[2,192,1024]{2,1,0:T(8,128)(2,1)}, u32[]{:S(2)}) copy-start(bf16[2,192,1024]{2,1,0:T(8,128)(2,1)} %copy-done.4) | copy-start | bytes 2359300
  32.4 170.7 %all-to-all-start.1 = ((bf16[8,2,2,64,1024]{4,3,2,1,0:T(8,128)(2,1)}), bf16[8,2,2,64,1024]{4,3,2,1,0:T(8,128)(2,1)}, u32[]{:S(2)}, u32[]{:S(2)}) async-start(bf16[8,2,2,64,1024]{4,3,2,1,0:T(8,128)(2,1)} %bitcast.325), calls=%async_computation.1 | async-start | bytes 8388608 | tf_op jit(solution)/shard_map/all_to_all | solution.py:239
  40.1 47.7 %collective-permute-start.1 = (bf16[96,1024]{1,0:T(8,128)(2,1)}, bf16[96,1024]{1,0:T(8,128)(2,1)}, u32[]{:S(2)}, u32[]{:S(2)}) collective-permute-start(bf16[96,1024]{1,0:T(8,128)(2,1)} %dynamic-slice_bitcast_fusion.1), channel_id=1, source_target_pairs={{0,8},{4,12},{8,0},{12,4},{16,24},{20,28},{24,16},{28,20},{1,9},{5... | collective-permute-start | bytes 589832 | tf_op jit(solution)/shard_map/ppermute | solution.py:105
  88.7 0.7 copy-start.14
  89.3 19.6 %copy-start.28 = (pred[4,8]{1,0:T(4,128)(4,1)S(1)}, pred[4,8]{1,0:T(4,128)(4,1)}, u32[]{:S(2)}) copy-start(pred[4,8]{1,0:T(4,128)(4,1)} %get-tuple-element.71) | copy-start | bytes 100
  89.3 19.2 %collective-permute-start.2 = (bf16[48,1024]{1,0:T(8,128)(2,1)S(1)}, bf16[48,1024]{1,0:T(8,128)(2,1)S(1)}, u32[]{:S(2)}, u32[]{:S(2)}) collective-permute-start(bf16[48,1024]{1,0:T(8,128)(2,1)S(1)} %dynamic-slice_bitcast_fusion.2), channel_id=1, source_target_pairs={{0,16},{4,20},{8,24},{12,28},{16,0},{20,4},{24,8},{28,12},{1,17},{... | collective-permute-start | bytes 294920 | tf_op jit(solution)/shard_map/ppermute | solution.py:105
  91.1 17.4 %copy-start.15 = (bf16[96,1024]{1,0:T(8,128)(2,1)S(1)}, bf16[96,1024]{1,0:T(8,128)(2,1)}, u32[]{:S(2)}) copy-start(bf16[96,1024]{1,0:T(8,128)(2,1)} %copy-done.14) | copy-start | bytes 589828
  108.5 7.9 %collective-permute-start.3 = (bf16[48,1024]{1,0:T(8,128)(2,1)S(1)}, bf16[48,1024]{1,0:T(8,128)(2,1)S(1)}, u32[]{:S(2)}, u32[]{:S(2)}) collective-permute-start(bf16[48,1024]{1,0:T(8,128)(2,1)S(1)} %bitcast_add_fusion.2), channel_id=1, source_target_pairs={{0,16},{4,20},{8,24},{12,28},{16,0},{20,4},{24,8},{28,12},{1,17},{... | collective-permute-start | bytes 294920 | tf_op jit(solution)/shard_map/ppermute | solution.py:109
  108.9 9.5 %copy-start.27 = (pred[4,8]{1,0:T(4,128)(4,1)S(1)}, pred[4,8]{1,0:T(4,128)(4,1)}, u32[]{:S(2)}) copy-start(pred[4,8]{1,0:T(4,128)(4,1)} %get-tuple-element.70) | copy-start | bytes 100
  116.4 7.6 %copy-start.7 = (bf16[1,4,64,8,128]{4,2,3,1,0:T(8,128)(2,1)S(1)}, bf16[1,4,64,8,128]{4,2,3,1,0:T(8,128)(2,1)}, u32[]{:S(2)}) copy-start(bf16[1,4,64,8,128]{4,2,3,1,0:T(8,128)(2,1)} %copy.774) | copy-start | bytes 1572868
  116.4 7.6 %copy-start.26 = (pred[4,8]{1,0:T(4,128)(4,1)S(1)}, pred[4,8]{1,0:T(4,128)(4,1)}, u32[]{:S(2)}) copy-start(pred[4,8]{1,0:T(4,128)(4,1)} %get-tuple-element.69) | copy-start | bytes 100
  116.6 6.4 %collective-permute-start.4 = (bf16[96,1024]{1,0:T(8,128)(2,1)S(1)}, bf16[96,1024]{1,0:T(8,128)(2,1)S(1)}, u32[]{:S(2)}, u32[]{:S(2)}) collective-permute-start(bf16[96,1024]{1,0:T(8,128)(2,1)S(1)} %get-tuple-element.59), channel_id=1, source_target_pairs={{0,8},{4,12},{8,0},{12,4},{16,24},{20,28},{24,16},{28,20},{1,9},{5... | collective-permute-start | bytes 589832 | tf_op jit(solution)/shard_map/ppermute | solution.py:109
  124.1 20.1 %collective-permute-start.5 = (bf16[192,1024]{1,0:T(8,128)(2,1)}, bf16[192,1024]{1,0:T(8,128)(2,1)}, u32[]{:S(2)}, u32[]{:S(2)}) collective-permute-start(bf16[192,1024]{1,0:T(8,128)(2,1)} %get-tuple-element.49), channel_id=1, source_target_pairs={{0,4},{4,0},{8,12},{12,8},{16,20},{20,16},{24,28},{28,24},{1,5},{5... | collective-permute-start | bytes 1179656 | tf_op jit(solution)/shard_map/ppermute | solution.py:109
  145.5 1.1 copy-start.11
  148.3 3.1 copy-start.6
  150.8 4.7 %collective-permute-start.6 = (f32[64,8,130]{2,1,0:T(8,128)}, f32[64,8,130]{2,1,0:T(8,128)}, u32[]{:S(2)}, u32[]{:S(2)}) collective-permute-start(f32[64,8,130]{2,1,0:T(8,128)} %bitcast.316), channel_id=1, source_target_pairs={{0,4},{4,0},{8,12},{12,8},{16,20},{20,16},{24,28},{28,24},{1,5},{5... | collective-permute-start | bytes 798728 | tf_op jit(solution)/shard_map/ppermute | solution.py:105
  160.3 8.3 %collective-permute-start.7 = (f32[32,8,130]{2,1,0:T(8,128)S(1)}, f32[32,8,130]{2,1,0:T(8,128)S(1)}, u32[]{:S(2)}, u32[]{:S(2)}) collective-permute-start(f32[32,8,130]{2,1,0:T(8,128)S(1)} %get-tuple-element.40), channel_id=1, source_target_pairs={{0,8},{4,12},{8,0},{12,4},{16,24},{20,28},{24,16},{28,20},{1,9},{5... | collective-permute-start | bytes 399368 | tf_op jit(solution)/shard_map/ppermute | solution.py:105
  169.3 1.5 copy-start.12
  169.6 5.0 %collective-permute-start.8 = (f32[16,8,130]{2,1,0:T(8,128)S(1)}, f32[16,8,130]{2,1,0:T(8,128)S(1)}, u32[]{:S(2)}, u32[]{:S(2)}) collective-permute-start(f32[16,8,130]{2,1,0:T(8,128)S(1)} %get-tuple-element.47), channel_id=1, source_target_pairs={{0,16},{4,20},{8,24},{12,28},{16,0},{20,4},{24,8},{28,12},{1,17},{... | collective-permute-start | bytes 199688 | tf_op jit(solution)/shard_map/ppermute | solution.py:105
  175.3 5.0 %collective-permute-start.9 = (f32[16,8,130]{2,1,0:T(8,128)S(1)}, f32[16,8,130]{2,1,0:T(8,128)S(1)}, u32[]{:S(2)}, u32[]{:S(2)}) collective-permute-start(f32[16,8,130]{2,1,0:T(8,128)S(1)} %pad_maximum_fusion.11), channel_id=1, source_target_pairs={{0,16},{4,20},{8,24},{12,28},{16,0},{20,4},{24,8},{28,12},{1,17},{... | collective-permute-start | bytes 199688 | tf_op jit(solution)/shard_map/ppermute | solution.py:109
  180.4 6.4 %collective-permute-start.10 = (f32[32,8,130]{2,1,0:T(8,128)S(1)}, f32[32,8,130]{2,1,0:T(8,128)S(1)}, u32[]{:S(2)}, u32[]{:S(2)}) collective-permute-start(f32[32,8,130]{2,1,0:T(8,128)S(1)} %get-tuple-element.55), channel_id=1, source_target_pairs={{0,8},{4,12},{8,0},{12,4},{16,24},{20,28},{24,16},{28,20},{1,9},{5... | collective-permute-start | bytes 399368 | tf_op jit(solution)/shard_map/ppermute | solution.py:109
  187.9 6.9 %collective-permute-start.11 = (f32[64,8,130]{2,1,0:T(8,128)}, f32[64,8,130]{2,1,0:T(8,128)}, u32[]{:S(2)}, u32[]{:S(2)}) collective-permute-start(f32[64,8,130]{2,1,0:T(8,128)} %get-tuple-element.43), channel_id=1, source_target_pairs={{0,4},{4,0},{8,12},{12,8},{16,20},{20,16},{24,28},{28,24},{1,5},{5... | collective-permute-start | bytes 798728 | tf_op jit(solution)/shard_map/ppermute | solution.py:109
  203.0 51.9 %all-to-all-start = ((bf16[4,1024,128]{1,2,0:T(8,128)(2,1)}), bf16[4,1024,128]{1,2,0:T(8,128)(2,1)}, u32[]{:S(2)}, u32[]{:S(2)}) async-start(bf16[4,1024,128]{1,2,0:T(8,128)(2,1)} %bitcast.315), calls=%async_computation | async-start | bytes 2097152 | tf_op jit(solution)/shard_map/all_to_all | solution.py:140
  220.6 8.9 %copy-start.18 = (f32[4,8,64]{2,1,0:T(8,128)S(1)}, f32[4,8,64]{2,1,0:T(8,128)}, u32[]{:S(2)}) copy-start(f32[4,8,64]{2,1,0:T(8,128)} %get-tuple-element.86) | copy-start | bytes 24580
  220.6 8.9 %copy-start.19 = (f32[4,8,64]{2,1,0:T(8,128)S(1)}, f32[4,8,64]{2,1,0:T(8,128)}, u32[]{:S(2)}) copy-start(f32[4,8,64]{2,1,0:T(8,128)} %get-tuple-element.88) | copy-start | bytes 24580
  220.6 8.9 %copy-start.20 = (f32[4,8,64]{2,1,0:T(8,128)S(1)}, f32[4,8,64]{2,1,0:T(8,128)}, u32[]{:S(2)}) copy-start(f32[4,8,64]{2,1,0:T(8,128)} %get-tuple-element.84) | copy-start | bytes 24580
  220.6 8.9 %copy-start.21 = (f32[4,8,64]{2,1,0:T(8,128)S(1)}, f32[4,8,64]{2,1,0:T(8,128)}, u32[]{:S(2)}) copy-start(f32[4,8,64]{2,1,0:T(8,128)} %get-tuple-element.82) | copy-start | bytes 24580
  220.6 8.9 %copy-start.22 = (f32[4,8,64]{2,1,0:T(8,128)S(1)}, f32[4,8,64]{2,1,0:T(8,128)}, u32[]{:S(2)}) copy-start(f32[4,8,64]{2,1,0:T(8,128)} %get-tuple-element.80) | copy-start | bytes 24580
  229.6 4.7 %copy-start.10 = (bf16[1,4,64,8,128]{4,2,3,1,0:T(8,128)(2,1)S(1)}, bf16[1,4,64,8,128]{4,2,3,1,0:T(8,128)(2,1)}, u32[]{:S(2)}) copy-start(bf16[1,4,64,8,128]{4,2,3,1,0:T(8,128)(2,1)} %copy.778) | copy-start | bytes 1572868
  235.5 4.5 %copy-start.9 = (bf16[1,4,64,8,128]{4,2,3,1,0:T(8,128)(2,1)S(1)}, bf16[1,4,64,8,128]{4,2,3,1,0:T(8,128)(2,1)}, u32[]{:S(2)}) copy-start(bf16[1,4,64,8,128]{4,2,3,1,0:T(8,128)(2,1)} %copy.780) | copy-start | bytes 1572868
  238.1 3.2 %copy-start.1 = (bf16[4,8,64,192]{2,3,1,0:T(8,128)(2,1)S(1)}, bf16[4,8,64,192]{2,3,1,0:T(8,128)(2,1)}, u32[]{:S(2)}) copy-start(bf16[4,8,64,192]{2,3,1,0:T(8,128)(2,1)} %copy.730) | copy-start | bytes 2359300
  238.1 3.2 %copy-start.2 = (bf16[4,3,1,64,8,128]{5,4,3,2,1,0:T(8,128)(2,1)S(1)}, bf16[4,3,1,64,8,128]{5,4,3,2,1,0:T(8,128)(2,1)}, u32[]{:S(2)}) copy-start(bf16[4,3,1,64,8,128]{5,4,3,2,1,0:T(8,128)(2,1)} %get-tuple-element.25) | copy-start | bytes 4718596
  244.7 1.8 copy-start.3
  244.7 1.8 copy-start.8
  244.7 2.1 copy-start.13
  244.7 2.2 copy-start.16
  255.0 5.1 %copy-start.25 = (s32[2]{0:T(128)S(1)}, s32[2]{0:T(128)}, u32[]{:S(2)}) copy-start(s32[2]{0:T(128)} %get-tuple-element.12) | copy-start | bytes 28
  255.0 5.7 %copy-start.24 = (pred[2]{0:T(512)(128)(4,1)S(1)}, pred[2]{0:T(512)(128)(4,1)}, u32[]{:S(2)}) copy-start(pred[2]{0:T(512)(128)(4,1)} %copy-done.23) | copy-start | bytes 10
  255.0 53.4 %all-to-all-start.2 = ((bf16[4,1024,256]{1,2,0:T(8,128)(2,1)}), bf16[4,1024,256]{1,2,0:T(8,128)(2,1)S(1)}, u32[]{:S(2)}, u32[]{:S(2)}) async-start(bf16[4,1024,256]{1,2,0:T(8,128)(2,1)} %bitcast.331), calls=%async_computation.2 | async-start | bytes 4194304 | tf_op jit(solution)/shard_map/all_to_all | solution.py:140

commit v3 on v1

--- a/solution.py
+++ b/solution.py
@@ -123,23 +123,34 @@
 
 
 def softmax_merge(a, b):
-    mix_a, total_a, peak_a = a
-    mix_b, total_b, peak_b = b
+    width = a.shape[1] - 128
+    heads = width // HEAD_DIM
+    peak_a = a[:, width + heads : width + 2 * heads]
+    peak_b = b[:, width + heads : width + 2 * heads]
     peak = jnp.maximum(peak_a, peak_b)
     scale_a = jnp.exp(peak_a - peak)
     scale_b = jnp.exp(peak_b - peak)
-    mix = mix_a * scale_a[..., None] + mix_b * scale_b[..., None]
-    total = total_a * scale_a + total_b * scale_b
-    return (mix, total, peak)
-
-
-def project_over_head(rows, out_weight):
+    rows = a.shape[0]
+    mix = (
+        a[:, :width].reshape(rows, heads, HEAD_DIM) * scale_a[..., None]
+        + b[:, :width].reshape(rows, heads, HEAD_DIM) * scale_b[..., None]
+    ).reshape(rows, width)
+    total = a[:, width : width + heads] * scale_a + b[:, width : width + heads] * scale_b
+    pad = jnp.zeros((rows, 128 - 2 * heads), a.dtype)
+    return jnp.concatenate([mix, total, peak, pad], axis=1)
+
+
+def head_partials(rows, out_weight):
     head_count = lax.axis_size("head")
-    row_count, width_here = rows.shape
-    weight_view = out_weight.reshape(width_here, head_count, out_weight.shape[1] // head_count)
-    partial = jnp.einsum("td,dhc->htc", rows, weight_view, preferred_element_type=jnp.float32)
-    gathered = lax.all_to_all(partial.astype(jnp.bfloat16), "head", 0, 0, tiled=True)
-    return jnp.sum(gathered.astype(jnp.float32), axis=0)
+    partial = lax.dot_general(
+        out_weight, rows, (((0,), (1,)), ((), ())), preferred_element_type=jnp.float32
+    ).astype(jnp.bfloat16)
+    return partial.reshape(head_count, out_weight.shape[1] // head_count, rows.shape[0])
+
+
+def sum_over_head(partial):
+    gathered = lax.all_to_all(partial, "head", 0, 0, tiled=True)
+    return jnp.sum(gathered.astype(jnp.float32), axis=0).T
 
 
 def on_device(
@@ -214,10 +225,12 @@
         [window_valid, jnp.ones((blocks_here, GLOB + RAND, heads_here), dtype=bool)], axis=1
     )
     attended = block_attend(query_view, all_kv[0], all_kv[1], all_valid)
-    mixed = project_over_head(attended.reshape(tok_here, width_here), out_weight)
-    global_query = shared[0].reshape(GLOB, BLOCK, heads_here, HEAD_DIM)
-    key_grid = key_rot.reshape(tok_here, heads_here, HEAD_DIM)
-    value_grid = values.reshape(tok_here, heads_here, HEAD_DIM)
+    global_query = shared[0]
+    key_later = key_rot
+    value_later = values
+    global_query = global_query.reshape(GLOB, BLOCK, heads_here, HEAD_DIM)
+    key_grid = key_later.reshape(tok_here, heads_here, HEAD_DIM)
+    value_grid = value_later.reshape(tok_here, heads_here, HEAD_DIM)
     global_scores = jnp.einsum(
         "gqhd,khd->gqhk", global_query, key_grid, preferred_element_type=jnp.float32
     ) * (1.0 / math.sqrt(HEAD_DIM))
@@ -228,23 +241,26 @@
         "gqhk,khd->gqhd", expo.astype(jnp.bfloat16), value_grid, preferred_element_type=jnp.float32
     )
     row_total = GLOB * BLOCK
-    mix_sum, total_sum, _ = tree_reduce(
-        (
-            partial_mix.reshape(row_total, heads_here, HEAD_DIM),
+    packed = jnp.concatenate(
+        [
+            partial_mix.reshape(row_total, width_here),
             partial_total.reshape(row_total, heads_here),
             local_peak.reshape(row_total, heads_here),
-        ),
-        softmax_merge,
-        "seq",
-    )
+            jnp.zeros((row_total, 128 - 2 * heads_here), jnp.float32),
+        ],
+        axis=1,
+    )
+    reduced = tree_reduce(packed, softmax_merge, "seq")
+    mix_sum = reduced[:, :width_here].reshape(row_total, heads_here, HEAD_DIM)
+    total_sum = reduced[:, width_here : width_here + heads_here]
     global_out = (mix_sum / total_sum[..., None]).reshape(row_total, width_here).astype(jnp.bfloat16)
-    global_mixed = project_over_head(global_out, out_weight).reshape(GLOB, BLOCK, -1)
-    mixed = mixed.reshape(blocks_here, BLOCK, -1)
+    global_out = global_out.reshape(GLOB, BLOCK, width_here)
     block_index = jnp.arange(blocks_here)
     for global_slot in range(GLOB):
         hit = mine_global[global_slot] & (block_index == local_global[global_slot])
-        mixed = jnp.where(hit[:, None, None], global_mixed[global_slot][None], mixed)
-    return mixed.reshape(tok_here, -1).astype(jnp.bfloat16)
+        attended = jnp.where(hit[:, None, None], global_out[global_slot][None], attended)
+    mixed = sum_over_head(head_partials(attended.reshape(tok_here, width_here), out_weight))
+    return mixed.astype(jnp.bfloat16)
 
 
 def solution(mesh):

time: 246 us -> 235 us (0.955)
  blocking collectives: 0 us -> 53.5 us
  waiting for transfers between devices: 113 us -> 66.6 us
  starting transfers between devices: 36 us -> 22 us
  local copies, waits for them, and re-layouts: 49.5 us -> 59.8 us
  matrix products: 18.4 us -> 8.44 us
  other arithmetic: 24.5 us -> 20.1 us
    all_to_all x0 -> x1, blocking collectives: none -> 53.5 us  [sum_over_head(): gathered = lax.all_to_all(partial, 'head', 0, 0, tiled=True)]
    all_to_all x2 -> x0, waiting for transfers between devices: 42.5 us -> none  [project_over_head(): lax.all_to_all(partial.astype(jnp.bfloat16), 'head', 0, 0, tiled=True)]
    dot_general x2 -> x1, matrix products: 12.7 us -> 2.48 us  [head_partials(): lax.dot_general(out_weight, rows, (((0,), (1,)), ((), ())), preferred_ele...]
    all_to_all x2 -> x0, starting transfers between devices: 9.97 us -> none  [project_over_head(): lax.all_to_all(partial.astype(jnp.bfloat16), 'head', 0, 0, tiled=True)]
    ppermute x9 -> x6, waiting for transfers between devices: 17 us -> 9.6 us  [tree_reduce(): got = lax.ppermute(parts, axis, xor_perm(count, bit))]
    ppermute x12 -> x6, waiting for transfers between devices: 53 us -> 57 us  [tree_reduce(): got = lax.ppermute(send, axis, xor_perm(count, bit))]
    gather x2, local copies, waits for them, and re-layouts: 3.36 us -> 7 us  [on_device(): incoming[:, my_owners, my_ranks]]
    ppermute x12 -> x6, starting transfers between devices: 9.16 us -> 6.07 us  [tree_reduce(): got = lax.ppermute(send, axis, xor_perm(count, bit))]
  transfers between devices with their start and end apart: 26 -> 15, of which waited for: 18 -> 8; matrix products, arithmetic and copies ran while one was open for 32% -> 19% of each run, Pallas kernels for 0% -> 0%
where the time goes in v3:
time: 235 us; the launch traced here: 233 us
  waiting for transfers between devices  66.6 us (28%)
  local copies, waits for them, and re-layouts  59.8 us (25%)
  blocking collectives  53.5 us (23%)
  starting transfers between devices  22 us (9%)
  other arithmetic  20.1 us (9%)
  matrix products  8.44 us (4%)
    ppermute x6, waiting for transfers between devices, tree_reduce(): got = lax.ppermute(send, axis, xor_perm(count, bit))  57 us
    all_to_all x1, blocking collectives, sum_over_head(): gathered = lax.all_to_all(partial, 'head', 0, 0, tiled=True)  53.5 us
    unnamed x45, local copies, waits for them, and re-layouts  15.7 us
    slice x1, local copies, waits for them, and re-layouts, on_device(): attended = block_attend(query_view, all_kv[0], all_kv[1], all_valid)  10.2 us
    ppermute x6, waiting for transfers between devices, tree_reduce(): got = lax.ppermute(parts, axis, xor_perm(count, bit))  9.6 us
    gather x2, local copies, waits for them, and re-layouts, on_device(): incoming[:, my_owners, my_ranks]  7 us
    convert_element_type x7, local copies, waits for them, and re-layouts, rotate(): return turned.reshape(row_count, row_width).astype(jnp.bfloat16)  6.65 us
    ppermute x6, starting transfers between devices, tree_reduce(): got = lax.ppermute(send, axis, xor_perm(count, bit))  6.07 us
  transfers between devices with their start and end apart: 15, of which 8 were waited for; matrix products, arithmetic and copies ran while one was open for 19% of the time, Pallas kernels for 0%

profile of v3, /device:TPU:2, one launch (start us, length us, event | category | flops | bytes accessed | tf_op | source)
XLA Modules:
  0.0 232.8 jit_solution(8270378036522034151)
XLA Ops:
  1.4 1.2 copy.129
  2.8 1.2 copy.130
  4.0 1.1 convert.4
  5.7 1.5 multiply_subtract_fusion
  7.3 1.2 fusion.33
  8.4 1.9 collective-permute-start.12
  10.4 3.6 %collective-permute-start.13 = (bf16[2,128,1024]{1,2,0:T(8,128)(2,1)}, bf16[2,128,1024]{1,2,0:T(8,128)(2,1)}, u32[]{:S(2)}, u32[]{:S(2)}) collective-permute-start(bf16[2,128,1024]{1,2,0:T(8,128)(2,1)} %get-tuple-element.26), channel_id=1, source_target_pairs={{4,0},{8,4},{12,8},{16,12},{20,16},{24,20},{28,24},{5,1},{9,5},{13... | collective-permute-start | bytes 1572872 | tf_op jit(solution)/shard_map/ppermute | solution.py:28
  14.7 1.3 copy.161
  16.9 0.6 compare_select_fusion.3
  17.9 1.3 copy.160
  19.2 1.6 gather_fusion.1
  20.8 1.6 gather_fusion
  22.4 0.6 gather_fusion.2
  23.4 0.9 dynamic-slice_bitcast_fusion
  24.8 1.3 copy.164
  26.2 1.1 pad_maximum_fusion.1
  27.3 2.8 %gather_fusion.3 = bf16[16,2,64,1024]{3,2,1,0:T(8,128)(2,1)} fusion(bf16[2,4,64,1024]{3,2,1,0:T(8,128)(2,1)S(1)} %pad_maximum_fusion.1, s32[1024]{0:T(1024)S(1)} %get-tuple-element.67), kind=kCustom, calls=%fused_computation.3 | custom fusion | bytes 8388672 | tf_op jit(solution)/shard_map/gather | solution.py:210
  30.1 5.0 %all-to-all-start = ((bf16[2,8,2,64,1024]{4,3,0,2,1:T(8,128)(2,1)}), bf16[2,8,2,64,1024]{4,3,0,2,1:T(8,128)(2,1)}, u32[]{:S(2)}, u32[]{:S(2)}) async-start(bf16[2,8,2,64,1024]{4,3,0,2,1:T(8,128)(2,1)} %bitcast.272), calls=%async_computation | async-start | bytes 8388608 | tf_op jit(solution)/shard_map/all_to_all | solution.py:211
  35.6 50.2 %collective-permute-done.1 = bf16[96,1024]{1,0:T(8,128)(2,1)S(1)} collective-permute-done((bf16[96,1024]{1,0:T(8,128)(2,1)S(1)}, bf16[96,1024]{1,0:T(8,128)(2,1)S(1)}, u32[]{:S(2)}, u32[]{:S(2)}) %collective-permute-start.1) | collective-permute-done | bytes 196640 | tf_op jit(solution)/shard_map/ppermute | solution.py:105
  85.9 2.6 %collective-permute-start.2 = (bf16[48,1024]{1,0:T(8,128)(2,1)S(1)}, bf16[48,1024]{1,0:T(8,128)(2,1)S(1)}, u32[]{:S(2)}, u32[]{:S(2)}) collective-permute-start(bf16[48,1024]{1,0:T(8,128)(2,1)S(1)} %dynamic-slice_bitcast_fusion.6), channel_id=1, source_target_pairs={{0,16},{4,20},{8,24},{12,28},{16,0},{20,4},{24,8},{28,12},{1,17},{... | collective-permute-start | bytes 294920 | tf_op jit(solution)/shard_map/ppermute | solution.py:105
  88.6 1.4 reshape.539
  90.0 1.4 collective-permute-done.2
  91.5 1.8 collective-permute-start.3
  93.4 0.7 broadcast_in_dim.189
  94.3 1.9 collective-permute-done.3
  96.3 0.9 collective-permute-start.4
  97.1 1.3 fusion.98
  98.5 0.6 fusion.99
  99.1 2.9 %collective-permute-done.4 = bf16[96,1024]{1,0:T(8,128)(2,1)S(1)} collective-permute-done((bf16[96,1024]{1,0:T(8,128)(2,1)S(1)}, bf16[96,1024]{1,0:T(8,128)(2,1)S(1)}, u32[]{:S(2)}, u32[]{:S(2)}) %collective-permute-start.4) | collective-permute-done | bytes 196640 | tf_op jit(solution)/shard_map/ppermute | solution.py:109
  102.3 1.2 compare_and_fusion.1
  103.7 1.3 compare_and_fusion
  105.1 0.6 broadcast_in_dim.175
  105.9 1.0 fusion.44
  108.8 0.9 dynamic-slice_bitcast_fusion.2
  110.2 2.8 %pad_maximum_fusion = bf16[2,512,1024]{1,2,0:T(8,128)(2,1)} fusion(bf16[2,128,1024]{1,2,0:T(8,128)(2,1)} %collective-permute-done.13, bf16[1,256,1024]{1,2,0:T(8,128)(2,1)S(1)} %bitcast.281, bf16[1,256,1024]{1,2,0:T(8,128)(2,1)S(1)} %bitcast.268, bf16[2,128,1024]{1,2,0:T(8,128)(2,1)} %collective-permute-done.12), kind=kLoop, calls=%fused_computation.20 | loop fusion | flops 8388608 | bytes 4194304 | tf_op jit(solution)/shard_map/concatenate | solution.py:24
  113.0 3.2 %copy.140 = bf16[2,512,1024]{2,1,0:T(8,128)(2,1)S(1)} copy(bf16[2,512,1024]{1,2,0:T(8,128)(2,1)} %pad_maximum_fusion) | data formatting | bytes 4194304 | tf_op jit(solution)/shard_map/concatenate | solution.py:24
  116.2 1.1 fusion.21
  117.2 0.9 fusion.71
  118.4 1.2 fusion.50
  119.7 0.9 collective-permute-start.7
  120.6 1.1 fusion.20
  121.7 3.8 %collective-permute-done.7 = f32[32,1152]{1,0:T(8,128)S(1)} collective-permute-done((f32[32,1152]{1,0:T(8,128)S(1)}, f32[32,1152]{1,0:T(8,128)S(1)}, u32[]{:S(2)}, u32[]{:S(2)}) %collective-permute-start.7) | collective-permute-done | bytes 147488 | tf_op jit(solution)/shard_map/ppermute | solution.py:105
  126.0 1.8 collective-permute-start.8
  127.9 1.1 fusion.19
  128.9 1.5 collective-permute-done.8
  130.8 1.7 collective-permute-start.9
  132.6 1.1 fusion.18
  133.7 1.5 collective-permute-done.9
  135.3 0.9 collective-permute-start.10
  136.1 1.1 fusion.17
  137.2 3.3 %collective-permute-done.10 = f32[32,1152]{1,0:T(8,128)S(1)} collective-permute-done((f32[32,1152]{1,0:T(8,128)S(1)}, f32[32,1152]{1,0:T(8,128)S(1)}, u32[]{:S(2)}, u32[]{:S(2)}) %collective-permute-start.10) | collective-permute-done | bytes 147488 | tf_op jit(solution)/shard_map/ppermute | solution.py:109
  140.7 1.6 broadcast_dynamic-update-slice_fusion
  142.9 4.7 %gather_fusion.4 = bf16[12,2,64,1024]{3,2,1,0:T(8,128)(2,1)} fusion(bf16[2,8,2,64,1024]{4,3,0,2,1:T(8,128)(2,1)} %all-to-all-done, s32[12]{0:T(128)S(1)} %fusion.87), kind=kCustom, calls=%fused_computation.4 | custom fusion | bytes 6291552 | tf_op jit(solution)/shard_map/gather | solution.py:214
  147.5 2.4 %copy.146 = bf16[2,12,64,1024]{3,2,1,0:T(8,128)(2,1)S(1)} copy(bf16[2,12,64,1024]{3,2,0,1:T(8,128)(2,1)} %bitcast.273) | data formatting | bytes 6291456 | tf_op jit(solution)/shard_map/gather | solution.py:214
  149.9 2.2 constant_dynamic-update-slice_fusion
  152.1 10.2 %fusion.96 = (bf16[1,4,10,64,1024]{4,3,2,1,0:T(8,128)(2,1)}, bf16[1,4,10,64,1024]{4,3,2,1,0:T(8,128)(2,1)}) fusion(bf16[2,4,10,64,1024]{4,3,2,1,0:T(8,128)(2,1)} %constant_dynamic-update-slice_fusion), kind=kLoop, calls=%fused_computation.223 | loop fusion | bytes 20971520 | tf_op jit(solution)/shard_map/slice | solution.py:227
  162.3 4.0 %copy.178 = bf16[320,8,8,128]{3,2,1,0:T(8,128)(2,1)S(1)} copy(bf16[320,8,8,128]{3,1,2,0:T(8,128)(2,1)} %bitcast.264) | data formatting | bytes 10485760
  166.4 1.4 copy.179
  167.8 2.5 %fusion.4 = (f32[4,8,64]{2,1,0:T(8,128)S(1)}, f32[4,8,64,640]{3,2,1,0:T(8,128)S(1)}) fusion(pred[4,8,640]{2,1,0:T(8,128)(4,1)S(1)} %copy-done.6, bf16[4,640,8,128]{3,2,1,0:T(8,128)(2,1)S(1)} %bitcast.265, bf16[4,64,8,128]{1,0,3,2:T(4,128)(2,1)S(1)} %copy-done.2), kind=kOutput, calls=%fused_computation.12 | convolution fusion | flops 339474432 | bytes 11038720 | tf_op jit(solution)/shard_map/bqhd,bshd->bhqs/dot_general | solution.py:74
  170.3 1.6 fusion.5
  172.0 2.8 %divide_convert_fusion = bf16[4,64,8,128]{3,1,2,0:T(8,128)(2,1)S(1)} fusion(bf16[4,640,8,128]{3,2,1,0:T(8,128)(2,1)S(1)} %bitcast.279, f32[4,8,64,640]{3,2,1,0:T(8,128)S(1)} %get-tuple-element.66, f32[4,8,64]{2,1,0:T(8,128)S(1)} %get-tuple-element.65, pred[4,8,640]{2,1,0:T(8,128)(4,1)S(1)} %copy-done.6, f32[4,64,8]{1,2,0:T(8,128)S(1)} %bitcast.323), kind=kOutput, calls=%fused_computation.42 | convolution fusion | flops 341311488 | bytes 11046912 | tf_op jit(solution)/shard_map/bhqs,bshd->bqhd/dot_general | solution.py:83
  175.3 2.5 %convolution_convert_fusion = bf16[256,4096]{1,0:T(8,128)(2,1)S(1)} fusion(bf16[1024,4096]{1,0:T(8,128)(2,1)S(1)} %bitcast.325, bf16[256,1024]{1,0:T(8,128)(2,1)S(1)} %bitcast.303, bf16[256,1024]{1,0:T(8,128)(2,1)S(1)} %bitcast.304, bf16[32,8,8,128]{3,2,1,0:T(8,128)(2,1)S(1)} %bitcast.308, pred[256]{0:T(512)(128)(4,1)S(1)} %copy-done.12, ...), kind=kOutput, calls=%fused_computation.11 | convolution fusion | flops 2149056512 | bytes 12059136 | tf_op jit(solution)/shard_map/dot_general | solution.py:145
  178.0 53.5 %all_to_all.10 = bf16[4,1024,256]{1,2,0:T(8,128)(2,1)S(1)} all-to-all(bf16[4,1024,256]{1,2,0:T(8,128)(2,1)S(1)} %bitcast.275), channel_id=1, replica_groups=mesh['seq'=8,'head'=4] {'head'}, dimensions={0} | all-to-all | bytes 4194304 | tf_op jit(solution)/shard_map/all_to_all | solution.py:152
  231.5 1.3 reduce_sum.55
  (137 shorter events, 10.1 us)
Async XLA Ops:
  0.0 5.1 %copy-start.1 = (bf16[256,1024]{1,0:T(8,128)(2,1)S(1)}, bf16[256,1024]{1,0:T(8,128)(2,1)}, u32[]{:S(2)}) copy-start(bf16[256,1024]{1,0:T(8,128)(2,1)} %param.11) | copy-start | bytes 1572868
  5.1 9.3 %copy-start.9 = (s32[32,3]{0,1:T(4,128)S(1)}, s32[32,3]{0,1:T(4,128)}, u32[]{:S(2)}) copy-start(s32[32,3]{0,1:T(4,128)} %param.14) | copy-start | bytes 1156
  5.7 11.2 %copy-start.10 = (s32[2]{0:T(128)S(1)}, s32[2]{0:T(128)}, u32[]{:S(2)}) copy-start(s32[2]{0:T(128)} %param.13) | copy-start | bytes 28
  8.4 101.8 %collective-permute-start.12 = (bf16[2,128,1024]{1,2,0:T(8,128)(2,1)}, bf16[2,128,1024]{1,2,0:T(8,128)(2,1)}, u32[]{:S(2)}, u32[]{:S(2)}) collective-permute-start(bf16[2,128,1024]{1,2,0:T(8,128)(2,1)} %get-tuple-element.25), channel_id=1, source_target_pairs={{0,4},{4,8},{8,12},{12,16},{16,20},{20,24},{24,28},{1,5},{5,9},{9,... | collective-permute-start | bytes 1572872 | tf_op jit(solution)/shard_map/ppermute | solution.py:26
  10.4 99.8 %collective-permute-start.13 = (bf16[2,128,1024]{1,2,0:T(8,128)(2,1)}, bf16[2,128,1024]{1,2,0:T(8,128)(2,1)}, u32[]{:S(2)}, u32[]{:S(2)}) collective-permute-start(bf16[2,128,1024]{1,2,0:T(8,128)(2,1)} %get-tuple-element.26), channel_id=1, source_target_pairs={{4,0},{8,4},{12,8},{16,12},{20,16},{24,20},{28,24},{5,1},{9,5},{13... | collective-permute-start | bytes 1572872 | tf_op jit(solution)/shard_map/ppermute | solution.py:28
  16.9 6.5 %copy-start.7 = (pred[2]{0:T(512)(128)(4,1)}, pred[2]{0:T(512)(128)(4,1)S(1)}, u32[]{:S(2)}) copy-start(pred[2]{0:T(512)(128)(4,1)S(1)} %fusion.86) | copy-start | bytes 10
  23.4 1.0 copy-start.3
  24.4 10.8 %collective-permute-start = (bf16[192,1024]{1,0:T(8,128)(2,1)}, bf16[192,1024]{1,0:T(8,128)(2,1)S(1)}, u32[]{:S(2)}, u32[]{:S(2)}) collective-permute-start(bf16[192,1024]{1,0:T(8,128)(2,1)} %dynamic-slice_bitcast_fusion), channel_id=1, source_target_pairs={{0,4},{4,0},{8,12},{12,8},{16,20},{20,16},{24,28},{28,24},{1,5},{5... | collective-permute-start | bytes 1179656 | tf_op jit(solution)/shard_map/ppermute | solution.py:105
  30.1 5.0 %copy-start.11 = (s32[8]{0:T(128)S(1)}, s32[8]{0:T(128)}, u32[]{:S(2)}) copy-start(s32[8]{0:T(128)} %param.15) | copy-start | bytes 100
  30.1 5.1 %copy-start.4 = (bf16[2,192,1024]{2,1,0:T(8,128)(2,1)S(1)}, bf16[2,192,1024]{2,1,0:T(8,128)(2,1)}, u32[]{:S(2)}) copy-start(bf16[2,192,1024]{2,1,0:T(8,128)(2,1)} %copy-done.3) | copy-start | bytes 2359300
  30.1 112.7 %all-to-all-start = ((bf16[2,8,2,64,1024]{4,3,0,2,1:T(8,128)(2,1)}), bf16[2,8,2,64,1024]{4,3,0,2,1:T(8,128)(2,1)}, u32[]{:S(2)}, u32[]{:S(2)}) async-start(bf16[2,8,2,64,1024]{4,3,0,2,1:T(8,128)(2,1)} %bitcast.272), calls=%async_computation | async-start | bytes 8388608 | tf_op jit(solution)/shard_map/all_to_all | solution.py:211
  35.1 63.4 %copy-start.8 = (pred[2]{0:T(512)(128)(4,1)S(1)}, pred[2]{0:T(512)(128)(4,1)}, u32[]{:S(2)}) copy-start(pred[2]{0:T(512)(128)(4,1)} %copy-done.7) | copy-start | bytes 10
  35.3 50.6 %collective-permute-start.1 = (bf16[96,1024]{1,0:T(8,128)(2,1)S(1)}, bf16[96,1024]{1,0:T(8,128)(2,1)S(1)}, u32[]{:S(2)}, u32[]{:S(2)}) collective-permute-start(bf16[96,1024]{1,0:T(8,128)(2,1)S(1)} %dynamic-slice_bitcast_fusion.3), channel_id=1, source_target_pairs={{0,8},{4,12},{8,0},{12,4},{16,24},{20,28},{24,16},{28,20},{1,9},{5... | collective-permute-start | bytes 589832 | tf_op jit(solution)/shard_map/ppermute | solution.py:105
  85.9 5.5 %collective-permute-start.2 = (bf16[48,1024]{1,0:T(8,128)(2,1)S(1)}, bf16[48,1024]{1,0:T(8,128)(2,1)S(1)}, u32[]{:S(2)}, u32[]{:S(2)}) collective-permute-start(bf16[48,1024]{1,0:T(8,128)(2,1)S(1)} %dynamic-slice_bitcast_fusion.6), channel_id=1, source_target_pairs={{0,16},{4,20},{8,24},{12,28},{16,0},{20,4},{24,8},{28,12},{1,17},{... | collective-permute-start | bytes 294920 | tf_op jit(solution)/shard_map/ppermute | solution.py:105
  91.5 4.7 %collective-permute-start.3 = (bf16[48,1024]{1,0:T(8,128)(2,1)S(1)}, bf16[48,1024]{1,0:T(8,128)(2,1)S(1)}, u32[]{:S(2)}, u32[]{:S(2)}) collective-permute-start(bf16[48,1024]{1,0:T(8,128)(2,1)S(1)} %bitcast_add_fusion.2), channel_id=1, source_target_pairs={{0,16},{4,20},{8,24},{12,28},{16,0},{20,4},{24,8},{28,12},{1,17},{... | collective-permute-start | bytes 294920 | tf_op jit(solution)/shard_map/ppermute | solution.py:109
  96.3 5.7 %collective-permute-start.4 = (bf16[96,1024]{1,0:T(8,128)(2,1)S(1)}, bf16[96,1024]{1,0:T(8,128)(2,1)S(1)}, u32[]{:S(2)}, u32[]{:S(2)}) collective-permute-start(bf16[96,1024]{1,0:T(8,128)(2,1)S(1)} %get-tuple-element.45), channel_id=1, source_target_pairs={{0,8},{4,12},{8,0},{12,4},{16,24},{20,28},{24,16},{28,20},{1,9},{5... | collective-permute-start | bytes 589832 | tf_op jit(solution)/shard_map/ppermute | solution.py:109
  102.3 3.6 %collective-permute-start.5 = (bf16[192,1024]{1,0:T(8,128)(2,1)S(1)}, bf16[192,1024]{1,0:T(8,128)(2,1)S(1)}, u32[]{:S(2)}, u32[]{:S(2)}) collective-permute-start(bf16[192,1024]{1,0:T(8,128)(2,1)S(1)} %get-tuple-element.33), channel_id=1, source_target_pairs={{0,4},{4,0},{8,12},{12,8},{16,20},{20,16},{24,28},{28,24},{1,5},{5... | collective-permute-start | bytes 1179656 | tf_op jit(solution)/shard_map/ppermute | solution.py:109
  109.7 7.5 %collective-permute-start.6 = (f32[64,1152]{1,0:T(8,128)}, f32[64,1152]{1,0:T(8,128)}, u32[]{:S(2)}, u32[]{:S(2)}) collective-permute-start(f32[64,1152]{1,0:T(8,128)} %get-tuple-element.32), channel_id=1, source_target_pairs={{0,4},{4,0},{8,12},{12,8},{16,20},{20,16},{24,28},{28,24},{1,5},{5... | collective-permute-start | bytes 884744 | tf_op jit(solution)/shard_map/ppermute | solution.py:105
  119.7 5.8 %collective-permute-start.7 = (f32[32,1152]{1,0:T(8,128)S(1)}, f32[32,1152]{1,0:T(8,128)S(1)}, u32[]{:S(2)}, u32[]{:S(2)}) collective-permute-start(f32[32,1152]{1,0:T(8,128)S(1)} %get-tuple-element.42), channel_id=1, source_target_pairs={{0,8},{4,12},{8,0},{12,4},{16,24},{20,28},{24,16},{28,20},{1,9},{5... | collective-permute-start | bytes 442376 | tf_op jit(solution)/shard_map/ppermute | solution.py:105
  125.9 14.8 %copy-start.5 = (bf16[192,1024]{1,0:T(8,128)(2,1)S(1)}, bf16[192,1024]{1,0:T(8,128)(2,1)}, u32[]{:S(2)}) copy-start(bf16[192,1024]{1,0:T(8,128)(2,1)} %get-tuple-element.27) | copy-start | bytes 1179652
  126.0 4.4 %collective-permute-start.8 = (f32[16,1152]{1,0:T(8,128)S(1)}, f32[16,1152]{1,0:T(8,128)S(1)}, u32[]{:S(2)}, u32[]{:S(2)}) collective-permute-start(f32[16,1152]{1,0:T(8,128)S(1)} %get-tuple-element.54), channel_id=1, source_target_pairs={{0,16},{4,20},{8,24},{12,28},{16,0},{20,4},{24,8},{28,12},{1,17},{... | collective-permute-start | bytes 221192 | tf_op jit(solution)/shard_map/ppermute | solution.py:105
  130.8 4.4 %collective-permute-start.9 = (f32[16,1152]{1,0:T(8,128)S(1)}, f32[16,1152]{1,0:T(8,128)S(1)}, u32[]{:S(2)}, u32[]{:S(2)}) collective-permute-start(f32[16,1152]{1,0:T(8,128)S(1)} %concatenate.72), channel_id=1, source_target_pairs={{0,16},{4,20},{8,24},{12,28},{16,0},{20,4},{24,8},{28,12},{1,17},{... | collective-permute-start | bytes 221192 | tf_op jit(solution)/shard_map/ppermute | solution.py:109
  135.3 5.2 %collective-permute-start.10 = (f32[32,1152]{1,0:T(8,128)S(1)}, f32[32,1152]{1,0:T(8,128)S(1)}, u32[]{:S(2)}, u32[]{:S(2)}) collective-permute-start(f32[32,1152]{1,0:T(8,128)S(1)} %get-tuple-element.49), channel_id=1, source_target_pairs={{0,8},{4,12},{8,0},{12,4},{16,24},{20,28},{24,16},{28,20},{1,9},{5... | collective-permute-start | bytes 442376 | tf_op jit(solution)/shard_map/ppermute | solution.py:109
  140.6 1.8 collective-permute-start.11
  162.3 4.1 %copy-start = (bf16[1,4,10,64,1024]{4,3,2,1,0:T(8,128)(2,1)S(1)}, bf16[1,4,10,64,1024]{4,3,2,1,0:T(8,128)(2,1)}, u32[]{:S(2)}) copy-start(bf16[1,4,10,64,1024]{4,3,2,1,0:T(8,128)(2,1)} %get-tuple-element.20) | copy-start | bytes 15728644
  166.4 1.4 copy-start.2
  166.4 1.4 copy-start.6
  170.3 5.0 %slice-start = ((s8[8388608]{0:T(1024)(128)(4,1)}), s8[4194304]{0:T(1024)(128)(4,1)S(1)}, s32[]{:S(2)}) async-start(s8[8388608]{0:T(1024)(128)(4,1)} %bitcast.324), calls=%async_computation.2 | async-start | bytes 8388608
  171.9 3.3 %slice-start.1 = ((s8[8388608]{0:T(1024)(128)(4,1)}), s8[4194304]{0:T(1024)(128)(4,1)S(1)}, s32[]{:S(2)}) async-start(s8[8388608]{0:T(1024)(128)(4,1)} %bitcast.324), calls=%async_computation.3 | async-start | bytes 8388608
  172.0 3.3 %copy-start.12 = (pred[256]{0:T(512)(128)(4,1)S(1)}, pred[256]{0:T(512)(128)(4,1)}, u32[]{:S(2)}) copy-start(pred[256]{0:T(512)(128)(4,1)} %broadcast_in_dim.175) | copy-start | bytes 772

commit v4 on v3

--- a/solution.py
+++ b/solution.py
@@ -151,6 +151,39 @@
 def sum_over_head(partial):
     gathered = lax.all_to_all(partial, "head", 0, 0, tiled=True)
     return jnp.sum(gathered.astype(jnp.float32), axis=0).T
+
+
+def partial_attend(query_blocks, key_blocks, value_blocks, valid_slots):
+    count_q, slot_count = (key_blocks.shape[0], key_blocks.shape[1])
+    heads_here = query_blocks.shape[-1] // HEAD_DIM
+    query_grid = query_blocks.reshape(count_q, BLOCK, heads_here, HEAD_DIM)
+    key_grid = key_blocks.reshape(count_q, slot_count * BLOCK, heads_here, HEAD_DIM)
+    value_grid = value_blocks.reshape(count_q, slot_count * BLOCK, heads_here, HEAD_DIM)
+    scores = jnp.einsum(
+        "bqhd,bshd->bhqs", query_grid, key_grid, preferred_element_type=jnp.float32
+    ) * (1.0 / math.sqrt(HEAD_DIM))
+    present = jnp.repeat(jnp.transpose(valid_slots, (0, 2, 1)), BLOCK, axis=2)[:, :, None, :]
+    scores = jnp.where(present, scores, masked_score)
+    peak = jnp.max(scores, axis=3)
+    expo = jnp.exp(scores - peak[..., None])
+    total = jnp.sum(expo, axis=3)
+    mixture = jnp.einsum(
+        "bhqs,bshd->bqhd", expo.astype(jnp.bfloat16), value_grid, preferred_element_type=jnp.float32
+    )
+    return mixture, total, peak
+
+
+def merge_attend(first, second):
+    mix_a, total_a, peak_a = first
+    mix_b, total_b, peak_b = second
+    peak = jnp.maximum(peak_a, peak_b)
+    scale_a = jnp.exp(peak_a - peak)
+    scale_b = jnp.exp(peak_b - peak)
+    total = total_a * scale_a + total_b * scale_b
+    mix = mix_a * jnp.transpose(scale_a, (0, 2, 1))[..., None] + mix_b * jnp.transpose(scale_b, (0, 2, 1))[..., None]
+    mix = mix / jnp.transpose(total, (0, 2, 1))[..., None]
+    count_q = mix.shape[0]
+    return mix.reshape(count_q, BLOCK, -1).astype(jnp.bfloat16)
 
 
 def on_device(
@@ -192,26 +225,6 @@
     masked = jnp.where(mine_global[None, :, None, None], picked, jnp.zeros_like(picked))
     shared = tree_reduce(masked.reshape(3 * GLOB * BLOCK, width_here), add_merge, "seq")
     shared = shared.reshape(3, GLOB, BLOCK, width_here)
-    slot_total = blocks_here * RAND
-    capacity = (slot_total + seq_count - 1) // seq_count
-    flat_ids = random_blocks.reshape(seq_count, slot_total)
-    owners = flat_ids // blocks_here
-    slot_order = jnp.arange(slot_total)
-    same_owner = (owners[:, :, None] == owners[:, None, :]) & (
-        slot_order[None, None, :] < slot_order[None, :, None]
-    )
-    ranks = jnp.sum(same_owner.astype(jnp.int32), axis=2)
-    local_ids = flat_ids - owners * blocks_here
-    wanted = (owners[:, None, :] == seq_place) & (
-        ranks[:, None, :] == jnp.arange(capacity)[None, :, None]
-    )
-    send_local = jnp.sum(jnp.where(wanted, local_ids[:, None, :], 0), axis=2)
-    kv_blocks = pair_kv.reshape(2, blocks_here, BLOCK, width_here)
-    outgoing = kv_blocks[:, send_local]
-    incoming = lax.all_to_all(outgoing, "seq", split_axis=1, concat_axis=1, tiled=True)
-    my_owners = owners[seq_place]
-    my_ranks = ranks[seq_place]
-    random_kv = incoming[:, my_owners, my_ranks].reshape(2, blocks_here, RAND, BLOCK, width_here)
     slot_parts = [
         padded_blocks[:, offset_slot : offset_slot + blocks_here][:, :, None]
         for offset_slot in range(2 * WMAX + 1)
@@ -219,12 +232,10 @@
     slot_parts.append(
         jnp.broadcast_to(shared[1:3][:, None], (2, blocks_here, GLOB, BLOCK, width_here))
     )
-    slot_parts.append(random_kv)
-    all_kv = jnp.concatenate(slot_parts, axis=2)
-    all_valid = jnp.concatenate(
-        [window_valid, jnp.ones((blocks_here, GLOB + RAND, heads_here), dtype=bool)], axis=1
-    )
-    attended = block_attend(query_view, all_kv[0], all_kv[1], all_valid)
+    near_kv = jnp.concatenate(slot_parts, axis=2)
+    near_valid = jnp.concatenate(
+        [window_valid, jnp.ones((blocks_here, GLOB, heads_here), dtype=bool)], axis=1
+    )
     global_query = shared[0]
     key_later = key_rot
     value_later = values
@@ -251,6 +262,32 @@
         axis=1,
     )
     reduced = tree_reduce(packed, softmax_merge, "seq")
+    slot_total = blocks_here * RAND
+    capacity = (slot_total + seq_count - 1) // seq_count
+    flat_ids = random_blocks.reshape(seq_count, slot_total)
+    owners = flat_ids // blocks_here
+    slot_order = jnp.arange(slot_total)
+    same_owner = (owners[:, :, None] == owners[:, None, :]) & (
+        slot_order[None, None, :] < slot_order[None, :, None]
+    )
+    ranks = jnp.sum(same_owner.astype(jnp.int32), axis=2)
+    local_ids = flat_ids - owners * blocks_here
+    wanted = (owners[:, None, :] == seq_place) & (
+        ranks[:, None, :] == jnp.arange(capacity)[None, :, None]
+    )
+    send_local = jnp.sum(jnp.where(wanted, local_ids[:, None, :], 0), axis=2)
+    kv_blocks = pair_kv.reshape(2, blocks_here, BLOCK, width_here)
+    outgoing = kv_blocks[:, send_local]
+    outgoing, reduced = lax.optimization_barrier((outgoing, reduced))
+    incoming = lax.all_to_all(outgoing, "seq", split_axis=1, concat_axis=1, tiled=True)
+    my_owners = owners[seq_place]
+    my_ranks = ranks[seq_place]
+    random_kv = incoming[:, my_owners, my_ranks].reshape(2, blocks_here, RAND, BLOCK, width_here)
+    near_part = partial_attend(query_view, near_kv[0], near_kv[1], near_valid)
+    far_part = partial_attend(
+        query_view, random_kv[0], random_kv[1], jnp.ones((blocks_here, RAND, heads_here), dtype=bool)
+    )
+    attended = merge_attend(near_part, far_part)
     mix_sum = reduced[:, :width_here].reshape(row_total, heads_here, HEAD_DIM)
     total_sum = reduced[:, width_here : width_here + heads_here]
     global_out = (mix_sum / total_sum[..., None]).reshape(row_total, width_here).astype(jnp.bfloat16)

time: 235 us -> 223 us (0.949)
  waiting for transfers between devices: 66.6 us -> 55.6 us
  local copies, waits for them, and re-layouts: 59.8 us -> 54.9 us
  other arithmetic: 20.1 us -> 24.7 us
    ppermute x6, waiting for transfers between devices: 57 us -> 19.9 us  [tree_reduce(): got = lax.ppermute(send, axis, xor_perm(count, bit))]
    all_to_all x1, waiting for transfers between devices: 0.01 us -> 29.7 us  [on_device(): lax.all_to_all(outgoing, 'seq', split_axis=1, concat_axis=1, tiled=True)]
    slice x1 -> x4, local copies, waits for them, and re-layouts: 10.2 us -> 1.92 us  [the longest x1 1.52 us: on_device(): near_part = partial_attend(query_view, near_kv[0], near_kv[1], near_valid)]
    gather x1 -> x2, local copies, waits for them, and re-layouts: 2.79 us -> 7.72 us  [on_device(): outgoing = kv_blocks[:, send_local]]
    all_to_all x0 -> x1, local copies, waits for them, and re-layouts: none -> 4.88 us  [on_device(): lax.all_to_all(outgoing, 'seq', split_axis=1, concat_axis=1, tiled=True)]
    gather x2 -> x1, local copies, waits for them, and re-layouts: 7 us -> 2.94 us  [on_device(): incoming[:, my_owners, my_ranks]]
    ppermute x6, waiting for transfers between devices: 9.6 us -> 6.07 us  [tree_reduce(): got = lax.ppermute(parts, axis, xor_perm(count, bit))]
    unnamed x45 -> x54, local copies, waits for them, and re-layouts: 15.7 us -> 13.5 us
  transfers between devices with their start and end apart: 15 -> 15, of which waited for: 8 -> 10; matrix products, arithmetic and copies ran while one was open for 19% -> 25% of each run, Pallas kernels for 0% -> 0%
where the time goes in v4:
time: 223 us; the launch traced here: 222 us
  waiting for transfers between devices  55.6 us (25%)
  local copies, waits for them, and re-layouts  54.9 us (25%)
  blocking collectives  53.1 us (24%)
  other arithmetic  24.7 us (11%)
  starting transfers between devices  20.3 us (9%)
  matrix products  10.7 us (5%)
  between operations  2.34 us (1%)
    all_to_all x1, blocking collectives, sum_over_head(): gathered = lax.all_to_all(partial, 'head', 0, 0, tiled=True)  53.1 us
    all_to_all x1, waiting for transfers between devices, on_device(): lax.all_to_all(outgoing, 'seq', split_axis=1, concat_axis=1, tiled=True)  29.7 us
    ppermute x6, waiting for transfers between devices, tree_reduce(): got = lax.ppermute(send, axis, xor_perm(count, bit))  19.9 us
    unnamed x54, local copies, waits for them, and re-layouts  13.5 us
    gather x2, local copies, waits for them, and re-layouts, on_device(): outgoing = kv_blocks[:, send_local]  7.72 us
    convert_element_type x8, local copies, waits for them, and re-layouts, rotate(): return turned.reshape(row_count, row_width).astype(jnp.bfloat16)  7.54 us
    ppermute x6, waiting for transfers between devices, tree_reduce(): got = lax.ppermute(parts, axis, xor_perm(count, bit))  6.07 us
    ppermute x6, starting transfers between devices, tree_reduce(): got = lax.ppermute(parts, axis, xor_perm(count, bit))  5.76 us
  transfers between devices with their start and end apart: 15, of which 10 were waited for; matrix products, arithmetic and copies ran while one was open for 25% of the time, Pallas kernels for 0%

profile of v4, /device:TPU:2, one launch (start us, length us, event | category | flops | bytes accessed | tf_op | source)
XLA Modules:
  0.0 221.7 jit_solution(2950269400499776147)
XLA Ops:
  0.0 0.8 copy.144
  2.3 1.2 copy.142
  3.6 1.2 copy.149
  8.7 1.3 copy.178
  11.2 1.6 gather_fusion.1
  13.9 1.7 collective-permute-done
  15.8 6.9 %collective-permute-done.1 = bf16[96,1024]{1,0:T(8,128)(2,1)S(1)} collective-permute-done((bf16[96,1024]{1,0:T(8,128)(2,1)S(1)}, bf16[96,1024]{1,0:T(8,128)(2,1)S(1)}, u32[]{:S(2)}, u32[]{:S(2)}) %collective-permute-start.1) | collective-permute-done | bytes 196640 | tf_op jit(solution)/shard_map/ppermute | solution.py:105
  22.7 1.6 collective-permute-start.2
  24.3 3.1 %collective-permute-done.2 = bf16[48,1024]{1,0:T(8,128)(2,1)S(1)} collective-permute-done((bf16[48,1024]{1,0:T(8,128)(2,1)S(1)}, bf16[48,1024]{1,0:T(8,128)(2,1)S(1)}, u32[]{:S(2)}, u32[]{:S(2)}) %collective-permute-start.2) | collective-permute-done | bytes 98336 | tf_op jit(solution)/shard_map/ppermute | solution.py:105
  27.4 1.6 collective-permute-start.3
  29.0 3.1 %collective-permute-done.3 = bf16[48,1024]{1,0:T(8,128)(2,1)S(1)} collective-permute-done((bf16[48,1024]{1,0:T(8,128)(2,1)S(1)}, bf16[48,1024]{1,0:T(8,128)(2,1)S(1)}, u32[]{:S(2)}, u32[]{:S(2)}) %collective-permute-start.3) | collective-permute-done | bytes 98336 | tf_op jit(solution)/shard_map/ppermute | solution.py:109
  32.8 1.2 fusion.55
  34.0 1.9 collective-permute-start.12
  35.9 3.6 %collective-permute-start.13 = (bf16[2,128,1024]{1,2,0:T(8,128)(2,1)}, bf16[2,128,1024]{1,2,0:T(8,128)(2,1)}, u32[]{:S(2)}, u32[]{:S(2)}) collective-permute-start(bf16[2,128,1024]{1,2,0:T(8,128)(2,1)} %get-tuple-element.35), channel_id=1, source_target_pairs={{4,0},{8,4},{12,8},{16,12},{20,16},{24,20},{28,24},{5,1},{9,5},{13... | collective-permute-start | bytes 1572872 | tf_op jit(solution)/shard_map/ppermute | solution.py:28
  39.5 0.9 copy.188
  40.7 1.1 collective-permute-start.5
  43.2 1.0 fusion.66
  44.9 1.1 fusion.52
  45.9 0.7 copy.157
  46.7 1.4 copy.156
  48.1 1.4 convolution_bitcast_fusion
  49.5 0.8 copy.245
  50.4 1.2 concatenate.63
  54.6 5.5 %collective-permute-done.7 = f32[32,1152]{1,0:T(8,128)S(1)} collective-permute-done((f32[32,1152]{1,0:T(8,128)S(1)}, f32[32,1152]{1,0:T(8,128)S(1)}, u32[]{:S(2)}, u32[]{:S(2)}) %collective-permute-start.7) | collective-permute-done | bytes 147488 | tf_op jit(solution)/shard_map/ppermute | solution.py:105
  60.6 1.5 collective-permute-start.8
  62.7 2.3 %collective-permute-done.8 = f32[16,1152]{1,0:T(8,128)S(1)} collective-permute-done((f32[16,1152]{1,0:T(8,128)S(1)}, f32[16,1152]{1,0:T(8,128)S(1)}, u32[]{:S(2)}, u32[]{:S(2)}) %collective-permute-start.8) | collective-permute-done | bytes 73760 | tf_op jit(solution)/shard_map/ppermute | solution.py:105
  65.4 1.5 collective-permute-start.9
  67.5 2.3 %collective-permute-done.9 = f32[16,1152]{1,0:T(8,128)S(1)} collective-permute-done((f32[16,1152]{1,0:T(8,128)S(1)}, f32[16,1152]{1,0:T(8,128)S(1)}, u32[]{:S(2)}, u32[]{:S(2)}) %collective-permute-start.9) | collective-permute-done | bytes 73760 | tf_op jit(solution)/shard_map/ppermute | solution.py:109
  69.8 0.7 pad_maximum_fusion.9
  70.5 1.2 collective-permute-start.10
  71.7 1.8 compare_and_fusion.1
  73.9 1.3 copy.177
  75.5 1.1 pad_maximum_fusion.1
  76.6 1.0 fusion.80
  77.6 0.7 pad_maximum_fusion.7
  79.1 1.3 compare_and_fusion
  80.4 1.4 reshape.543
  81.8 1.6 copy.166
  83.5 0.8 broadcast_in_dim.199
  85.0 2.8 %gather_fusion = bf16[16,2,64,1024]{3,2,1,0:T(8,128)(2,1)} fusion(bf16[2,4,64,1024]{3,2,1,0:T(8,128)(2,1)S(1)} %pad_maximum_fusion.1, s32[1024]{0:T(1024)S(1)} %copy-done.10), kind=kCustom, calls=%fused_computation | custom fusion | bytes 8388672 | tf_op jit(solution)/shard_map/gather | solution.py:280
  87.8 4.9 %copy.243 = bf16[8,2,2,64,1024]{4,3,1,2,0:T(8,128)(2,1)} copy(bf16[8,2,2,64,1024]{4,3,2,1,0:T(8,128)(2,1)} %bitcast.311) | data formatting | bytes 8388608 | tf_op jit(solution)/shard_map/gather | solution.py:280
  93.0 1.0 fusion.71
  94.0 0.9 pad_maximum_fusion.3
  94.9 5.3 %all-to-all-start = ((bf16[2,8,2,64,1024]{4,3,2,0,1:T(8,128)(2,1)}), bf16[2,8,2,64,1024]{4,3,2,0,1:T(8,128)(2,1)}, u32[]{:S(2)}, u32[]{:S(2)}) async-start(bf16[2,8,2,64,1024]{4,3,2,0,1:T(8,128)(2,1)} %bitcast.310), calls=%async_computation | async-start | bytes 8388608 | tf_op jit(solution)/shard_map/all_to_all | solution.py:282
  100.2 2.8 %pad_maximum_fusion = bf16[2,512,1024]{1,2,0:T(8,128)(2,1)} fusion(bf16[2,128,1024]{1,2,0:T(8,128)(2,1)} %collective-permute-done.13, bf16[1,256,1024]{1,2,0:T(8,128)(2,1)S(1)} %bitcast.324, bf16[1,256,1024]{1,2,0:T(8,128)(2,1)S(1)} %bitcast.306, bf16[2,128,1024]{1,2,0:T(8,128)(2,1)} %collective-permute-done.12), kind=kLoop, calls=%fused_computation.17 | loop fusion | flops 8388608 | bytes 4194304 | tf_op jit(solution)/shard_map/concatenate | solution.py:24
  103.0 3.0 %copy.159 = bf16[2,512,1024]{2,1,0:T(8,128)(2,1)S(1)} copy(bf16[2,512,1024]{1,2,0:T(8,128)(2,1)} %pad_maximum_fusion) | data formatting | bytes 4194304 | tf_op jit(solution)/shard_map/concatenate | solution.py:24
  106.4 0.8 copy-done.7
  107.4 1.5 fusion.124
  109.0 1.0 copy.196
  109.9 2.7 %copy.197 = bf16[224,8,8,128]{3,2,1,0:T(8,128)(2,1)} copy(bf16[224,8,8,128]{3,1,2,0:T(8,128)(2,1)S(1)} %bitcast.312) | data formatting | bytes 7340032
  112.7 1.8 fusion
  114.6 2.0 copy-done
  116.6 1.5 fusion.5
  118.5 29.7 %all-to-all-done = bf16[2,8,2,64,1024]{4,3,2,0,1:T(8,128)(2,1)} async-done(((bf16[2,8,2,64,1024]{4,3,2,0,1:T(8,128)(2,1)}), bf16[2,8,2,64,1024]{4,3,2,0,1:T(8,128)(2,1)}, u32[]{:S(2)}, u32[]{:S(2)}) %all-to-all-start) | async-done | bytes 4194336 | tf_op jit(solution)/shard_map/all_to_all | solution.py:282
  148.1 4.9 %copy.169 = bf16[2,8,2,64,1024]{4,3,2,1,0:T(8,128)(2,1)} copy(bf16[2,8,2,64,1024]{4,3,2,0,1:T(8,128)(2,1)} %all-to-all-done) | data formatting | bytes 8388608 | tf_op jit(solution)/shard_map/all_to_all | solution.py:282
  153.0 2.9 %gather_fusion.4 = bf16[12,2,64,1024]{3,2,1,0:T(8,128)(2,1)S(1)} fusion(bf16[2,8,2,64,1024]{4,3,2,1,0:T(8,128)(2,1)} %copy.169, s32[12]{0:T(128)S(1)} %fusion.112), kind=kCustom, calls=%fused_computation.4 | custom fusion | bytes 6291552 | tf_op jit(solution)/shard_map/gather | solution.py:285
  157.0 1.2 multiply_reduce_fusion
  158.7 0.8 fusion.12
  159.5 1.1 copy-done.1
  160.6 2.1 fusion.32
  162.7 1.4 fusion.40
  164.6 2.5 %convolution_convert_fusion = bf16[256,4096]{1,0:T(8,128)(2,1)S(1)} fusion(bf16[1024,4096]{1,0:T(8,128)(2,1)S(1)} %bitcast.367, bf16[256,1024]{1,0:T(8,128)(2,1)S(1)} %bitcast.348, bf16[256,1024]{1,0:T(8,128)(2,1)S(1)} %bitcast.349, bf16[32,8,8,128]{3,2,1,0:T(8,128)(2,1)S(1)} %bitcast.353, pred[256]{0:T(512)(128)(4,1)S(1)} %broadcast_in_dim.188, ...), kind=kOutput, calls=%fused_computation.5 | convolution fusion | flops 2149056512 | bytes 12059136 | tf_op jit(solution)/shard_map/dot_general | solution.py:145
  167.3 53.1 %all_to_all.10 = bf16[4,1024,256]{1,2,0:T(8,128)(2,1)S(1)} all-to-all(bf16[4,1024,256]{1,2,0:T(8,128)(2,1)S(1)} %bitcast.316), channel_id=1, replica_groups=mesh['seq'=8,'head'=4] {'head'}, dimensions={0} | all-to-all | bytes 4194304 | tf_op jit(solution)/shard_map/all_to_all | solution.py:152
  220.4 1.3 reduce_sum.71
  (155 shorter events, 19.6 us)
Async XLA Ops:
  0.9 6.0 %copy-start.9 = (s32[8,12]{1,0:T(8,128)}, s32[8,12]{1,0:T(8,128)S(1)}, u32[]{:S(2)}) copy-start(s32[8,12]{1,0:T(8,128)S(1)} %get-tuple-element.66) | copy-start | bytes 1156
  5.3 2.4 %copy-start.14 = (s32[2]{0:T(128)S(1)}, s32[2]{0:T(128)}, u32[]{:S(2)}) copy-start(s32[2]{0:T(128)} %param.13) | copy-start | bytes 28
  5.8 7.0 %copy-start.2 = (bf16[256,1024]{1,0:T(8,128)(2,1)S(1)}, bf16[256,1024]{1,0:T(8,128)(2,1)}, u32[]{:S(2)}) copy-start(bf16[256,1024]{1,0:T(8,128)(2,1)} %param.11) | copy-start | bytes 1572868
  7.7 5.9 %copy-start.12 = (pred[2]{0:T(512)(128)(4,1)}, pred[2]{0:T(512)(128)(4,1)S(1)}, u32[]{:S(2)}) copy-start(pred[2]{0:T(512)(128)(4,1)S(1)} %fusion.111) | copy-start | bytes 10
  13.8 1.8 collective-permute-start
  15.7 7.0 %collective-permute-start.1 = (bf16[96,1024]{1,0:T(8,128)(2,1)S(1)}, bf16[96,1024]{1,0:T(8,128)(2,1)S(1)}, u32[]{:S(2)}, u32[]{:S(2)}) collective-permute-start(bf16[96,1024]{1,0:T(8,128)(2,1)S(1)} %dynamic-slice_bitcast_fusion.3), channel_id=1, source_target_pairs={{0,8},{4,12},{8,0},{12,4},{16,24},{20,28},{24,16},{28,20},{1,9},{5... | collective-permute-start | bytes 589832 | tf_op jit(solution)/shard_map/ppermute | solution.py:105
  22.7 4.7 %collective-permute-start.2 = (bf16[48,1024]{1,0:T(8,128)(2,1)S(1)}, bf16[48,1024]{1,0:T(8,128)(2,1)S(1)}, u32[]{:S(2)}, u32[]{:S(2)}) collective-permute-start(bf16[48,1024]{1,0:T(8,128)(2,1)S(1)} %dynamic-slice_bitcast_fusion.6), channel_id=1, source_target_pairs={{0,16},{4,20},{8,24},{12,28},{16,0},{20,4},{24,8},{28,12},{1,17},{... | collective-permute-start | bytes 294920 | tf_op jit(solution)/shard_map/ppermute | solution.py:105
  27.4 4.7 %collective-permute-start.3 = (bf16[48,1024]{1,0:T(8,128)(2,1)S(1)}, bf16[48,1024]{1,0:T(8,128)(2,1)S(1)}, u32[]{:S(2)}, u32[]{:S(2)}) collective-permute-start(bf16[48,1024]{1,0:T(8,128)(2,1)S(1)} %bitcast_add_fusion.2), channel_id=1, source_target_pairs={{0,16},{4,20},{8,24},{12,28},{16,0},{20,4},{24,8},{28,12},{1,17},{... | collective-permute-start | bytes 294920 | tf_op jit(solution)/shard_map/ppermute | solution.py:109
  32.2 8.2 %collective-permute-start.4 = (bf16[96,1024]{1,0:T(8,128)(2,1)S(1)}, bf16[96,1024]{1,0:T(8,128)(2,1)S(1)}, u32[]{:S(2)}, u32[]{:S(2)}) collective-permute-start(bf16[96,1024]{1,0:T(8,128)(2,1)S(1)} %get-tuple-element.54), channel_id=1, source_target_pairs={{0,8},{4,12},{8,0},{12,4},{16,24},{20,28},{24,16},{28,20},{1,9},{5... | collective-permute-start | bytes 589832 | tf_op jit(solution)/shard_map/ppermute | solution.py:109
  34.0 66.2 %collective-permute-start.12 = (bf16[2,128,1024]{1,2,0:T(8,128)(2,1)}, bf16[2,128,1024]{1,2,0:T(8,128)(2,1)}, u32[]{:S(2)}, u32[]{:S(2)}) collective-permute-start(bf16[2,128,1024]{1,2,0:T(8,128)(2,1)} %get-tuple-element.34), channel_id=1, source_target_pairs={{0,4},{4,8},{8,12},{12,16},{16,20},{20,24},{24,28},{1,5},{5,9},{9,... | collective-permute-start | bytes 1572872 | tf_op jit(solution)/shard_map/ppermute | solution.py:26
  35.9 64.3 %collective-permute-start.13 = (bf16[2,128,1024]{1,2,0:T(8,128)(2,1)}, bf16[2,128,1024]{1,2,0:T(8,128)(2,1)}, u32[]{:S(2)}, u32[]{:S(2)}) collective-permute-start(bf16[2,128,1024]{1,2,0:T(8,128)(2,1)} %get-tuple-element.35), channel_id=1, source_target_pairs={{4,0},{8,4},{12,8},{16,12},{20,16},{24,20},{28,24},{5,1},{9,5},{13... | collective-permute-start | bytes 1572872 | tf_op jit(solution)/shard_map/ppermute | solution.py:28
  40.7 2.5 %collective-permute-start.5 = (bf16[192,1024]{1,0:T(8,128)(2,1)S(1)}, bf16[192,1024]{1,0:T(8,128)(2,1)S(1)}, u32[]{:S(2)}, u32[]{:S(2)}) collective-permute-start(bf16[192,1024]{1,0:T(8,128)(2,1)S(1)} %get-tuple-element.42), channel_id=1, source_target_pairs={{0,4},{4,0},{8,12},{12,8},{16,20},{20,16},{24,28},{28,24},{1,5},{5... | collective-permute-start | bytes 1179656 | tf_op jit(solution)/shard_map/ppermute | solution.py:109
  49.5 4.5 %copy-start.15 = (pred[4,5]{1,0:T(4,128)(4,1)S(1)}, pred[4,5]{1,0:T(4,128)(4,1)}, u32[]{:S(2)}) copy-start(pred[4,5]{1,0:T(4,128)(4,1)} %fusion.103) | copy-start | bytes 64
  49.5 4.5 %copy-start.13 = (pred[2]{0:T(512)(128)(4,1)S(1)}, pred[2]{0:T(512)(128)(4,1)}, u32[]{:S(2)}) copy-start(pred[2]{0:T(512)(128)(4,1)} %copy-done.12) | copy-start | bytes 10
  50.4 11.7 %copy-start.11 = (s32[2]{0:T(128)S(1)}, s32[2]{0:T(128)}, u32[]{:S(2)}) copy-start(s32[2]{0:T(128)} %get-tuple-element.25) | copy-start | bytes 28
  51.6 1.6 collective-permute-start.6
  53.9 6.2 %collective-permute-start.7 = (f32[32,1152]{1,0:T(8,128)S(1)}, f32[32,1152]{1,0:T(8,128)S(1)}, u32[]{:S(2)}, u32[]{:S(2)}) collective-permute-start(f32[32,1152]{1,0:T(8,128)S(1)} %get-tuple-element.51), channel_id=1, source_target_pairs={{0,8},{4,12},{8,0},{12,4},{16,24},{20,28},{24,16},{28,20},{1,9},{5... | collective-permute-start | bytes 442376 | tf_op jit(solution)/shard_map/ppermute | solution.py:105
  60.6 4.4 %collective-permute-start.8 = (f32[16,1152]{1,0:T(8,128)S(1)}, f32[16,1152]{1,0:T(8,128)S(1)}, u32[]{:S(2)}, u32[]{:S(2)}) collective-permute-start(f32[16,1152]{1,0:T(8,128)S(1)} %get-tuple-element.63), channel_id=1, source_target_pairs={{0,16},{4,20},{8,24},{12,28},{16,0},{20,4},{24,8},{28,12},{1,17},{... | collective-permute-start | bytes 221192 | tf_op jit(solution)/shard_map/ppermute | solution.py:105
  65.4 4.4 %collective-permute-start.9 = (f32[16,1152]{1,0:T(8,128)S(1)}, f32[16,1152]{1,0:T(8,128)S(1)}, u32[]{:S(2)}, u32[]{:S(2)}) collective-permute-start(f32[16,1152]{1,0:T(8,128)S(1)} %concatenate.72), channel_id=1, source_target_pairs={{0,16},{4,20},{8,24},{12,28},{16,0},{20,4},{24,8},{28,12},{1,17},{... | collective-permute-start | bytes 221192 | tf_op jit(solution)/shard_map/ppermute | solution.py:109
  70.5 6.1 %collective-permute-start.10 = (f32[32,1152]{1,0:T(8,128)}, f32[32,1152]{1,0:T(8,128)}, u32[]{:S(2)}, u32[]{:S(2)}) collective-permute-start(f32[32,1152]{1,0:T(8,128)} %get-tuple-element.58), channel_id=1, source_target_pairs={{0,8},{4,12},{8,0},{12,4},{16,24},{20,28},{24,16},{28,20},{1,9},{5... | collective-permute-start | bytes 442376 | tf_op jit(solution)/shard_map/ppermute | solution.py:109
  75.3 9.7 %copy-start.10 = (s32[1024]{0:T(1024)S(1)}, s32[1024]{0:T(1024)}, u32[]{:S(2)}) copy-start(s32[1024]{0:T(1024)} %get-tuple-element.81) | copy-start | bytes 12292
  78.4 14.6 %collective-permute-start.11 = (f32[64,1152]{1,0:T(8,128)}, f32[64,1152]{1,0:T(8,128)}, u32[]{:S(2)}, u32[]{:S(2)}) collective-permute-start(f32[64,1152]{1,0:T(8,128)} %get-tuple-element.46), channel_id=1, source_target_pairs={{0,4},{4,0},{8,12},{12,8},{16,20},{20,16},{24,28},{28,24},{1,5},{5... | collective-permute-start | bytes 884744 | tf_op jit(solution)/shard_map/ppermute | solution.py:109
  83.5 29.2 %copy-start.3 = (bf16[4,64,8,128]{3,1,2,0:T(8,128)(2,1)}, bf16[4,64,8,128]{3,1,2,0:T(8,128)(2,1)S(1)}, u32[]{:S(2)}) copy-start(bf16[4,64,8,128]{3,1,2,0:T(8,128)(2,1)S(1)} %copy.166) | copy-start | bytes 1572868
  87.8 4.9 %copy-start.16 = (pred[4]{0:T(512)(128)(4,1)S(1)}, pred[4]{0:T(512)(128)(4,1)}, u32[]{:S(2)}) copy-start(pred[4]{0:T(512)(128)(4,1)} %compare_and_fusion.1) | copy-start | bytes 16
  94.9 53.2 %all-to-all-start = ((bf16[2,8,2,64,1024]{4,3,2,0,1:T(8,128)(2,1)}), bf16[2,8,2,64,1024]{4,3,2,0,1:T(8,128)(2,1)}, u32[]{:S(2)}, u32[]{:S(2)}) async-start(bf16[2,8,2,64,1024]{4,3,2,0,1:T(8,128)(2,1)} %bitcast.310), calls=%async_computation | async-start | bytes 8388608 | tf_op jit(solution)/shard_map/all_to_all | solution.py:282
  106.1 1.0 copy-start.7
  109.9 2.8 %copy-start.8 = (pred[4,8,448]{2,1,0:T(8,128)(4,1)S(1)}, pred[4,8,448]{2,1,0:T(8,128)(4,1)}, u32[]{:S(2)}) copy-start(pred[4,8,448]{2,1,0:T(8,128)(4,1)} %broadcast_in_dim.200) | copy-start | bytes 43012
  114.5 2.0 copy-start
  114.5 3.6 %slice-start = ((f32[128,1152]{1,0:T(8,128)}), f32[128,8]{1,0:T(8,128)S(1)}, s32[]{:S(2)}) async-start(f32[128,1152]{1,0:T(8,128)} %pad_maximum_fusion.3), calls=%async_computation.2 | async-start | bytes 131072 | tf_op jit(solution)/shard_map/slice | solution.py:292
  114.5 3.8 %copy-start.6 = (f32[128,1152]{1,0:T(8,128)S(1)}, f32[128,1152]{1,0:T(8,128)}, u32[]{:S(2)}) copy-start(f32[128,1152]{1,0:T(8,128)} %pad_maximum_fusion.3) | copy-start | bytes 1769476
  156.0 1.0 copy-start.4
  157.0 2.5 %copy-start.5 = (bf16[224,8,8,128]{3,2,1,0:T(8,128)(2,1)S(1)}, bf16[224,8,8,128]{3,2,1,0:T(8,128)(2,1)}, u32[]{:S(2)}) copy-start(bf16[224,8,8,128]{3,2,1,0:T(8,128)(2,1)} %copy.197) | copy-start | bytes 11010052
  158.2 2.4 %copy-start.1 = (f32[4,8,64,448]{3,2,1,0:T(8,128)S(1)}, f32[4,8,64,448]{3,2,1,0:T(8,128)}, u32[]{:S(2)}) copy-start(f32[4,8,64,448]{3,2,1,0:T(8,128)} %copy-done) | copy-start | bytes 11010052
  158.7 5.9 %slice-start.1 = ((s8[8388608]{0:T(1024)(128)(4,1)}), s8[4194304]{0:T(1024)(128)(4,1)S(1)}, s32[]{:S(2)}) async-start(s8[8388608]{0:T(1024)(128)(4,1)} %bitcast.366), calls=%async_computation.3 | async-start | bytes 8388608
  160.6 4.0 %slice-start.2 = ((s8[8388608]{0:T(1024)(128)(4,1)}), s8[4194304]{0:T(1024)(128)(4,1)S(1)}, s32[]{:S(2)}) async-start(s8[8388608]{0:T(1024)(128)(4,1)} %bitcast.366), calls=%async_computation.4 | async-start | bytes 8388608

commit v5 on v4

--- a/solution.py
+++ b/solution.py
@@ -245,8 +245,8 @@
     global_scores = jnp.einsum(
         "gqhd,khd->gqhk", global_query, key_grid, preferred_element_type=jnp.float32
     ) * (1.0 / math.sqrt(HEAD_DIM))
-    local_peak = jnp.max(global_scores, axis=3)
-    expo = jnp.exp(global_scores - local_peak[..., None])
+    peak = lax.pmax(jnp.max(global_scores, axis=3), "seq")
+    expo = jnp.exp(global_scores - peak[..., None])
     partial_total = jnp.sum(expo, axis=3)
     partial_mix = jnp.einsum(
         "gqhk,khd->gqhd", expo.astype(jnp.bfloat16), value_grid, preferred_element_type=jnp.float32
@@ -256,12 +256,11 @@
         [
             partial_mix.reshape(row_total, width_here),
             partial_total.reshape(row_total, heads_here),
-            local_peak.reshape(row_total, heads_here),
-            jnp.zeros((row_total, 128 - 2 * heads_here), jnp.float32),
+            jnp.zeros((row_total, 128 - heads_here), jnp.float32),
         ],
         axis=1,
     )
-    reduced = tree_reduce(packed, softmax_merge, "seq")
+    reduced = lax.psum(packed, "seq")
     slot_total = blocks_here * RAND
     capacity = (slot_total + seq_count - 1) // seq_count
     flat_ids = random_blocks.reshape(seq_count, slot_total)
@@ -278,7 +277,7 @@
     send_local = jnp.sum(jnp.where(wanted, local_ids[:, None, :], 0), axis=2)
     kv_blocks = pair_kv.reshape(2, blocks_here, BLOCK, width_here)
     outgoing = kv_blocks[:, send_local]
-    outgoing, reduced = lax.optimization_barrier((outgoing, reduced))
+    outgoing, shared = lax.optimization_barrier((outgoing, shared))
     incoming = lax.all_to_all(outgoing, "seq", split_axis=1, concat_axis=1, tiled=True)
     my_owners = owners[seq_place]
     my_ranks = ranks[seq_place]
@@ -291,13 +290,14 @@
     mix_sum = reduced[:, :width_here].reshape(row_total, heads_here, HEAD_DIM)
     total_sum = reduced[:, width_here : width_here + heads_here]
     global_out = (mix_sum / total_sum[..., None]).reshape(row_total, width_here).astype(jnp.bfloat16)
-    global_out = global_out.reshape(GLOB, BLOCK, width_here)
+    mixed = sum_over_head(head_partials(attended.reshape(tok_here, width_here), out_weight))
+    global_mixed = sum_over_head(head_partials(global_out, out_weight)).reshape(GLOB, BLOCK, -1)
+    mixed = mixed.reshape(blocks_here, BLOCK, -1)
     block_index = jnp.arange(blocks_here)
     for global_slot in range(GLOB):
         hit = mine_global[global_slot] & (block_index == local_global[global_slot])
-        attended = jnp.where(hit[:, None, None], global_out[global_slot][None], attended)
-    mixed = sum_over_head(head_partials(attended.reshape(tok_here, width_here), out_weight))
-    return mixed.astype(jnp.bfloat16)
+        mixed = jnp.where(hit[:, None, None], global_mixed[global_slot][None], mixed)
+    return mixed.reshape(tok_here, -1).astype(jnp.bfloat16)
 
 
 def solution(mesh):

time: 223 us -> 292 us (1.31)
  waiting for transfers between devices: 55.6 us -> 140 us
  blocking collectives: 53.1 us -> 12.1 us
  between operations: 2.34 us -> 15.6 us
  matrix products: 10.7 us -> 16.3 us
  starting transfers between devices: 20.3 us -> 25.2 us
  other arithmetic: 24.7 us -> 21.2 us
  local copies, waits for them, and re-layouts: 54.9 us -> 58.4 us
    all_to_all x1 -> x0, blocking collectives: 53.1 us -> none  [sum_over_head(): gathered = lax.all_to_all(partial, 'head', 0, 0, tiled=True)]
    psum x0 -> x1, waiting for transfers between devices: none -> 48.9 us  [on_device(): reduced = lax.psum(packed, 'seq')]
    all_to_all x0 -> x2, waiting for transfers between devices: none -> 42.8 us  [sum_over_head(): gathered = lax.all_to_all(partial, 'head', 0, 0, tiled=True)]
    all_to_all x1, waiting for transfers between devices: 29.7 us -> 0.01 us  [on_device(): lax.all_to_all(outgoing, 'seq', split_axis=1, concat_axis=1, tiled=True)]
    ppermute x6 -> x3, waiting for transfers between devices: 19.9 us -> 40.1 us  [tree_reduce(): got = lax.ppermute(send, axis, xor_perm(count, bit))]
    pmax x0 -> x1, blocking collectives: none -> 12.1 us  [on_device(): peak = lax.pmax(jnp.max(global_scores, axis=3), 'seq')]
    all_to_all x0 -> x2, starting transfers between devices: none -> 8.55 us  [sum_over_head(): gathered = lax.all_to_all(partial, 'head', 0, 0, tiled=True)]
    dot_general x1 -> x2, matrix products: 2.47 us -> 7.29 us  [head_partials(): lax.dot_general(out_weight, rows, (((0,), (1,)), ((), ())), preferred_ele...]
  transfers between devices with their start and end apart: 15 -> 12, of which waited for: 10 -> 8; matrix products, arithmetic and copies ran while one was open for 25% -> 29% of each run, Pallas kernels for 0% -> 0%
where the time goes in v5:
time: 292 us; the launch traced here: 289 us
  waiting for transfers between devices  140 us (48%)
  local copies, waits for them, and re-layouts  58.4 us (20%)
  starting transfers between devices  25.2 us (9%)
  other arithmetic  21.2 us (7%)
  matrix products  16.3 us (6%)
  between operations  15.6 us (5%)
  blocking collectives  12.1 us (4%)
    psum x1, waiting for transfers between devices, on_device(): reduced = lax.psum(packed, 'seq')  48.9 us
    all_to_all x2, waiting for transfers between devices, sum_over_head(): gathered = lax.all_to_all(partial, 'head', 0, 0, tiled=True)  42.8 us
    ppermute x3, waiting for transfers between devices, tree_reduce(): got = lax.ppermute(send, axis, xor_perm(count, bit))  40.1 us
    unnamed x49, local copies, waits for them, and re-layouts  14.7 us
    pmax x1, blocking collectives, on_device(): peak = lax.pmax(jnp.max(global_scores, axis=3), 'seq')  12.1 us
    all_to_all x2, starting transfers between devices, sum_over_head(): gathered = lax.all_to_all(partial, 'head', 0, 0, tiled=True)  8.55 us
    ppermute x3, waiting for transfers between devices, tree_reduce(): got = lax.ppermute(parts, axis, xor_perm(count, bit))  8.14 us
    gather x2, local copies, waits for them, and re-layouts, on_device(): outgoing = kv_blocks[:, send_local]  7.66 us
  transfers between devices with their start and end apart: 12, of which 8 were waited for; matrix products, arithmetic and copies ran while one was open for 29% of the time, Pallas kernels for 0%

profile of v5, /device:TPU:2, one launch (start us, length us, event | category | flops | bytes accessed | tf_op | source)
XLA Modules:
  0.0 288.6 jit_solution(16467802916628495655)
XLA Ops:
  6.5 1.3 copy.140
  9.3 1.2 copy.139
  10.6 1.1 convert.2
  12.2 1.5 multiply_subtract_fusion
  13.8 1.2 fusion.57
  15.0 1.9 collective-permute-start.7
  16.9 2.4 collective-permute-start.6
  22.1 1.3 gather_fusion.1
  25.2 1.0 pad_maximum_fusion.2
  26.3 0.8 dynamic-slice_bitcast_fusion
  27.1 2.0 collective-permute-start
  29.5 1.4 copy.182
  30.9 1.1 pad_maximum_fusion.1
  32.0 2.8 gather_fusion.3
  34.8 4.9 %copy.232 = bf16[8,2,2,64,1024]{4,3,1,2,0:T(8,128)(2,1)} copy(bf16[8,2,2,64,1024]{4,3,2,1,0:T(8,128)(2,1)} %bitcast.258) | data formatting | bytes 8388608 | tf_op jit(solution)/shard_map/gather | solution.py:279
  39.7 4.7 %all-to-all-start.1 = ((bf16[2,8,2,64,1024]{4,3,2,0,1:T(8,128)(2,1)}), bf16[2,8,2,64,1024]{4,3,2,0,1:T(8,128)(2,1)}, u32[]{:S(2)}, u32[]{:S(2)}) async-start(bf16[2,8,2,64,1024]{4,3,2,0,1:T(8,128)(2,1)} %bitcast.257), calls=%async_computation.1 | async-start | bytes 8388608 | tf_op jit(solution)/shard_map/all_to_all | solution.py:281
  45.0 1.0 bitcast_add_fusion
  46.1 0.8 dynamic-slice_bitcast_fusion.1
  46.9 1.5 reshape.514
  48.5 0.7 broadcast_in_dim.180
  49.2 1.6 copy.157
  50.9 0.9 copy.186
  51.8 2.8 pad_maximum_fusion
  54.6 3.0 %copy.150 = bf16[2,512,1024]{2,1,0:T(8,128)(2,1)S(1)} copy(bf16[2,512,1024]{1,2,0:T(8,128)(2,1)} %pad_maximum_fusion) | data formatting | bytes 4194304 | tf_op jit(solution)/shard_map/concatenate | solution.py:24
  57.6 37.2 %collective-permute-done.1 = bf16[96,1024]{1,0:T(8,128)(2,1)} collective-permute-done((bf16[96,1024]{1,0:T(8,128)(2,1)}, bf16[96,1024]{1,0:T(8,128)(2,1)}, u32[]{:S(2)}, u32[]{:S(2)}) %collective-permute-start.1) | collective-permute-done | bytes 196640 | tf_op jit(solution)/shard_map/ppermute | solution.py:105
  94.8 0.9 bitcast_add_fusion.1
  95.8 1.8 collective-permute-start.2
  97.6 2.9 collective-permute-done.2
  100.5 1.8 collective-permute-start.3
  102.3 2.9 collective-permute-done.3
  105.3 1.9 collective-permute-start.4
  107.3 3.7 %collective-permute-done.4 = bf16[96,1024]{1,0:T(8,128)(2,1)S(1)} collective-permute-done((bf16[96,1024]{1,0:T(8,128)(2,1)S(1)}, bf16[96,1024]{1,0:T(8,128)(2,1)S(1)}, u32[]{:S(2)}, u32[]{:S(2)}) %collective-permute-start.4) | collective-permute-done | bytes 196640 | tf_op jit(solution)/shard_map/ppermute | solution.py:109
  111.5 1.6 collective-permute-done.5
  113.7 1.5 fusion.103
  115.2 2.7 copy.190
  117.9 2.8 copy.189
  121.4 12.1 %pmax.7 = f32[2,64,8]{1,0,2:T(2,128)S(1)} all-reduce(f32[2,64,8]{1,0,2:T(2,128)S(1)} %bitcast_reduce_fusion), channel_id=1, replica_groups=mesh['seq'=8,'head'=4] {'seq'}, use_global_device_ids=true, to_apply=%region_1.2 | all-reduce | flops 1024 | bytes 8192 | tf_op jit(solution)/shard_map/pmax | solution.py:248
  134.9 0.9 concatenate.27
  135.8 3.9 %fusion = (f32[4,8,64]{2,1,0:T(8,128)S(1)}, f32[4,8,64,448]{3,2,1,0:T(8,128)S(1)}) fusion(pred[4,8,448]{2,1,0:T(8,128)(4,1)S(1)} %copy-done.10, bf16[4,64,8,128]{3,1,2,0:T(8,128)(2,1)S(1)} %copy.157, bf16[4,448,8,128]{3,2,1,0:T(8,128)(2,1)} %bitcast.261), kind=kOutput, calls=%fused_computation.11 | convolution fusion | flops 237631488 | bytes 7886848 | tf_op jit(solution)/shard_map/bqhd,bshd->bhqs/dot_general | solution.py:162
  139.7 2.0 copy-done
  141.7 1.5 fusion.5
  143.1 48.9 %all-reduce.3.cloned.1.call-done = f32[128,1152]{1,0:T(8,128)} async-done(((f32[128,1152]{1,0:T(8,128)}), f32[128,1152]{1,0:T(8,128)}) %all-reduce.3.cloned.1.call-update) | async-done | bytes 589840 | tf_op jit(solution)/shard_map/psum | solution.py:263
  192.1 0.8 slice.124
  193.1 4.9 %convolution_convert_fusion.1 = bf16[128,4096]{1,0:T(8,128)(2,1)S(1)} fusion(bf16[1024,4096]{1,0:T(8,128)(2,1)} %param.12, f32[16,8,8,128]{3,2,1,0:T(8,128)S(1)} %bitcast.294, f32[128,1152]{1,0:T(8,128)} %all-reduce.3.cloned.1.call-done), kind=kOutput, calls=%fused_computation.6 | convolution fusion | flops 1074528256 | bytes 10485760 | tf_op jit(solution)/shard_map/dot_general | solution.py:145
  198.0 1.1 copy.234
  199.1 4.6 %all-to-all-start = ((bf16[4,1024,128]{1,2,0:T(8,128)(2,1)}), bf16[4,1024,128]{1,2,0:T(8,128)(2,1)S(1)}, u32[]{:S(2)}, u32[]{:S(2)}) async-start(bf16[4,1024,128]{1,2,0:T(8,128)(2,1)} %bitcast.244), calls=%async_computation | async-start | bytes 2097152 | tf_op jit(solution)/shard_map/all_to_all | solution.py:152
  203.7 4.9 %copy.166 = bf16[2,8,2,64,1024]{4,3,2,1,0:T(8,128)(2,1)} copy(bf16[2,8,2,64,1024]{4,3,2,0,1:T(8,128)(2,1)} %all-to-all-done.1) | data formatting | bytes 8388608 | tf_op jit(solution)/shard_map/all_to_all | solution.py:281
  208.6 4.7 %gather_fusion.4 = bf16[12,2,64,1024]{3,2,1,0:T(8,128)(2,1)} fusion(bf16[2,8,2,64,1024]{4,3,2,1,0:T(8,128)(2,1)} %copy.166, s32[12]{0:T(128)S(1)} %fusion.93), kind=kCustom, calls=%fused_computation.4 | custom fusion | bytes 6291552 | tf_op jit(solution)/shard_map/gather | solution.py:284
  213.2 2.2 fusion.104
  215.9 1.2 multiply_reduce_fusion
  217.6 0.8 fusion.12
  218.4 1.1 copy-done.1
  219.5 2.1 fusion.32
  221.6 1.2 fusion.40
  223.1 2.4 convolution_convert_fusion
  225.5 1.6 copy.233
  227.1 1.1 all-to-all-done
  228.2 1.0 copy-done.5
  229.2 4.0 %all-to-all-start.2 = ((bf16[4,1024,256]{1,2,0:T(8,128)(2,1)}), bf16[4,1024,256]{1,2,0:T(8,128)(2,1)S(1)}, u32[]{:S(2)}, u32[]{:S(2)}) async-start(bf16[4,1024,256]{1,2,0:T(8,128)(2,1)} %bitcast.263), calls=%async_computation.2 | async-start | bytes 4194304 | tf_op jit(solution)/shard_map/all_to_all | solution.py:152
  234.4 1.3 compare_and_fusion
  235.9 1.3 compare_and_fusion.1
  237.4 1.4 convert_reduce_fusion.1
  238.8 41.6 %all-to-all-done.2 = bf16[4,1024,256]{1,2,0:T(8,128)(2,1)S(1)} async-done(((bf16[4,1024,256]{1,2,0:T(8,128)(2,1)}), bf16[4,1024,256]{1,2,0:T(8,128)(2,1)S(1)}, u32[]{:S(2)}, u32[]{:S(2)}) %all-to-all-start.2) | async-done | bytes 2097184 | tf_op jit(solution)/shard_map/all_to_all | solution.py:152
  280.8 0.9 fusion.50
  (117 shorter events, 13.3 us)
Async XLA Ops:
  6.5 5.1 %copy-start.2 = (bf16[256,1024]{1,0:T(8,128)(2,1)S(1)}, bf16[256,1024]{1,0:T(8,128)(2,1)}, u32[]{:S(2)}) copy-start(bf16[256,1024]{1,0:T(8,128)(2,1)} %param.11) | copy-start | bytes 1572868
  11.9 3.1 %copy-start.3 = (bf16[256,1024]{0,1:T(8,128)(2,1)}, bf16[256,1024]{0,1:T(8,128)(2,1)S(1)}, u32[]{:S(2)}) copy-start(bf16[256,1024]{0,1:T(8,128)(2,1)S(1)} %copy.149) | copy-start | bytes 1572868
  12.2 7.2 %copy-start.11 = (s32[32,3]{0,1:T(4,128)S(1)}, s32[32,3]{0,1:T(4,128)}, u32[]{:S(2)}) copy-start(s32[32,3]{0,1:T(4,128)} %param.14) | copy-start | bytes 1156
  13.7 7.1 %copy-start.12 = (s32[2]{0:T(128)S(1)}, s32[2]{0:T(128)}, u32[]{:S(2)}) copy-start(s32[2]{0:T(128)} %param.13) | copy-start | bytes 28
  15.0 36.8 %collective-permute-start.7 = (bf16[2,128,1024]{1,2,0:T(8,128)(2,1)}, bf16[2,128,1024]{1,2,0:T(8,128)(2,1)}, u32[]{:S(2)}, u32[]{:S(2)}) collective-permute-start(bf16[2,128,1024]{1,2,0:T(8,128)(2,1)} %get-tuple-element.19), channel_id=1, source_target_pairs={{4,0},{8,4},{12,8},{16,12},{20,16},{24,20},{28,24},{5,1},{9,5},{13... | collective-permute-start | bytes 1572872 | tf_op jit(solution)/shard_map/ppermute | solution.py:28
  16.9 34.8 %collective-permute-start.6 = (bf16[2,128,1024]{1,2,0:T(8,128)(2,1)}, bf16[2,128,1024]{1,2,0:T(8,128)(2,1)}, u32[]{:S(2)}, u32[]{:S(2)}) collective-permute-start(bf16[2,128,1024]{1,2,0:T(8,128)(2,1)} %get-tuple-element.18), channel_id=1, source_target_pairs={{0,4},{4,8},{8,12},{12,16},{16,20},{20,24},{24,28},{1,5},{5,9},{9,... | collective-permute-start | bytes 1572872 | tf_op jit(solution)/shard_map/ppermute | solution.py:26
  27.1 17.9 %collective-permute-start = (bf16[192,1024]{1,0:T(8,128)(2,1)}, bf16[192,1024]{1,0:T(8,128)(2,1)}, u32[]{:S(2)}, u32[]{:S(2)}) collective-permute-start(bf16[192,1024]{1,0:T(8,128)(2,1)} %dynamic-slice_bitcast_fusion), channel_id=1, source_target_pairs={{0,4},{4,0},{8,12},{12,8},{16,20},{20,16},{24,28},{28,24},{1,5},{5... | collective-permute-start | bytes 1179656 | tf_op jit(solution)/shard_map/ppermute | solution.py:105
  39.7 5.1 %copy-start.13 = (s32[8]{0:T(128)S(1)}, s32[8]{0:T(128)}, u32[]{:S(2)}) copy-start(s32[8]{0:T(128)} %param.15) | copy-start | bytes 100
  39.7 159.4 %all-to-all-start.1 = ((bf16[2,8,2,64,1024]{4,3,2,0,1:T(8,128)(2,1)}), bf16[2,8,2,64,1024]{4,3,2,0,1:T(8,128)(2,1)}, u32[]{:S(2)}, u32[]{:S(2)}) async-start(bf16[2,8,2,64,1024]{4,3,2,0,1:T(8,128)(2,1)} %bitcast.257), calls=%async_computation.1 | async-start | bytes 8388608 | tf_op jit(solution)/shard_map/all_to_all | solution.py:281
  44.3 7.4 %copy-start.4 = (bf16[256,1024]{0,1:T(8,128)(2,1)S(1)}, bf16[256,1024]{0,1:T(8,128)(2,1)}, u32[]{:S(2)}) copy-start(bf16[256,1024]{0,1:T(8,128)(2,1)} %copy-done.3) | copy-start | bytes 1572868
  44.4 147.7 %all-reduce.3.cloned.1.call-start = ((), (), s32[]{:S(2)}) async-start(), calls=%async_computation.3 | async-start | bytes 1179648 | tf_op jit(solution)/shard_map/psum | solution.py:263
  46.1 5.7 %copy-start.8 = (bf16[192,1024]{1,0:T(8,128)(2,1)}, bf16[192,1024]{1,0:T(8,128)(2,1)S(1)}, u32[]{:S(2)}) copy-start(bf16[192,1024]{1,0:T(8,128)(2,1)S(1)} %bitcast_add_fusion) | copy-start | bytes 1179652
  46.9 47.9 %collective-permute-start.1 = (bf16[96,1024]{1,0:T(8,128)(2,1)}, bf16[96,1024]{1,0:T(8,128)(2,1)}, u32[]{:S(2)}, u32[]{:S(2)}) collective-permute-start(bf16[96,1024]{1,0:T(8,128)(2,1)} %dynamic-slice_bitcast_fusion.1), channel_id=1, source_target_pairs={{0,8},{4,12},{8,0},{12,4},{16,24},{20,28},{24,16},{28,20},{1,9},{5... | collective-permute-start | bytes 589832 | tf_op jit(solution)/shard_map/ppermute | solution.py:105
  54.6 40.2 %copy-start.9 = (bf16[192,1024]{1,0:T(8,128)(2,1)S(1)}, bf16[192,1024]{1,0:T(8,128)(2,1)}, u32[]{:S(2)}) copy-start(bf16[192,1024]{1,0:T(8,128)(2,1)} %copy-done.8) | copy-start | bytes 1179652
  95.8 4.7 %collective-permute-start.2 = (bf16[48,1024]{1,0:T(8,128)(2,1)S(1)}, bf16[48,1024]{1,0:T(8,128)(2,1)S(1)}, u32[]{:S(2)}, u32[]{:S(2)}) collective-permute-start(bf16[48,1024]{1,0:T(8,128)(2,1)S(1)} %dynamic-slice_bitcast_fusion.2), channel_id=1, source_target_pairs={{0,16},{4,20},{8,24},{12,28},{16,0},{20,4},{24,8},{28,12},{1,17},{... | collective-permute-start | bytes 294920 | tf_op jit(solution)/shard_map/ppermute | solution.py:105
  100.5 4.7 %collective-permute-start.3 = (bf16[48,1024]{1,0:T(8,128)(2,1)S(1)}, bf16[48,1024]{1,0:T(8,128)(2,1)S(1)}, u32[]{:S(2)}, u32[]{:S(2)}) collective-permute-start(bf16[48,1024]{1,0:T(8,128)(2,1)S(1)} %bitcast_add_fusion.2), channel_id=1, source_target_pairs={{0,16},{4,20},{8,24},{12,28},{16,0},{20,4},{24,8},{28,12},{1,17},{... | collective-permute-start | bytes 294920 | tf_op jit(solution)/shard_map/ppermute | solution.py:109
  105.3 5.7 %collective-permute-start.4 = (bf16[96,1024]{1,0:T(8,128)(2,1)S(1)}, bf16[96,1024]{1,0:T(8,128)(2,1)S(1)}, u32[]{:S(2)}, u32[]{:S(2)}) collective-permute-start(bf16[96,1024]{1,0:T(8,128)(2,1)S(1)} %get-tuple-element.28), channel_id=1, source_target_pairs={{0,8},{4,12},{8,0},{12,4},{16,24},{20,28},{24,16},{28,20},{1,9},{5... | collective-permute-start | bytes 589832 | tf_op jit(solution)/shard_map/ppermute | solution.py:109
  111.3 1.8 collective-permute-start.5
  120.7 12.7 %copy-start.7 = (bf16[32,8,8,128]{3,2,1,0:T(8,128)(2,1)S(1)}, bf16[32,8,8,128]{3,2,1,0:T(8,128)(2,1)}, u32[]{:S(2)}) copy-start(bf16[32,8,8,128]{3,2,1,0:T(8,128)(2,1)} %copy.186) | copy-start | bytes 1572868
  121.4 14.4 %copy-start.10 = (pred[4,8,448]{2,1,0:T(8,128)(4,1)S(1)}, pred[4,8,448]{2,1,0:T(8,128)(4,1)}, u32[]{:S(2)}) copy-start(pred[4,8,448]{2,1,0:T(8,128)(4,1)} %broadcast_in_dim.180) | copy-start | bytes 43012
  139.7 2.0 copy-start
  199.1 29.1 %all-to-all-start = ((bf16[4,1024,128]{1,2,0:T(8,128)(2,1)}), bf16[4,1024,128]{1,2,0:T(8,128)(2,1)S(1)}, u32[]{:S(2)}, u32[]{:S(2)}) async-start(bf16[4,1024,128]{1,2,0:T(8,128)(2,1)} %bitcast.244), calls=%async_computation | async-start | bytes 2097152 | tf_op jit(solution)/shard_map/all_to_all | solution.py:152
  215.9 2.5 copy-start.6
  217.1 2.4 copy-start.1
  217.6 5.5 %slice-start = ((s8[8388608]{0:T(1024)(128)(4,1)}), s8[4194304]{0:T(1024)(128)(4,1)S(1)}, s32[]{:S(2)}) async-start(s8[8388608]{0:T(1024)(128)(4,1)} %bitcast.301), calls=%async_computation.4 | async-start | bytes 8388608
  219.5 3.6 %slice-start.1 = ((s8[8388608]{0:T(1024)(128)(4,1)}), s8[4194304]{0:T(1024)(128)(4,1)S(1)}, s32[]{:S(2)}) async-start(s8[8388608]{0:T(1024)(128)(4,1)} %bitcast.301), calls=%async_computation.5 | async-start | bytes 8388608
  228.2 1.0 copy-start.5
  229.2 51.3 %all-to-all-start.2 = ((bf16[4,1024,256]{1,2,0:T(8,128)(2,1)}), bf16[4,1024,256]{1,2,0:T(8,128)(2,1)S(1)}, u32[]{:S(2)}, u32[]{:S(2)}) async-start(bf16[4,1024,256]{1,2,0:T(8,128)(2,1)} %bitcast.263), calls=%async_computation.2 | async-start | bytes 4194304 | tf_op jit(solution)/shard_map/all_to_all | solution.py:152
Sparse Core Ops, SparseCore 0:
  135.9 56.1 all-reduce.2

commit v6 on v4

--- a/solution.py
+++ b/solution.py
@@ -208,8 +208,23 @@
     query_rot = rotate(queries, first_row, frequency, mscale)
     key_rot = rotate(keys, first_row, frequency, mscale)
     pair_kv = jnp.stack([key_rot, values])
-    padded = padded_2(pair_kv, (("seq", 1),), WMAX * BLOCK)
-    padded_blocks = padded.reshape(2, blocks_here + 2 * WMAX, BLOCK, width_here)
+    halo = WMAX * BLOCK
+    seq_ends = seq_count - 1
+    from_left = lax.ppermute(
+        pair_kv[:, tok_here - halo :], "seq", [(i, (i + 1) % seq_count) for i in range(seq_ends)]
+    ).reshape(2, WMAX, BLOCK, width_here)
+    from_right = lax.ppermute(
+        pair_kv[:, :halo], "seq", [((i + 1) % seq_count, i) for i in range(seq_ends)]
+    ).reshape(2, WMAX, BLOCK, width_here)
+    local_blocks = pair_kv.reshape(2, blocks_here, BLOCK, width_here)
+
+    def padded_block(index):
+        if index < WMAX:
+            return from_left[:, index]
+        if index < WMAX + blocks_here:
+            return local_blocks[:, index - WMAX]
+        return from_right[:, index - WMAX - blocks_here]
+
     offsets = jnp.arange(-WMAX, WMAX + 1)
     window_ids = seq_place * blocks_here + jnp.arange(blocks_here)[:, None] + offsets[None, :]
     inside = (window_ids >= 0) & (window_ids < block_total)
@@ -226,13 +241,13 @@
     shared = tree_reduce(masked.reshape(3 * GLOB * BLOCK, width_here), add_merge, "seq")
     shared = shared.reshape(3, GLOB, BLOCK, width_here)
     slot_parts = [
-        padded_blocks[:, offset_slot : offset_slot + blocks_here][:, :, None]
-        for offset_slot in range(2 * WMAX + 1)
+        jnp.stack(
+            [padded_block(block + offset_slot) for offset_slot in range(2 * WMAX + 1)], axis=1
+        )
+        for block in range(blocks_here)
     ]
-    slot_parts.append(
-        jnp.broadcast_to(shared[1:3][:, None], (2, blocks_here, GLOB, BLOCK, width_here))
-    )
-    near_kv = jnp.concatenate(slot_parts, axis=2)
+    global_kv = jnp.broadcast_to(shared[1:3][:, None], (2, blocks_here, GLOB, BLOCK, width_here))
+    near_kv = jnp.concatenate([jnp.stack(slot_parts, axis=1), global_kv], axis=2)
     near_valid = jnp.concatenate(
         [window_valid, jnp.ones((blocks_here, GLOB, heads_here), dtype=bool)], axis=1
     )
@@ -276,13 +291,15 @@
         ranks[:, None, :] == jnp.arange(capacity)[None, :, None]
     )
     send_local = jnp.sum(jnp.where(wanted, local_ids[:, None, :], 0), axis=2)
-    kv_blocks = pair_kv.reshape(2, blocks_here, BLOCK, width_here)
-    outgoing = kv_blocks[:, send_local]
+    kv_blocks = jnp.stack([key_rot.reshape(blocks_here, BLOCK, width_here), value_view], axis=1)
+    outgoing = kv_blocks[send_local]
     outgoing, reduced = lax.optimization_barrier((outgoing, reduced))
-    incoming = lax.all_to_all(outgoing, "seq", split_axis=1, concat_axis=1, tiled=True)
+    incoming = lax.all_to_all(outgoing, "seq", split_axis=0, concat_axis=0, tiled=True)
     my_owners = owners[seq_place]
     my_ranks = ranks[seq_place]
-    random_kv = incoming[:, my_owners, my_ranks].reshape(2, blocks_here, RAND, BLOCK, width_here)
+    random_k = incoming[my_owners, my_ranks, 0].reshape(blocks_here, RAND, BLOCK, width_here)
+    random_v = incoming[my_owners, my_ranks, 1].reshape(blocks_here, RAND, BLOCK, width_here)
+    random_kv = (random_k, random_v)
     near_part = partial_attend(query_view, near_kv[0], near_kv[1], near_valid)
     far_part = partial_attend(
         query_view, random_kv[0], random_kv[1], jnp.ones((blocks_here, RAND, heads_here), dtype=bool)

time: 223 us -> 213 us (0.955)
  local copies, waits for them, and re-layouts: 54.9 us -> 45.7 us
  other arithmetic: 24.7 us -> 18.8 us
  waiting for transfers between devices: 55.6 us -> 61.4 us
    all_to_all x1 -> x0, local copies, waits for them, and re-layouts: 4.88 us -> none  [on_device(): lax.all_to_all(outgoing, 'seq', split_axis=1, concat_axis=1, tiled=True)]
    ppermute x6, waiting for transfers between devices: 6.07 us -> 10.9 us  [tree_reduce(): got = lax.ppermute(parts, axis, xor_perm(count, bit))]
    convert_element_type x8 -> x10, local copies, waits for them, and re-layouts: 7.54 us -> 11 us  [rotate(): return turned.reshape(row_count, row_width).astype(jnp.bfloat16)]
    concatenate x2 -> x0, local copies, waits for them, and re-layouts: 3.25 us -> none  [the longest x1 2.98 us: padded_2(): jnp.concatenate([lax.ppermute(tail, axis, [(i, (i + 1) % count) for i in...]
    ppermute x0 -> x2, local copies, waits for them, and re-layouts: none -> 2.49 us  [the longest x1 1.25 us: on_device(): lax.ppermute(pair_kv[:, tok_here - halo:], 'seq', [(i, (i + 1) % seq_coun...]
    concatenate x2, other arithmetic: 3.49 us -> 1.08 us  [the longest x1 1.07 us: on_device(): jnp.concatenate([jnp.stack(slot_parts, axis=1), global_kv], axis=2)]
    unnamed x54 -> x47, local copies, waits for them, and re-layouts: 13.5 us -> 13.3 us
  transfers between devices with their start and end apart: 15 -> 15, of which waited for: 10 -> 11; matrix products, arithmetic and copies ran while one was open for 25% -> 22% of each run, Pallas kernels for 0% -> 0%
where the time goes in v6:
time: 213 us; the launch traced here: 212 us
  waiting for transfers between devices  61.4 us (29%)
  blocking collectives  53.1 us (25%)
  local copies, waits for them, and re-layouts  45.7 us (21%)
  starting transfers between devices  20.8 us (10%)
  other arithmetic  18.8 us (9%)
  matrix products  9.67 us (5%)
  between operations  2.37 us (1%)
    all_to_all x1, blocking collectives, sum_over_head(): gathered = lax.all_to_all(partial, 'head', 0, 0, tiled=True)  53.1 us
    all_to_all x1, waiting for transfers between devices, on_device(): lax.all_to_all(outgoing, 'seq', split_axis=0, concat_axis=0, tiled=True)  31.5 us
    ppermute x6, waiting for transfers between devices, tree_reduce(): got = lax.ppermute(send, axis, xor_perm(count, bit))  19 us
    unnamed x47, local copies, waits for them, and re-layouts  13.3 us
    convert_element_type x10, local copies, waits for them, and re-layouts, rotate(): return turned.reshape(row_count, row_width).astype(jnp.bfloat16)  11 us
    ppermute x6, waiting for transfers between devices, tree_reduce(): got = lax.ppermute(parts, axis, xor_perm(count, bit))  10.9 us
    all_to_all x1, starting transfers between devices, on_device(): lax.all_to_all(outgoing, 'seq', split_axis=0, concat_axis=0, tiled=True)  5.53 us
    ppermute x6, starting transfers between devices, tree_reduce(): got = lax.ppermute(parts, axis, xor_perm(count, bit))  5.19 us
  transfers between devices with their start and end apart: 15, of which 11 were waited for; matrix products, arithmetic and copies ran while one was open for 22% of the time, Pallas kernels for 0%

profile of v6, /device:TPU:2, one launch (start us, length us, event | category | flops | bytes accessed | tf_op | source)
XLA Modules:
  0.0 211.9 jit_solution(6602666340532261478)
XLA Ops:
  1.4 1.2 copy.129
  3.7 1.0 copy.138
  6.1 1.2 fusion.53
  7.3 1.9 collective-permute-start.12
  9.2 3.6 %collective-permute-start.13 = (bf16[2,128,1024]{1,2,0:T(8,128)(2,1)}, bf16[2,128,1024]{1,2,0:T(8,128)(2,1)}, u32[]{:S(2)}, u32[]{:S(2)}) collective-permute-start(bf16[2,128,1024]{1,2,0:T(8,128)(2,1)} %get-tuple-element.38), channel_id=1, source_target_pairs={{4,0},{8,4},{12,8},{16,12},{20,16},{24,20},{28,24},{5,1},{9,5},{13... | collective-permute-start | bytes 1572872 | tf_op jit(solution)/shard_map/ppermute | solution.py:216
  14.0 1.4 reshape.557
  15.4 1.6 copy.154
  17.6 1.3 gather_fusion.1
  18.8 0.6 copy.155
  20.1 1.0 pad_maximum_fusion.3
  21.2 0.8 dynamic-slice_bitcast_fusion
  22.9 1.1 collective-permute-done
  24.2 6.9 %collective-permute-done.1 = bf16[96,1024]{1,0:T(8,128)(2,1)S(1)} collective-permute-done((bf16[96,1024]{1,0:T(8,128)(2,1)S(1)}, bf16[96,1024]{1,0:T(8,128)(2,1)S(1)}, u32[]{:S(2)}, u32[]{:S(2)}) %collective-permute-start.1) | collective-permute-done | bytes 196640 | tf_op jit(solution)/shard_map/ppermute | solution.py:105
  31.1 1.6 collective-permute-start.2
  32.7 3.1 %collective-permute-done.2 = bf16[48,1024]{1,0:T(8,128)(2,1)S(1)} collective-permute-done((bf16[48,1024]{1,0:T(8,128)(2,1)S(1)}, bf16[48,1024]{1,0:T(8,128)(2,1)S(1)}, u32[]{:S(2)}, u32[]{:S(2)}) %collective-permute-start.2) | collective-permute-done | bytes 98336 | tf_op jit(solution)/shard_map/ppermute | solution.py:105
  35.8 1.6 collective-permute-start.3
  37.4 3.1 %collective-permute-done.3 = bf16[48,1024]{1,0:T(8,128)(2,1)S(1)} collective-permute-done((bf16[48,1024]{1,0:T(8,128)(2,1)S(1)}, bf16[48,1024]{1,0:T(8,128)(2,1)S(1)}, u32[]{:S(2)}, u32[]{:S(2)}) %collective-permute-start.3) | collective-permute-done | bytes 98336 | tf_op jit(solution)/shard_map/ppermute | solution.py:109
  40.6 1.0 collective-permute-start.4
  41.8 4.6 %collective-permute-done.4 = bf16[96,1024]{1,0:T(8,128)(2,1)S(1)} collective-permute-done((bf16[96,1024]{1,0:T(8,128)(2,1)S(1)}, bf16[96,1024]{1,0:T(8,128)(2,1)S(1)}, u32[]{:S(2)}, u32[]{:S(2)}) %collective-permute-start.4) | collective-permute-done | bytes 196640 | tf_op jit(solution)/shard_map/ppermute | solution.py:109
  46.8 1.6 collective-permute-done.5
  48.4 1.1 fusion.64
  51.8 1.4 collective-permute-done.6
  53.8 1.0 collective-permute-start.7
  56.0 3.8 %collective-permute-done.7 = f32[32,1152]{1,0:T(8,128)S(1)} collective-permute-done((f32[32,1152]{1,0:T(8,128)S(1)}, f32[32,1152]{1,0:T(8,128)S(1)}, u32[]{:S(2)}, u32[]{:S(2)}) %collective-permute-start.7) | collective-permute-done | bytes 147488 | tf_op jit(solution)/shard_map/ppermute | solution.py:105
  60.2 1.6 collective-permute-start.8
  61.8 2.8 %collective-permute-done.8 = f32[16,1152]{1,0:T(8,128)S(1)} collective-permute-done((f32[16,1152]{1,0:T(8,128)S(1)}, f32[16,1152]{1,0:T(8,128)S(1)}, u32[]{:S(2)}, u32[]{:S(2)}) %collective-permute-start.8) | collective-permute-done | bytes 73760 | tf_op jit(solution)/shard_map/ppermute | solution.py:105
  65.0 1.5 collective-permute-start.9
  66.5 1.2 compare_and_fusion.1
  67.8 1.6 collective-permute-done.9
  69.4 0.7 pad_maximum_fusion.10
  70.1 0.9 collective-permute-start.10
  71.0 1.2 compare_and_fusion
  72.3 1.4 reshape.560
  73.7 1.4 reshape.559
  76.2 1.6 copy.143
  77.8 1.6 copy.158
  79.4 0.6 copy.153
  80.2 1.0 fusion.78
  81.3 2.8 %gather_fusion = bf16[16,2,64,1024]{3,2,1,0:T(8,128)(2,1)} fusion(bf16[4,2,64,1024]{3,2,0,1:T(8,128)(2,1)S(1)} %pad_maximum_fusion.2, s32[1024]{0:T(1024)S(1)} %pad_clamp_fusion.1), kind=kCustom, calls=%fused_computation | custom fusion | bytes 8388672 | tf_op jit(solution)/shard_map/gather | solution.py:295
  84.3 1.0 fusion.69
  85.3 0.9 pad_maximum_fusion.4
  86.2 5.5 %all-to-all-start = ((bf16[8,2,2,64,1024]{4,3,2,1,0:T(8,128)(2,1)}), bf16[8,2,2,64,1024]{4,3,2,1,0:T(8,128)(2,1)}, u32[]{:S(2)}, u32[]{:S(2)}) async-start(bf16[8,2,2,64,1024]{4,3,2,1,0:T(8,128)(2,1)} %bitcast.281), calls=%async_computation | async-start | bytes 8388608 | tf_op jit(solution)/shard_map/all_to_all | solution.py:297
  91.8 1.2 copy.139
  93.1 0.7 slice.231
  93.8 1.2 copy.141
  95.2 0.8 copy-done.10
  97.4 1.1 pad_maximum_fusion
  98.5 1.5 fusion.122
  100.0 1.0 copy.173
  101.0 2.7 %copy.174 = bf16[224,8,8,128]{3,2,1,0:T(8,128)(2,1)} copy(bf16[224,8,8,128]{3,1,2,0:T(8,128)(2,1)S(1)} %bitcast.287) | data formatting | bytes 7340032
  103.7 1.8 fusion
  105.6 1.5 fusion.5
  107.9 31.5 %all-to-all-done = bf16[8,2,2,64,1024]{4,3,2,1,0:T(8,128)(2,1)} async-done(((bf16[8,2,2,64,1024]{4,3,2,1,0:T(8,128)(2,1)}), bf16[8,2,2,64,1024]{4,3,2,1,0:T(8,128)(2,1)}, u32[]{:S(2)}, u32[]{:S(2)}) %all-to-all-start) | async-done | bytes 4194336 | tf_op jit(solution)/shard_map/all_to_all | solution.py:297
  139.5 2.8 %gather_fusion.4 = bf16[12,64,1024]{2,1,0:T(8,128)(2,1)S(1)} fusion(bf16[8,2,2,64,1024]{4,3,2,1,0:T(8,128)(2,1)} %all-to-all-done, s32[12]{0:T(128)S(1)} %bitcast.334), kind=kCustom, calls=%fused_computation.4 | custom fusion | bytes 3145872 | tf_op jit(solution)/shard_map/gather | solution.py:300
  142.3 1.6 copy.175
  144.0 2.8 %gather_fusion.5 = bf16[12,64,1024]{2,1,0:T(8,128)(2,1)S(1)} fusion(bf16[8,2,2,64,1024]{4,3,2,1,0:T(8,128)(2,1)} %all-to-all-done, s32[12]{0:T(128)S(1)} %get-tuple-element.12), kind=kCustom, calls=%fused_computation.5 | custom fusion | bytes 3145872 | tf_op jit(solution)/shard_map/gather | solution.py:301
  147.3 0.9 copy-done.3
  148.2 1.2 multiply_reduce_fusion
  149.4 0.8 fusion.12
  150.8 2.1 fusion.32
  152.9 1.4 fusion.42
  154.8 2.5 %convolution_convert_fusion = bf16[256,4096]{1,0:T(8,128)(2,1)S(1)} fusion(bf16[1024,4096]{1,0:T(8,128)(2,1)S(1)} %bitcast.342, bf16[256,1024]{1,0:T(8,128)(2,1)S(1)} %bitcast.323, bf16[256,1024]{1,0:T(8,128)(2,1)S(1)} %bitcast.322, bf16[32,8,8,128]{3,2,1,0:T(8,128)(2,1)S(1)} %bitcast.327, pred[256]{0:T(512)(128)(4,1)S(1)} %broadcast_in_dim.175, ...), kind=kOutput, calls=%fused_computation.7 | convolution fusion | flops 2149056512 | bytes 12059136 | tf_op jit(solution)/shard_map/dot_general | solution.py:145
  157.5 53.1 %all_to_all.10 = bf16[4,1024,256]{1,2,0:T(8,128)(2,1)S(1)} all-to-all(bf16[4,1024,256]{1,2,0:T(8,128)(2,1)S(1)} %bitcast.290), channel_id=1, replica_groups=mesh['seq'=8,'head'=4] {'head'}, dimensions={0} | all-to-all | bytes 4194304 | tf_op jit(solution)/shard_map/all_to_all | solution.py:152
  210.6 1.3 reduce_sum.71
  (155 shorter events, 17.0 us)
Async XLA Ops:
  0.0 2.8 %copy-start.11 = (bf16[256,1024]{1,0:T(8,128)(2,1)S(1)}, bf16[256,1024]{1,0:T(8,128)(2,1)}, u32[]{:S(2)}) copy-start(bf16[256,1024]{1,0:T(8,128)(2,1)} %param.10) | copy-start | bytes 1572868
  2.7 1.0 copy-start.2
  5.0 1.0 copy-start.8
  5.5 7.8 %copy-start.14 = (s32[2]{0:T(128)S(1)}, s32[2]{0:T(128)}, u32[]{:S(2)}) copy-start(s32[2]{0:T(128)} %param.13) | copy-start | bytes 28
  7.3 84.5 %collective-permute-start.12 = (bf16[2,128,1024]{1,2,0:T(8,128)(2,1)}, bf16[2,128,1024]{1,2,0:T(8,128)(2,1)}, u32[]{:S(2)}, u32[]{:S(2)}) collective-permute-start(bf16[2,128,1024]{1,2,0:T(8,128)(2,1)} %get-tuple-element.37), channel_id=1, source_target_pairs={{0,4},{4,8},{8,12},{12,16},{16,20},{20,24},{24,28},{1,5},{5,9},{9,... | collective-permute-start | bytes 1572872 | tf_op jit(solution)/shard_map/ppermute | solution.py:213
  9.2 84.6 %collective-permute-start.13 = (bf16[2,128,1024]{1,2,0:T(8,128)(2,1)}, bf16[2,128,1024]{1,2,0:T(8,128)(2,1)}, u32[]{:S(2)}, u32[]{:S(2)}) collective-permute-start(bf16[2,128,1024]{1,2,0:T(8,128)(2,1)} %get-tuple-element.38), channel_id=1, source_target_pairs={{4,0},{8,4},{12,8},{16,12},{20,16},{24,20},{28,24},{5,1},{9,5},{13... | collective-permute-start | bytes 1572872 | tf_op jit(solution)/shard_map/ppermute | solution.py:216
  20.0 2.0 copy-start.13
  22.0 1.9 collective-permute-start
  24.0 22.7 %copy-start.15 = (s32[8]{0:T(128)S(1)}, s32[8]{0:T(128)}, u32[]{:S(2)}) copy-start(s32[8]{0:T(128)} %param.15) | copy-start | bytes 100
  24.0 7.0 %collective-permute-start.1 = (bf16[96,1024]{1,0:T(8,128)(2,1)S(1)}, bf16[96,1024]{1,0:T(8,128)(2,1)S(1)}, u32[]{:S(2)}, u32[]{:S(2)}) collective-permute-start(bf16[96,1024]{1,0:T(8,128)(2,1)S(1)} %dynamic-slice_bitcast_fusion.3), channel_id=1, source_target_pairs={{0,8},{4,12},{8,0},{12,4},{16,24},{20,28},{24,16},{28,20},{1,9},{5... | collective-permute-start | bytes 589832 | tf_op jit(solution)/shard_map/ppermute | solution.py:105
  31.1 4.7 %collective-permute-start.2 = (bf16[48,1024]{1,0:T(8,128)(2,1)S(1)}, bf16[48,1024]{1,0:T(8,128)(2,1)S(1)}, u32[]{:S(2)}, u32[]{:S(2)}) collective-permute-start(bf16[48,1024]{1,0:T(8,128)(2,1)S(1)} %dynamic-slice_bitcast_fusion.6), channel_id=1, source_target_pairs={{0,16},{4,20},{8,24},{12,28},{16,0},{20,4},{24,8},{28,12},{1,17},{... | collective-permute-start | bytes 294920 | tf_op jit(solution)/shard_map/ppermute | solution.py:105
  35.8 4.7 %collective-permute-start.3 = (bf16[48,1024]{1,0:T(8,128)(2,1)S(1)}, bf16[48,1024]{1,0:T(8,128)(2,1)S(1)}, u32[]{:S(2)}, u32[]{:S(2)}) collective-permute-start(bf16[48,1024]{1,0:T(8,128)(2,1)S(1)} %bitcast_add_fusion.2), channel_id=1, source_target_pairs={{0,16},{4,20},{8,24},{12,28},{16,0},{20,4},{24,8},{28,12},{1,17},{... | collective-permute-start | bytes 294920 | tf_op jit(solution)/shard_map/ppermute | solution.py:109
  40.6 5.7 %collective-permute-start.4 = (bf16[96,1024]{1,0:T(8,128)(2,1)S(1)}, bf16[96,1024]{1,0:T(8,128)(2,1)S(1)}, u32[]{:S(2)}, u32[]{:S(2)}) collective-permute-start(bf16[96,1024]{1,0:T(8,128)(2,1)S(1)} %get-tuple-element.57), channel_id=1, source_target_pairs={{0,8},{4,12},{8,0},{12,4},{16,24},{20,28},{24,16},{28,20},{1,9},{5... | collective-permute-start | bytes 589832 | tf_op jit(solution)/shard_map/ppermute | solution.py:109
  46.6 1.8 collective-permute-start.5
  49.4 0.8 copy-start.5
  51.4 3.4 %copy-start.12 = (s32[2]{0:T(128)S(1)}, s32[2]{0:T(128)}, u32[]{:S(2)}) copy-start(s32[2]{0:T(128)} %get-tuple-element.27) | copy-start | bytes 28
  51.5 1.6 collective-permute-start.6
  53.8 6.0 %collective-permute-start.7 = (f32[32,1152]{1,0:T(8,128)S(1)}, f32[32,1152]{1,0:T(8,128)S(1)}, u32[]{:S(2)}, u32[]{:S(2)}) collective-permute-start(f32[32,1152]{1,0:T(8,128)S(1)} %get-tuple-element.54), channel_id=1, source_target_pairs={{0,8},{4,12},{8,0},{12,4},{16,24},{20,28},{24,16},{28,20},{1,9},{5... | collective-permute-start | bytes 442376 | tf_op jit(solution)/shard_map/ppermute | solution.py:105
  60.2 4.4 %collective-permute-start.8 = (f32[16,1152]{1,0:T(8,128)S(1)}, f32[16,1152]{1,0:T(8,128)S(1)}, u32[]{:S(2)}, u32[]{:S(2)}) collective-permute-start(f32[16,1152]{1,0:T(8,128)S(1)} %get-tuple-element.66), channel_id=1, source_target_pairs={{0,16},{4,20},{8,24},{12,28},{16,0},{20,4},{24,8},{28,12},{1,17},{... | collective-permute-start | bytes 221192 | tf_op jit(solution)/shard_map/ppermute | solution.py:105
  65.0 4.4 %collective-permute-start.9 = (f32[16,1152]{1,0:T(8,128)S(1)}, f32[16,1152]{1,0:T(8,128)S(1)}, u32[]{:S(2)}, u32[]{:S(2)}) collective-permute-start(f32[16,1152]{1,0:T(8,128)S(1)} %concatenate.72), channel_id=1, source_target_pairs={{0,16},{4,20},{8,24},{12,28},{16,0},{20,4},{24,8},{28,12},{1,17},{... | collective-permute-start | bytes 221192 | tf_op jit(solution)/shard_map/ppermute | solution.py:109
  70.1 10.1 %collective-permute-start.10 = (f32[32,1152]{1,0:T(8,128)}, f32[32,1152]{1,0:T(8,128)}, u32[]{:S(2)}, u32[]{:S(2)}) collective-permute-start(f32[32,1152]{1,0:T(8,128)} %get-tuple-element.61), channel_id=1, source_target_pairs={{0,8},{4,12},{8,0},{12,4},{16,24},{20,28},{24,16},{28,20},{1,9},{5... | collective-permute-start | bytes 442376 | tf_op jit(solution)/shard_map/ppermute | solution.py:109
  81.2 3.1 %collective-permute-start.11 = (f32[64,1152]{1,0:T(8,128)S(1)}, f32[64,1152]{1,0:T(8,128)}, u32[]{:S(2)}, u32[]{:S(2)}) collective-permute-start(f32[64,1152]{1,0:T(8,128)S(1)} %get-tuple-element.49), channel_id=1, source_target_pairs={{0,4},{4,0},{8,12},{12,8},{16,20},{20,16},{24,28},{28,24},{1,5},{5... | collective-permute-start | bytes 884744 | tf_op jit(solution)/shard_map/ppermute | solution.py:109
  86.2 53.3 %all-to-all-start = ((bf16[8,2,2,64,1024]{4,3,2,1,0:T(8,128)(2,1)}), bf16[8,2,2,64,1024]{4,3,2,1,0:T(8,128)(2,1)}, u32[]{:S(2)}, u32[]{:S(2)}) async-start(bf16[8,2,2,64,1024]{4,3,2,1,0:T(8,128)(2,1)} %bitcast.281), calls=%async_computation | async-start | bytes 8388608 | tf_op jit(solution)/shard_map/all_to_all | solution.py:297
  95.0 1.0 copy-start.10
  96.0 1.0 copy-start.6
  96.0 1.1 copy-start.9
  105.6 2.0 copy-start
  105.6 2.0 slice-start
  105.6 2.2 %copy-start.7 = (f32[128,1152]{1,0:T(8,128)S(1)}, f32[128,1152]{1,0:T(8,128)}, u32[]{:S(2)}) copy-start(f32[128,1152]{1,0:T(8,128)} %pad_maximum_fusion.4) | copy-start | bytes 1769476
  146.8 1.4 copy-start.3
  146.8 3.4 %copy-start.4 = (bf16[224,8,8,128]{3,2,1,0:T(8,128)(2,1)S(1)}, bf16[224,8,8,128]{3,2,1,0:T(8,128)(2,1)}, u32[]{:S(2)}) copy-start(bf16[224,8,8,128]{3,2,1,0:T(8,128)(2,1)} %copy.174) | copy-start | bytes 11010052
  148.2 2.6 %copy-start.1 = (f32[4,8,64,448]{3,2,1,0:T(8,128)S(1)}, f32[4,8,64,448]{3,2,1,0:T(8,128)}, u32[]{:S(2)}) copy-start(f32[4,8,64,448]{3,2,1,0:T(8,128)} %copy-done) | copy-start | bytes 11010052
  149.4 5.3 %slice-start.1 = ((s8[8388608]{0:T(1024)(128)(4,1)}), s8[4194304]{0:T(1024)(128)(4,1)S(1)}, s32[]{:S(2)}) async-start(s8[8388608]{0:T(1024)(128)(4,1)} %bitcast.341), calls=%async_computation.3 | async-start | bytes 8388608
  150.8 4.0 %slice-start.2 = ((s8[8388608]{0:T(1024)(128)(4,1)}), s8[4194304]{0:T(1024)(128)(4,1)S(1)}, s32[]{:S(2)}) async-start(s8[8388608]{0:T(1024)(128)(4,1)} %bitcast.341), calls=%async_computation.4 | async-start | bytes 8388608

commit v7 on v6

--- a/solution.py
+++ b/solution.py
@@ -276,7 +276,6 @@
         ],
         axis=1,
     )
-    reduced = tree_reduce(packed, softmax_merge, "seq")
     slot_total = blocks_here * RAND
     capacity = (slot_total + seq_count - 1) // seq_count
     flat_ids = random_blocks.reshape(seq_count, slot_total)
@@ -293,7 +292,7 @@
     send_local = jnp.sum(jnp.where(wanted, local_ids[:, None, :], 0), axis=2)
     kv_blocks = jnp.stack([key_rot.reshape(blocks_here, BLOCK, width_here), value_view], axis=1)
     outgoing = kv_blocks[send_local]
-    outgoing, reduced = lax.optimization_barrier((outgoing, reduced))
+    outgoing, shared = lax.optimization_barrier((outgoing, shared))
     incoming = lax.all_to_all(outgoing, "seq", split_axis=0, concat_axis=0, tiled=True)
     my_owners = owners[seq_place]
     my_ranks = ranks[seq_place]
@@ -301,6 +300,8 @@
     random_v = incoming[my_owners, my_ranks, 1].reshape(blocks_here, RAND, BLOCK, width_here)
     random_kv = (random_k, random_v)
     near_part = partial_attend(query_view, near_kv[0], near_kv[1], near_valid)
+    packed, near_part = lax.optimization_barrier((packed, near_part))
+    reduced = tree_reduce(packed, softmax_merge, "seq")
     far_part = partial_attend(
         query_view, random_kv[0], random_kv[1], jnp.ones((blocks_here, RAND, heads_here), dtype=bool)
     )

time: 213 us -> 218 us (1.023)
  waiting for transfers between devices: 61.4 us -> 64.7 us
  local copies, waits for them, and re-layouts: 45.7 us -> 42.8 us
  other arithmetic: 18.8 us -> 21.4 us
    ppermute x6, waiting for transfers between devices: 19 us -> 55.9 us  [tree_reduce(): got = lax.ppermute(send, axis, xor_perm(count, bit))]
    all_to_all x1, waiting for transfers between devices: 31.5 us -> 0.01 us  [on_device(): lax.all_to_all(outgoing, 'seq', split_axis=0, concat_axis=0, tiled=True)]
    another operation x2, other arithmetic: 0.57 us -> 3.49 us  [on_device(): jnp.stack(slot_parts, axis=1)]
    convert_element_type x10, local copies, waits for them, and re-layouts: 11 us -> 8.54 us  [rotate(): return turned.reshape(row_count, row_width).astype(jnp.bfloat16)]
    unnamed x47 -> x60, local copies, waits for them, and re-layouts: 13.3 us -> 11.2 us
  transfers between devices with their start and end apart: 15 -> 15, of which waited for: 11 -> 8; matrix products, arithmetic and copies ran while one was open for 22% -> 15% of each run, Pallas kernels for 0% -> 0%
where the time goes in v7:
time: 218 us; the launch traced here: 215 us
  waiting for transfers between devices  64.7 us (30%)
  blocking collectives  53.5 us (25%)
  local copies, waits for them, and re-layouts  42.8 us (20%)
  other arithmetic  21.4 us (10%)
  starting transfers between devices  20.2 us (9%)
  matrix products  10.3 us (5%)
  between operations  2.47 us (1%)
    ppermute x6, waiting for transfers between devices, tree_reduce(): got = lax.ppermute(send, axis, xor_perm(count, bit))  55.9 us
    all_to_all x1, blocking collectives, sum_over_head(): gathered = lax.all_to_all(partial, 'head', 0, 0, tiled=True)  53.5 us
    unnamed x60, local copies, waits for them, and re-layouts  11.2 us
    ppermute x6, waiting for transfers between devices, tree_reduce(): got = lax.ppermute(parts, axis, xor_perm(count, bit))  8.76 us
    convert_element_type x10, local copies, waits for them, and re-layouts, rotate(): return turned.reshape(row_count, row_width).astype(jnp.bfloat16)  8.54 us
    all_to_all x1, starting transfers between devices, on_device(): lax.all_to_all(outgoing, 'seq', split_axis=0, concat_axis=0, tiled=True)  5.42 us
    ppermute x6, starting transfers between devices, tree_reduce(): got = lax.ppermute(send, axis, xor_perm(count, bit))  5.27 us
  transfers between devices with their start and end apart: 15, of which 8 were waited for; matrix products, arithmetic and copies ran while one was open for 15% of the time, Pallas kernels for 0%

profile of v7, /device:TPU:2, one launch (start us, length us, event | category | flops | bytes accessed | tf_op | source)
XLA Modules:
  0.0 215.3 jit_solution(1047764619521291339)
XLA Ops:
  1.4 1.2 copy.123
  3.1 0.6 copy-done
  3.7 1.0 copy.133
  5.5 0.6 copy-done.10
  6.1 1.2 fusion.50
  7.2 2.0 collective-permute-start.6
  9.3 3.6 %collective-permute-start.7 = (bf16[2,128,1024]{1,2,0:T(8,128)(2,1)}, bf16[2,128,1024]{1,2,0:T(8,128)(2,1)}, u32[]{:S(2)}, u32[]{:S(2)}) collective-permute-start(bf16[2,128,1024]{1,2,0:T(8,128)(2,1)} %get-tuple-element.39), channel_id=1, source_target_pairs={{4,0},{8,4},{12,8},{16,12},{20,16},{24,20},{28,24},{5,1},{9,5},{13... | collective-permute-start | bytes 1572872 | tf_op jit(solution)/shard_map/ppermute | solution.py:216
  13.4 0.6 copy.154
  15.0 1.3 copy.153
  16.9 1.6 gather_fusion
  18.5 0.6 gather_fusion.2
  19.6 0.8 copy-done.7
  20.9 1.4 reshape.564
  22.3 0.6 copy.158
  23.0 2.3 %copy.138 = bf16[4,64,8,128]{3,1,2,0:T(8,128)(2,1)} copy(bf16[4,64,8,128]{1,0,3,2:T(4,128)(2,1)} %reshape.564) | data formatting | bytes 1048576 | tf_op jit(solution)/shard_map/convert_element_type | solution.py:65
  25.6 1.0 bitcast_add_fusion
  27.4 0.9 copy.165
  28.3 1.0 fusion.46
  29.3 4.7 %collective-permute-done.1 = bf16[96,1024]{1,0:T(8,128)(2,1)S(1)} collective-permute-done((bf16[96,1024]{1,0:T(8,128)(2,1)S(1)}, bf16[96,1024]{1,0:T(8,128)(2,1)S(1)}, u32[]{:S(2)}, u32[]{:S(2)}) %collective-permute-start.1) | collective-permute-done | bytes 196640 | tf_op jit(solution)/shard_map/ppermute | solution.py:105
  34.1 1.6 collective-permute-start.2
  35.7 3.1 %collective-permute-done.2 = bf16[48,1024]{1,0:T(8,128)(2,1)S(1)} collective-permute-done((bf16[48,1024]{1,0:T(8,128)(2,1)S(1)}, bf16[48,1024]{1,0:T(8,128)(2,1)S(1)}, u32[]{:S(2)}, u32[]{:S(2)}) %collective-permute-start.2) | collective-permute-done | bytes 98336 | tf_op jit(solution)/shard_map/ppermute | solution.py:105
  38.8 1.6 collective-permute-start.3
  40.7 0.7 copy.144
  41.4 2.1 collective-permute-done.3
  43.6 1.1 collective-permute-start.4
  44.7 0.6 broadcast_compare_fusion
  45.3 1.2 copy.134
  46.5 0.7 slice.211
  47.3 1.2 copy.136
  48.6 0.8 collective-permute-done.4
  49.7 1.3 maximum_bitcast_fusion
  51.0 2.2 %maximum_bitcast_fusion.1 = (bf16[2,1,5,64,1024]{4,3,2,0,1:T(8,128)(2,1)}, bf16[2,1,5,64,1024]{4,3,2,0,1:T(8,128)(2,1)}, bf16[2,1,5,64,1024]{4,3,2,0,1:T(8,128)(2,1)}) fusion(bf16[1,4,64,1024]{3,2,1,0:T(8,128)(2,1)S(1)} %bitcast.275, bf16[1,4,64,1024]{3,2,1,0:T(8,128)(2,1)S(1)} %copy.158, bf16[2,1,64,1024]{3,2,1,0:T(8,128)(2,1)S(1)} %copy-done.11, ...), kind=kLoop, calls=%fused_computation.38 | loop fusion | flops 3932160 | bytes 6029312 | tf_op jit(solution)/shard_map/stack | solution.py:250
  53.2 1.0 fusion.61
  55.6 1.2 pad_maximum_fusion.4
  57.9 1.2 pad_maximum_fusion
  59.1 1.5 fusion.118
  60.6 1.0 copy.167
  61.6 1.0 copy.168
  62.6 1.8 fusion
  64.5 1.5 fusion.5
  66.0 2.5 %fusion.21 = f32[4,64,8,128]{3,1,2,0:T(8,128)} fusion(bf16[4,448,8,128]{3,2,1,0:T(8,128)(2,1)S(1)} %bitcast.284, f32[4,8,64,448]{3,2,1,0:T(8,128)S(1)} %get-tuple-element.82, f32[4,8,64]{2,1,0:T(8,128)S(1)} %get-tuple-element.11, pred[4,8,448]{2,1,0:T(8,128)(4,1)S(1)} %broadcast_in_dim.170), kind=kOutput, calls=%fused_computation.31 | convolution fusion | flops 238551040 | bytes 8411136 | tf_op jit(solution)/shard_map/bhqs,bshd->bqhd/dot_general | solution.py:170
  70.6 0.9 collective-permute-done.8
  72.1 1.1 collective-permute-start.9
  73.6 0.6 copy.162
  74.4 2.8 %gather_fusion.3 = bf16[16,2,64,1024]{3,2,1,0:T(8,128)(2,1)} fusion(bf16[4,2,64,1024]{3,2,0,1:T(8,128)(2,1)S(1)} %pad_maximum_fusion.2, s32[1024]{0:T(1024)S(1)} %pad_clamp_fusion), kind=kCustom, calls=%fused_computation.3 | custom fusion | bytes 8388672 | tf_op jit(solution)/shard_map/gather | solution.py:294
  77.2 5.4 %all-to-all-start = ((bf16[8,2,2,64,1024]{4,3,2,1,0:T(8,128)(2,1)}), bf16[8,2,2,64,1024]{4,3,2,1,0:T(8,128)(2,1)}, u32[]{:S(2)}, u32[]{:S(2)}) async-start(bf16[8,2,2,64,1024]{4,3,2,1,0:T(8,128)(2,1)} %bitcast.271), calls=%async_computation | async-start | bytes 8388608 | tf_op jit(solution)/shard_map/all_to_all | solution.py:296
  83.1 1.6 collective-permute-start.10
  84.7 47.2 %collective-permute-done.10 = f32[16,1152]{1,0:T(8,128)S(1)} collective-permute-done((f32[16,1152]{1,0:T(8,128)S(1)}, f32[16,1152]{1,0:T(8,128)S(1)}, u32[]{:S(2)}, u32[]{:S(2)}) %collective-permute-start.10) | collective-permute-done | bytes 73760 | tf_op jit(solution)/shard_map/ppermute | solution.py:105
  132.6 0.6 fusion.121
  133.2 3.4 %collective-permute-done.11 = f32[16,1152]{1,0:T(8,128)S(1)} collective-permute-done((f32[16,1152]{1,0:T(8,128)S(1)}, f32[16,1152]{1,0:T(8,128)S(1)}, u32[]{:S(2)}, u32[]{:S(2)}) %collective-permute-start.11) | collective-permute-done | bytes 73760 | tf_op jit(solution)/shard_map/ppermute | solution.py:109
  136.6 0.6 collective-permute-start.12
  137.3 0.6 fusion.120
  137.9 1.3 compare_and_fusion.1
  139.4 2.5 %collective-permute-done.12 = f32[32,1152]{1,0:T(8,128)S(1)} collective-permute-done((f32[32,1152]{1,0:T(8,128)S(1)}, f32[32,1152]{1,0:T(8,128)S(1)}, u32[]{:S(2)}, u32[]{:S(2)}) %collective-permute-start.12) | collective-permute-done | bytes 147488 | tf_op jit(solution)/shard_map/ppermute | solution.py:109
  142.0 1.3 compare_and_fusion
  144.2 2.8 %gather_fusion.4 = bf16[12,64,1024]{2,1,0:T(8,128)(2,1)S(1)} fusion(bf16[8,2,2,64,1024]{4,3,2,1,0:T(8,128)(2,1)} %all-to-all-done, s32[12]{0:T(128)S(1)} %bitcast.329), kind=kCustom, calls=%fused_computation.4 | custom fusion | bytes 3145872 | tf_op jit(solution)/shard_map/gather | solution.py:299
  147.5 1.2 multiply_reduce_fusion
  148.7 4.0 %gather_fusion.5 = bf16[12,64,1024]{2,1,0:T(8,128)(2,1)} fusion(bf16[8,2,2,64,1024]{4,3,2,1,0:T(8,128)(2,1)} %all-to-all-done, s32[12]{0:T(128)S(1)} %get-tuple-element.13), kind=kCustom, calls=%fused_computation.5 | custom fusion | bytes 3145872 | tf_op jit(solution)/shard_map/gather | solution.py:300
  152.8 2.0 copy.177
  154.8 0.7 fusion.12
  155.6 1.6 fusion.37
  157.8 2.5 %convolution_convert_fusion = bf16[256,4096]{1,0:T(8,128)(2,1)S(1)} fusion(bf16[1024,4096]{1,0:T(8,128)(2,1)S(1)} %bitcast.338, bf16[256,1024]{1,0:T(8,128)(2,1)S(1)} %bitcast.314, bf16[256,1024]{1,0:T(8,128)(2,1)S(1)} %bitcast.315, bf16[32,8,8,128]{3,2,1,0:T(8,128)(2,1)S(1)} %bitcast.319, pred[256]{0:T(512)(128)(4,1)S(1)} %broadcast_in_dim.179, ...), kind=kOutput, calls=%fused_computation.7 | convolution fusion | flops 2149056512 | bytes 12059136 | tf_op jit(solution)/shard_map/dot_general | solution.py:145
  160.5 53.5 %all_to_all.10 = bf16[4,1024,256]{1,2,0:T(8,128)(2,1)S(1)} all-to-all(bf16[4,1024,256]{1,2,0:T(8,128)(2,1)S(1)} %bitcast.280), channel_id=1, replica_groups=mesh['seq'=8,'head'=4] {'head'}, dimensions={0} | all-to-all | bytes 4194304 | tf_op jit(solution)/shard_map/all_to_all | solution.py:152
  214.0 1.3 reduce_sum.65
  (166 shorter events, 15.0 us)
Async XLA Ops:
  0.0 2.8 %copy-start.12 = (bf16[256,1024]{1,0:T(8,128)(2,1)S(1)}, bf16[256,1024]{1,0:T(8,128)(2,1)}, u32[]{:S(2)}) copy-start(bf16[256,1024]{1,0:T(8,128)(2,1)} %param.9) | copy-start | bytes 1572868
  2.7 1.0 copy-start
  5.0 1.0 copy-start.10
  7.2 6.8 %copy-start.19 = (s32[2]{0:T(128)S(1)}, s32[2]{0:T(128)}, u32[]{:S(2)}) copy-start(s32[2]{0:T(128)} %param.13) | copy-start | bytes 28
  7.2 38.0 %collective-permute-start.6 = (bf16[2,128,1024]{1,2,0:T(8,128)(2,1)}, bf16[2,128,1024]{1,2,0:T(8,128)(2,1)}, u32[]{:S(2)}, u32[]{:S(2)}) collective-permute-start(bf16[2,128,1024]{1,2,0:T(8,128)(2,1)} %get-tuple-element.38), channel_id=1, source_target_pairs={{0,4},{4,8},{8,12},{12,16},{16,20},{20,24},{24,28},{1,5},{5,9},{9,... | collective-permute-start | bytes 1572872 | tf_op jit(solution)/shard_map/ppermute | solution.py:213
  9.3 38.0 %collective-permute-start.7 = (bf16[2,128,1024]{1,2,0:T(8,128)(2,1)}, bf16[2,128,1024]{1,2,0:T(8,128)(2,1)}, u32[]{:S(2)}, u32[]{:S(2)}) collective-permute-start(bf16[2,128,1024]{1,2,0:T(8,128)(2,1)} %get-tuple-element.39), channel_id=1, source_target_pairs={{4,0},{8,4},{12,8},{16,12},{20,16},{24,20},{28,24},{5,1},{9,5},{13... | collective-permute-start | bytes 1572872 | tf_op jit(solution)/shard_map/ppermute | solution.py:216
  14.0 5.1 %copy-start.15 = (pred[2]{0:T(512)(128)(4,1)}, pred[2]{0:T(512)(128)(4,1)S(1)}, u32[]{:S(2)}) copy-start(pred[2]{0:T(512)(128)(4,1)S(1)} %fusion.107) | copy-start | bytes 10
  19.5 0.9 copy-start.7
  20.4 5.2 %collective-permute-start = (bf16[192,1024]{1,0:T(8,128)(2,1)S(1)}, bf16[192,1024]{1,0:T(8,128)(2,1)S(1)}, u32[]{:S(2)}, u32[]{:S(2)}) collective-permute-start(bf16[192,1024]{1,0:T(8,128)(2,1)S(1)} %dynamic-slice_bitcast_fusion), channel_id=1, source_target_pairs={{0,4},{4,0},{8,12},{12,8},{16,20},{20,16},{24,28},{28,24},{1,5},{5... | collective-permute-start | bytes 1179656 | tf_op jit(solution)/shard_map/ppermute | solution.py:105
  20.9 4.4 %copy-start.18 = (s32[32,3]{0,1:T(4,128)S(1)}, s32[32,3]{0,1:T(4,128)}, u32[]{:S(2)}) copy-start(s32[32,3]{0,1:T(4,128)} %param.14) | copy-start | bytes 1156
  20.9 4.6 %copy-start.20 = (s32[8]{0:T(128)S(1)}, s32[8]{0:T(128)}, u32[]{:S(2)}) copy-start(s32[8]{0:T(128)} %param.15) | copy-start | bytes 100
  26.7 7.4 %collective-permute-start.1 = (bf16[96,1024]{1,0:T(8,128)(2,1)S(1)}, bf16[96,1024]{1,0:T(8,128)(2,1)S(1)}, u32[]{:S(2)}, u32[]{:S(2)}) collective-permute-start(bf16[96,1024]{1,0:T(8,128)(2,1)S(1)} %dynamic-slice_bitcast_fusion.3), channel_id=1, source_target_pairs={{0,8},{4,12},{8,0},{12,4},{16,24},{20,28},{24,16},{28,20},{1,9},{5... | collective-permute-start | bytes 589832 | tf_op jit(solution)/shard_map/ppermute | solution.py:105
  34.1 4.7 %collective-permute-start.2 = (bf16[48,1024]{1,0:T(8,128)(2,1)S(1)}, bf16[48,1024]{1,0:T(8,128)(2,1)S(1)}, u32[]{:S(2)}, u32[]{:S(2)}) collective-permute-start(bf16[48,1024]{1,0:T(8,128)(2,1)S(1)} %dynamic-slice_bitcast_fusion.6), channel_id=1, source_target_pairs={{0,16},{4,20},{8,24},{12,28},{16,0},{20,4},{24,8},{28,12},{1,17},{... | collective-permute-start | bytes 294920 | tf_op jit(solution)/shard_map/ppermute | solution.py:105
  38.8 4.7 %collective-permute-start.3 = (bf16[48,1024]{1,0:T(8,128)(2,1)S(1)}, bf16[48,1024]{1,0:T(8,128)(2,1)S(1)}, u32[]{:S(2)}, u32[]{:S(2)}) collective-permute-start(bf16[48,1024]{1,0:T(8,128)(2,1)S(1)} %bitcast_add_fusion.2), channel_id=1, source_target_pairs={{0,16},{4,20},{8,24},{12,28},{16,0},{20,4},{24,8},{28,12},{1,17},{... | collective-permute-start | bytes 294920 | tf_op jit(solution)/shard_map/ppermute | solution.py:109
  43.6 5.7 %collective-permute-start.4 = (bf16[96,1024]{1,0:T(8,128)(2,1)S(1)}, bf16[96,1024]{1,0:T(8,128)(2,1)S(1)}, u32[]{:S(2)}, u32[]{:S(2)}) collective-permute-start(bf16[96,1024]{1,0:T(8,128)(2,1)S(1)} %get-tuple-element.58), channel_id=1, source_target_pairs={{0,8},{4,12},{8,0},{12,4},{16,24},{20,28},{24,16},{28,20},{1,9},{5... | collective-permute-start | bytes 589832 | tf_op jit(solution)/shard_map/ppermute | solution.py:109
  48.5 1.1 copy-start.5
  49.5 1.5 copy-start.11
  49.6 3.6 %collective-permute-start.5 = (bf16[192,1024]{1,0:T(8,128)(2,1)S(1)}, bf16[192,1024]{1,0:T(8,128)(2,1)S(1)}, u32[]{:S(2)}, u32[]{:S(2)}) collective-permute-start(bf16[192,1024]{1,0:T(8,128)(2,1)S(1)} %get-tuple-element.46), channel_id=1, source_target_pairs={{0,4},{4,0},{8,12},{12,8},{16,20},{20,16},{24,28},{28,24},{1,5},{5... | collective-permute-start | bytes 1179656 | tf_op jit(solution)/shard_map/ppermute | solution.py:109
  49.7 1.3 copy-start.6
  54.2 0.8 copy-start.8
  55.6 1.5 copy-start.1
  55.6 1.9 copy-start.2
  55.6 2.3 %copy-start.3 = (bf16[2,1,5,64,1024]{4,3,2,0,1:T(8,128)(2,1)S(1)}, bf16[2,1,5,64,1024]{4,3,2,0,1:T(8,128)(2,1)}, u32[]{:S(2)}) copy-start(bf16[2,1,5,64,1024]{4,3,2,0,1:T(8,128)(2,1)} %get-tuple-element.37) | copy-start | bytes 3932164
  61.6 1.0 copy-start.4
  66.0 2.7 %copy-start.9 = (bf16[32,8,8,128]{3,2,1,0:T(8,128)(2,1)S(1)}, bf16[32,8,8,128]{3,2,1,0:T(8,128)(2,1)}, u32[]{:S(2)}) copy-start(bf16[32,8,8,128]{3,2,1,0:T(8,128)(2,1)} %copy.165) | copy-start | bytes 1572868
  69.1 1.2 copy-start.13
  69.1 1.2 copy-start.17
  69.7 1.8 collective-permute-start.8
  72.1 10.5 %collective-permute-start.9 = (f32[32,1152]{1,0:T(8,128)S(1)}, f32[32,1152]{1,0:T(8,128)S(1)}, u32[]{:S(2)}, u32[]{:S(2)}) collective-permute-start(f32[32,1152]{1,0:T(8,128)S(1)} %get-tuple-element.55), channel_id=1, source_target_pairs={{0,8},{4,12},{8,0},{12,4},{16,24},{20,28},{24,16},{28,20},{1,9},{5... | collective-permute-start | bytes 442376 | tf_op jit(solution)/shard_map/ppermute | solution.py:105
  77.2 67.0 %all-to-all-start = ((bf16[8,2,2,64,1024]{4,3,2,1,0:T(8,128)(2,1)}), bf16[8,2,2,64,1024]{4,3,2,1,0:T(8,128)(2,1)}, u32[]{:S(2)}, u32[]{:S(2)}) async-start(bf16[8,2,2,64,1024]{4,3,2,1,0:T(8,128)(2,1)} %bitcast.271), calls=%async_computation | async-start | bytes 8388608 | tf_op jit(solution)/shard_map/all_to_all | solution.py:296
  82.6 49.9 %copy-start.16 = (pred[2]{0:T(512)(128)(4,1)S(1)}, pred[2]{0:T(512)(128)(4,1)}, u32[]{:S(2)}) copy-start(pred[2]{0:T(512)(128)(4,1)} %copy-done.15) | copy-start | bytes 10
  82.6 54.6 %copy-start.14 = (s32[2]{0:T(128)S(1)}, s32[2]{0:T(128)}, u32[]{:S(2)}) copy-start(s32[2]{0:T(128)} %get-tuple-element.28) | copy-start | bytes 28
  83.1 48.7 %collective-permute-start.10 = (f32[16,1152]{1,0:T(8,128)S(1)}, f32[16,1152]{1,0:T(8,128)S(1)}, u32[]{:S(2)}, u32[]{:S(2)}) collective-permute-start(f32[16,1152]{1,0:T(8,128)S(1)} %get-tuple-element.67), channel_id=1, source_target_pairs={{0,16},{4,20},{8,24},{12,28},{16,0},{20,4},{24,8},{28,12},{1,17},{... | collective-permute-start | bytes 221192 | tf_op jit(solution)/shard_map/ppermute | solution.py:105
  132.2 4.4 %collective-permute-start.11 = (f32[16,1152]{1,0:T(8,128)S(1)}, f32[16,1152]{1,0:T(8,128)S(1)}, u32[]{:S(2)}, u32[]{:S(2)}) collective-permute-start(f32[16,1152]{1,0:T(8,128)S(1)} %concatenate.71), channel_id=1, source_target_pairs={{0,16},{4,20},{8,24},{12,28},{16,0},{20,4},{24,8},{28,12},{1,17},{... | collective-permute-start | bytes 221192 | tf_op jit(solution)/shard_map/ppermute | solution.py:109
  136.6 5.2 %collective-permute-start.12 = (f32[32,1152]{1,0:T(8,128)S(1)}, f32[32,1152]{1,0:T(8,128)S(1)}, u32[]{:S(2)}, u32[]{:S(2)}) collective-permute-start(f32[32,1152]{1,0:T(8,128)S(1)} %get-tuple-element.62), channel_id=1, source_target_pairs={{0,8},{4,12},{8,0},{12,4},{16,24},{20,28},{24,16},{28,20},{1,9},{5... | collective-permute-start | bytes 442376 | tf_op jit(solution)/shard_map/ppermute | solution.py:109
  142.0 1.7 collective-permute-start.13
  152.8 2.8 %copy-start.21 = (f32[4,64,8,128]{3,1,2,0:T(8,128)S(1)}, f32[4,64,8,128]{3,1,2,0:T(8,128)}, u32[]{:S(2)}) copy-start(f32[4,64,8,128]{3,1,2,0:T(8,128)} %fusion.21) | copy-start | bytes 3145732
  152.8 4.9 %slice-start = ((s8[8388608]{0:T(1024)(128)(4,1)}), s8[4194304]{0:T(1024)(128)(4,1)S(1)}, s32[]{:S(2)}) async-start(s8[8388608]{0:T(1024)(128)(4,1)} %bitcast.337), calls=%async_computation.2 | async-start | bytes 8388608
  155.6 2.2 %slice-start.1 = ((s8[8388608]{0:T(1024)(128)(4,1)}), s8[4194304]{0:T(1024)(128)(4,1)S(1)}, s32[]{:S(2)}) async-start(s8[8388608]{0:T(1024)(128)(4,1)} %bitcast.337), calls=%async_computation.3 | async-start | bytes 8388608

commit v8 on v6

--- a/solution.py
+++ b/solution.py
@@ -291,8 +291,8 @@
         ranks[:, None, :] == jnp.arange(capacity)[None, :, None]
     )
     send_local = jnp.sum(jnp.where(wanted, local_ids[:, None, :], 0), axis=2)
-    kv_blocks = jnp.stack([key_rot.reshape(blocks_here, BLOCK, width_here), value_view], axis=1)
-    outgoing = kv_blocks[send_local]
+    key_blocks = key_rot.reshape(blocks_here, BLOCK, width_here)
+    outgoing = jnp.stack([key_blocks[send_local], value_view[send_local]], axis=2)
     outgoing, reduced = lax.optimization_barrier((outgoing, reduced))
     incoming = lax.all_to_all(outgoing, "seq", split_axis=0, concat_axis=0, tiled=True)
     my_owners = owners[seq_place]
@@ -301,19 +301,32 @@
     random_v = incoming[my_owners, my_ranks, 1].reshape(blocks_here, RAND, BLOCK, width_here)
     random_kv = (random_k, random_v)
     near_part = partial_attend(query_view, near_kv[0], near_kv[1], near_valid)
-    far_part = partial_attend(
-        query_view, random_kv[0], random_kv[1], jnp.ones((blocks_here, RAND, heads_here), dtype=bool)
-    )
-    attended = merge_attend(near_part, far_part)
     mix_sum = reduced[:, :width_here].reshape(row_total, heads_here, HEAD_DIM)
     total_sum = reduced[:, width_here : width_here + heads_here]
     global_out = (mix_sum / total_sum[..., None]).reshape(row_total, width_here).astype(jnp.bfloat16)
     global_out = global_out.reshape(GLOB, BLOCK, width_here)
-    block_index = jnp.arange(blocks_here)
-    for global_slot in range(GLOB):
-        hit = mine_global[global_slot] & (block_index == local_global[global_slot])
-        attended = jnp.where(hit[:, None, None], global_out[global_slot][None], attended)
-    mixed = sum_over_head(head_partials(attended.reshape(tok_here, width_here), out_weight))
+    pieces = 2 if blocks_here % 2 == 0 else 1
+    span = blocks_here // pieces
+    outputs = []
+    for piece in range(pieces):
+        lo = piece * span
+        hi = lo + span
+        near_piece = jax.tree.map(lambda x: x[lo:hi], near_part)
+        far_part = partial_attend(
+            query_view[lo:hi],
+            random_k[lo:hi],
+            random_v[lo:hi],
+            jnp.ones((span, RAND, heads_here), dtype=bool),
+        )
+        attended = merge_attend(near_piece, far_part)
+        block_index = jnp.arange(lo, hi)
+        for global_slot in range(GLOB):
+            hit = mine_global[global_slot] & (block_index == local_global[global_slot])
+            attended = jnp.where(hit[:, None, None], global_out[global_slot][None], attended)
+        outputs.append(
+            sum_over_head(head_partials(attended.reshape(span * BLOCK, width_here), out_weight))
+        )
+    mixed = jnp.concatenate(outputs, axis=0)
     return mixed.astype(jnp.bfloat16)
 
 

time: 213 us -> 233 us (1.094)
  blocking collectives: 53.1 us -> 0 us
  waiting for transfers between devices: 61.4 us -> 104 us
  starting transfers between devices: 20.8 us -> 33.1 us
  other arithmetic: 18.8 us -> 29.4 us
  matrix products: 9.67 us -> 14.2 us
  local copies, waits for them, and re-layouts: 45.7 us -> 49 us
    all_to_all x1 -> x0, blocking collectives: 53.1 us -> none  [sum_over_head(): gathered = lax.all_to_all(partial, 'head', 0, 0, tiled=True)]
    all_to_all x0 -> x2, waiting for transfers between devices: none -> 45.1 us  [sum_over_head(): gathered = lax.all_to_all(partial, 'head', 0, 0, tiled=True)]
    all_to_all x0 -> x2, starting transfers between devices: none -> 8.28 us  [sum_over_head(): gathered = lax.all_to_all(partial, 'head', 0, 0, tiled=True)]
    convert_element_type x10 -> x7, local copies, waits for them, and re-layouts: 11 us -> 5.24 us  [rotate(): return turned.reshape(row_count, row_width).astype(jnp.bfloat16)]
    another operation x1, other arithmetic: 0.1 us -> 4.57 us  [on_device(): jnp.stack([key_blocks[send_local], value_view[send_local]], axis=2)]
    ppermute x6, waiting for transfers between devices: 19 us -> 15.1 us  [tree_reduce(): got = lax.ppermute(send, axis, xor_perm(count, bit))]
    all_to_all x1, waiting for transfers between devices: 31.5 us -> 35 us  [on_device(): lax.all_to_all(outgoing, 'seq', split_axis=0, concat_axis=0, tiled=True)]
    dot_general x1 -> x2, matrix products: 2.48 us -> 5.93 us  [head_partials(): lax.dot_general(out_weight, rows, (((0,), (1,)), ((), ())), preferred_ele...]
  transfers between devices with their start and end apart: 15 -> 17, of which waited for: 11 -> 11; matrix products, arithmetic and copies ran while one was open for 22% -> 26% of each run, Pallas kernels for 0% -> 0%
where the time goes in v8:
time: 233 us; the launch traced here: 232 us
  waiting for transfers between devices  104 us (45%)
  local copies, waits for them, and re-layouts  49 us (21%)
  starting transfers between devices  33.1 us (14%)
  other arithmetic  29.4 us (13%)
  matrix products  14.2 us (6%)
  between operations  2.39 us (1%)
    all_to_all x2, waiting for transfers between devices, sum_over_head(): gathered = lax.all_to_all(partial, 'head', 0, 0, tiled=True)  45.1 us
    all_to_all x1, waiting for transfers between devices, on_device(): lax.all_to_all(outgoing, 'seq', split_axis=0, concat_axis=0, tiled=True)  35 us
    ppermute x6, waiting for transfers between devices, tree_reduce(): got = lax.ppermute(send, axis, xor_perm(count, bit))  15.1 us
    unnamed x63, local copies, waits for them, and re-layouts  9.84 us
    ppermute x6, waiting for transfers between devices, tree_reduce(): got = lax.ppermute(parts, axis, xor_perm(count, bit))  8.67 us
    all_to_all x2, starting transfers between devices, sum_over_head(): gathered = lax.all_to_all(partial, 'head', 0, 0, tiled=True)  8.28 us
    ppermute x6, starting transfers between devices, tree_reduce(): got = lax.ppermute(parts, axis, xor_perm(count, bit))  7.73 us
    ppermute x6, starting transfers between devices, tree_reduce(): got = lax.ppermute(send, axis, xor_perm(count, bit))  6.53 us
  transfers between devices with their start and end apart: 17, of which 11 were waited for; matrix products, arithmetic and copies ran while one was open for 26% of the time, Pallas kernels for 0%

profile of v8, /device:TPU:2, one launch (start us, length us, event | category | flops | bytes accessed | tf_op | source)
XLA Modules:
  0.0 231.9 jit_solution(17950090240110441362)
XLA Ops:
  0.0 1.2 copy.154
  2.7 1.2 copy.147
  7.1 1.3 gather_fusion.3
  8.8 1.3 copy.185
  10.2 1.6 gather_fusion.2
  11.9 1.0 pad_maximum_fusion.3
  14.1 1.2 fusion.43
  15.3 2.4 %collective-permute-start.12 = (bf16[2,128,1024]{1,2,0:T(8,128)(2,1)}, bf16[2,128,1024]{1,2,0:T(8,128)(2,1)}, u32[]{:S(2)}, u32[]{:S(2)}) collective-permute-start(bf16[2,128,1024]{1,2,0:T(8,128)(2,1)} %get-tuple-element.38), channel_id=1, source_target_pairs={{0,4},{4,8},{8,12},{12,16},{16,20},{20,24},{24,28},{1,5},{5,9},{9,... | collective-permute-start | bytes 1572872 | tf_op jit(solution)/shard_map/ppermute | solution.py:213
  17.7 3.1 %collective-permute-start.13 = (bf16[2,128,1024]{1,2,0:T(8,128)(2,1)}, bf16[2,128,1024]{1,2,0:T(8,128)(2,1)}, u32[]{:S(2)}, u32[]{:S(2)}) collective-permute-start(bf16[2,128,1024]{1,2,0:T(8,128)(2,1)} %get-tuple-element.39), channel_id=1, source_target_pairs={{4,0},{8,4},{12,8},{16,12},{20,16},{24,20},{28,24},{5,1},{9,5},{13... | collective-permute-start | bytes 1572872 | tf_op jit(solution)/shard_map/ppermute | solution.py:216
  21.9 2.0 gather_fusion.1
  24.0 2.1 gather_fusion
  27.2 1.0 bitcast_add_fusion
  28.4 6.6 %collective-permute-done.1 = bf16[96,1024]{1,0:T(8,128)(2,1)S(1)} collective-permute-done((bf16[96,1024]{1,0:T(8,128)(2,1)S(1)}, bf16[96,1024]{1,0:T(8,128)(2,1)S(1)}, u32[]{:S(2)}, u32[]{:S(2)}) %collective-permute-start.1) | collective-permute-done | bytes 196640 | tf_op jit(solution)/shard_map/ppermute | solution.py:105
  35.0 2.4 %collective-permute-start.2 = (bf16[48,1024]{1,0:T(8,128)(2,1)S(1)}, bf16[48,1024]{1,0:T(8,128)(2,1)S(1)}, u32[]{:S(2)}, u32[]{:S(2)}) collective-permute-start(bf16[48,1024]{1,0:T(8,128)(2,1)S(1)} %dynamic-slice_bitcast_fusion.6), channel_id=1, source_target_pairs={{0,16},{4,20},{8,24},{12,28},{16,0},{20,4},{24,8},{28,12},{1,17},{... | collective-permute-start | bytes 294920 | tf_op jit(solution)/shard_map/ppermute | solution.py:105
  37.5 2.6 %collective-permute-done.2 = bf16[48,1024]{1,0:T(8,128)(2,1)S(1)} collective-permute-done((bf16[48,1024]{1,0:T(8,128)(2,1)S(1)}, bf16[48,1024]{1,0:T(8,128)(2,1)S(1)}, u32[]{:S(2)}, u32[]{:S(2)}) %collective-permute-start.2) | collective-permute-done | bytes 98336 | tf_op jit(solution)/shard_map/ppermute | solution.py:105
  40.1 2.1 collective-permute-start.3
  42.2 2.6 %collective-permute-done.3 = bf16[48,1024]{1,0:T(8,128)(2,1)S(1)} collective-permute-done((bf16[48,1024]{1,0:T(8,128)(2,1)S(1)}, bf16[48,1024]{1,0:T(8,128)(2,1)S(1)}, u32[]{:S(2)}, u32[]{:S(2)}) %collective-permute-start.3) | collective-permute-done | bytes 98336 | tf_op jit(solution)/shard_map/ppermute | solution.py:109
  44.9 2.2 collective-permute-start.4
  47.1 3.6 %collective-permute-done.4 = bf16[96,1024]{1,0:T(8,128)(2,1)S(1)} collective-permute-done((bf16[96,1024]{1,0:T(8,128)(2,1)S(1)}, bf16[96,1024]{1,0:T(8,128)(2,1)S(1)}, u32[]{:S(2)}, u32[]{:S(2)}) %collective-permute-start.4) | collective-permute-done | bytes 196640 | tf_op jit(solution)/shard_map/ppermute | solution.py:109
  51.7 1.1 collective-permute-done.5
  52.7 1.0 fusion.53
  54.4 1.1 fusion.33
  57.5 1.0 concatenate.67
  58.8 4.6 %pad_maximum_fusion.1 = bf16[8,2,2,64,1024]{4,3,1,2,0:T(8,128)(2,1)} fusion(bf16[8,2,1,64,1024]{4,3,1,2,0:T(8,128)(2,1)} %bitcast.323, bf16[8,2,1,64,1024]{4,3,1,2,0:T(8,128)(2,1)} %bitcast.324), kind=kLoop, calls=%fused_computation.10 | loop fusion | flops 2097152 | bytes 8388608 | tf_op jit(solution)/shard_map/stack | solution.py:295
  64.8 2.1 collective-permute-start.7
  68.1 3.2 %collective-permute-done.7 = f32[32,1152]{1,0:T(8,128)S(1)} collective-permute-done((f32[32,1152]{1,0:T(8,128)S(1)}, f32[32,1152]{1,0:T(8,128)S(1)}, u32[]{:S(2)}, u32[]{:S(2)}) %collective-permute-start.7) | collective-permute-done | bytes 147488 | tf_op jit(solution)/shard_map/ppermute | solution.py:105
  71.8 1.7 collective-permute-start.8
  73.5 2.7 %collective-permute-done.8 = f32[16,1152]{1,0:T(8,128)S(1)} collective-permute-done((f32[16,1152]{1,0:T(8,128)S(1)}, f32[16,1152]{1,0:T(8,128)S(1)}, u32[]{:S(2)}, u32[]{:S(2)}) %collective-permute-start.8) | collective-permute-done | bytes 73760 | tf_op jit(solution)/shard_map/ppermute | solution.py:105
  76.6 1.7 collective-permute-start.9
  78.2 1.3 compare_and_fusion
  79.5 1.4 collective-permute-done.9
  81.7 1.7 collective-permute-start.10
  83.4 1.2 compare_and_fusion.1
  85.1 1.4 reshape.629
  86.5 2.0 reshape.630
  90.0 1.1 reshape.631
  92.8 1.2 copy.163
  94.1 1.0 fusion.67
  95.0 0.9 pad_maximum_fusion.9
  96.8 1.2 copy.165
  98.9 3.0 %maximum_bitcast_fusion.1 = (bf16[2,1,5,64,1024]{4,3,2,0,1:T(8,128)(2,1)S(1)}, bf16[2,1,5,64,1024]{4,3,2,0,1:T(8,128)(2,1)}, bf16[2,1,5,64,1024]{4,3,2,0,1:T(8,128)(2,1)}) fusion(bf16[1,4,64,1024]{3,2,1,0:T(8,128)(2,1)S(1)} %bitcast.314, bf16[1,4,64,1024]{3,2,1,0:T(8,128)(2,1)} %copy-done.3, bf16[2,1,64,1024]{3,2,1,0:T(8,128)(2,1)} %slice.295, ...), kind=kLoop, calls=%fused_computation.31 | loop fusion | flops 3932160 | bytes 6029312 | tf_op jit(solution)/shard_map/stack | solution.py:250
  101.9 1.1 fusion.58
  103.0 0.9 pad_maximum_fusion.4
  103.9 5.0 %all-to-all-start = ((bf16[8,2,2,64,1024]{4,3,1,2,0:T(8,128)(2,1)}), bf16[8,2,2,64,1024]{4,3,1,2,0:T(8,128)(2,1)}, u32[]{:S(2)}, u32[]{:S(2)}) async-start(bf16[8,2,2,64,1024]{4,3,1,2,0:T(8,128)(2,1)} %pad_maximum_fusion.1), calls=%async_computation | async-start | bytes 8388608 | tf_op jit(solution)/shard_map/all_to_all | solution.py:297
  109.3 1.0 copy-done.1
  110.7 1.0 pad_maximum_fusion
  111.7 1.5 fusion.117
  113.3 1.0 copy.208
  114.2 1.0 copy.207
  115.4 1.8 fusion
  117.2 1.6 fusion.5
  118.8 2.5 %fusion.12 = f32[4,64,8,128]{3,1,2,0:T(8,128)} fusion(bf16[4,448,8,128]{3,2,1,0:T(8,128)(2,1)S(1)} %bitcast.327, f32[4,8,64,448]{3,2,1,0:T(8,128)S(1)} %get-tuple-element.89, f32[4,8,64]{2,1,0:T(8,128)S(1)} %get-tuple-element.88, pred[4,8,448]{2,1,0:T(8,128)(4,1)S(1)} %copy-done.12), kind=kOutput, calls=%fused_computation.24 | convolution fusion | flops 238551040 | bytes 8411136 | tf_op jit(solution)/shard_map/bhqs,bshd->bqhd/dot_general | solution.py:170
  121.7 35.0 %all-to-all-done = bf16[8,2,2,64,1024]{4,3,1,2,0:T(8,128)(2,1)} async-done(((bf16[8,2,2,64,1024]{4,3,1,2,0:T(8,128)(2,1)}), bf16[8,2,2,64,1024]{4,3,1,2,0:T(8,128)(2,1)}, u32[]{:S(2)}, u32[]{:S(2)}) %all-to-all-start) | async-done | bytes 4194336 | tf_op jit(solution)/shard_map/all_to_all | solution.py:297
  156.7 2.8 %gather_fusion.6 = bf16[12,64,1024]{2,1,0:T(8,128)(2,1)S(1)} fusion(bf16[8,2,2,64,1024]{4,3,1,2,0:T(8,128)(2,1)} %all-to-all-done, s32[12]{0:T(128)S(1)} %get-tuple-element.9), kind=kCustom, calls=%fused_computation.6 | custom fusion | bytes 3145872 | tf_op jit(solution)/shard_map/gather | solution.py:301
  159.9 2.8 %gather_fusion.5 = bf16[12,64,1024]{2,1,0:T(8,128)(2,1)S(1)} fusion(bf16[8,2,2,64,1024]{4,3,1,2,0:T(8,128)(2,1)} %all-to-all-done, s32[12]{0:T(128)S(1)} %bitcast.374), kind=kCustom, calls=%fused_computation.5 | custom fusion | bytes 3145872 | tf_op jit(solution)/shard_map/gather | solution.py:300
  167.3 1.0 fusion.25
  169.2 1.3 convolution_convert_fusion
  170.5 1.1 copy.261
  171.6 4.8 %all-to-all-start.2 = ((bf16[4,1024,128]{1,2,0:T(8,128)(2,1)}), bf16[4,1024,128]{1,2,0:T(8,128)(2,1)S(1)}, u32[]{:S(2)}, u32[]{:S(2)}) async-start(bf16[4,1024,128]{1,2,0:T(8,128)(2,1)} %bitcast.305), calls=%async_computation.2 | async-start | bytes 2097152 | tf_op jit(solution)/shard_map/all_to_all | solution.py:152
  176.3 4.6 %convolution_convert_fusion.1 = bf16[128,4096]{1,0:T(8,128)(2,1)S(1)} fusion(bf16[128,1024]{1,0:T(8,128)(2,1)S(1)} %get-tuple-element.58, bf16[1024,4096]{1,0:T(8,128)(2,1)} %param.12), kind=kOutput, calls=%fused_computation.9 | convolution fusion | flops 1074266112 | bytes 9699328 | tf_op jit(solution)/shard_map/dot_general | solution.py:145
  181.0 1.1 copy.262
  182.1 20.1 %all-to-all-done.2 = bf16[4,1024,128]{1,2,0:T(8,128)(2,1)S(1)} async-done(((bf16[4,1024,128]{1,2,0:T(8,128)(2,1)}), bf16[4,1024,128]{1,2,0:T(8,128)(2,1)S(1)}, u32[]{:S(2)}, u32[]{:S(2)}) %all-to-all-start.2) | async-done | bytes 1048608 | tf_op jit(solution)/shard_map/all_to_all | solution.py:152
  202.1 3.5 %all-to-all-start.1 = ((bf16[4,1024,128]{1,2,0:T(8,128)(2,1)}), bf16[4,1024,128]{1,2,0:T(8,128)(2,1)S(1)}, u32[]{:S(2)}, u32[]{:S(2)}) async-start(bf16[4,1024,128]{1,2,0:T(8,128)(2,1)} %bitcast.306), calls=%async_computation.1 | async-start | bytes 2097152 | tf_op jit(solution)/shard_map/all_to_all | solution.py:152
  205.9 25.0 %all-to-all-done.1 = bf16[4,1024,128]{1,2,0:T(8,128)(2,1)S(1)} async-done(((bf16[4,1024,128]{1,2,0:T(8,128)(2,1)}), bf16[4,1024,128]{1,2,0:T(8,128)(2,1)S(1)}, u32[]{:S(2)}, u32[]{:S(2)}) %all-to-all-start.1) | async-done | bytes 1048608 | tf_op jit(solution)/shard_map/all_to_all | solution.py:152
  (188 shorter events, 28.6 us)
Async XLA Ops:
  4.4 1.5 copy-start.20
  4.4 2.1 copy-start
  6.0 7.1 %copy-start.14 = (pred[2]{0:T(512)(128)(4,1)}, pred[2]{0:T(512)(128)(4,1)S(1)}, u32[]{:S(2)}) copy-start(pred[2]{0:T(512)(128)(4,1)S(1)} %fusion.107) | copy-start | bytes 10
  11.8 9.1 %copy-start.17 = (s32[32,3]{0,1:T(4,128)S(1)}, s32[32,3]{0,1:T(4,128)}, u32[]{:S(2)}) copy-start(s32[32,3]{0,1:T(4,128)} %param.14) | copy-start | bytes 1156
  13.9 13.3 %collective-permute-start = (bf16[192,1024]{1,0:T(8,128)(2,1)}, bf16[192,1024]{1,0:T(8,128)(2,1)}, u32[]{:S(2)}, u32[]{:S(2)}) collective-permute-start(bf16[192,1024]{1,0:T(8,128)(2,1)} %dynamic-slice_bitcast_fusion), channel_id=1, source_target_pairs={{0,4},{4,0},{8,12},{12,8},{16,20},{20,16},{24,28},{28,24},{1,5},{5... | collective-permute-start | bytes 1179656 | tf_op jit(solution)/shard_map/ppermute | solution.py:105
  15.3 77.5 %collective-permute-start.12 = (bf16[2,128,1024]{1,2,0:T(8,128)(2,1)}, bf16[2,128,1024]{1,2,0:T(8,128)(2,1)}, u32[]{:S(2)}, u32[]{:S(2)}) collective-permute-start(bf16[2,128,1024]{1,2,0:T(8,128)(2,1)} %get-tuple-element.38), channel_id=1, source_target_pairs={{0,4},{4,8},{8,12},{12,16},{16,20},{20,24},{24,28},{1,5},{5,9},{9,... | collective-permute-start | bytes 1572872 | tf_op jit(solution)/shard_map/ppermute | solution.py:213
  17.7 79.1 %collective-permute-start.13 = (bf16[2,128,1024]{1,2,0:T(8,128)(2,1)}, bf16[2,128,1024]{1,2,0:T(8,128)(2,1)}, u32[]{:S(2)}, u32[]{:S(2)}) collective-permute-start(bf16[2,128,1024]{1,2,0:T(8,128)(2,1)} %get-tuple-element.39), channel_id=1, source_target_pairs={{4,0},{8,4},{12,8},{16,12},{20,16},{24,20},{28,24},{5,1},{9,5},{13... | collective-permute-start | bytes 1572872 | tf_op jit(solution)/shard_map/ppermute | solution.py:216
  24.0 4.3 %copy-start.21 = (s32[8]{0:T(128)S(1)}, s32[8]{0:T(128)}, u32[]{:S(2)}) copy-start(s32[8]{0:T(128)} %param.15) | copy-start | bytes 100
  28.2 6.7 %collective-permute-start.1 = (bf16[96,1024]{1,0:T(8,128)(2,1)S(1)}, bf16[96,1024]{1,0:T(8,128)(2,1)S(1)}, u32[]{:S(2)}, u32[]{:S(2)}) collective-permute-start(bf16[96,1024]{1,0:T(8,128)(2,1)S(1)} %dynamic-slice_bitcast_fusion.3), channel_id=1, source_target_pairs={{0,8},{4,12},{8,0},{12,4},{16,24},{20,28},{24,16},{28,20},{1,9},{5... | collective-permute-start | bytes 589832 | tf_op jit(solution)/shard_map/ppermute | solution.py:105
  35.0 5.0 %collective-permute-start.2 = (bf16[48,1024]{1,0:T(8,128)(2,1)S(1)}, bf16[48,1024]{1,0:T(8,128)(2,1)S(1)}, u32[]{:S(2)}, u32[]{:S(2)}) collective-permute-start(bf16[48,1024]{1,0:T(8,128)(2,1)S(1)} %dynamic-slice_bitcast_fusion.6), channel_id=1, source_target_pairs={{0,16},{4,20},{8,24},{12,28},{16,0},{20,4},{24,8},{28,12},{1,17},{... | collective-permute-start | bytes 294920 | tf_op jit(solution)/shard_map/ppermute | solution.py:105
  40.1 4.7 %collective-permute-start.3 = (bf16[48,1024]{1,0:T(8,128)(2,1)S(1)}, bf16[48,1024]{1,0:T(8,128)(2,1)S(1)}, u32[]{:S(2)}, u32[]{:S(2)}) collective-permute-start(bf16[48,1024]{1,0:T(8,128)(2,1)S(1)} %bitcast_add_fusion.2), channel_id=1, source_target_pairs={{0,16},{4,20},{8,24},{12,28},{16,0},{20,4},{24,8},{28,12},{1,17},{... | collective-permute-start | bytes 294920 | tf_op jit(solution)/shard_map/ppermute | solution.py:109
  44.9 5.8 %collective-permute-start.4 = (bf16[96,1024]{1,0:T(8,128)(2,1)S(1)}, bf16[96,1024]{1,0:T(8,128)(2,1)S(1)}, u32[]{:S(2)}, u32[]{:S(2)}) collective-permute-start(bf16[96,1024]{1,0:T(8,128)(2,1)S(1)} %get-tuple-element.62), channel_id=1, source_target_pairs={{0,8},{4,12},{8,0},{12,4},{16,24},{20,28},{24,16},{28,20},{1,9},{5... | collective-permute-start | bytes 589832 | tf_op jit(solution)/shard_map/ppermute | solution.py:109
  50.9 5.3 %copy-start.9 = (bf16[32,8,8,128]{3,2,1,0:T(8,128)(2,1)S(1)}, bf16[32,8,8,128]{3,2,1,0:T(8,128)(2,1)}, u32[]{:S(2)}) copy-start(bf16[32,8,8,128]{3,2,1,0:T(8,128)(2,1)} %copy.199) | copy-start | bytes 1572868
  51.0 1.8 collective-permute-start.5
  58.6 5.6 %collective-permute-start.6 = (f32[64,1152]{1,0:T(8,128)S(1)}, f32[64,1152]{1,0:T(8,128)S(1)}, u32[]{:S(2)}, u32[]{:S(2)}) collective-permute-start(f32[64,1152]{1,0:T(8,128)S(1)} %get-tuple-element.45), channel_id=1, source_target_pairs={{0,4},{4,0},{8,12},{12,8},{16,20},{20,16},{24,28},{28,24},{1,5},{5... | collective-permute-start | bytes 884744 | tf_op jit(solution)/shard_map/ppermute | solution.py:105
  63.3 3.6 %copy-start.16 = (s32[2]{0:T(128)S(1)}, s32[2]{0:T(128)}, u32[]{:S(2)}) copy-start(s32[2]{0:T(128)} %get-tuple-element.24) | copy-start | bytes 28
  63.3 4.2 %copy-start.15 = (pred[2]{0:T(512)(128)(4,1)S(1)}, pred[2]{0:T(512)(128)(4,1)}, u32[]{:S(2)}) copy-start(pred[2]{0:T(512)(128)(4,1)} %copy-done.14) | copy-start | bytes 10
  63.3 10.2 %copy-start.13 = (pred[4,5,8]{1,2,0:T(8,128)(4,1)S(1)}, pred[4,5,8]{1,2,0:T(8,128)(4,1)}, u32[]{:S(2)}) copy-start(pred[4,5,8]{1,2,0:T(8,128)(4,1)} %broadcast_and_fusion) | copy-start | bytes 484
  64.8 6.5 %collective-permute-start.7 = (f32[32,1152]{1,0:T(8,128)S(1)}, f32[32,1152]{1,0:T(8,128)S(1)}, u32[]{:S(2)}, u32[]{:S(2)}) collective-permute-start(f32[32,1152]{1,0:T(8,128)S(1)} %get-tuple-element.57), channel_id=1, source_target_pairs={{0,8},{4,12},{8,0},{12,4},{16,24},{20,28},{24,16},{28,20},{1,9},{5... | collective-permute-start | bytes 442376 | tf_op jit(solution)/shard_map/ppermute | solution.py:105
  71.8 4.4 %collective-permute-start.8 = (f32[16,1152]{1,0:T(8,128)S(1)}, f32[16,1152]{1,0:T(8,128)S(1)}, u32[]{:S(2)}, u32[]{:S(2)}) collective-permute-start(f32[16,1152]{1,0:T(8,128)S(1)} %get-tuple-element.71), channel_id=1, source_target_pairs={{0,16},{4,20},{8,24},{12,28},{16,0},{20,4},{24,8},{28,12},{1,17},{... | collective-permute-start | bytes 221192 | tf_op jit(solution)/shard_map/ppermute | solution.py:105
  76.6 4.4 %collective-permute-start.9 = (f32[16,1152]{1,0:T(8,128)S(1)}, f32[16,1152]{1,0:T(8,128)S(1)}, u32[]{:S(2)}, u32[]{:S(2)}) collective-permute-start(f32[16,1152]{1,0:T(8,128)S(1)} %concatenate.76), channel_id=1, source_target_pairs={{0,16},{4,20},{8,24},{12,28},{16,0},{20,4},{24,8},{28,12},{1,17},{... | collective-permute-start | bytes 221192 | tf_op jit(solution)/shard_map/ppermute | solution.py:109
  81.7 12.4 %collective-permute-start.10 = (f32[32,1152]{1,0:T(8,128)}, f32[32,1152]{1,0:T(8,128)}, u32[]{:S(2)}, u32[]{:S(2)}) collective-permute-start(f32[32,1152]{1,0:T(8,128)} %get-tuple-element.66), channel_id=1, source_target_pairs={{0,8},{4,12},{8,0},{12,4},{16,24},{20,28},{24,16},{28,20},{1,9},{5... | collective-permute-start | bytes 442376 | tf_op jit(solution)/shard_map/ppermute | solution.py:109
  85.1 9.0 %copy-start.11 = (f32[1,32,1152]{2,1,0:T(8,128)S(1)}, f32[1,32,1152]{2,1,0:T(8,128)}, u32[]{:S(2)}) copy-start(f32[1,32,1152]{2,1,0:T(8,128)} %get-tuple-element.67) | copy-start | bytes 442372
  89.1 6.8 %copy-start.3 = (bf16[1,4,64,1024]{3,2,1,0:T(8,128)(2,1)}, bf16[1,4,64,1024]{3,2,1,0:T(8,128)(2,1)S(1)}, u32[]{:S(2)}) copy-start(bf16[1,4,64,1024]{3,2,1,0:T(8,128)(2,1)S(1)} %copy.188) | copy-start | bytes 1572868
  95.9 6.0 %collective-permute-start.11 = (f32[64,1152]{1,0:T(8,128)}, f32[64,1152]{1,0:T(8,128)}, u32[]{:S(2)}, u32[]{:S(2)}) collective-permute-start(f32[64,1152]{1,0:T(8,128)} %get-tuple-element.52), channel_id=1, source_target_pairs={{0,4},{4,0},{8,12},{12,8},{16,20},{20,16},{24,28},{28,24},{1,5},{5... | collective-permute-start | bytes 884744 | tf_op jit(solution)/shard_map/ppermute | solution.py:109
  98.0 0.8 copy-start.5
  103.9 5.0 %copy-start.10 = (bf16[192,1024]{1,0:T(8,128)(2,1)S(1)}, bf16[192,1024]{1,0:T(8,128)(2,1)}, u32[]{:S(2)}) copy-start(bf16[192,1024]{1,0:T(8,128)(2,1)} %get-tuple-element.40) | copy-start | bytes 1179652
  103.9 52.8 %all-to-all-start = ((bf16[8,2,2,64,1024]{4,3,1,2,0:T(8,128)(2,1)}), bf16[8,2,2,64,1024]{4,3,1,2,0:T(8,128)(2,1)}, u32[]{:S(2)}, u32[]{:S(2)}) async-start(bf16[8,2,2,64,1024]{4,3,1,2,0:T(8,128)(2,1)} %pad_maximum_fusion.1), calls=%async_computation | async-start | bytes 8388608 | tf_op jit(solution)/shard_map/all_to_all | solution.py:297
  109.0 1.3 copy-start.1
  109.0 1.7 copy-start.2
  114.2 1.2 copy-start.4
  114.2 1.2 copy-start.12
  118.8 2.6 %slice-start.2 = ((f32[128,1152]{1,0:T(8,128)}), f32[128,8]{1,0:T(8,128)S(1)}, s32[]{:S(2)}) async-start(f32[128,1152]{1,0:T(8,128)} %pad_maximum_fusion.4), calls=%async_computation.5 | async-start | bytes 131072 | tf_op jit(solution)/shard_map/slice | solution.py:305
  118.8 2.8 %copy-start.6 = (f32[128,1152]{1,0:T(8,128)S(1)}, f32[128,1152]{1,0:T(8,128)}, u32[]{:S(2)}) copy-start(f32[128,1152]{1,0:T(8,128)} %pad_maximum_fusion.4) | copy-start | bytes 1769476
  162.7 1.0 copy-start.7
  162.9 2.0 copy-start.8
  163.3 2.8 %copy-start.22 = (f32[4,64,8,128]{3,1,2,0:T(8,128)S(1)}, f32[4,64,8,128]{3,1,2,0:T(8,128)}, u32[]{:S(2)}) copy-start(f32[4,64,8,128]{3,1,2,0:T(8,128)} %fusion.12) | copy-start | bytes 3145732
  164.9 3.8 %slice-start = ((s8[8388608]{0:T(1024)(128)(4,1)}), s8[4194304]{0:T(1024)(128)(4,1)S(1)}, s32[]{:S(2)}) async-start(s8[8388608]{0:T(1024)(128)(4,1)} %bitcast.308), calls=%async_computation.3 | async-start | bytes 8388608
  166.9 1.6 copy-start.18
  166.9 1.6 copy-start.19
  166.9 2.2 slice-start.1
  171.6 30.6 %all-to-all-start.2 = ((bf16[4,1024,128]{1,2,0:T(8,128)(2,1)}), bf16[4,1024,128]{1,2,0:T(8,128)(2,1)S(1)}, u32[]{:S(2)}, u32[]{:S(2)}) async-start(bf16[4,1024,128]{1,2,0:T(8,128)(2,1)} %bitcast.305), calls=%async_computation.2 | async-start | bytes 2097152 | tf_op jit(solution)/shard_map/all_to_all | solution.py:152
  202.1 28.7 %all-to-all-start.1 = ((bf16[4,1024,128]{1,2,0:T(8,128)(2,1)}), bf16[4,1024,128]{1,2,0:T(8,128)(2,1)S(1)}, u32[]{:S(2)}, u32[]{:S(2)}) async-start(bf16[4,1024,128]{1,2,0:T(8,128)(2,1)} %bitcast.306), calls=%async_computation.1 | async-start | bytes 2097152 | tf_op jit(solution)/shard_map/all_to_all | solution.py:152

commit v9 on v6

--- a/solution.py
+++ b/solution.py
@@ -50,6 +50,25 @@
     half_dim = HEAD_DIM // 2
     position = (first_row + jnp.arange(row_count)).astype(jnp.float32)
     angle_table = position[:, None] * frequency[None, :]
+    cosine = jnp.cos(angle_table)[:, None, :] * mscale
+    sine_part = jnp.sin(angle_table)[:, None, :] * mscale
+    halves_view = source.astype(jnp.float32).reshape(row_count, row_width // HEAD_DIM, 2, half_dim)
+    lower_half = halves_view[:, :, 0]
+    upper_half = halves_view[:, :, 1]
+    turned = jnp.stack(
+        [
+            lower_half * cosine - upper_half * sine_part,
+            upper_half * cosine + lower_half * sine_part,
+        ],
+        axis=2,
+    )
+    return turned.reshape(row_count, row_width).astype(jnp.bfloat16)
+
+
+def rotate_at(source, position, frequency, mscale):
+    row_count, row_width = source.shape
+    half_dim = HEAD_DIM // 2
+    angle_table = position.astype(jnp.float32)[:, None] * frequency[None, :]
     cosine = jnp.cos(angle_table)[:, None, :] * mscale
     sine_part = jnp.sin(angle_table)[:, None, :] * mscale
     halves_view = source.astype(jnp.float32).reshape(row_count, row_width // HEAD_DIM, 2, half_dim)
@@ -236,7 +255,17 @@
     query_view = query_rot.reshape(blocks_here, BLOCK, width_here)
     key_view = key_rot.reshape(blocks_here, BLOCK, width_here)
     value_view = values.reshape(blocks_here, BLOCK, width_here)
-    picked = jnp.stack([query_view[local_global], key_view[local_global], value_view[local_global]])
+    raw_q = queries.reshape(blocks_here, BLOCK, width_here)[local_global].reshape(GLOB * BLOCK, width_here)
+    raw_k = keys.reshape(blocks_here, BLOCK, width_here)[local_global].reshape(GLOB * BLOCK, width_here)
+    picked_rows = (first_row + local_global * BLOCK)[:, None] + jnp.arange(BLOCK)[None, :]
+    picked_rows = picked_rows.reshape(GLOB * BLOCK)
+    picked = jnp.stack(
+        [
+            rotate_at(raw_q, picked_rows, frequency, mscale).reshape(GLOB, BLOCK, width_here),
+            rotate_at(raw_k, picked_rows, frequency, mscale).reshape(GLOB, BLOCK, width_here),
+            value_view[local_global],
+        ]
+    )
     masked = jnp.where(mine_global[None, :, None, None], picked, jnp.zeros_like(picked))
     shared = tree_reduce(masked.reshape(3 * GLOB * BLOCK, width_here), add_merge, "seq")
     shared = shared.reshape(3, GLOB, BLOCK, width_here)

time: 213 us -> 214 us (level)
  other arithmetic: 18.8 us -> 25.5 us
  local copies, waits for them, and re-layouts: 45.7 us -> 41.4 us
    another operation x1 -> x5, other arithmetic: 1.04 us -> 6.84 us  [on_device(): jnp.stack([query_view[local_global], key_view[local_global], value_view[l...]
    convert_element_type x10 -> x6, local copies, waits for them, and re-layouts: 11 us -> 7.27 us  [rotate(): return turned.reshape(row_count, row_width).astype(jnp.bfloat16)]
    unnamed x47 -> x61, local copies, waits for them, and re-layouts: 13.3 us -> 10.4 us
    convert_element_type x0 -> x5, local copies, waits for them, and re-layouts: none -> 2.33 us  [the longest x2 1.57 us: rotate_at(): source.astype(jnp.float32)]
  transfers between devices with their start and end apart: 15 -> 15, of which waited for: 11 -> 11; matrix products, arithmetic and copies ran while one was open for 22% -> 25% of each run, Pallas kernels for 0% -> 0%
where the time goes in v9:
time: 214 us; the launch traced here: 213 us
  waiting for transfers between devices  59.8 us (28%)
  blocking collectives  53.1 us (25%)
  local copies, waits for them, and re-layouts  41.4 us (19%)
  other arithmetic  25.5 us (12%)
  starting transfers between devices  20.8 us (10%)
  matrix products  9.7 us (5%)
  between operations  2.6 us (1%)
    all_to_all x1, blocking collectives, sum_over_head(): gathered = lax.all_to_all(partial, 'head', 0, 0, tiled=True)  53.1 us
    all_to_all x1, waiting for transfers between devices, on_device(): lax.all_to_all(outgoing, 'seq', split_axis=0, concat_axis=0, tiled=True)  31.5 us
    ppermute x6, waiting for transfers between devices, tree_reduce(): got = lax.ppermute(send, axis, xor_perm(count, bit))  17.4 us
    ppermute x6, waiting for transfers between devices, tree_reduce(): got = lax.ppermute(parts, axis, xor_perm(count, bit))  10.9 us
    unnamed x61, local copies, waits for them, and re-layouts  10.4 us
    convert_element_type x6, local copies, waits for them, and re-layouts, rotate(): return turned.reshape(row_count, row_width).astype(jnp.bfloat16)  7.27 us
    all_to_all x1, starting transfers between devices, on_device(): lax.all_to_all(outgoing, 'seq', split_axis=0, concat_axis=0, tiled=True)  5.54 us
    ppermute x6, starting transfers between devices, tree_reduce(): got = lax.ppermute(parts, axis, xor_perm(count, bit))  5.19 us
  transfers between devices with their start and end apart: 15, of which 11 were waited for; matrix products, arithmetic and copies ran while one was open for 25% of the time, Pallas kernels for 0%

profile of v9, /device:TPU:2, one launch (start us, length us, event | category | flops | bytes accessed | tf_op | source)
XLA Modules:
  0.0 212.9 jit_solution(503123720822842048)
XLA Ops:
  1.4 1.2 copy.115
  3.6 1.2 fusion.53
  4.8 1.9 collective-permute-start.12
  6.7 3.6 %collective-permute-start.13 = (bf16[2,128,1024]{1,2,0:T(8,128)(2,1)}, bf16[2,128,1024]{1,2,0:T(8,128)(2,1)}, u32[]{:S(2)}, u32[]{:S(2)}) collective-permute-start(bf16[2,128,1024]{1,2,0:T(8,128)(2,1)} %get-tuple-element.42), channel_id=1, source_target_pairs={{4,0},{8,4},{12,8},{16,12},{20,16},{24,20},{28,24},{5,1},{9,5},{13... | collective-permute-start | bytes 1572872 | tf_op jit(solution)/shard_map/ppermute | solution.py:235
  11.1 1.0 fusion.90
  12.1 1.3 gather_fusion.3
  14.5 0.8 reshape.606
  15.3 0.8 reshape.607
  16.1 3.7 %subtract_convert_fusion.2 = (bf16[128,8,1,64]{3,2,1,0:T(2,128)(2,1)S(1)}, bf16[128,8,1,64]{3,2,1,0:T(2,128)(2,1)S(1)}, bf16[128,8,1,64]{3,2,1,0:T(2,128)(2,1)S(1)}, bf16[128,8,1,64]{3,2,1,0:T(2,128)(2,1)S(1)}) fusion(f32[128,8,2,64]{3,2,1,0:T(2,128)S(1)} %reshape.606, f32[128,64]{1,0:T(8,128)} %get-tuple-element.78, f32[128,64]{1,0:T(8,128)} %get-tuple-element.77, ...), kind=kLoop, calls=%fused_computation.89 | loop fusion | flops 1048576 | bytes 1638400 | tf_op jit(solution)/shard_map/convert.9
  19.8 2.8 %pad_maximum_fusion.7 = (bf16[128,8,2,64]{3,2,1,0:T(2,128)(2,1)S(1)}, bf16[128,8,2,64]{3,2,1,0:T(2,128)(2,1)S(1)}) fusion(bf16[128,8,1,64]{3,2,1,0:T(2,128)(2,1)S(1)} %get-tuple-element.33, bf16[128,8,1,64]{3,2,1,0:T(2,128)(2,1)S(1)} %get-tuple-element.32, bf16[128,8,1,64]{3,2,1,0:T(2,128)(2,1)S(1)} %get-tuple-element.71, ...), kind=kLoop, calls=%fused_computation.78 | loop fusion | flops 1048576 | bytes 1048576 | tf_op jit(solution)/shard_map/stack | solution.py:77
  25.6 0.6 compare_select_fusion
  26.2 6.3 %collective-permute-done.1 = bf16[96,1024]{1,0:T(8,128)(2,1)S(1)} collective-permute-done((bf16[96,1024]{1,0:T(8,128)(2,1)S(1)}, bf16[96,1024]{1,0:T(8,128)(2,1)S(1)}, u32[]{:S(2)}, u32[]{:S(2)}) %collective-permute-start.1) | collective-permute-done | bytes 196640 | tf_op jit(solution)/shard_map/ppermute | solution.py:124
  32.6 1.6 collective-permute-start.2
  34.2 3.1 %collective-permute-done.2 = bf16[48,1024]{1,0:T(8,128)(2,1)S(1)} collective-permute-done((bf16[48,1024]{1,0:T(8,128)(2,1)S(1)}, bf16[48,1024]{1,0:T(8,128)(2,1)S(1)}, u32[]{:S(2)}, u32[]{:S(2)}) %collective-permute-start.2) | collective-permute-done | bytes 98336 | tf_op jit(solution)/shard_map/ppermute | solution.py:124
  37.3 1.6 collective-permute-start.3
  38.9 3.1 %collective-permute-done.3 = bf16[48,1024]{1,0:T(8,128)(2,1)S(1)} collective-permute-done((bf16[48,1024]{1,0:T(8,128)(2,1)S(1)}, bf16[48,1024]{1,0:T(8,128)(2,1)S(1)}, u32[]{:S(2)}, u32[]{:S(2)}) %collective-permute-start.3) | collective-permute-done | bytes 98336 | tf_op jit(solution)/shard_map/ppermute | solution.py:128
  42.1 1.0 collective-permute-start.4
  43.1 4.7 %collective-permute-done.4 = bf16[96,1024]{1,0:T(8,128)(2,1)S(1)} collective-permute-done((bf16[96,1024]{1,0:T(8,128)(2,1)S(1)}, bf16[96,1024]{1,0:T(8,128)(2,1)S(1)}, u32[]{:S(2)}, u32[]{:S(2)}) %collective-permute-start.4) | collective-permute-done | bytes 196640 | tf_op jit(solution)/shard_map/ppermute | solution.py:128
  48.2 1.6 collective-permute-done.5
  49.8 1.0 fusion.64
  52.9 0.7 dynamic-slice_bitcast_fusion.2
  53.8 0.7 fusion.127
  56.1 1.0 collective-permute-start.7
  57.1 0.6 fusion.126
  57.8 4.3 %collective-permute-done.7 = f32[32,1152]{1,0:T(8,128)S(1)} collective-permute-done((f32[32,1152]{1,0:T(8,128)S(1)}, f32[32,1152]{1,0:T(8,128)S(1)}, u32[]{:S(2)}, u32[]{:S(2)}) %collective-permute-start.7) | collective-permute-done | bytes 147488 | tf_op jit(solution)/shard_map/ppermute | solution.py:124
  62.5 1.6 collective-permute-start.8
  64.1 2.8 %collective-permute-done.8 = f32[16,1152]{1,0:T(8,128)S(1)} collective-permute-done((f32[16,1152]{1,0:T(8,128)S(1)}, f32[16,1152]{1,0:T(8,128)S(1)}, u32[]{:S(2)}, u32[]{:S(2)}) %collective-permute-start.8) | collective-permute-done | bytes 73760 | tf_op jit(solution)/shard_map/ppermute | solution.py:124
  67.3 1.5 collective-permute-start.9
  68.8 1.3 compare_and_fusion.1
  70.1 1.5 collective-permute-done.9
  71.7 0.7 pad_maximum_fusion.13
  72.4 0.9 collective-permute-start.10
  73.3 1.2 compare_and_fusion
  74.5 1.4 reshape.662
  77.1 1.4 reshape.663
  78.5 1.6 copy.133
  80.1 1.8 copy.146
  81.9 0.6 copy.143
  82.7 1.0 fusion.78
  83.8 2.8 %gather_fusion = bf16[16,2,64,1024]{3,2,1,0:T(8,128)(2,1)} fusion(bf16[4,2,64,1024]{3,2,0,1:T(8,128)(2,1)S(1)} %pad_maximum_fusion.2, s32[1024]{0:T(1024)S(1)} %pad_clamp_fusion.1), kind=kCustom, calls=%fused_computation | custom fusion | bytes 8388672 | tf_op jit(solution)/shard_map/gather | solution.py:324
  86.8 1.0 fusion.69
  87.8 0.9 pad_maximum_fusion.4
  88.7 5.5 %all-to-all-start = ((bf16[8,2,2,64,1024]{4,3,2,1,0:T(8,128)(2,1)}), bf16[8,2,2,64,1024]{4,3,2,1,0:T(8,128)(2,1)}, u32[]{:S(2)}, u32[]{:S(2)}) async-start(bf16[8,2,2,64,1024]{4,3,2,1,0:T(8,128)(2,1)} %bitcast.271), calls=%async_computation | async-start | bytes 8388608 | tf_op jit(solution)/shard_map/all_to_all | solution.py:326
  94.3 1.2 copy.128
  95.6 0.7 slice.251
  96.3 1.2 copy.130
  97.7 0.8 copy-done.13
  99.9 1.1 pad_maximum_fusion
  101.0 1.5 fusion.124
  102.5 1.0 copy.161
  103.5 2.7 %copy.162 = bf16[224,8,8,128]{3,2,1,0:T(8,128)(2,1)} copy(bf16[224,8,8,128]{3,1,2,0:T(8,128)(2,1)S(1)} %bitcast.277) | data formatting | bytes 7340032
  106.2 1.8 fusion
  108.1 1.5 fusion.5
  110.5 31.5 %all-to-all-done = bf16[8,2,2,64,1024]{4,3,2,1,0:T(8,128)(2,1)} async-done(((bf16[8,2,2,64,1024]{4,3,2,1,0:T(8,128)(2,1)}), bf16[8,2,2,64,1024]{4,3,2,1,0:T(8,128)(2,1)}, u32[]{:S(2)}, u32[]{:S(2)}) %all-to-all-start) | async-done | bytes 4194336 | tf_op jit(solution)/shard_map/all_to_all | solution.py:326
  142.0 2.8 %gather_fusion.4 = bf16[12,64,1024]{2,1,0:T(8,128)(2,1)S(1)} fusion(bf16[8,2,2,64,1024]{4,3,2,1,0:T(8,128)(2,1)} %all-to-all-done, s32[12]{0:T(128)S(1)} %bitcast.326), kind=kCustom, calls=%fused_computation.4 | custom fusion | bytes 3145872 | tf_op jit(solution)/shard_map/gather | solution.py:329
  145.3 2.8 %gather_fusion.5 = bf16[12,64,1024]{2,1,0:T(8,128)(2,1)S(1)} fusion(bf16[8,2,2,64,1024]{4,3,2,1,0:T(8,128)(2,1)} %all-to-all-done, s32[12]{0:T(128)S(1)} %get-tuple-element.12), kind=kCustom, calls=%fused_computation.5 | custom fusion | bytes 3145872 | tf_op jit(solution)/shard_map/gather | solution.py:330
  149.2 1.2 multiply_reduce_fusion
  150.4 0.8 fusion.12
  151.2 0.6 copy-done.1
  151.8 2.1 fusion.32
  153.9 1.4 fusion.42
  155.9 2.5 %convolution_convert_fusion = bf16[256,4096]{1,0:T(8,128)(2,1)S(1)} fusion(bf16[1024,4096]{1,0:T(8,128)(2,1)S(1)} %bitcast.334, bf16[256,1024]{1,0:T(8,128)(2,1)S(1)} %bitcast.315, bf16[256,1024]{1,0:T(8,128)(2,1)S(1)} %bitcast.314, bf16[32,8,8,128]{3,2,1,0:T(8,128)(2,1)S(1)} %bitcast.319, pred[256]{0:T(512)(128)(4,1)S(1)} %broadcast_in_dim.185, ...), kind=kOutput, calls=%fused_computation.7 | convolution fusion | flops 2149056512 | bytes 12059136 | tf_op jit(solution)/shard_map/dot_general | solution.py:164
  158.5 53.1 %all_to_all.10 = bf16[4,1024,256]{1,2,0:T(8,128)(2,1)S(1)} all-to-all(bf16[4,1024,256]{1,2,0:T(8,128)(2,1)S(1)} %bitcast.282), channel_id=1, replica_groups=mesh['seq'=8,'head'=4] {'head'}, dimensions={0} | all-to-all | bytes 4194304 | tf_op jit(solution)/shard_map/all_to_all | solution.py:171
  211.6 1.3 reduce_sum.71
  (177 shorter events, 16.7 us)
Async XLA Ops:
  0.0 2.8 %copy-start.2 = (bf16[256,1024]{1,0:T(8,128)(2,1)S(1)}, bf16[256,1024]{1,0:T(8,128)(2,1)}, u32[]{:S(2)}) copy-start(bf16[256,1024]{1,0:T(8,128)(2,1)} %param.11) | copy-start | bytes 1572868
  3.3 7.0 %copy-start.21 = (s32[2]{0:T(128)S(1)}, s32[2]{0:T(128)}, u32[]{:S(2)}) copy-start(s32[2]{0:T(128)} %param.13) | copy-start | bytes 28
  3.5 9.8 %copy-start.10 = (bf16[256,1024]{1,0:T(8,128)(2,1)S(1)}, bf16[256,1024]{1,0:T(8,128)(2,1)}, u32[]{:S(2)}) copy-start(bf16[256,1024]{1,0:T(8,128)(2,1)} %param.10) | copy-start | bytes 1572868
  3.5 10.4 %copy-start.11 = (bf16[256,1024]{1,0:T(8,128)(2,1)S(1)}, bf16[256,1024]{1,0:T(8,128)(2,1)}, u32[]{:S(2)}) copy-start(bf16[256,1024]{1,0:T(8,128)(2,1)} %param.9) | copy-start | bytes 1572868
  4.8 89.6 %collective-permute-start.12 = (bf16[2,128,1024]{1,2,0:T(8,128)(2,1)}, bf16[2,128,1024]{1,2,0:T(8,128)(2,1)}, u32[]{:S(2)}, u32[]{:S(2)}) collective-permute-start(bf16[2,128,1024]{1,2,0:T(8,128)(2,1)} %get-tuple-element.41), channel_id=1, source_target_pairs={{0,4},{4,8},{8,12},{12,16},{16,20},{20,24},{24,28},{1,5},{5,9},{9,... | collective-permute-start | bytes 1572872 | tf_op jit(solution)/shard_map/ppermute | solution.py:232
  6.7 89.6 %collective-permute-start.13 = (bf16[2,128,1024]{1,2,0:T(8,128)(2,1)}, bf16[2,128,1024]{1,2,0:T(8,128)(2,1)}, u32[]{:S(2)}, u32[]{:S(2)}) collective-permute-start(bf16[2,128,1024]{1,2,0:T(8,128)(2,1)} %get-tuple-element.42), channel_id=1, source_target_pairs={{4,0},{8,4},{12,8},{16,12},{20,16},{24,20},{28,24},{5,1},{9,5},{13... | collective-permute-start | bytes 1572872 | tf_op jit(solution)/shard_map/ppermute | solution.py:235
  10.4 3.5 %copy-start.17 = (pred[2]{0:T(512)(128)(4,1)}, pred[2]{0:T(512)(128)(4,1)S(1)}, u32[]{:S(2)}) copy-start(pred[2]{0:T(512)(128)(4,1)S(1)} %fusion.111) | copy-start | bytes 10
  10.4 0.5 copy-start.15
  19.8 3.6 %copy-start.14 = (bf16[2,64,1024]{2,1,0:T(8,128)(2,1)S(1)}, bf16[2,64,1024]{2,1,0:T(8,128)(2,1)}, u32[]{:S(2)}) copy-start(bf16[2,64,1024]{2,1,0:T(8,128)(2,1)} %gather_fusion.3) | copy-start | bytes 786436
  23.3 0.7 copy-start.20
  23.6 1.8 collective-permute-start
  24.8 18.2 %copy-start.22 = (s32[8]{0:T(128)S(1)}, s32[8]{0:T(128)}, u32[]{:S(2)}) copy-start(s32[8]{0:T(128)} %param.15) | copy-start | bytes 100
  25.5 7.0 %collective-permute-start.1 = (bf16[96,1024]{1,0:T(8,128)(2,1)S(1)}, bf16[96,1024]{1,0:T(8,128)(2,1)S(1)}, u32[]{:S(2)}, u32[]{:S(2)}) collective-permute-start(bf16[96,1024]{1,0:T(8,128)(2,1)S(1)} %dynamic-slice_bitcast_fusion.3), channel_id=1, source_target_pairs={{0,8},{4,12},{8,0},{12,4},{16,24},{20,28},{24,16},{28,20},{1,9},{5... | collective-permute-start | bytes 589832 | tf_op jit(solution)/shard_map/ppermute | solution.py:124
  32.6 4.7 %collective-permute-start.2 = (bf16[48,1024]{1,0:T(8,128)(2,1)S(1)}, bf16[48,1024]{1,0:T(8,128)(2,1)S(1)}, u32[]{:S(2)}, u32[]{:S(2)}) collective-permute-start(bf16[48,1024]{1,0:T(8,128)(2,1)S(1)} %dynamic-slice_bitcast_fusion.6), channel_id=1, source_target_pairs={{0,16},{4,20},{8,24},{12,28},{16,0},{20,4},{24,8},{28,12},{1,17},{... | collective-permute-start | bytes 294920 | tf_op jit(solution)/shard_map/ppermute | solution.py:124
  37.3 4.7 %collective-permute-start.3 = (bf16[48,1024]{1,0:T(8,128)(2,1)S(1)}, bf16[48,1024]{1,0:T(8,128)(2,1)S(1)}, u32[]{:S(2)}, u32[]{:S(2)}) collective-permute-start(bf16[48,1024]{1,0:T(8,128)(2,1)S(1)} %bitcast_add_fusion.2), channel_id=1, source_target_pairs={{0,16},{4,20},{8,24},{12,28},{16,0},{20,4},{24,8},{28,12},{1,17},{... | collective-permute-start | bytes 294920 | tf_op jit(solution)/shard_map/ppermute | solution.py:128
  42.1 5.7 %collective-permute-start.4 = (bf16[96,1024]{1,0:T(8,128)(2,1)S(1)}, bf16[96,1024]{1,0:T(8,128)(2,1)S(1)}, u32[]{:S(2)}, u32[]{:S(2)}) collective-permute-start(bf16[96,1024]{1,0:T(8,128)(2,1)S(1)} %get-tuple-element.61), channel_id=1, source_target_pairs={{0,8},{4,12},{8,0},{12,4},{16,24},{20,28},{24,16},{28,20},{1,9},{5... | collective-permute-start | bytes 589832 | tf_op jit(solution)/shard_map/ppermute | solution.py:128
  48.0 1.8 collective-permute-start.5
  50.9 0.7 copy-start.6
  52.6 1.2 copy-start.18
  52.6 1.8 copy-start.12
  53.7 1.8 collective-permute-start.6
  54.9 2.1 %copy-start.16 = (s32[2]{0:T(128)S(1)}, s32[2]{0:T(128)}, u32[]{:S(2)}) copy-start(s32[2]{0:T(128)} %copy-done.15) | copy-start | bytes 28
  56.1 6.0 %collective-permute-start.7 = (f32[32,1152]{1,0:T(8,128)S(1)}, f32[32,1152]{1,0:T(8,128)S(1)}, u32[]{:S(2)}, u32[]{:S(2)}) collective-permute-start(f32[32,1152]{1,0:T(8,128)S(1)} %get-tuple-element.58), channel_id=1, source_target_pairs={{0,8},{4,12},{8,0},{12,4},{16,24},{20,28},{24,16},{28,20},{1,9},{5... | collective-permute-start | bytes 442376 | tf_op jit(solution)/shard_map/ppermute | solution.py:124
  62.5 4.4 %collective-permute-start.8 = (f32[16,1152]{1,0:T(8,128)S(1)}, f32[16,1152]{1,0:T(8,128)S(1)}, u32[]{:S(2)}, u32[]{:S(2)}) collective-permute-start(f32[16,1152]{1,0:T(8,128)S(1)} %get-tuple-element.70), channel_id=1, source_target_pairs={{0,16},{4,20},{8,24},{12,28},{16,0},{20,4},{24,8},{28,12},{1,17},{... | collective-permute-start | bytes 221192 | tf_op jit(solution)/shard_map/ppermute | solution.py:124
  67.2 9.5 %copy-start.19 = (s32[8,2,1]{0,1,2:T(2,128)S(1)}, s32[8,2,1]{0,1,2:T(2,128)}, u32[]{:S(2)}) copy-start(s32[8,2,1]{0,1,2:T(2,128)} %compare_select_fusion) | copy-start | bytes 196
  67.3 4.4 %collective-permute-start.9 = (f32[16,1152]{1,0:T(8,128)S(1)}, f32[16,1152]{1,0:T(8,128)S(1)}, u32[]{:S(2)}, u32[]{:S(2)}) collective-permute-start(f32[16,1152]{1,0:T(8,128)S(1)} %concatenate.72), channel_id=1, source_target_pairs={{0,16},{4,20},{8,24},{12,28},{16,0},{20,4},{24,8},{28,12},{1,17},{... | collective-permute-start | bytes 221192 | tf_op jit(solution)/shard_map/ppermute | solution.py:128
  72.4 10.3 %collective-permute-start.10 = (f32[32,1152]{1,0:T(8,128)}, f32[32,1152]{1,0:T(8,128)}, u32[]{:S(2)}, u32[]{:S(2)}) collective-permute-start(f32[32,1152]{1,0:T(8,128)} %get-tuple-element.65), channel_id=1, source_target_pairs={{0,8},{4,12},{8,0},{12,4},{16,24},{20,28},{24,16},{28,20},{1,9},{5... | collective-permute-start | bytes 442376 | tf_op jit(solution)/shard_map/ppermute | solution.py:128
  80.1 26.1 %copy-start.3 = (bf16[4,64,8,128]{3,1,2,0:T(8,128)(2,1)}, bf16[4,64,8,128]{3,1,2,0:T(8,128)(2,1)S(1)}, u32[]{:S(2)}) copy-start(bf16[4,64,8,128]{3,1,2,0:T(8,128)(2,1)S(1)} %copy.133) | copy-start | bytes 1572868
  83.7 3.1 %collective-permute-start.11 = (f32[64,1152]{1,0:T(8,128)S(1)}, f32[64,1152]{1,0:T(8,128)}, u32[]{:S(2)}, u32[]{:S(2)}) collective-permute-start(f32[64,1152]{1,0:T(8,128)S(1)} %get-tuple-element.53), channel_id=1, source_target_pairs={{0,4},{4,0},{8,12},{12,8},{16,20},{20,16},{24,28},{28,24},{1,5},{5... | collective-permute-start | bytes 884744 | tf_op jit(solution)/shard_map/ppermute | solution.py:128
  88.7 53.3 %all-to-all-start = ((bf16[8,2,2,64,1024]{4,3,2,1,0:T(8,128)(2,1)}), bf16[8,2,2,64,1024]{4,3,2,1,0:T(8,128)(2,1)}, u32[]{:S(2)}, u32[]{:S(2)}) async-start(bf16[8,2,2,64,1024]{4,3,2,1,0:T(8,128)(2,1)} %bitcast.271), calls=%async_computation | async-start | bytes 8388608 | tf_op jit(solution)/shard_map/all_to_all | solution.py:326
  97.5 1.0 copy-start.13
  98.5 1.0 copy-start.7
  98.5 1.1 copy-start.9
  108.0 2.1 copy-start
  108.1 2.0 slice-start
  108.1 2.2 %copy-start.8 = (f32[128,1152]{1,0:T(8,128)S(1)}, f32[128,1152]{1,0:T(8,128)}, u32[]{:S(2)}) copy-start(f32[128,1152]{1,0:T(8,128)} %pad_maximum_fusion.4) | copy-start | bytes 1769476
  148.1 1.0 copy-start.4
  148.2 3.0 %copy-start.5 = (bf16[224,8,8,128]{3,2,1,0:T(8,128)(2,1)S(1)}, bf16[224,8,8,128]{3,2,1,0:T(8,128)(2,1)}, u32[]{:S(2)}) copy-start(bf16[224,8,8,128]{3,2,1,0:T(8,128)(2,1)} %copy.162) | copy-start | bytes 11010052
  149.2 2.6 %copy-start.1 = (f32[4,8,64,448]{3,2,1,0:T(8,128)S(1)}, f32[4,8,64,448]{3,2,1,0:T(8,128)}, u32[]{:S(2)}) copy-start(f32[4,8,64,448]{3,2,1,0:T(8,128)} %copy-done) | copy-start | bytes 11010052
  150.4 5.4 %slice-start.1 = ((s8[8388608]{0:T(1024)(128)(4,1)}), s8[4194304]{0:T(1024)(128)(4,1)S(1)}, s32[]{:S(2)}) async-start(s8[8388608]{0:T(1024)(128)(4,1)} %bitcast.333), calls=%async_computation.3 | async-start | bytes 8388608
  151.8 4.0 %slice-start.2 = ((s8[8388608]{0:T(1024)(128)(4,1)}), s8[4194304]{0:T(1024)(128)(4,1)S(1)}, s32[]{:S(2)}) async-start(s8[8388608]{0:T(1024)(128)(4,1)} %bitcast.333), calls=%async_computation.4 | async-start | bytes 8388608

commit v10 on v6

--- a/solution.py
+++ b/solution.py
@@ -169,6 +169,27 @@
     total = jnp.sum(expo, axis=3)
     mixture = jnp.einsum(
         "bhqs,bshd->bqhd", expo.astype(jnp.bfloat16), value_grid, preferred_element_type=jnp.float32
+    )
+    return mixture, total, peak
+
+
+def shared_attend(query_blocks, key_chunks, value_chunks, chunk_valid):
+    count_q = query_blocks.shape[0]
+    chunk_count = key_chunks.shape[0]
+    heads_here = query_blocks.shape[-1] // HEAD_DIM
+    query_grid = query_blocks.reshape(count_q, BLOCK, heads_here, HEAD_DIM)
+    key_grid = key_chunks.reshape(chunk_count * BLOCK, heads_here, HEAD_DIM)
+    value_grid = value_chunks.reshape(chunk_count * BLOCK, heads_here, HEAD_DIM)
+    scores = jnp.einsum(
+        "bqhd,shd->bhqs", query_grid, key_grid, preferred_element_type=jnp.float32
+    ) * (1.0 / math.sqrt(HEAD_DIM))
+    present = jnp.repeat(chunk_valid, BLOCK, axis=1)[:, None, None, :]
+    scores = jnp.where(present, scores, masked_score)
+    peak = jnp.max(scores, axis=3)
+    expo = jnp.exp(scores - peak[..., None])
+    total = jnp.sum(expo, axis=3)
+    mixture = jnp.einsum(
+        "bhqs,shd->bqhd", expo.astype(jnp.bfloat16), value_grid, preferred_element_type=jnp.float32
     )
     return mixture, total, peak
 
@@ -297,13 +318,14 @@
     incoming = lax.all_to_all(outgoing, "seq", split_axis=0, concat_axis=0, tiled=True)
     my_owners = owners[seq_place]
     my_ranks = ranks[seq_place]
-    random_k = incoming[my_owners, my_ranks, 0].reshape(blocks_here, RAND, BLOCK, width_here)
-    random_v = incoming[my_owners, my_ranks, 1].reshape(blocks_here, RAND, BLOCK, width_here)
-    random_kv = (random_k, random_v)
+    chunk_count = seq_count * capacity
+    slot_chunk = (my_owners * capacity + my_ranks).reshape(blocks_here, RAND)
+    chunk_valid = jnp.any(
+        slot_chunk[:, :, None] == jnp.arange(chunk_count)[None, None, :], axis=1
+    )
+    incoming = incoming.reshape(chunk_count, 2, BLOCK, width_here)
     near_part = partial_attend(query_view, near_kv[0], near_kv[1], near_valid)
-    far_part = partial_attend(
-        query_view, random_kv[0], random_kv[1], jnp.ones((blocks_here, RAND, heads_here), dtype=bool)
-    )
+    far_part = shared_attend(query_view, incoming[:, 0], incoming[:, 1], chunk_valid)
     attended = merge_attend(near_part, far_part)
     mix_sum = reduced[:, :width_here].reshape(row_total, heads_here, HEAD_DIM)
     total_sum = reduced[:, width_here : width_here + heads_here]

time: 213 us -> 228 us (1.070)
  other arithmetic: 18.8 us -> 32 us
  starting transfers between devices: 20.8 us -> 25 us
    gather x2 -> x0, local copies, waits for them, and re-layouts: 5.68 us -> none  [the longest x1 2.84 us: on_device(): incoming[my_owners, my_ranks, 0]]
    all_to_all x1, waiting for transfers between devices: 31.5 us -> 27.5 us  [on_device(): lax.all_to_all(outgoing, 'seq', split_axis=0, concat_axis=0, tiled=True)]
    reduce_sum x0 -> x1, other arithmetic: none -> 3.79 us  [shared_attend(): total = jnp.sum(expo, axis=3)]
    convert_element_type x10, local copies, waits for them, and re-layouts: 11 us -> 8.4 us  [rotate(): return turned.reshape(row_count, row_width).astype(jnp.bfloat16)]
    all_to_all x0 -> x1, local copies, waits for them, and re-layouts: none -> 2.63 us  [on_device(): lax.all_to_all(outgoing, 'seq', split_axis=0, concat_axis=0, tiled=True)]
    ppermute x6, waiting for transfers between devices: 19 us -> 21.5 us  [tree_reduce(): got = lax.ppermute(send, axis, xor_perm(count, bit))]
    unnamed x47 -> x51, local copies, waits for them, and re-layouts: 13.3 us -> 12.1 us
  transfers between devices with their start and end apart: 15 -> 15, of which waited for: 11 -> 10; matrix products, arithmetic and copies ran while one was open for 22% -> 23% of each run, Pallas kernels for 0% -> 0%
where the time goes in v10:
time: 228 us; the launch traced here: 227 us
  waiting for transfers between devices  61.2 us (27%)
  blocking collectives  53.1 us (23%)
  local copies, waits for them, and re-layouts  43.5 us (19%)
  other arithmetic  32 us (14%)
  starting transfers between devices  25 us (11%)
  matrix products  9.86 us (4%)
  between operations  2.4 us (1%)
    all_to_all x1, blocking collectives, sum_over_head(): gathered = lax.all_to_all(partial, 'head', 0, 0, tiled=True)  53.1 us
    all_to_all x1, waiting for transfers between devices, on_device(): lax.all_to_all(outgoing, 'seq', split_axis=0, concat_axis=0, tiled=True)  27.5 us
    ppermute x6, waiting for transfers between devices, tree_reduce(): got = lax.ppermute(send, axis, xor_perm(count, bit))  21.5 us
    ppermute x6, waiting for transfers between devices, tree_reduce(): got = lax.ppermute(parts, axis, xor_perm(count, bit))  12.3 us
    unnamed x51, local copies, waits for them, and re-layouts  12.1 us
    convert_element_type x10, local copies, waits for them, and re-layouts, rotate(): return turned.reshape(row_count, row_width).astype(jnp.bfloat16)  8.4 us
    ppermute x6, starting transfers between devices, tree_reduce(): got = lax.ppermute(parts, axis, xor_perm(count, bit))  6.97 us
    ppermute x6, starting transfers between devices, tree_reduce(): got = lax.ppermute(send, axis, xor_perm(count, bit))  6.25 us
  transfers between devices with their start and end apart: 15, of which 10 were waited for; matrix products, arithmetic and copies ran while one was open for 23% of the time, Pallas kernels for 0%

profile of v10, /device:TPU:2, one launch (start us, length us, event | category | flops | bytes accessed | tf_op | source)
XLA Modules:
  0.0 226.9 jit_solution(7260894549136884593)
XLA Ops:
  0.0 1.3 copy.226
  2.7 1.2 copy.220
  7.2 1.3 gather_fusion.2
  10.2 1.0 pad_maximum_fusion.3
  11.8 1.2 fusion.58
  12.9 2.4 %collective-permute-start.12 = (bf16[2,128,1024]{1,2,0:T(8,128)(2,1)}, bf16[2,128,1024]{1,2,0:T(8,128)(2,1)}, u32[]{:S(2)}, u32[]{:S(2)}) collective-permute-start(bf16[2,128,1024]{1,2,0:T(8,128)(2,1)} %get-tuple-element.37), channel_id=1, source_target_pairs={{0,4},{4,8},{8,12},{12,16},{16,20},{20,24},{24,28},{1,5},{5,9},{9,... | collective-permute-start | bytes 1572872 | tf_op jit(solution)/shard_map/ppermute | solution.py:234
  15.3 3.2 %collective-permute-start.13 = (bf16[2,128,1024]{1,2,0:T(8,128)(2,1)}, bf16[2,128,1024]{1,2,0:T(8,128)(2,1)}, u32[]{:S(2)}, u32[]{:S(2)}) collective-permute-start(bf16[2,128,1024]{1,2,0:T(8,128)(2,1)} %get-tuple-element.38), channel_id=1, source_target_pairs={{4,0},{8,4},{12,8},{16,12},{20,16},{24,20},{28,24},{5,1},{9,5},{13... | collective-permute-start | bytes 1572872 | tf_op jit(solution)/shard_map/ppermute | solution.py:237
  20.1 12.3 %collective-permute-done.1 = bf16[96,1024]{1,0:T(8,128)(2,1)S(1)} collective-permute-done((bf16[96,1024]{1,0:T(8,128)(2,1)S(1)}, bf16[96,1024]{1,0:T(8,128)(2,1)S(1)}, u32[]{:S(2)}, u32[]{:S(2)}) %collective-permute-start.1) | collective-permute-done | bytes 196640 | tf_op jit(solution)/shard_map/ppermute | solution.py:105
  32.5 2.6 %collective-permute-start.2 = (bf16[48,1024]{1,0:T(8,128)(2,1)S(1)}, bf16[48,1024]{1,0:T(8,128)(2,1)S(1)}, u32[]{:S(2)}, u32[]{:S(2)}) collective-permute-start(bf16[48,1024]{1,0:T(8,128)(2,1)S(1)} %dynamic-slice_bitcast_fusion.6), channel_id=1, source_target_pairs={{0,16},{4,20},{8,24},{12,28},{16,0},{20,4},{24,8},{28,12},{1,17},{... | collective-permute-start | bytes 294920 | tf_op jit(solution)/shard_map/ppermute | solution.py:105
  35.1 3.0 %collective-permute-done.2 = bf16[48,1024]{1,0:T(8,128)(2,1)S(1)} collective-permute-done((bf16[48,1024]{1,0:T(8,128)(2,1)S(1)}, bf16[48,1024]{1,0:T(8,128)(2,1)S(1)}, u32[]{:S(2)}, u32[]{:S(2)}) %collective-permute-start.2) | collective-permute-done | bytes 98336 | tf_op jit(solution)/shard_map/ppermute | solution.py:105
  38.1 1.7 collective-permute-start.3
  39.8 3.0 %collective-permute-done.3 = bf16[48,1024]{1,0:T(8,128)(2,1)S(1)} collective-permute-done((bf16[48,1024]{1,0:T(8,128)(2,1)S(1)}, bf16[48,1024]{1,0:T(8,128)(2,1)S(1)}, u32[]{:S(2)}, u32[]{:S(2)}) %collective-permute-start.3) | collective-permute-done | bytes 98336 | tf_op jit(solution)/shard_map/ppermute | solution.py:109
  42.9 2.3 collective-permute-start.4
  45.8 3.0 %collective-permute-done.4 = bf16[96,1024]{1,0:T(8,128)(2,1)S(1)} collective-permute-done((bf16[96,1024]{1,0:T(8,128)(2,1)S(1)}, bf16[96,1024]{1,0:T(8,128)(2,1)S(1)}, u32[]{:S(2)}, u32[]{:S(2)}) %collective-permute-start.4) | collective-permute-done | bytes 196640 | tf_op jit(solution)/shard_map/ppermute | solution.py:109
  50.9 1.0 fusion.69
  52.6 1.1 fusion.54
  53.7 0.7 copy.234
  54.8 0.8 copy.233
  55.7 1.0 concatenate.57
  56.9 0.8 select_reduce_fusion
  59.1 2.1 collective-permute-start.7
  62.0 3.6 %collective-permute-done.7 = f32[32,1152]{1,0:T(8,128)S(1)} collective-permute-done((f32[32,1152]{1,0:T(8,128)S(1)}, f32[32,1152]{1,0:T(8,128)S(1)}, u32[]{:S(2)}, u32[]{:S(2)}) %collective-permute-start.7) | collective-permute-done | bytes 147488 | tf_op jit(solution)/shard_map/ppermute | solution.py:105
  66.0 1.2 collective-permute-start.8
  67.9 2.5 %collective-permute-done.8 = f32[16,1152]{1,0:T(8,128)S(1)} collective-permute-done((f32[16,1152]{1,0:T(8,128)S(1)}, f32[16,1152]{1,0:T(8,128)S(1)}, u32[]{:S(2)}, u32[]{:S(2)}) %collective-permute-start.8) | collective-permute-done | bytes 73760 | tf_op jit(solution)/shard_map/ppermute | solution.py:105
  70.8 1.2 collective-permute-start.9
  72.6 2.6 %collective-permute-done.9 = f32[16,1152]{1,0:T(8,128)S(1)} collective-permute-done((f32[16,1152]{1,0:T(8,128)S(1)}, f32[16,1152]{1,0:T(8,128)S(1)}, u32[]{:S(2)}, u32[]{:S(2)}) %collective-permute-start.9) | collective-permute-done | bytes 73760 | tf_op jit(solution)/shard_map/ppermute | solution.py:109
  75.3 1.8 collective-permute-start.10
  77.4 3.1 %collective-permute-done.10 = f32[32,1152]{1,0:T(8,128)S(1)} collective-permute-done((f32[32,1152]{1,0:T(8,128)S(1)}, f32[32,1152]{1,0:T(8,128)S(1)}, u32[]{:S(2)}, u32[]{:S(2)}) %collective-permute-start.10) | collective-permute-done | bytes 147488 | tf_op jit(solution)/shard_map/ppermute | solution.py:109
  80.5 0.9 pad_maximum_fusion.8
  81.4 1.8 compare_and_fusion
  83.2 1.4 reshape.509
  85.4 2.3 %copy.256 = bf16[4,1,64,1024]{3,2,0,1:T(8,128)(2,1)} copy(bf16[4,1,64,1024]{2,0,3,1:T(4,128)(2,1)} %reshape.509) | data formatting | bytes 1048576 | tf_op jit(solution)/shard_map/convert_element_type | solution.py:65
  87.7 1.2 copy.247
  90.5 0.7 broadcast_in_dim.180
  91.8 1.1 pad_maximum_fusion.2
  93.0 2.9 %gather_fusion = bf16[16,2,64,1024]{3,2,1,0:T(8,128)(2,1)} fusion(bf16[4,2,64,1024]{3,2,0,1:T(8,128)(2,1)S(1)} %pad_maximum_fusion.2, s32[1024]{0:T(1024)} %pad_clamp_fusion.1), kind=kCustom, calls=%fused_computation | custom fusion | bytes 8388672 | tf_op jit(solution)/shard_map/gather | solution.py:316
  95.9 1.0 fusion.56
  96.9 1.1 fusion.74
  98.0 0.9 pad_maximum_fusion.4
  98.9 6.2 %all-to-all-start = ((bf16[8,2,2,64,1024]{4,3,2,1,0:T(8,128)(2,1)}), bf16[8,2,2,64,1024]{4,3,2,1,0:T(8,128)(2,1)}, u32[]{:S(2)}, u32[]{:S(2)}) async-start(bf16[8,2,2,64,1024]{4,3,2,1,0:T(8,128)(2,1)} %bitcast.293), calls=%async_computation | async-start | bytes 8388608 | tf_op jit(solution)/shard_map/all_to_all | solution.py:318
  105.0 1.3 compare_and_fusion.1
  107.0 1.2 copy.236
  108.3 0.7 slice.233
  109.0 1.2 copy.238
  110.3 1.3 maximum_bitcast_fusion
  111.6 1.4 maximum_bitcast_fusion.1
  113.3 1.1 pad_maximum_fusion
  114.4 1.5 fusion.122
  115.9 1.0 copy.276
  116.9 2.7 %copy.277 = bf16[224,8,8,128]{3,2,1,0:T(8,128)(2,1)} copy(bf16[224,8,8,128]{3,1,2,0:T(8,128)(2,1)S(1)} %bitcast.299) | data formatting | bytes 7340032
  119.6 1.8 fusion.5
  121.4 2.0 copy-done
  123.4 1.5 fusion.10
  125.3 27.5 %all-to-all-done = bf16[8,2,2,64,1024]{4,3,2,1,0:T(8,128)(2,1)} async-done(((bf16[8,2,2,64,1024]{4,3,2,1,0:T(8,128)(2,1)}), bf16[8,2,2,64,1024]{4,3,2,1,0:T(8,128)(2,1)}, u32[]{:S(2)}, u32[]{:S(2)}) %all-to-all-start) | async-done | bytes 4194336 | tf_op jit(solution)/shard_map/all_to_all | solution.py:318
  152.8 2.6 %copy.245 = bf16[8,2,2,64,1024]{4,3,1,0,2:T(8,128)(2,1)S(1)} copy(bf16[8,2,2,64,1024]{4,3,2,1,0:T(8,128)(2,1)} %all-to-all-done) | data formatting | bytes 8388608 | tf_op jit(solution)/shard_map/all_to_all | solution.py:318
  156.9 1.3 fusion.15
  158.2 1.2 fusion.2
  159.4 3.8 %fusion = (f32[4,8,64]{2,0,1:T(4,128)S(1)}, bf16[4,8,64,1024]{3,2,0,1:T(8,128)(2,1)S(1)}) fusion(f32[8,1024,4,64]{1,3,2,0:T(8,128)S(1)} %bitcast.286, f32[4,8,64]{2,0,1:T(4,128)S(1)} %fusion.2, pred[4,1024]{1,0:T(4,128)(4,1)S(1)} %copy-done.9, f32[8,1024,256]{1,2,0:S(1)} %fusion.15), kind=kLoop, calls=%fused_computation.6 | loop fusion | flops 16775168 | bytes 20992000 | tf_op jit(solution)/shard_map/reduce_sum | solution.py:190
  163.9 1.5 fusion.41
  166.0 1.1 copy-done.5
  167.2 2.2 divide_convert_fusion
  169.9 2.5 %convolution_convert_fusion = bf16[256,4096]{1,0:T(8,128)(2,1)S(1)} fusion(bf16[1024,4096]{1,0:T(8,128)(2,1)S(1)} %bitcast.355, bf16[256,1024]{1,0:T(8,128)(2,1)S(1)} %bitcast.335, bf16[256,1024]{1,0:T(8,128)(2,1)S(1)} %bitcast.336, bf16[32,8,8,128]{3,2,1,0:T(8,128)(2,1)S(1)} %bitcast.340, pred[256]{0:T(512)(128)(4,1)S(1)} %copy-done.16, ...), kind=kOutput, calls=%fused_computation.10 | convolution fusion | flops 2149056512 | bytes 12059136 | tf_op jit(solution)/shard_map/dot_general | solution.py:145
  172.5 53.1 %all_to_all.10 = bf16[4,1024,256]{1,2,0:T(8,128)(2,1)S(1)} all-to-all(bf16[4,1024,256]{1,2,0:T(8,128)(2,1)S(1)} %bitcast.302), channel_id=1, replica_groups=mesh['seq'=8,'head'=4] {'head'}, dimensions={0} | all-to-all | bytes 4194304 | tf_op jit(solution)/shard_map/all_to_all | solution.py:152
  225.6 1.3 reduce_sum.71
  (164 shorter events, 23.4 us)
Async XLA Ops:
  0.0 4.1 %copy-start.14 = (s32[2]{0:T(128)S(1)}, s32[2]{0:T(128)}, u32[]{:S(2)}) copy-start(s32[2]{0:T(128)} %param.13) | copy-start | bytes 28
  4.2 5.9 %copy-start.11 = (pred[2]{0:T(512)(128)(4,1)}, pred[2]{0:T(512)(128)(4,1)S(1)}, u32[]{:S(2)}) copy-start(pred[2]{0:T(512)(128)(4,1)S(1)} %fusion.110) | copy-start | bytes 10
  5.1 1.5 copy-start.2
  5.5 5.8 %copy-start.3 = (bf16[256,8,2,64]{0,3,2,1:T(8,128)(2,1)}, bf16[256,8,2,64]{0,3,2,1:T(8,128)(2,1)S(1)}, u32[]{:S(2)}) copy-start(bf16[256,8,2,64]{0,3,2,1:T(8,128)(2,1)S(1)} %get-tuple-element.82) | copy-start | bytes 1572868
  9.5 9.1 %copy-start.13 = (s32[32,3]{0,1:T(4,128)S(1)}, s32[32,3]{0,1:T(4,128)}, u32[]{:S(2)}) copy-start(s32[32,3]{0,1:T(4,128)} %param.14) | copy-start | bytes 1156
  11.5 33.7 %copy-start.15 = (s32[8]{0:T(128)S(1)}, s32[8]{0:T(128)}, u32[]{:S(2)}) copy-start(s32[8]{0:T(128)} %param.15) | copy-start | bytes 100
  11.5 7.9 %collective-permute-start = (bf16[192,1024]{1,0:T(8,128)(2,1)S(1)}, bf16[192,1024]{1,0:T(8,128)(2,1)S(1)}, u32[]{:S(2)}, u32[]{:S(2)}) collective-permute-start(bf16[192,1024]{1,0:T(8,128)(2,1)S(1)} %dynamic-slice_bitcast_fusion), channel_id=1, source_target_pairs={{0,4},{4,0},{8,12},{12,8},{16,20},{20,16},{24,28},{28,24},{1,5},{5... | collective-permute-start | bytes 1179656 | tf_op jit(solution)/shard_map/ppermute | solution.py:105
  12.9 94.1 %collective-permute-start.12 = (bf16[2,128,1024]{1,2,0:T(8,128)(2,1)}, bf16[2,128,1024]{1,2,0:T(8,128)(2,1)}, u32[]{:S(2)}, u32[]{:S(2)}) collective-permute-start(bf16[2,128,1024]{1,2,0:T(8,128)(2,1)} %get-tuple-element.37), channel_id=1, source_target_pairs={{0,4},{4,8},{8,12},{12,16},{16,20},{20,24},{24,28},{1,5},{5,9},{9,... | collective-permute-start | bytes 1572872 | tf_op jit(solution)/shard_map/ppermute | solution.py:234
  15.3 93.7 %collective-permute-start.13 = (bf16[2,128,1024]{1,2,0:T(8,128)(2,1)}, bf16[2,128,1024]{1,2,0:T(8,128)(2,1)}, u32[]{:S(2)}, u32[]{:S(2)}) collective-permute-start(bf16[2,128,1024]{1,2,0:T(8,128)(2,1)} %get-tuple-element.38), channel_id=1, source_target_pairs={{4,0},{8,4},{12,8},{16,12},{20,16},{24,20},{28,24},{5,1},{9,5},{13... | collective-permute-start | bytes 1572872 | tf_op jit(solution)/shard_map/ppermute | solution.py:237
  19.5 12.9 %collective-permute-start.1 = (bf16[96,1024]{1,0:T(8,128)(2,1)S(1)}, bf16[96,1024]{1,0:T(8,128)(2,1)S(1)}, u32[]{:S(2)}, u32[]{:S(2)}) collective-permute-start(bf16[96,1024]{1,0:T(8,128)(2,1)S(1)} %dynamic-slice_bitcast_fusion.3), channel_id=1, source_target_pairs={{0,8},{4,12},{8,0},{12,4},{16,24},{20,28},{24,16},{28,20},{1,9},{5... | collective-permute-start | bytes 589832 | tf_op jit(solution)/shard_map/ppermute | solution.py:105
  32.5 5.6 %collective-permute-start.2 = (bf16[48,1024]{1,0:T(8,128)(2,1)S(1)}, bf16[48,1024]{1,0:T(8,128)(2,1)S(1)}, u32[]{:S(2)}, u32[]{:S(2)}) collective-permute-start(bf16[48,1024]{1,0:T(8,128)(2,1)S(1)} %dynamic-slice_bitcast_fusion.6), channel_id=1, source_target_pairs={{0,16},{4,20},{8,24},{12,28},{16,0},{20,4},{24,8},{28,12},{1,17},{... | collective-permute-start | bytes 294920 | tf_op jit(solution)/shard_map/ppermute | solution.py:105
  38.1 4.7 %collective-permute-start.3 = (bf16[48,1024]{1,0:T(8,128)(2,1)S(1)}, bf16[48,1024]{1,0:T(8,128)(2,1)S(1)}, u32[]{:S(2)}, u32[]{:S(2)}) collective-permute-start(bf16[48,1024]{1,0:T(8,128)(2,1)S(1)} %bitcast_add_fusion.2), channel_id=1, source_target_pairs={{0,16},{4,20},{8,24},{12,28},{16,0},{20,4},{24,8},{28,12},{1,17},{... | collective-permute-start | bytes 294920 | tf_op jit(solution)/shard_map/ppermute | solution.py:109
  42.9 5.9 %collective-permute-start.4 = (bf16[96,1024]{1,0:T(8,128)(2,1)S(1)}, bf16[96,1024]{1,0:T(8,128)(2,1)S(1)}, u32[]{:S(2)}, u32[]{:S(2)}) collective-permute-start(bf16[96,1024]{1,0:T(8,128)(2,1)S(1)} %get-tuple-element.57), channel_id=1, source_target_pairs={{0,8},{4,12},{8,0},{12,4},{16,24},{20,28},{24,16},{28,20},{1,9},{5... | collective-permute-start | bytes 589832 | tf_op jit(solution)/shard_map/ppermute | solution.py:109
  49.1 1.8 collective-permute-start.5
  54.8 6.6 %copy-start.12 = (pred[2]{0:T(512)(128)(4,1)S(1)}, pred[2]{0:T(512)(128)(4,1)}, u32[]{:S(2)}) copy-start(pred[2]{0:T(512)(128)(4,1)} %copy-done.11) | copy-start | bytes 10
  54.8 12.4 %copy-start.10 = (s32[2]{0:T(128)S(1)}, s32[2]{0:T(128)}, u32[]{:S(2)}) copy-start(s32[2]{0:T(128)} %get-tuple-element.25) | copy-start | bytes 28
  56.7 1.7 collective-permute-start.6
  58.8 25.7 %copy-start.4 = (bf16[256,8,2,64]{0,3,2,1:T(8,128)(2,1)S(1)}, bf16[256,8,2,64]{0,3,2,1:T(8,128)(2,1)}, u32[]{:S(2)}) copy-start(bf16[256,8,2,64]{0,3,2,1:T(8,128)(2,1)} %copy-done.3) | copy-start | bytes 1572868
  59.1 6.5 %collective-permute-start.7 = (f32[32,1152]{1,0:T(8,128)S(1)}, f32[32,1152]{1,0:T(8,128)S(1)}, u32[]{:S(2)}, u32[]{:S(2)}) collective-permute-start(f32[32,1152]{1,0:T(8,128)S(1)} %get-tuple-element.54), channel_id=1, source_target_pairs={{0,8},{4,12},{8,0},{12,4},{16,24},{20,28},{24,16},{28,20},{1,9},{5... | collective-permute-start | bytes 442376 | tf_op jit(solution)/shard_map/ppermute | solution.py:105
  66.0 4.4 %collective-permute-start.8 = (f32[16,1152]{1,0:T(8,128)S(1)}, f32[16,1152]{1,0:T(8,128)S(1)}, u32[]{:S(2)}, u32[]{:S(2)}) collective-permute-start(f32[16,1152]{1,0:T(8,128)S(1)} %get-tuple-element.66), channel_id=1, source_target_pairs={{0,16},{4,20},{8,24},{12,28},{16,0},{20,4},{24,8},{28,12},{1,17},{... | collective-permute-start | bytes 221192 | tf_op jit(solution)/shard_map/ppermute | solution.py:105
  70.8 4.4 %collective-permute-start.9 = (f32[16,1152]{1,0:T(8,128)S(1)}, f32[16,1152]{1,0:T(8,128)S(1)}, u32[]{:S(2)}, u32[]{:S(2)}) collective-permute-start(f32[16,1152]{1,0:T(8,128)S(1)} %concatenate.66), channel_id=1, source_target_pairs={{0,16},{4,20},{8,24},{12,28},{16,0},{20,4},{24,8},{28,12},{1,17},{... | collective-permute-start | bytes 221192 | tf_op jit(solution)/shard_map/ppermute | solution.py:109
  75.3 5.2 %collective-permute-start.10 = (f32[32,1152]{1,0:T(8,128)S(1)}, f32[32,1152]{1,0:T(8,128)S(1)}, u32[]{:S(2)}, u32[]{:S(2)}) collective-permute-start(f32[32,1152]{1,0:T(8,128)S(1)} %get-tuple-element.61), channel_id=1, source_target_pairs={{0,8},{4,12},{8,0},{12,4},{16,24},{20,28},{24,16},{28,20},{1,9},{5... | collective-permute-start | bytes 442376 | tf_op jit(solution)/shard_map/ppermute | solution.py:109
  81.4 15.5 %collective-permute-start.11 = (f32[64,1152]{1,0:T(8,128)}, f32[64,1152]{1,0:T(8,128)}, u32[]{:S(2)}, u32[]{:S(2)}) collective-permute-start(f32[64,1152]{1,0:T(8,128)} %get-tuple-element.49), channel_id=1, source_target_pairs={{0,4},{4,0},{8,12},{12,8},{16,20},{20,16},{24,28},{28,24},{1,5},{5... | collective-permute-start | bytes 884744 | tf_op jit(solution)/shard_map/ppermute | solution.py:109
  98.9 53.9 %all-to-all-start = ((bf16[8,2,2,64,1024]{4,3,2,1,0:T(8,128)(2,1)}), bf16[8,2,2,64,1024]{4,3,2,1,0:T(8,128)(2,1)}, u32[]{:S(2)}, u32[]{:S(2)}) async-start(bf16[8,2,2,64,1024]{4,3,2,1,0:T(8,128)(2,1)} %bitcast.293), calls=%async_computation | async-start | bytes 8388608 | tf_op jit(solution)/shard_map/all_to_all | solution.py:318
  110.3 2.7 %copy-start.8 = (bf16[192,1024]{1,0:T(8,128)(2,1)S(1)}, bf16[192,1024]{1,0:T(8,128)(2,1)}, u32[]{:S(2)}) copy-start(bf16[192,1024]{1,0:T(8,128)(2,1)} %get-tuple-element.39) | copy-start | bytes 1179652
  121.4 2.0 copy-start
  121.4 3.5 %slice-start = ((f32[128,1152]{1,0:T(8,128)}), f32[128,8]{1,0:T(8,128)S(1)}, s32[]{:S(2)}) async-start(f32[128,1152]{1,0:T(8,128)} %pad_maximum_fusion.4), calls=%async_computation.2 | async-start | bytes 131072 | tf_op jit(solution)/shard_map/slice | solution.py:331
  121.4 3.7 %copy-start.6 = (f32[128,1152]{1,0:T(8,128)S(1)}, f32[128,1152]{1,0:T(8,128)}, u32[]{:S(2)}) copy-start(f32[128,1152]{1,0:T(8,128)} %pad_maximum_fusion.4) | copy-start | bytes 1769476
  155.9 1.0 copy-start.7
  156.9 1.3 copy-start.9
  163.8 2.2 copy-start.1
  163.8 3.3 %copy-start.5 = (bf16[224,8,8,128]{3,2,1,0:T(8,128)(2,1)S(1)}, bf16[224,8,8,128]{3,2,1,0:T(8,128)(2,1)}, u32[]{:S(2)}) copy-start(bf16[224,8,8,128]{3,2,1,0:T(8,128)(2,1)} %copy.277) | copy-start | bytes 11010052
  163.8 6.0 %slice-start.1 = ((s8[8388608]{0:T(1024)(128)(4,1)}), s8[4194304]{0:T(1024)(128)(4,1)S(1)}, s32[]{:S(2)}) async-start(s8[8388608]{0:T(1024)(128)(4,1)} %bitcast.354), calls=%async_computation.3 | async-start | bytes 8388608
  167.1 2.7 %slice-start.2 = ((s8[8388608]{0:T(1024)(128)(4,1)}), s8[4194304]{0:T(1024)(128)(4,1)S(1)}, s32[]{:S(2)}) async-start(s8[8388608]{0:T(1024)(128)(4,1)} %bitcast.354), calls=%async_computation.4 | async-start | bytes 8388608
  167.2 2.7 %copy-start.16 = (pred[256]{0:T(512)(128)(4,1)S(1)}, pred[256]{0:T(512)(128)(4,1)}, u32[]{:S(2)}) copy-start(pred[256]{0:T(512)(128)(4,1)} %broadcast_in_dim.181) | copy-start | bytes 772
  167.2 2.7 %copy-start.17 = (pred[256]{0:T(512)(128)(4,1)S(1)}, pred[256]{0:T(512)(128)(4,1)}, u32[]{:S(2)}) copy-start(pred[256]{0:T(512)(128)(4,1)} %broadcast_in_dim.165) | copy-start | bytes 772

commit v11 on v6

--- a/solution.py
+++ b/solution.py
@@ -50,18 +50,13 @@
     half_dim = HEAD_DIM // 2
     position = (first_row + jnp.arange(row_count)).astype(jnp.float32)
     angle_table = position[:, None] * frequency[None, :]
-    cosine = jnp.cos(angle_table)[:, None, :] * mscale
-    sine_part = jnp.sin(angle_table)[:, None, :] * mscale
-    halves_view = source.astype(jnp.float32).reshape(row_count, row_width // HEAD_DIM, 2, half_dim)
-    lower_half = halves_view[:, :, 0]
-    upper_half = halves_view[:, :, 1]
-    turned = jnp.stack(
-        [
-            lower_half * cosine - upper_half * sine_part,
-            upper_half * cosine + lower_half * sine_part,
-        ],
-        axis=2,
-    )
+    cosine = jnp.cos(angle_table) * mscale
+    sine_part = jnp.sin(angle_table) * mscale
+    cosine = jnp.concatenate([cosine, cosine], axis=1)[:, None, :]
+    sine_part = jnp.concatenate([sine_part, sine_part], axis=1)[:, None, :]
+    grid = source.astype(jnp.float32).reshape(row_count, row_width // HEAD_DIM, HEAD_DIM)
+    turned_half = jnp.concatenate([-grid[..., half_dim:], grid[..., :half_dim]], axis=2)
+    turned = grid * cosine + turned_half * sine_part
     return turned.reshape(row_count, row_width).astype(jnp.bfloat16)
 
 

time: 213 us -> 209 us (0.981)
  local copies, waits for them, and re-layouts: 45.7 us -> 29 us
  other arithmetic: 18.8 us -> 25.1 us
  starting transfers between devices: 20.8 us -> 25.2 us
    convert_element_type x10 -> x0, local copies, waits for them, and re-layouts: 11 us -> none  [rotate(): return turned.reshape(row_count, row_width).astype(jnp.bfloat16)]
    ppermute x6, waiting for transfers between devices: 19 us -> 25 us  [tree_reduce(): got = lax.ppermute(send, axis, xor_perm(count, bit))]
    unnamed x47 -> x53, local copies, waits for them, and re-layouts: 13.3 us -> 7.6 us
    ppermute x2 -> x0, local copies, waits for them, and re-layouts: 2.49 us -> none  [the longest x1 1.25 us: on_device(): lax.ppermute(pair_kv[:, tok_here - halo:], 'seq', [(i, (i + 1) % seq_coun...]
    all_to_all x1, waiting for transfers between devices: 31.5 us -> 29.4 us  [on_device(): lax.all_to_all(outgoing, 'seq', split_axis=0, concat_axis=0, tiled=True)]
  transfers between devices with their start and end apart: 15 -> 15, of which waited for: 11 -> 10; matrix products, arithmetic and copies ran while one was open for 22% -> 17% of each run, Pallas kernels for 0% -> 0%
where the time goes in v11:
time: 209 us; the launch traced here: 208 us
  waiting for transfers between devices  63.5 us (30%)
  blocking collectives  53.1 us (25%)
  local copies, waits for them, and re-layouts  29 us (14%)
  starting transfers between devices  25.2 us (12%)
  other arithmetic  25.1 us (12%)
  matrix products  9.67 us (5%)
  between operations  2.4 us (1%)
    all_to_all x1, blocking collectives, sum_over_head(): gathered = lax.all_to_all(partial, 'head', 0, 0, tiled=True)  53.1 us
    all_to_all x1, waiting for transfers between devices, on_device(): lax.all_to_all(outgoing, 'seq', split_axis=0, concat_axis=0, tiled=True)  29.4 us
    ppermute x6, waiting for transfers between devices, tree_reduce(): got = lax.ppermute(send, axis, xor_perm(count, bit))  25 us
    ppermute x6, waiting for transfers between devices, tree_reduce(): got = lax.ppermute(parts, axis, xor_perm(count, bit))  9.07 us
    unnamed x53, local copies, waits for them, and re-layouts  7.6 us
    ppermute x6, starting transfers between devices, tree_reduce(): got = lax.ppermute(parts, axis, xor_perm(count, bit))  6.96 us
    ppermute x6, starting transfers between devices, tree_reduce(): got = lax.ppermute(send, axis, xor_perm(count, bit))  6.61 us
    all_to_all x1, starting transfers between devices, on_device(): lax.all_to_all(outgoing, 'seq', split_axis=0, concat_axis=0, tiled=True)  6.1 us
  transfers between devices with their start and end apart: 15, of which 10 were waited for; matrix products, arithmetic and copies ran while one was open for 17% of the time, Pallas kernels for 0%

profile of v11, /device:TPU:2, one launch (start us, length us, event | category | flops | bytes accessed | tf_op | source)
XLA Modules:
  0.0 207.9 jit_solution(8564886063050102272)
XLA Ops:
  1.4 0.7 fusion.118
  2.1 1.2 compare_select_fusion.3
  3.5 1.1 convert_bitcast_fusion
  5.8 0.8 pad_maximum_fusion.11
  7.1 0.7 slice_negate_fusion
  8.0 0.6 maximum_multiply_fusion.1
  9.1 1.0 fusion.48
  10.0 0.6 gather_fusion.2
  10.6 0.6 gather_fusion.1
  11.6 1.1 fusion.57
  12.7 2.4 %collective-permute-start.12 = (bf16[2,128,1024]{2,1,0:T(8,128)(2,1)}, bf16[2,128,1024]{2,1,0:T(8,128)(2,1)}, u32[]{:S(2)}, u32[]{:S(2)}) collective-permute-start(bf16[2,128,1024]{2,1,0:T(8,128)(2,1)} %get-tuple-element.33), channel_id=1, source_target_pairs={{0,4},{4,8},{8,12},{12,16},{16,20},{20,24},{24,28},{1,5},{5,9},{9,... | collective-permute-start | bytes 1572872 | tf_op jit(solution)/shard_map/ppermute | solution.py:208
  15.1 3.2 %collective-permute-start.13 = (bf16[2,128,1024]{2,1,0:T(8,128)(2,1)}, bf16[2,128,1024]{2,1,0:T(8,128)(2,1)}, u32[]{:S(2)}, u32[]{:S(2)}) collective-permute-start(bf16[2,128,1024]{2,1,0:T(8,128)(2,1)} %get-tuple-element.34), channel_id=1, source_target_pairs={{4,0},{8,4},{12,8},{16,12},{20,16},{24,20},{28,24},{5,1},{9,5},{13... | collective-permute-start | bytes 1572872 | tf_op jit(solution)/shard_map/ppermute | solution.py:211
  18.6 13.5 %collective-permute-done.1 = bf16[96,1024]{1,0:T(8,128)(2,1)S(1)} collective-permute-done((bf16[96,1024]{1,0:T(8,128)(2,1)S(1)}, bf16[96,1024]{1,0:T(8,128)(2,1)S(1)}, u32[]{:S(2)}, u32[]{:S(2)}) %collective-permute-start.1) | collective-permute-done | bytes 196640 | tf_op jit(solution)/shard_map/ppermute | solution.py:100
  32.2 2.6 %collective-permute-start.2 = (bf16[48,1024]{1,0:T(8,128)(2,1)S(1)}, bf16[48,1024]{1,0:T(8,128)(2,1)S(1)}, u32[]{:S(2)}, u32[]{:S(2)}) collective-permute-start(bf16[48,1024]{1,0:T(8,128)(2,1)S(1)} %dynamic-slice_bitcast_fusion.6), channel_id=1, source_target_pairs={{0,16},{4,20},{8,24},{12,28},{16,0},{20,4},{24,8},{28,12},{1,17},{... | collective-permute-start | bytes 294920 | tf_op jit(solution)/shard_map/ppermute | solution.py:100
  34.9 2.9 %collective-permute-done.2 = bf16[48,1024]{1,0:T(8,128)(2,1)S(1)} collective-permute-done((bf16[48,1024]{1,0:T(8,128)(2,1)S(1)}, bf16[48,1024]{1,0:T(8,128)(2,1)S(1)}, u32[]{:S(2)}, u32[]{:S(2)}) %collective-permute-start.2) | collective-permute-done | bytes 98336 | tf_op jit(solution)/shard_map/ppermute | solution.py:100
  37.9 1.7 collective-permute-start.3
  39.6 3.0 %collective-permute-done.3 = bf16[48,1024]{1,0:T(8,128)(2,1)S(1)} collective-permute-done((bf16[48,1024]{1,0:T(8,128)(2,1)S(1)}, bf16[48,1024]{1,0:T(8,128)(2,1)S(1)}, u32[]{:S(2)}, u32[]{:S(2)}) %collective-permute-start.3) | collective-permute-done | bytes 98336 | tf_op jit(solution)/shard_map/ppermute | solution.py:104
  42.7 2.3 %collective-permute-start.4 = (bf16[96,1024]{1,0:T(8,128)(2,1)S(1)}, bf16[96,1024]{1,0:T(8,128)(2,1)S(1)}, u32[]{:S(2)}, u32[]{:S(2)}) collective-permute-start(bf16[96,1024]{1,0:T(8,128)(2,1)S(1)} %get-tuple-element.59), channel_id=1, source_target_pairs={{0,8},{4,12},{8,0},{12,4},{16,24},{20,28},{24,16},{28,20},{1,9},{5... | collective-permute-start | bytes 589832 | tf_op jit(solution)/shard_map/ppermute | solution.py:104
  45.5 3.1 %collective-permute-done.4 = bf16[96,1024]{1,0:T(8,128)(2,1)S(1)} collective-permute-done((bf16[96,1024]{1,0:T(8,128)(2,1)S(1)}, bf16[96,1024]{1,0:T(8,128)(2,1)S(1)}, u32[]{:S(2)}, u32[]{:S(2)}) %collective-permute-start.4) | collective-permute-done | bytes 196640 | tf_op jit(solution)/shard_map/ppermute | solution.py:104
  48.7 0.8 pad_maximum_fusion.7
  49.7 0.6 reshape.423
  50.3 0.6 iota_add_fusion.1
  50.9 0.6 fusion.119
  51.5 1.1 fusion.73
  53.2 1.1 fusion.53
  54.3 0.7 copy.83
  55.5 0.8 copy.82
  56.3 1.0 concatenate.81
  58.0 1.1 collective-permute-done.6
  59.8 2.1 %collective-permute-start.7 = (f32[32,1152]{1,0:T(8,128)S(1)}, f32[32,1152]{1,0:T(8,128)S(1)}, u32[]{:S(2)}, u32[]{:S(2)}) collective-permute-start(f32[32,1152]{1,0:T(8,128)S(1)} %get-tuple-element.56), channel_id=1, source_target_pairs={{0,8},{4,12},{8,0},{12,4},{16,24},{20,28},{24,16},{28,20},{1,9},{5... | collective-permute-start | bytes 442376 | tf_op jit(solution)/shard_map/ppermute | solution.py:100
  62.0 4.3 %collective-permute-done.7 = f32[32,1152]{1,0:T(8,128)S(1)} collective-permute-done((f32[32,1152]{1,0:T(8,128)S(1)}, f32[32,1152]{1,0:T(8,128)S(1)}, u32[]{:S(2)}, u32[]{:S(2)}) %collective-permute-start.7) | collective-permute-done | bytes 147488 | tf_op jit(solution)/shard_map/ppermute | solution.py:100
  66.8 1.2 collective-permute-start.8
  68.1 3.1 %collective-permute-done.8 = f32[16,1152]{1,0:T(8,128)S(1)} collective-permute-done((f32[16,1152]{1,0:T(8,128)S(1)}, f32[16,1152]{1,0:T(8,128)S(1)}, u32[]{:S(2)}, u32[]{:S(2)}) %collective-permute-start.8) | collective-permute-done | bytes 73760 | tf_op jit(solution)/shard_map/ppermute | solution.py:100
  71.6 1.2 collective-permute-start.9
  73.3 2.7 %collective-permute-done.9 = f32[16,1152]{1,0:T(8,128)S(1)} collective-permute-done((f32[16,1152]{1,0:T(8,128)S(1)}, f32[16,1152]{1,0:T(8,128)S(1)}, u32[]{:S(2)}, u32[]{:S(2)}) %collective-permute-start.9) | collective-permute-done | bytes 73760 | tf_op jit(solution)/shard_map/ppermute | solution.py:104
  76.0 1.8 collective-permute-start.10
  77.8 2.8 %gather_fusion = bf16[16,2,64,1024]{3,2,1,0:T(8,128)(2,1)} fusion(bf16[4,2,64,1024]{3,2,0,1:T(8,128)(2,1)S(1)} %pad_maximum_fusion.2, s32[1024]{0:T(1024)S(1)} %pad_clamp_fusion.1), kind=kCustom, calls=%fused_computation | custom fusion | bytes 8388672 | tf_op jit(solution)/shard_map/gather | solution.py:290
  80.6 0.6 fusion.134
  81.5 1.2 compare_and_fusion.1
  83.2 6.1 %all-to-all-start = ((bf16[8,2,2,64,1024]{4,3,2,1,0:T(8,128)(2,1)}), bf16[8,2,2,64,1024]{4,3,2,1,0:T(8,128)(2,1)}, u32[]{:S(2)}, u32[]{:S(2)}) async-start(bf16[8,2,2,64,1024]{4,3,2,1,0:T(8,128)(2,1)} %bitcast.290), calls=%async_computation | async-start | bytes 8388608 | tf_op jit(solution)/shard_map/all_to_all | solution.py:292
  89.3 1.3 compare_and_fusion
  91.5 0.7 or_bitcast_fusion
  92.2 1.0 slice.231
  93.2 1.0 slice.232
  94.2 1.2 maximum_bitcast_fusion
  95.4 1.5 maximum_bitcast_fusion.1
  97.2 1.1 pad_maximum_fusion
  98.2 1.5 fusion.131
  99.7 1.0 copy.116
  100.7 2.7 %copy.117 = bf16[224,8,8,128]{3,2,1,0:T(8,128)(2,1)} copy(bf16[224,8,8,128]{3,1,2,0:T(8,128)(2,1)S(1)} %bitcast.297) | data formatting | bytes 7340032
  103.4 1.8 fusion
  105.3 1.6 fusion.5
  107.7 29.4 %all-to-all-done = bf16[8,2,2,64,1024]{4,3,2,1,0:T(8,128)(2,1)} async-done(((bf16[8,2,2,64,1024]{4,3,2,1,0:T(8,128)(2,1)}), bf16[8,2,2,64,1024]{4,3,2,1,0:T(8,128)(2,1)}, u32[]{:S(2)}, u32[]{:S(2)}) %all-to-all-start) | async-done | bytes 4194336 | tf_op jit(solution)/shard_map/all_to_all | solution.py:292
  137.1 2.8 %gather_fusion.4 = bf16[12,64,1024]{2,1,0:T(8,128)(2,1)S(1)} fusion(bf16[8,2,2,64,1024]{4,3,2,1,0:T(8,128)(2,1)} %all-to-all-done, s32[12]{0:T(128)S(1)} %bitcast.347), kind=kCustom, calls=%fused_computation.4 | custom fusion | bytes 3145872 | tf_op jit(solution)/shard_map/gather | solution.py:295
  140.4 2.8 %gather_fusion.5 = bf16[12,64,1024]{2,1,0:T(8,128)(2,1)S(1)} fusion(bf16[8,2,2,64,1024]{4,3,2,1,0:T(8,128)(2,1)} %all-to-all-done, s32[12]{0:T(128)S(1)} %get-tuple-element.12), kind=kCustom, calls=%fused_computation.5 | custom fusion | bytes 3145872 | tf_op jit(solution)/shard_map/gather | solution.py:296
  143.7 0.6 copy-done.4
  144.3 1.2 multiply_reduce_fusion
  145.5 0.8 fusion.12
  146.3 0.6 copy-done.1
  146.9 2.1 fusion.32
  149.0 1.4 fusion.42
  150.9 2.5 %convolution_convert_fusion = bf16[256,4096]{1,0:T(8,128)(2,1)S(1)} fusion(bf16[1024,4096]{1,0:T(8,128)(2,1)S(1)} %bitcast.356, bf16[256,1024]{1,0:T(8,128)(2,1)S(1)} %bitcast.335, bf16[256,1024]{1,0:T(8,128)(2,1)S(1)} %bitcast.334, bf16[32,8,8,128]{3,2,1,0:T(8,128)(2,1)S(1)} %bitcast.339, pred[256]{0:T(512)(128)(4,1)S(1)} %broadcast_in_dim.175, ...), kind=kOutput, calls=%fused_computation.7 | convolution fusion | flops 2149056512 | bytes 12059136 | tf_op jit(solution)/shard_map/dot_general | solution.py:140
  153.6 53.1 %all_to_all.10 = bf16[4,1024,256]{1,2,0:T(8,128)(2,1)S(1)} all-to-all(bf16[4,1024,256]{1,2,0:T(8,128)(2,1)S(1)} %bitcast.302), channel_id=1, replica_groups=mesh['seq'=8,'head'=4] {'head'}, dimensions={0} | all-to-all | bytes 4194304 | tf_op jit(solution)/shard_map/all_to_all | solution.py:147
  206.6 1.3 reduce_sum.71
  (151 shorter events, 12.4 us)
Async XLA Ops:
  0.0 4.9 %copy-start.7 = (bf16[256,1024]{1,0:T(8,128)(2,1)S(1)}, bf16[256,1024]{1,0:T(8,128)(2,1)}, u32[]{:S(2)}) copy-start(bf16[256,1024]{1,0:T(8,128)(2,1)} %param.10) | copy-start | bytes 1572868
  2.1 2.6 %copy-start.11 = (pred[2]{0:T(512)(128)(4,1)}, pred[2]{0:T(512)(128)(4,1)S(1)}, u32[]{:S(2)}) copy-start(pred[2]{0:T(512)(128)(4,1)S(1)} %fusion.118) | copy-start | bytes 10
  4.9 1.7 copy-start.2
  7.1 0.9 copy-start.9
  8.0 1.0 copy-start.6
  11.3 7.0 %copy-start.14 = (s32[32,3]{0,1:T(4,128)S(1)}, s32[32,3]{0,1:T(4,128)}, u32[]{:S(2)}) copy-start(s32[32,3]{0,1:T(4,128)} %param.14) | copy-start | bytes 1156
  11.5 7.0 %collective-permute-start = (bf16[192,1024]{1,0:T(8,128)(2,1)S(1)}, bf16[192,1024]{1,0:T(8,128)(2,1)S(1)}, u32[]{:S(2)}, u32[]{:S(2)}) collective-permute-start(bf16[192,1024]{1,0:T(8,128)(2,1)S(1)} %dynamic-slice_bitcast_fusion), channel_id=1, source_target_pairs={{0,4},{4,0},{8,12},{12,8},{16,20},{20,16},{24,28},{28,24},{1,5},{5... | collective-permute-start | bytes 1179656 | tf_op jit(solution)/shard_map/ppermute | solution.py:100
  12.7 79.6 %collective-permute-start.12 = (bf16[2,128,1024]{2,1,0:T(8,128)(2,1)}, bf16[2,128,1024]{2,1,0:T(8,128)(2,1)}, u32[]{:S(2)}, u32[]{:S(2)}) collective-permute-start(bf16[2,128,1024]{2,1,0:T(8,128)(2,1)} %get-tuple-element.33), channel_id=1, source_target_pairs={{0,4},{4,8},{8,12},{12,16},{16,20},{20,24},{24,28},{1,5},{5,9},{9,... | collective-permute-start | bytes 1572872 | tf_op jit(solution)/shard_map/ppermute | solution.py:208
  15.1 78.2 %collective-permute-start.13 = (bf16[2,128,1024]{2,1,0:T(8,128)(2,1)}, bf16[2,128,1024]{2,1,0:T(8,128)(2,1)}, u32[]{:S(2)}, u32[]{:S(2)}) collective-permute-start(bf16[2,128,1024]{2,1,0:T(8,128)(2,1)} %get-tuple-element.34), channel_id=1, source_target_pairs={{4,0},{8,4},{12,8},{16,12},{20,16},{24,20},{28,24},{5,1},{9,5},{13... | collective-permute-start | bytes 1572872 | tf_op jit(solution)/shard_map/ppermute | solution.py:211
  18.5 13.7 %collective-permute-start.1 = (bf16[96,1024]{1,0:T(8,128)(2,1)S(1)}, bf16[96,1024]{1,0:T(8,128)(2,1)S(1)}, u32[]{:S(2)}, u32[]{:S(2)}) collective-permute-start(bf16[96,1024]{1,0:T(8,128)(2,1)S(1)} %dynamic-slice_bitcast_fusion.3), channel_id=1, source_target_pairs={{0,8},{4,12},{8,0},{12,4},{16,24},{20,28},{24,16},{28,20},{1,9},{5... | collective-permute-start | bytes 589832 | tf_op jit(solution)/shard_map/ppermute | solution.py:100
  18.6 30.9 %copy-start.10 = (s32[8,12]{1,0:T(8,128)}, s32[8,12]{1,0:T(8,128)S(1)}, u32[]{:S(2)}) copy-start(s32[8,12]{1,0:T(8,128)S(1)} %get-tuple-element.71) | copy-start | bytes 1156
  32.2 5.6 %collective-permute-start.2 = (bf16[48,1024]{1,0:T(8,128)(2,1)S(1)}, bf16[48,1024]{1,0:T(8,128)(2,1)S(1)}, u32[]{:S(2)}, u32[]{:S(2)}) collective-permute-start(bf16[48,1024]{1,0:T(8,128)(2,1)S(1)} %dynamic-slice_bitcast_fusion.6), channel_id=1, source_target_pairs={{0,16},{4,20},{8,24},{12,28},{16,0},{20,4},{24,8},{28,12},{1,17},{... | collective-permute-start | bytes 294920 | tf_op jit(solution)/shard_map/ppermute | solution.py:100
  37.9 4.7 %collective-permute-start.3 = (bf16[48,1024]{1,0:T(8,128)(2,1)S(1)}, bf16[48,1024]{1,0:T(8,128)(2,1)S(1)}, u32[]{:S(2)}, u32[]{:S(2)}) collective-permute-start(bf16[48,1024]{1,0:T(8,128)(2,1)S(1)} %bitcast_add_fusion.2), channel_id=1, source_target_pairs={{0,16},{4,20},{8,24},{12,28},{16,0},{20,4},{24,8},{28,12},{1,17},{... | collective-permute-start | bytes 294920 | tf_op jit(solution)/shard_map/ppermute | solution.py:104
  42.7 5.9 %collective-permute-start.4 = (bf16[96,1024]{1,0:T(8,128)(2,1)S(1)}, bf16[96,1024]{1,0:T(8,128)(2,1)S(1)}, u32[]{:S(2)}, u32[]{:S(2)}) collective-permute-start(bf16[96,1024]{1,0:T(8,128)(2,1)S(1)} %get-tuple-element.59), channel_id=1, source_target_pairs={{0,8},{4,12},{8,0},{12,4},{16,24},{20,28},{24,16},{28,20},{1,9},{5... | collective-permute-start | bytes 589832 | tf_op jit(solution)/shard_map/ppermute | solution.py:104
  49.6 1.9 collective-permute-start.5
  55.4 2.5 %copy-start.16 = (s32[8]{0:T(128)S(1)}, s32[8]{0:T(128)}, u32[]{:S(2)}) copy-start(s32[8]{0:T(128)} %param.15) | copy-start | bytes 100
  55.5 2.5 %copy-start.17 = (s32[5]{0:T(128)S(1)}, s32[5]{0:T(128)}, u32[]{:S(2)}) copy-start(s32[5]{0:T(128)} %fusion.119) | copy-start | bytes 64
  57.3 4.6 %copy-start.18 = (s32[4]{0:T(128)S(1)}, s32[4]{0:T(128)}, u32[]{:S(2)}) copy-start(s32[4]{0:T(128)} %iota_add_fusion.1) | copy-start | bytes 52
  57.4 1.8 collective-permute-start.6
  59.8 6.5 %collective-permute-start.7 = (f32[32,1152]{1,0:T(8,128)S(1)}, f32[32,1152]{1,0:T(8,128)S(1)}, u32[]{:S(2)}, u32[]{:S(2)}) collective-permute-start(f32[32,1152]{1,0:T(8,128)S(1)} %get-tuple-element.56), channel_id=1, source_target_pairs={{0,8},{4,12},{8,0},{12,4},{16,24},{20,28},{24,16},{28,20},{1,9},{5... | collective-permute-start | bytes 442376 | tf_op jit(solution)/shard_map/ppermute | solution.py:100
  66.6 6.1 %copy-start.13 = (s32[2]{0:T(128)S(1)}, s32[2]{0:T(128)}, u32[]{:S(2)}) copy-start(s32[2]{0:T(128)} %get-tuple-element.27) | copy-start | bytes 28
  66.7 11.1 %copy-start.15 = (s32[16]{0:T(128)S(1)}, s32[16]{0:T(128)}, u32[]{:S(2)}) copy-start(s32[16]{0:T(128)} %reshape.423) | copy-start | bytes 196
  66.8 4.4 %collective-permute-start.8 = (f32[16,1152]{1,0:T(8,128)S(1)}, f32[16,1152]{1,0:T(8,128)S(1)}, u32[]{:S(2)}, u32[]{:S(2)}) collective-permute-start(f32[16,1152]{1,0:T(8,128)S(1)} %get-tuple-element.68), channel_id=1, source_target_pairs={{0,16},{4,20},{8,24},{12,28},{16,0},{20,4},{24,8},{28,12},{1,17},{... | collective-permute-start | bytes 221192 | tf_op jit(solution)/shard_map/ppermute | solution.py:100
  71.6 4.4 %collective-permute-start.9 = (f32[16,1152]{1,0:T(8,128)S(1)}, f32[16,1152]{1,0:T(8,128)S(1)}, u32[]{:S(2)}, u32[]{:S(2)}) collective-permute-start(f32[16,1152]{1,0:T(8,128)S(1)} %concatenate.90), channel_id=1, source_target_pairs={{0,16},{4,20},{8,24},{12,28},{16,0},{20,4},{24,8},{28,12},{1,17},{... | collective-permute-start | bytes 221192 | tf_op jit(solution)/shard_map/ppermute | solution.py:104
  76.0 5.3 %collective-permute-start.10 = (f32[32,1152]{1,0:T(8,128)S(1)}, f32[32,1152]{1,0:T(8,128)S(1)}, u32[]{:S(2)}, u32[]{:S(2)}) collective-permute-start(f32[32,1152]{1,0:T(8,128)S(1)} %get-tuple-element.63), channel_id=1, source_target_pairs={{0,8},{4,12},{8,0},{12,4},{16,24},{20,28},{24,16},{28,20},{1,9},{5... | collective-permute-start | bytes 442376 | tf_op jit(solution)/shard_map/ppermute | solution.py:104
  77.8 2.8 %copy-start.12 = (pred[2]{0:T(512)(128)(4,1)S(1)}, pred[2]{0:T(512)(128)(4,1)}, u32[]{:S(2)}) copy-start(pred[2]{0:T(512)(128)(4,1)} %copy-done.11) | copy-start | bytes 10
  81.4 1.6 collective-permute-start.11
  83.2 53.8 %all-to-all-start = ((bf16[8,2,2,64,1024]{4,3,2,1,0:T(8,128)(2,1)}), bf16[8,2,2,64,1024]{4,3,2,1,0:T(8,128)(2,1)}, u32[]{:S(2)}, u32[]{:S(2)}) async-start(bf16[8,2,2,64,1024]{4,3,2,1,0:T(8,128)(2,1)} %bitcast.290), calls=%async_computation | async-start | bytes 8388608 | tf_op jit(solution)/shard_map/all_to_all | solution.py:292
  91.2 12.2 %copy-start.3 = (bf16[32,8,8,128]{3,2,1,0:T(8,128)(2,1)}, bf16[32,8,8,128]{3,2,1,0:T(8,128)(2,1)S(1)}, u32[]{:S(2)}) copy-start(bf16[32,8,8,128]{3,2,1,0:T(8,128)(2,1)S(1)} %copy.115) | copy-start | bytes 1572868
  95.4 1.5 copy-start.8
  105.3 2.0 copy-start
  143.2 1.0 copy-start.4
  143.2 3.1 %copy-start.5 = (bf16[224,8,8,128]{3,2,1,0:T(8,128)(2,1)S(1)}, bf16[224,8,8,128]{3,2,1,0:T(8,128)(2,1)}, u32[]{:S(2)}) copy-start(bf16[224,8,8,128]{3,2,1,0:T(8,128)(2,1)} %copy.117) | copy-start | bytes 11010052
  144.3 2.6 %copy-start.1 = (f32[4,8,64,448]{3,2,1,0:T(8,128)S(1)}, f32[4,8,64,448]{3,2,1,0:T(8,128)}, u32[]{:S(2)}) copy-start(f32[4,8,64,448]{3,2,1,0:T(8,128)} %copy-done) | copy-start | bytes 11010052
  145.5 5.4 %slice-start = ((s8[8388608]{0:T(1024)(128)(4,1)}), s8[4194304]{0:T(1024)(128)(4,1)S(1)}, s32[]{:S(2)}) async-start(s8[8388608]{0:T(1024)(128)(4,1)} %bitcast.355), calls=%async_computation.2 | async-start | bytes 8388608
  146.9 4.0 %slice-start.1 = ((s8[8388608]{0:T(1024)(128)(4,1)}), s8[4194304]{0:T(1024)(128)(4,1)S(1)}, s32[]{:S(2)}) async-start(s8[8388608]{0:T(1024)(128)(4,1)} %bitcast.355), calls=%async_computation.3 | async-start | bytes 8388608

commit v12 on v11

--- a/solution.py
+++ b/solution.py
@@ -203,14 +203,6 @@
     query_rot = rotate(queries, first_row, frequency, mscale)
     key_rot = rotate(keys, first_row, frequency, mscale)
     pair_kv = jnp.stack([key_rot, values])
-    halo = WMAX * BLOCK
-    seq_ends = seq_count - 1
-    from_left = lax.ppermute(
-        pair_kv[:, tok_here - halo :], "seq", [(i, (i + 1) % seq_count) for i in range(seq_ends)]
-    ).reshape(2, WMAX, BLOCK, width_here)
-    from_right = lax.ppermute(
-        pair_kv[:, :halo], "seq", [((i + 1) % seq_count, i) for i in range(seq_ends)]
-    ).reshape(2, WMAX, BLOCK, width_here)
     local_blocks = pair_kv.reshape(2, blocks_here, BLOCK, width_here)
 
     def padded_block(index):
@@ -235,6 +227,15 @@
     masked = jnp.where(mine_global[None, :, None, None], picked, jnp.zeros_like(picked))
     shared = tree_reduce(masked.reshape(3 * GLOB * BLOCK, width_here), add_merge, "seq")
     shared = shared.reshape(3, GLOB, BLOCK, width_here)
+    halo = WMAX * BLOCK
+    seq_ends = seq_count - 1
+    halo_kv, shared = lax.optimization_barrier((pair_kv, shared))
+    from_left = lax.ppermute(
+        halo_kv[:, tok_here - halo :], "seq", [(i, (i + 1) % seq_count) for i in range(seq_ends)]
+    ).reshape(2, WMAX, BLOCK, width_here)
+    from_right = lax.ppermute(
+        halo_kv[:, :halo], "seq", [((i + 1) % seq_count, i) for i in range(seq_ends)]
+    ).reshape(2, WMAX, BLOCK, width_here)
     slot_parts = [
         jnp.stack(
             [padded_block(block + offset_slot) for offset_slot in range(2 * WMAX + 1)], axis=1
@@ -271,6 +272,7 @@
         ],
         axis=1,
     )
+    packed, from_left, from_right = lax.optimization_barrier((packed, from_left, from_right))
     reduced = tree_reduce(packed, softmax_merge, "seq")
     slot_total = blocks_here * RAND
     capacity = (slot_total + seq_count - 1) // seq_count

time: 209 us -> 207 us (level)
  waiting for transfers between devices: 63.5 us -> 74.2 us
  starting transfers between devices: 25.2 us -> 17.5 us
  other arithmetic: 25.1 us -> 18.5 us
    ppermute x2, waiting for transfers between devices: 0.01 us -> 7.53 us  [the longest x1 4.63 us: on_device(): lax.ppermute(halo_kv[:, :halo], 'seq', [((i + 1) % seq_count, i) for i in...]
    ppermute x6, waiting for transfers between devices: 9.07 us -> 15.8 us  [tree_reduce(): got = lax.ppermute(parts, axis, xor_perm(count, bit))]
    ppermute x6, starting transfers between devices: 6.96 us -> 2.69 us  [tree_reduce(): got = lax.ppermute(parts, axis, xor_perm(count, bit))]
    ppermute x6, waiting for transfers between devices: 25 us -> 22.1 us  [tree_reduce(): got = lax.ppermute(send, axis, xor_perm(count, bit))]
    ppermute x6, starting transfers between devices: 6.61 us -> 4.24 us  [tree_reduce(): got = lax.ppermute(send, axis, xor_perm(count, bit))]
    unnamed x53 -> x37, local copies, waits for them, and re-layouts: 7.6 us -> 8.19 us
  transfers between devices with their start and end apart: 15 -> 15, of which waited for: 10 -> 15; matrix products, arithmetic and copies ran while one was open for 17% -> 13% of each run, Pallas kernels for 0% -> 0%
where the time goes in v12:
time: 207 us
  waiting for transfers between devices  74.2 us (36%)
  blocking collectives  53.1 us (26%)
  local copies, waits for them, and re-layouts  29.6 us (14%)
  other arithmetic  18.5 us (9%)
  starting transfers between devices  17.5 us (8%)
  matrix products  11.6 us (6%)
  between operations  2.39 us (1%)
    all_to_all x1, blocking collectives, sum_over_head(): gathered = lax.all_to_all(partial, 'head', 0, 0, tiled=True)  53.1 us
    all_to_all x1, waiting for transfers between devices, on_device(): lax.all_to_all(outgoing, 'seq', split_axis=0, concat_axis=0, tiled=True)  28.8 us
    ppermute x6, waiting for transfers between devices, tree_reduce(): got = lax.ppermute(send, axis, xor_perm(count, bit))  22.1 us
    ppermute x6, waiting for transfers between devices, tree_reduce(): got = lax.ppermute(parts, axis, xor_perm(count, bit))  15.8 us
    unnamed x37, local copies, waits for them, and re-layouts  8.19 us
    dot_general x2, matrix products, partial_attend(): jnp.einsum('bhqs,bshd->bqhd', expo.astype(jnp.bfloat16), value_grid, pref...  5.35 us
    all_to_all x1, starting transfers between devices, on_device(): lax.all_to_all(outgoing, 'seq', split_axis=0, concat_axis=0, tiled=True)  4.98 us
    ppermute x1, waiting for transfers between devices, on_device(): lax.ppermute(halo_kv[:, :halo], 'seq', [((i + 1) % seq_count, i) for i in...  4.63 us
  transfers between devices with their start and end apart: 15, of which 15 were waited for; matrix products, arithmetic and copies ran while one was open for 13% of the time, Pallas kernels for 0%

profile of v12, /device:TPU:2, one launch (start us, length us, event | category | flops | bytes accessed | tf_op | source)
XLA Modules:
  0.0 206.8 jit_solution(16202080305219445905)
XLA Ops:
  1.4 1.1 convert_bitcast_fusion.1
  3.5 0.5 fusion.88
  4.2 0.7 slice_negate_fusion
  4.9 0.6 maximum_multiply_fusion.1
  5.9 1.0 fusion.48
  6.9 0.6 gather_fusion.2
  7.5 0.6 gather_fusion.1
  8.0 0.6 gather_fusion.3
  9.5 1.4 collective-permute-done
  11.1 6.8 %collective-permute-done.1 = bf16[96,1024]{1,0:T(8,128)(2,1)S(1)} collective-permute-done((bf16[96,1024]{1,0:T(8,128)(2,1)S(1)}, bf16[96,1024]{1,0:T(8,128)(2,1)S(1)}, u32[]{:S(2)}, u32[]{:S(2)}) %collective-permute-start.1) | collective-permute-done | bytes 196640 | tf_op jit(solution)/shard_map/ppermute | solution.py:100
  18.0 1.6 collective-permute-start.2
  19.6 3.1 %collective-permute-done.2 = bf16[48,1024]{1,0:T(8,128)(2,1)S(1)} collective-permute-done((bf16[48,1024]{1,0:T(8,128)(2,1)S(1)}, bf16[48,1024]{1,0:T(8,128)(2,1)S(1)}, u32[]{:S(2)}, u32[]{:S(2)}) %collective-permute-start.2) | collective-permute-done | bytes 98336 | tf_op jit(solution)/shard_map/ppermute | solution.py:100
  22.7 1.6 collective-permute-start.3
  24.3 0.3 convert_reduce_fusion
  24.7 2.7 %collective-permute-done.3 = bf16[48,1024]{1,0:T(8,128)(2,1)S(1)} collective-permute-done((bf16[48,1024]{1,0:T(8,128)(2,1)S(1)}, bf16[48,1024]{1,0:T(8,128)(2,1)S(1)}, u32[]{:S(2)}, u32[]{:S(2)}) %collective-permute-start.3) | collective-permute-done | bytes 98336 | tf_op jit(solution)/shard_map/ppermute | solution.py:104
  27.5 0.4 collective-permute-start.4
  27.8 5.4 %collective-permute-done.4 = bf16[96,1024]{1,0:T(8,128)(2,1)S(1)} collective-permute-done((bf16[96,1024]{1,0:T(8,128)(2,1)S(1)}, bf16[96,1024]{1,0:T(8,128)(2,1)S(1)}, u32[]{:S(2)}, u32[]{:S(2)}) %collective-permute-start.4) | collective-permute-done | bytes 196640 | tf_op jit(solution)/shard_map/ppermute | solution.py:104
  33.9 1.3 collective-permute-done.5
  35.6 1.1 fusion.132
  36.8 2.0 collective-permute-start.6
  38.8 3.5 %collective-permute-start.7 = (bf16[2,128,1024]{2,1,0:T(8,128)(2,1)}, bf16[2,128,1024]{2,1,0:T(8,128)(2,1)}, u32[]{:S(2)}, u32[]{:S(2)}) collective-permute-start(bf16[2,128,1024]{2,1,0:T(8,128)(2,1)} %get-tuple-element.39), channel_id=1, source_target_pairs={{4,0},{8,4},{12,8},{16,12},{20,16},{24,20},{28,24},{5,1},{9,5},{13... | collective-permute-start | bytes 1572872 | tf_op jit(solution)/shard_map/ppermute | solution.py:236
  43.1 0.5 fusion.53
  43.7 0.4 convolution_bitcast_fusion
  44.7 2.9 %collective-permute-done.6 = bf16[2,128,1024]{2,1,0:T(8,128)(2,1)} collective-permute-done((bf16[2,128,1024]{2,1,0:T(8,128)(2,1)}, bf16[2,128,1024]{2,1,0:T(8,128)(2,1)}, u32[]{:S(2)}, u32[]{:S(2)}) %collective-permute-start.6) | collective-permute-done | bytes 524320 | tf_op jit(solution)/shard_map/ppermute | solution.py:233
  47.6 4.6 %collective-permute-done.7 = bf16[2,128,1024]{2,1,0:T(8,128)(2,1)} collective-permute-done((bf16[2,128,1024]{2,1,0:T(8,128)(2,1)}, bf16[2,128,1024]{2,1,0:T(8,128)(2,1)}, u32[]{:S(2)}, u32[]{:S(2)}) %collective-permute-start.7) | collective-permute-done | bytes 524320 | tf_op jit(solution)/shard_map/ppermute | solution.py:236
  52.2 1.8 collective-permute-start.8
  54.2 1.1 collective-permute-done.8
  55.9 0.6 collective-permute-start.9
  56.5 5.6 %collective-permute-done.9 = f32[32,1152]{1,0:T(8,128)S(1)} collective-permute-done((f32[32,1152]{1,0:T(8,128)S(1)}, f32[32,1152]{1,0:T(8,128)S(1)}, u32[]{:S(2)}, u32[]{:S(2)}) %collective-permute-start.9) | collective-permute-done | bytes 147488 | tf_op jit(solution)/shard_map/ppermute | solution.py:100
  62.9 4.1 %collective-permute-done.10 = f32[16,1152]{1,0:T(8,128)S(1)} collective-permute-done((f32[16,1152]{1,0:T(8,128)S(1)}, f32[16,1152]{1,0:T(8,128)S(1)}, u32[]{:S(2)}, u32[]{:S(2)}) %collective-permute-start.10) | collective-permute-done | bytes 73760 | tf_op jit(solution)/shard_map/ppermute | solution.py:100
  67.5 4.2 %collective-permute-done.11 = f32[16,1152]{1,0:T(8,128)S(1)} collective-permute-done((f32[16,1152]{1,0:T(8,128)S(1)}, f32[16,1152]{1,0:T(8,128)S(1)}, u32[]{:S(2)}, u32[]{:S(2)}) %collective-permute-start.11) | collective-permute-done | bytes 73760 | tf_op jit(solution)/shard_map/ppermute | solution.py:104
  71.8 0.6 collective-permute-start.12
  72.4 2.8 %gather_fusion = bf16[16,2,64,1024]{3,2,1,0:T(8,128)(2,1)} fusion(bf16[4,2,64,1024]{3,2,0,1:T(8,128)(2,1)S(1)} %pad_maximum_fusion.2, s32[1024]{0:T(1024)S(1)} %pad_clamp_fusion.1), kind=kCustom, calls=%fused_computation | custom fusion | bytes 8388672 | tf_op jit(solution)/shard_map/gather | solution.py:292
  75.2 0.6 fusion.135
  75.8 1.2 collective-permute-done.12
  77.2 0.6 fusion.134
  77.8 0.9 collective-permute-done.13
  78.9 0.9 pad_maximum_fusion.6
  79.8 5.0 %all-to-all-start = ((bf16[8,2,2,64,1024]{4,3,2,1,0:T(8,128)(2,1)}), bf16[8,2,2,64,1024]{4,3,2,1,0:T(8,128)(2,1)}, u32[]{:S(2)}, u32[]{:S(2)}) async-start(bf16[8,2,2,64,1024]{4,3,2,1,0:T(8,128)(2,1)} %bitcast.295), calls=%async_computation | async-start | bytes 8388608 | tf_op jit(solution)/shard_map/all_to_all | solution.py:294
  85.1 1.3 compare_and_fusion.1
  86.5 1.3 compare_and_fusion
  88.3 1.0 slice.224
  89.3 1.0 slice.225
  90.3 1.2 maximum_bitcast_fusion
  91.5 1.4 maximum_bitcast_fusion.1
  93.1 1.1 pad_maximum_fusion
  94.2 1.5 fusion.131
  95.7 1.0 copy.117
  96.7 2.7 %copy.118 = bf16[224,8,8,128]{3,2,1,0:T(8,128)(2,1)} copy(bf16[224,8,8,128]{3,1,2,0:T(8,128)(2,1)S(1)} %bitcast.302) | data formatting | bytes 7340032
  99.4 1.8 fusion
  101.3 1.6 fusion.5
  102.9 0.4 copy-done
  103.7 28.8 %all-to-all-done = bf16[8,2,2,64,1024]{4,3,2,1,0:T(8,128)(2,1)} async-done(((bf16[8,2,2,64,1024]{4,3,2,1,0:T(8,128)(2,1)}), bf16[8,2,2,64,1024]{4,3,2,1,0:T(8,128)(2,1)}, u32[]{:S(2)}, u32[]{:S(2)}) %all-to-all-start) | async-done | bytes 4194336 | tf_op jit(solution)/shard_map/all_to_all | solution.py:294
  132.5 2.8 %gather_fusion.4 = bf16[12,64,1024]{2,1,0:T(8,128)(2,1)S(1)} fusion(bf16[8,2,2,64,1024]{4,3,2,1,0:T(8,128)(2,1)} %all-to-all-done, s32[12]{0:T(128)S(1)} %bitcast.357), kind=kCustom, calls=%fused_computation.4 | custom fusion | bytes 3145872 | tf_op jit(solution)/shard_map/gather | solution.py:297
  135.3 0.4 copy.119
  135.8 1.2 multiply_reduce_fusion
  137.0 4.0 %gather_fusion.5 = bf16[12,64,1024]{2,1,0:T(8,128)(2,1)} fusion(bf16[8,2,2,64,1024]{4,3,2,1,0:T(8,128)(2,1)} %all-to-all-done, s32[12]{0:T(128)S(1)} %get-tuple-element.18), kind=kCustom, calls=%fused_computation.5 | custom fusion | bytes 3145872 | tf_op jit(solution)/shard_map/gather | solution.py:298
  141.0 2.0 copy.120
  143.1 0.7 fusion.12
  143.9 4.0 %fusion.32 = f32[4,64,8,128]{3,1,2,0:T(8,128)S(1)} fusion(bf16[4,448,8,128]{3,2,1,0:T(8,128)(2,1)} %bitcast.316, f32[4,8,64,448]{3,2,1,0:T(8,128)S(1)} %copy-done.1, f32[4,8,64]{2,1,0:T(8,128)S(1)} %get-tuple-element.85, pred[4,8,448]{2,1,0:T(8,128)(4,1)S(1)} %broadcast_in_dim.179, f32[4,64,8]{1,2,0:T(8,128)S(1)} %get-tuple-element.17), kind=kOutput, calls=%fused_computation.34 | convolution fusion | flops 238813184 | bytes 8419328 | tf_op jit(solution)/shard_map/bhqs,bshd->bqhd/dot_general | solution.py:165
  147.8 1.4 fusion.42
  149.7 2.5 %convolution_convert_fusion = bf16[256,4096]{1,0:T(8,128)(2,1)S(1)} fusion(bf16[1024,4096]{1,0:T(8,128)(2,1)S(1)} %bitcast.366, bf16[256,1024]{1,0:T(8,128)(2,1)S(1)} %bitcast.342, bf16[256,1024]{1,0:T(8,128)(2,1)S(1)} %bitcast.343, bf16[32,8,8,128]{3,2,1,0:T(8,128)(2,1)S(1)} %bitcast.347, pred[256]{0:T(512)(128)(4,1)S(1)} %broadcast_in_dim.173, ...), kind=kOutput, calls=%fused_computation.7 | convolution fusion | flops 2149056512 | bytes 12059136 | tf_op jit(solution)/shard_map/dot_general | solution.py:140
  152.4 53.1 %all_to_all.10 = bf16[4,1024,256]{1,2,0:T(8,128)(2,1)S(1)} all-to-all(bf16[4,1024,256]{1,2,0:T(8,128)(2,1)S(1)} %bitcast.307), channel_id=1, replica_groups=mesh['seq'=8,'head'=4] {'head'}, dimensions={0} | all-to-all | bytes 4194304 | tf_op jit(solution)/shard_map/all_to_all | solution.py:147
  205.5 1.3 reduce_sum.71
  (139 shorter events, 9.5 us)
Async XLA Ops:
  0.0 2.8 %copy-start.6 = (bf16[256,1024]{1,0:T(8,128)(2,1)S(1)}, bf16[256,1024]{1,0:T(8,128)(2,1)}, u32[]{:S(2)}) copy-start(bf16[256,1024]{1,0:T(8,128)(2,1)} %param.9) | copy-start | bytes 1572868
  2.8 0.7 copy-start.9
  4.9 1.0 copy-start.7
  5.9 2.1 %copy-start.2 = (bf16[256,1024]{1,0:T(8,128)(2,1)S(1)}, bf16[256,1024]{1,0:T(8,128)(2,1)}, u32[]{:S(2)}) copy-start(bf16[256,1024]{1,0:T(8,128)(2,1)} %param.11) | copy-start | bytes 1572868
  8.6 0.7 copy-start.8
  9.1 1.8 collective-permute-start
  10.9 7.0 %collective-permute-start.1 = (bf16[96,1024]{1,0:T(8,128)(2,1)S(1)}, bf16[96,1024]{1,0:T(8,128)(2,1)S(1)}, u32[]{:S(2)}, u32[]{:S(2)}) collective-permute-start(bf16[96,1024]{1,0:T(8,128)(2,1)S(1)} %dynamic-slice_bitcast_fusion.3), channel_id=1, source_target_pairs={{0,8},{4,12},{8,0},{12,4},{16,24},{20,28},{24,16},{28,20},{1,9},{5... | collective-permute-start | bytes 589832 | tf_op jit(solution)/shard_map/ppermute | solution.py:100
  18.0 4.7 %collective-permute-start.2 = (bf16[48,1024]{1,0:T(8,128)(2,1)S(1)}, bf16[48,1024]{1,0:T(8,128)(2,1)S(1)}, u32[]{:S(2)}, u32[]{:S(2)}) collective-permute-start(bf16[48,1024]{1,0:T(8,128)(2,1)S(1)} %dynamic-slice_bitcast_fusion.6), channel_id=1, source_target_pairs={{0,16},{4,20},{8,24},{12,28},{16,0},{20,4},{24,8},{28,12},{1,17},{... | collective-permute-start | bytes 294920 | tf_op jit(solution)/shard_map/ppermute | solution.py:100
  22.7 4.7 %collective-permute-start.3 = (bf16[48,1024]{1,0:T(8,128)(2,1)S(1)}, bf16[48,1024]{1,0:T(8,128)(2,1)S(1)}, u32[]{:S(2)}, u32[]{:S(2)}) collective-permute-start(bf16[48,1024]{1,0:T(8,128)(2,1)S(1)} %bitcast_add_fusion.2), channel_id=1, source_target_pairs={{0,16},{4,20},{8,24},{12,28},{16,0},{20,4},{24,8},{28,12},{1,17},{... | collective-permute-start | bytes 294920 | tf_op jit(solution)/shard_map/ppermute | solution.py:104
  27.5 5.7 %collective-permute-start.4 = (bf16[96,1024]{1,0:T(8,128)(2,1)S(1)}, bf16[96,1024]{1,0:T(8,128)(2,1)S(1)}, u32[]{:S(2)}, u32[]{:S(2)}) collective-permute-start(bf16[96,1024]{1,0:T(8,128)(2,1)S(1)} %get-tuple-element.65), channel_id=1, source_target_pairs={{0,8},{4,12},{8,0},{12,4},{16,24},{20,28},{24,16},{28,20},{1,9},{5... | collective-permute-start | bytes 589832 | tf_op jit(solution)/shard_map/ppermute | solution.py:104
  33.5 1.8 collective-permute-start.5
  35.6 6.9 %copy-start.3 = (bf16[384,1024]{1,0:T(8,128)(2,1)}, bf16[384,1024]{1,0:T(8,128)(2,1)S(1)}, u32[]{:S(2)}) copy-start(bf16[384,1024]{1,0:T(8,128)(2,1)S(1)} %pad_maximum_fusion.5) | copy-start | bytes 2359300
  36.8 10.8 %collective-permute-start.6 = (bf16[2,128,1024]{2,1,0:T(8,128)(2,1)}, bf16[2,128,1024]{2,1,0:T(8,128)(2,1)}, u32[]{:S(2)}, u32[]{:S(2)}) collective-permute-start(bf16[2,128,1024]{2,1,0:T(8,128)(2,1)} %get-tuple-element.40), channel_id=1, source_target_pairs={{0,4},{4,8},{8,12},{12,16},{16,20},{20,24},{24,28},{1,5},{5,9},{9,... | collective-permute-start | bytes 1572872 | tf_op jit(solution)/shard_map/ppermute | solution.py:233
  38.8 13.4 %collective-permute-start.7 = (bf16[2,128,1024]{2,1,0:T(8,128)(2,1)}, bf16[2,128,1024]{2,1,0:T(8,128)(2,1)}, u32[]{:S(2)}, u32[]{:S(2)}) collective-permute-start(bf16[2,128,1024]{2,1,0:T(8,128)(2,1)} %get-tuple-element.39), channel_id=1, source_target_pairs={{4,0},{8,4},{12,8},{16,12},{20,16},{24,20},{28,24},{5,1},{9,5},{13... | collective-permute-start | bytes 1572872 | tf_op jit(solution)/shard_map/ppermute | solution.py:236
  44.1 10.0 %copy-start.10 = (s32[8]{0:T(128)S(1)}, s32[8]{0:T(128)}, u32[]{:S(2)}) copy-start(s32[8]{0:T(128)} %param.15) | copy-start | bytes 100
  52.2 3.0 %collective-permute-start.8 = (f32[64,1152]{1,0:T(8,128)S(1)}, f32[64,1152]{1,0:T(8,128)S(1)}, u32[]{:S(2)}, u32[]{:S(2)}) collective-permute-start(f32[64,1152]{1,0:T(8,128)S(1)} %get-tuple-element.52), channel_id=1, source_target_pairs={{0,4},{4,0},{8,12},{12,8},{16,20},{20,16},{24,28},{28,24},{1,5},{5... | collective-permute-start | bytes 884744 | tf_op jit(solution)/shard_map/ppermute | solution.py:100
  55.9 6.2 %collective-permute-start.9 = (f32[32,1152]{1,0:T(8,128)S(1)}, f32[32,1152]{1,0:T(8,128)S(1)}, u32[]{:S(2)}, u32[]{:S(2)}) collective-permute-start(f32[32,1152]{1,0:T(8,128)S(1)} %get-tuple-element.62), channel_id=1, source_target_pairs={{0,8},{4,12},{8,0},{12,4},{16,24},{20,28},{24,16},{28,20},{1,9},{5... | collective-permute-start | bytes 442376 | tf_op jit(solution)/shard_map/ppermute | solution.py:100
  62.6 4.4 %collective-permute-start.10 = (f32[16,1152]{1,0:T(8,128)S(1)}, f32[16,1152]{1,0:T(8,128)S(1)}, u32[]{:S(2)}, u32[]{:S(2)}) collective-permute-start(f32[16,1152]{1,0:T(8,128)S(1)} %get-tuple-element.74), channel_id=1, source_target_pairs={{0,16},{4,20},{8,24},{12,28},{16,0},{20,4},{24,8},{28,12},{1,17},{... | collective-permute-start | bytes 221192 | tf_op jit(solution)/shard_map/ppermute | solution.py:100
  67.4 4.4 %collective-permute-start.11 = (f32[16,1152]{1,0:T(8,128)S(1)}, f32[16,1152]{1,0:T(8,128)S(1)}, u32[]{:S(2)}, u32[]{:S(2)}) collective-permute-start(f32[16,1152]{1,0:T(8,128)S(1)} %concatenate.87), channel_id=1, source_target_pairs={{0,16},{4,20},{8,24},{12,28},{16,0},{20,4},{24,8},{28,12},{1,17},{... | collective-permute-start | bytes 221192 | tf_op jit(solution)/shard_map/ppermute | solution.py:104
  71.8 5.2 %collective-permute-start.12 = (f32[32,1152]{1,0:T(8,128)S(1)}, f32[32,1152]{1,0:T(8,128)S(1)}, u32[]{:S(2)}, u32[]{:S(2)}) collective-permute-start(f32[32,1152]{1,0:T(8,128)S(1)} %get-tuple-element.69), channel_id=1, source_target_pairs={{0,8},{4,12},{8,0},{12,4},{16,24},{20,28},{24,16},{28,20},{1,9},{5... | collective-permute-start | bytes 442376 | tf_op jit(solution)/shard_map/ppermute | solution.py:104
  77.1 1.6 collective-permute-start.13
  79.8 52.7 %all-to-all-start = ((bf16[8,2,2,64,1024]{4,3,2,1,0:T(8,128)(2,1)}), bf16[8,2,2,64,1024]{4,3,2,1,0:T(8,128)(2,1)}, u32[]{:S(2)}, u32[]{:S(2)}) async-start(bf16[8,2,2,64,1024]{4,3,2,1,0:T(8,128)(2,1)} %bitcast.295), calls=%async_computation | async-start | bytes 8388608 | tf_op jit(solution)/shard_map/all_to_all | solution.py:294
  84.7 3.5 %copy-start.4 = (bf16[384,1024]{1,0:T(8,128)(2,1)S(1)}, bf16[384,1024]{1,0:T(8,128)(2,1)}, u32[]{:S(2)}) copy-start(bf16[384,1024]{1,0:T(8,128)(2,1)} %copy-done.3) | copy-start | bytes 2359300
  101.3 2.0 copy-start
  101.3 2.0 slice-start
  101.3 2.2 %copy-start.5 = (f32[128,1152]{1,0:T(8,128)S(1)}, f32[128,1152]{1,0:T(8,128)}, u32[]{:S(2)}) copy-start(f32[128,1152]{1,0:T(8,128)} %pad_maximum_fusion.6) | copy-start | bytes 1769476
  141.0 2.8 %copy-start.1 = (f32[4,8,64,448]{3,2,1,0:T(8,128)S(1)}, f32[4,8,64,448]{3,2,1,0:T(8,128)}, u32[]{:S(2)}) copy-start(f32[4,8,64,448]{3,2,1,0:T(8,128)} %copy-done) | copy-start | bytes 11010052
  143.0 6.7 %slice-start.1 = ((s8[8388608]{0:T(1024)(128)(4,1)}), s8[4194304]{0:T(1024)(128)(4,1)S(1)}, s32[]{:S(2)}) async-start(s8[8388608]{0:T(1024)(128)(4,1)} %bitcast.365), calls=%async_computation.3 | async-start | bytes 8388608
  143.8 5.9 %slice-start.2 = ((s8[8388608]{0:T(1024)(128)(4,1)}), s8[4194304]{0:T(1024)(128)(4,1)S(1)}, s32[]{:S(2)}) async-start(s8[8388608]{0:T(1024)(128)(4,1)} %bitcast.365), calls=%async_computation.4 | async-start | bytes 8388608

commit v13 on v12

--- a/solution.py
+++ b/solution.py
@@ -288,14 +288,17 @@
         ranks[:, None, :] == jnp.arange(capacity)[None, :, None]
     )
     send_local = jnp.sum(jnp.where(wanted, local_ids[:, None, :], 0), axis=2)
-    kv_blocks = jnp.stack([key_rot.reshape(blocks_here, BLOCK, width_here), value_view], axis=1)
-    outgoing = kv_blocks[send_local]
-    outgoing, reduced = lax.optimization_barrier((outgoing, reduced))
-    incoming = lax.all_to_all(outgoing, "seq", split_axis=0, concat_axis=0, tiled=True)
+    key_blocks = key_rot.reshape(blocks_here, BLOCK, width_here)
+    out_k = key_blocks[send_local]
+    out_v = value_view[send_local]
+    out_k, out_v, reduced = lax.optimization_barrier((out_k, out_v, reduced))
+    in_k = lax.all_to_all(out_k, "seq", split_axis=0, concat_axis=0, tiled=True)
+    out_v, in_k = lax.optimization_barrier((out_v, in_k))
+    in_v = lax.all_to_all(out_v, "seq", split_axis=0, concat_axis=0, tiled=True)
     my_owners = owners[seq_place]
     my_ranks = ranks[seq_place]
-    random_k = incoming[my_owners, my_ranks, 0].reshape(blocks_here, RAND, BLOCK, width_here)
-    random_v = incoming[my_owners, my_ranks, 1].reshape(blocks_here, RAND, BLOCK, width_here)
+    random_k = in_k[my_owners, my_ranks].reshape(blocks_here, RAND, BLOCK, width_here)
+    random_v = in_v[my_owners, my_ranks].reshape(blocks_here, RAND, BLOCK, width_here)
     random_kv = (random_k, random_v)
     near_part = partial_attend(query_view, near_kv[0], near_kv[1], near_valid)
     far_part = partial_attend(

time: 207 us -> 219 us (1.058)
  waiting for transfers between devices: 74.2 us -> 61.5 us
  local copies, waits for them, and re-layouts: 29.6 us -> 37.6 us
  other arithmetic: 18.5 us -> 26 us
  starting transfers between devices: 17.5 us -> 23.2 us
  matrix products: 11.6 us -> 14.4 us
    all_to_all x1 -> x2, starting transfers between devices: 4.98 us -> 10.8 us  [the longest x1 5.76 us: on_device(): in_v = lax.all_to_all(out_v, 'seq', split_axis=0, concat_axis=0, tiled=True)]
    ppermute x6, waiting for transfers between devices: 15.8 us -> 10.8 us  [tree_reduce(): got = lax.ppermute(parts, axis, xor_perm(count, bit))]
    unnamed x37 -> x47, local copies, waits for them, and re-layouts: 8.19 us -> 12.9 us
    dot_general x1, matrix products: 2.47 us -> 5.82 us  [head_partials(): lax.dot_general(out_weight, rows, (((0,), (1,)), ((), ())), preferred_ele...]
    ppermute x1, waiting for transfers between devices: 2.9 us -> 0.01 us  [on_device(): lax.ppermute(halo_kv[:, tok_here - halo:], 'seq', [(i, (i + 1) % seq_coun...]
    ppermute x6, waiting for transfers between devices: 22.1 us -> 19.8 us  [tree_reduce(): got = lax.ppermute(send, axis, xor_perm(count, bit))]
    all_to_all x1 -> x2, waiting for transfers between devices: 28.8 us -> 27.5 us  [the longest x1 16.1 us: on_device(): in_v = lax.all_to_all(out_v, 'seq', split_axis=0, concat_axis=0, tiled=True)]
    gather x3 -> x4, local copies, waits for them, and re-layouts: 9.67 us -> 9.38 us  [the longest x1 3.46 us: on_device(): in_v[my_owners, my_ranks].reshape(blocks_here, RAND, BLOCK, width_here)]
  transfers between devices with their start and end apart: 15 -> 16, of which waited for: 15 -> 12; matrix products, arithmetic and copies ran while one was open for 13% -> 22% of each run, Pallas kernels for 0% -> 0%
where the time goes in v13:
time: 219 us; the launch traced here: 218 us
  waiting for transfers between devices  61.5 us (28%)
  blocking collectives  53.1 us (24%)
  local copies, waits for them, and re-layouts  37.6 us (17%)
  other arithmetic  26 us (12%)
  starting transfers between devices  23.2 us (11%)
  matrix products  14.4 us (7%)
  between operations  2.29 us (1%)
    all_to_all x1, blocking collectives, sum_over_head(): gathered = lax.all_to_all(partial, 'head', 0, 0, tiled=True)  53.1 us
    ppermute x6, waiting for transfers between devices, tree_reduce(): got = lax.ppermute(send, axis, xor_perm(count, bit))  19.8 us
    all_to_all x1, waiting for transfers between devices, on_device(): in_v = lax.all_to_all(out_v, 'seq', split_axis=0, concat_axis=0, tiled=True)  16.1 us
    unnamed x47, local copies, waits for them, and re-layouts  12.9 us
    all_to_all x1, waiting for transfers between devices, on_device(): in_k = lax.all_to_all(out_k, 'seq', split_axis=0, concat_axis=0, tiled=True)  11.4 us
    ppermute x6, waiting for transfers between devices, tree_reduce(): got = lax.ppermute(parts, axis, xor_perm(count, bit))  10.8 us
    dot_general x1, matrix products, head_partials(): lax.dot_general(out_weight, rows, (((0,), (1,)), ((), ())), preferred_ele...  5.82 us
    all_to_all x1, starting transfers between devices, on_device(): in_v = lax.all_to_all(out_v, 'seq', split_axis=0, concat_axis=0, tiled=True)  5.76 us
  transfers between devices with their start and end apart: 16, of which 12 were waited for; matrix products, arithmetic and copies ran while one was open for 22% of the time, Pallas kernels for 0%

profile of v13, /device:TPU:2, one launch (start us, length us, event | category | flops | bytes accessed | tf_op | source)
XLA Modules:
  0.0 218.0 jit_solution(2156353183962587407)
XLA Ops:
  1.4 1.1 convert_bitcast_fusion.1
  4.7 0.7 slice_negate_fusion
  5.4 0.6 maximum_multiply_fusion.1
  6.4 1.0 fusion.48
  10.7 0.7 collective-permute-done
  12.1 6.3 %collective-permute-done.1 = bf16[96,1024]{1,0:T(8,128)(2,1)S(1)} collective-permute-done((bf16[96,1024]{1,0:T(8,128)(2,1)S(1)}, bf16[96,1024]{1,0:T(8,128)(2,1)S(1)}, u32[]{:S(2)}, u32[]{:S(2)}) %collective-permute-start.1) | collective-permute-done | bytes 196640 | tf_op jit(solution)/shard_map/ppermute | solution.py:100
  18.5 1.6 collective-permute-start.2
  20.1 3.1 %collective-permute-done.2 = bf16[48,1024]{1,0:T(8,128)(2,1)S(1)} collective-permute-done((bf16[48,1024]{1,0:T(8,128)(2,1)S(1)}, bf16[48,1024]{1,0:T(8,128)(2,1)S(1)}, u32[]{:S(2)}, u32[]{:S(2)}) %collective-permute-start.2) | collective-permute-done | bytes 98336 | tf_op jit(solution)/shard_map/ppermute | solution.py:100
  23.2 1.6 collective-permute-start.3
  24.8 0.6 fusion.110
  25.6 2.3 %collective-permute-done.3 = bf16[48,1024]{1,0:T(8,128)(2,1)S(1)} collective-permute-done((bf16[48,1024]{1,0:T(8,128)(2,1)S(1)}, bf16[48,1024]{1,0:T(8,128)(2,1)S(1)}, u32[]{:S(2)}, u32[]{:S(2)}) %collective-permute-start.3) | collective-permute-done | bytes 98336 | tf_op jit(solution)/shard_map/ppermute | solution.py:104
  28.4 5.4 %collective-permute-done.4 = bf16[96,1024]{1,0:T(8,128)(2,1)S(1)} collective-permute-done((bf16[96,1024]{1,0:T(8,128)(2,1)S(1)}, bf16[96,1024]{1,0:T(8,128)(2,1)S(1)}, u32[]{:S(2)}, u32[]{:S(2)}) %collective-permute-start.4) | collective-permute-done | bytes 196640 | tf_op jit(solution)/shard_map/ppermute | solution.py:104
  34.1 0.9 copy.107
  35.1 0.7 broadcast_compare_fusion
  36.1 1.0 fusion.132
  37.2 2.3 %collective-permute-start.6 = (bf16[2,128,1024]{2,1,0:T(8,128)(2,1)}, bf16[2,128,1024]{2,1,0:T(8,128)(2,1)}, u32[]{:S(2)}, u32[]{:S(2)}) collective-permute-start(bf16[2,128,1024]{2,1,0:T(8,128)(2,1)} %get-tuple-element.44), channel_id=1, source_target_pairs={{0,4},{4,8},{8,12},{12,16},{16,20},{20,24},{24,28},{1,5},{5,9},{9,... | collective-permute-start | bytes 1572872 | tf_op jit(solution)/shard_map/ppermute | solution.py:233
  39.5 3.2 %collective-permute-start.7 = (bf16[2,128,1024]{2,1,0:T(8,128)(2,1)}, bf16[2,128,1024]{2,1,0:T(8,128)(2,1)}, u32[]{:S(2)}, u32[]{:S(2)}) collective-permute-start(bf16[2,128,1024]{2,1,0:T(8,128)(2,1)} %get-tuple-element.43), channel_id=1, source_target_pairs={{4,0},{8,4},{12,8},{16,12},{20,16},{24,20},{28,24},{5,1},{9,5},{13... | collective-permute-start | bytes 1572872 | tf_op jit(solution)/shard_map/ppermute | solution.py:236
  43.5 1.1 fusion.53
  44.6 0.8 copy.98
  45.4 1.4 convolution_bitcast_fusion
  47.2 0.9 copy.180
  48.1 1.2 concatenate.76
  49.2 3.4 %collective-permute-done.7 = bf16[2,128,1024]{2,1,0:T(8,128)(2,1)} collective-permute-done((bf16[2,128,1024]{2,1,0:T(8,128)(2,1)}, bf16[2,128,1024]{2,1,0:T(8,128)(2,1)}, u32[]{:S(2)}, u32[]{:S(2)}) %collective-permute-start.7) | collective-permute-done | bytes 524320 | tf_op jit(solution)/shard_map/ppermute | solution.py:236
  52.7 1.8 collective-permute-start.8
  54.5 0.6 fusion.134
  56.3 0.6 collective-permute-start.9
  57.7 4.8 %collective-permute-done.9 = f32[32,1152]{1,0:T(8,128)S(1)} collective-permute-done((f32[32,1152]{1,0:T(8,128)S(1)}, f32[32,1152]{1,0:T(8,128)S(1)}, u32[]{:S(2)}, u32[]{:S(2)}) %collective-permute-start.9) | collective-permute-done | bytes 147488 | tf_op jit(solution)/shard_map/ppermute | solution.py:100
  63.1 4.3 %collective-permute-done.10 = f32[16,1152]{1,0:T(8,128)S(1)} collective-permute-done((f32[16,1152]{1,0:T(8,128)S(1)}, f32[16,1152]{1,0:T(8,128)S(1)}, u32[]{:S(2)}, u32[]{:S(2)}) %collective-permute-start.10) | collective-permute-done | bytes 73760 | tf_op jit(solution)/shard_map/ppermute | solution.py:100
  67.8 1.3 compare_and_fusion.1
  69.1 3.0 %collective-permute-done.11 = f32[16,1152]{1,0:T(8,128)S(1)} collective-permute-done((f32[16,1152]{1,0:T(8,128)S(1)}, f32[16,1152]{1,0:T(8,128)S(1)}, u32[]{:S(2)}, u32[]{:S(2)}) %collective-permute-start.11) | collective-permute-done | bytes 73760 | tf_op jit(solution)/shard_map/ppermute | solution.py:104
  72.2 0.7 pad_maximum_fusion.9
  73.4 1.2 compare_and_fusion
  74.6 2.0 gather_fusion
  76.6 2.0 gather_fusion.1
  78.7 0.9 copy.116
  80.2 0.8 slice.181
  81.0 1.0 fusion.87
  82.1 1.2 maximum_bitcast_fusion
  83.3 1.0 slice.224
  84.3 1.0 slice.225
  85.2 3.1 %maximum_bitcast_fusion.1 = (bf16[2,1,5,64,1024]{4,3,2,1,0:T(8,128)(2,1)}, bf16[2,1,5,64,1024]{4,3,2,1,0:T(8,128)(2,1)}, bf16[2,1,5,64,1024]{4,3,2,1,0:T(8,128)(2,1)}) fusion(bf16[1,4,64,1024]{3,2,1,0:T(8,128)(2,1)S(1)} %bitcast.297, bf16[1,4,64,1024]{3,2,1,0:T(8,128)(2,1)S(1)} %bitcast.291, bf16[2,1,64,1024]{3,2,1,0:T(8,128)(2,1)S(1)} %slice.224, ...), kind=kLoop, calls=%fused_computation.44 | loop fusion | flops 3932160 | bytes 6029312 | tf_op jit(solution)/shard_map/stack | solution.py:246
  88.5 0.9 pad_maximum_fusion.5
  89.3 5.0 %all-to-all-start = ((bf16[8,2,64,1024]{3,2,1,0:T(8,128)(2,1)}), bf16[8,2,64,1024]{3,2,1,0:T(8,128)(2,1)S(1)}, u32[]{:S(2)}, u32[]{:S(2)}) async-start(bf16[8,2,64,1024]{3,2,1,0:T(8,128)(2,1)} %bitcast.6), calls=%async_computation | async-start | bytes 4194304 | tf_op jit(solution)/shard_map/all_to_all | solution.py:295
  94.3 1.4 broadcast_in_dim.178
  96.2 2.8 %pad_maximum_fusion = bf16[2,4,7,64,1024]{4,3,2,1,0:T(8,128)(2,1)S(1)} fusion(bf16[2,4,2,64,1024]{4,3,2,1,0:T(8,128)(2,1)S(1)} %broadcast_in_dim.178, bf16[2,1,5,64,1024]{4,3,2,1,0:T(8,128)(2,1)S(1)} %copy-done.4, bf16[2,1,5,64,1024]{4,3,2,1,0:T(8,128)(2,1)} %get-tuple-element.42, bf16[2,1,5,64,1024]{4,3,2,1,0:T(8,128)(2,1)S(1)} %copy-done.3, ...), kind=kLoop, calls=%fused_computation.7 | loop fusion | flops 14680064 | bytes 14680064 | tf_op jit(solution)/shard_map/concatenate | solution.py:246
  99.0 1.5 fusion.131
  100.5 1.0 copy.117
  101.5 2.8 %copy.118 = bf16[224,8,8,128]{3,2,1,0:T(8,128)(2,1)} copy(bf16[224,8,8,128]{3,1,2,0:T(8,128)(2,1)S(1)} %bitcast.301) | data formatting | bytes 7340032
  104.3 1.9 fusion
  106.1 1.5 fusion.5
  108.1 11.4 %all-to-all-done = bf16[8,2,64,1024]{3,2,1,0:T(8,128)(2,1)S(1)} async-done(((bf16[8,2,64,1024]{3,2,1,0:T(8,128)(2,1)}), bf16[8,2,64,1024]{3,2,1,0:T(8,128)(2,1)S(1)}, u32[]{:S(2)}, u32[]{:S(2)}) %all-to-all-start) | async-done | bytes 2097184 | tf_op jit(solution)/shard_map/all_to_all | solution.py:295
  119.5 5.8 %all-to-all-start.1 = ((bf16[8,2,64,1024]{3,2,1,0:T(8,128)(2,1)}), bf16[8,2,64,1024]{3,2,1,0:T(8,128)(2,1)}, u32[]{:S(2)}, u32[]{:S(2)}) async-start(bf16[8,2,64,1024]{3,2,1,0:T(8,128)(2,1)} %bitcast.8), calls=%async_computation.1 | async-start | bytes 4194304 | tf_op jit(solution)/shard_map/all_to_all | solution.py:297
  125.6 1.9 gather_fusion.5
  127.5 2.0 copy.119
  129.5 1.2 multiply_reduce_fusion
  130.7 0.7 fusion.12
  131.8 2.6 %fusion.32 = f32[4,64,8,128]{3,1,2,0:T(8,128)} fusion(bf16[4,448,8,128]{3,2,1,0:T(8,128)(2,1)S(1)} %bitcast.315, f32[4,8,64,448]{3,2,1,0:T(8,128)S(1)} %copy-done.2, f32[4,8,64]{2,1,0:T(8,128)S(1)} %get-tuple-element.89, pred[4,8,448]{2,1,0:T(8,128)(4,1)S(1)} %broadcast_in_dim.180, f32[4,64,8]{1,2,0:T(8,128)S(1)} %get-tuple-element.23), kind=kOutput, calls=%fused_computation.35 | convolution fusion | flops 238813184 | bytes 8419328 | tf_op jit(solution)/shard_map/bhqs,bshd->bqhd/dot_general | solution.py:165
  134.4 16.1 %all-to-all-done.1 = bf16[8,2,64,1024]{3,2,1,0:T(8,128)(2,1)} async-done(((bf16[8,2,64,1024]{3,2,1,0:T(8,128)(2,1)}), bf16[8,2,64,1024]{3,2,1,0:T(8,128)(2,1)}, u32[]{:S(2)}, u32[]{:S(2)}) %all-to-all-start.1) | async-done | bytes 2097184 | tf_op jit(solution)/shard_map/all_to_all | solution.py:297
  150.5 3.5 %gather_fusion.6 = bf16[12,64,1024]{2,1,0:T(8,128)(2,1)} fusion(bf16[8,2,64,1024]{3,2,1,0:T(8,128)(2,1)} %all-to-all-done.1, s32[12]{0:T(128)S(1)} %fusion.119), kind=kCustom, calls=%fused_computation.6 | custom fusion | bytes 3145824 | tf_op jit(solution)/shard_map/gather | solution.py:301
  154.0 1.9 copy.120
  155.9 1.2 fusion.42
  157.6 5.8 %convolution_convert_fusion = bf16[256,4096]{1,0:T(8,128)(2,1)S(1)} fusion(bf16[1024,4096]{1,0:T(8,128)(2,1)} %param.12, bf16[256,1024]{1,0:T(8,128)(2,1)S(1)} %bitcast.341, bf16[256,1024]{1,0:T(8,128)(2,1)S(1)} %bitcast.342, bf16[32,8,8,128]{3,2,1,0:T(8,128)(2,1)S(1)} %bitcast.346, pred[256]{0:T(512)(128)(4,1)S(1)} %broadcast_in_dim.174, ...), kind=kOutput, calls=%fused_computation.8 | convolution fusion | flops 2149056512 | bytes 12059136 | tf_op jit(solution)/shard_map/dot_general | solution.py:140
  163.6 53.1 %all_to_all.15 = bf16[4,1024,256]{1,2,0:T(8,128)(2,1)S(1)} all-to-all(bf16[4,1024,256]{1,2,0:T(8,128)(2,1)S(1)} %bitcast.306), channel_id=1, replica_groups=mesh['seq'=8,'head'=4] {'head'}, dimensions={0} | all-to-all | bytes 4194304 | tf_op jit(solution)/shard_map/all_to_all | solution.py:147
  216.7 1.3 reduce_sum.71
  (150 shorter events, 15.5 us)
Async XLA Ops:
  0.0 2.8 %copy-start.8 = (bf16[256,1024]{1,0:T(8,128)(2,1)S(1)}, bf16[256,1024]{1,0:T(8,128)(2,1)}, u32[]{:S(2)}) copy-start(bf16[256,1024]{1,0:T(8,128)(2,1)} %param.9) | copy-start | bytes 1572868
  2.8 0.7 copy-start.14
  5.4 1.0 copy-start.9
  6.4 2.1 copy-start
  9.1 0.7 copy-start.13
  9.6 1.8 collective-permute-start
  11.4 7.0 %collective-permute-start.1 = (bf16[96,1024]{1,0:T(8,128)(2,1)S(1)}, bf16[96,1024]{1,0:T(8,128)(2,1)S(1)}, u32[]{:S(2)}, u32[]{:S(2)}) collective-permute-start(bf16[96,1024]{1,0:T(8,128)(2,1)S(1)} %dynamic-slice_bitcast_fusion.3), channel_id=1, source_target_pairs={{0,8},{4,12},{8,0},{12,4},{16,24},{20,28},{24,16},{28,20},{1,9},{5... | collective-permute-start | bytes 589832 | tf_op jit(solution)/shard_map/ppermute | solution.py:100
  18.5 4.7 %collective-permute-start.2 = (bf16[48,1024]{1,0:T(8,128)(2,1)S(1)}, bf16[48,1024]{1,0:T(8,128)(2,1)S(1)}, u32[]{:S(2)}, u32[]{:S(2)}) collective-permute-start(bf16[48,1024]{1,0:T(8,128)(2,1)S(1)} %dynamic-slice_bitcast_fusion.6), channel_id=1, source_target_pairs={{0,16},{4,20},{8,24},{12,28},{16,0},{20,4},{24,8},{28,12},{1,17},{... | collective-permute-start | bytes 294920 | tf_op jit(solution)/shard_map/ppermute | solution.py:100
  23.2 4.7 %collective-permute-start.3 = (bf16[48,1024]{1,0:T(8,128)(2,1)S(1)}, bf16[48,1024]{1,0:T(8,128)(2,1)S(1)}, u32[]{:S(2)}, u32[]{:S(2)}) collective-permute-start(bf16[48,1024]{1,0:T(8,128)(2,1)S(1)} %bitcast_add_fusion.2), channel_id=1, source_target_pairs={{0,16},{4,20},{8,24},{12,28},{16,0},{20,4},{24,8},{28,12},{1,17},{... | collective-permute-start | bytes 294920 | tf_op jit(solution)/shard_map/ppermute | solution.py:104
  28.0 5.7 %collective-permute-start.4 = (bf16[96,1024]{1,0:T(8,128)(2,1)S(1)}, bf16[96,1024]{1,0:T(8,128)(2,1)S(1)}, u32[]{:S(2)}, u32[]{:S(2)}) collective-permute-start(bf16[96,1024]{1,0:T(8,128)(2,1)S(1)} %get-tuple-element.69), channel_id=1, source_target_pairs={{0,8},{4,12},{8,0},{12,4},{16,24},{20,28},{24,16},{28,20},{1,9},{5... | collective-permute-start | bytes 589832 | tf_op jit(solution)/shard_map/ppermute | solution.py:104
  33.9 1.2 copy-start.15
  34.0 1.8 collective-permute-start.5
  37.2 12.0 %collective-permute-start.6 = (bf16[2,128,1024]{2,1,0:T(8,128)(2,1)}, bf16[2,128,1024]{2,1,0:T(8,128)(2,1)}, u32[]{:S(2)}, u32[]{:S(2)}) collective-permute-start(bf16[2,128,1024]{2,1,0:T(8,128)(2,1)} %get-tuple-element.44), channel_id=1, source_target_pairs={{0,4},{4,8},{8,12},{12,16},{16,20},{20,24},{24,28},{1,5},{5,9},{9,... | collective-permute-start | bytes 1572872 | tf_op jit(solution)/shard_map/ppermute | solution.py:233
  39.5 13.1 %collective-permute-start.7 = (bf16[2,128,1024]{2,1,0:T(8,128)(2,1)}, bf16[2,128,1024]{2,1,0:T(8,128)(2,1)}, u32[]{:S(2)}, u32[]{:S(2)}) collective-permute-start(bf16[2,128,1024]{2,1,0:T(8,128)(2,1)} %get-tuple-element.43), channel_id=1, source_target_pairs={{4,0},{8,4},{12,8},{16,12},{20,16},{24,20},{28,24},{5,1},{9,5},{13... | collective-permute-start | bytes 1572872 | tf_op jit(solution)/shard_map/ppermute | solution.py:236
  46.8 7.7 %copy-start.10 = (s32[2]{0:T(128)S(1)}, s32[2]{0:T(128)}, u32[]{:S(2)}) copy-start(s32[2]{0:T(128)} %get-tuple-element.37) | copy-start | bytes 28
  46.9 8.3 %copy-start.12 = (pred[5,8]{0,1:T(8,128)(4,1)S(1)}, pred[5,8]{0,1:T(8,128)(4,1)}, u32[]{:S(2)}) copy-start(pred[5,8]{0,1:T(8,128)(4,1)} %broadcast_compare_fusion) | copy-start | bytes 124
  46.9 8.3 %copy-start.16 = (pred[4,5]{1,0:T(4,128)(4,1)S(1)}, pred[4,5]{1,0:T(4,128)(4,1)}, u32[]{:S(2)}) copy-start(pred[4,5]{1,0:T(4,128)(4,1)} %fusion.110) | copy-start | bytes 64
  52.6 4.3 %copy-start.11 = (s32[8,2,1]{0,1,2:T(2,128)S(1)}, s32[8,2,1]{0,1,2:T(2,128)}, u32[]{:S(2)}) copy-start(s32[8,2,1]{0,1,2:T(2,128)} %compare_select_fusion) | copy-start | bytes 196
  52.7 3.0 %collective-permute-start.8 = (f32[64,1152]{1,0:T(8,128)S(1)}, f32[64,1152]{1,0:T(8,128)S(1)}, u32[]{:S(2)}, u32[]{:S(2)}) collective-permute-start(f32[64,1152]{1,0:T(8,128)S(1)} %get-tuple-element.56), channel_id=1, source_target_pairs={{0,4},{4,0},{8,12},{12,8},{16,20},{20,16},{24,28},{28,24},{1,5},{5... | collective-permute-start | bytes 884744 | tf_op jit(solution)/shard_map/ppermute | solution.py:100
  56.3 6.2 %collective-permute-start.9 = (f32[32,1152]{1,0:T(8,128)S(1)}, f32[32,1152]{1,0:T(8,128)S(1)}, u32[]{:S(2)}, u32[]{:S(2)}) collective-permute-start(f32[32,1152]{1,0:T(8,128)S(1)} %get-tuple-element.66), channel_id=1, source_target_pairs={{0,8},{4,12},{8,0},{12,4},{16,24},{20,28},{24,16},{28,20},{1,9},{5... | collective-permute-start | bytes 442376 | tf_op jit(solution)/shard_map/ppermute | solution.py:100
  63.0 4.4 %collective-permute-start.10 = (f32[16,1152]{1,0:T(8,128)S(1)}, f32[16,1152]{1,0:T(8,128)S(1)}, u32[]{:S(2)}, u32[]{:S(2)}) collective-permute-start(f32[16,1152]{1,0:T(8,128)S(1)} %get-tuple-element.78), channel_id=1, source_target_pairs={{0,16},{4,20},{8,24},{12,28},{16,0},{20,4},{24,8},{28,12},{1,17},{... | collective-permute-start | bytes 221192 | tf_op jit(solution)/shard_map/ppermute | solution.py:100
  67.8 4.4 %collective-permute-start.11 = (f32[16,1152]{1,0:T(8,128)S(1)}, f32[16,1152]{1,0:T(8,128)S(1)}, u32[]{:S(2)}, u32[]{:S(2)}) collective-permute-start(f32[16,1152]{1,0:T(8,128)S(1)} %concatenate.85), channel_id=1, source_target_pairs={{0,16},{4,20},{8,24},{12,28},{16,0},{20,4},{24,8},{28,12},{1,17},{... | collective-permute-start | bytes 221192 | tf_op jit(solution)/shard_map/ppermute | solution.py:104
  72.9 8.2 %collective-permute-start.12 = (f32[32,1152]{1,0:T(8,128)}, f32[32,1152]{1,0:T(8,128)}, u32[]{:S(2)}, u32[]{:S(2)}) collective-permute-start(f32[32,1152]{1,0:T(8,128)} %get-tuple-element.73), channel_id=1, source_target_pairs={{0,8},{4,12},{8,0},{12,4},{16,24},{20,28},{24,16},{28,20},{1,9},{5... | collective-permute-start | bytes 442376 | tf_op jit(solution)/shard_map/ppermute | solution.py:104
  82.0 6.3 %collective-permute-start.13 = (f32[64,1152]{1,0:T(8,128)S(1)}, f32[64,1152]{1,0:T(8,128)S(1)}, u32[]{:S(2)}, u32[]{:S(2)}) collective-permute-start(f32[64,1152]{1,0:T(8,128)S(1)} %get-tuple-element.61), channel_id=1, source_target_pairs={{0,4},{4,0},{8,12},{12,8},{16,20},{20,16},{24,28},{28,24},{1,5},{5... | collective-permute-start | bytes 884744 | tf_op jit(solution)/shard_map/ppermute | solution.py:104
  89.3 30.2 %all-to-all-start = ((bf16[8,2,64,1024]{3,2,1,0:T(8,128)(2,1)}), bf16[8,2,64,1024]{3,2,1,0:T(8,128)(2,1)S(1)}, u32[]{:S(2)}, u32[]{:S(2)}) async-start(bf16[8,2,64,1024]{3,2,1,0:T(8,128)(2,1)} %bitcast.6), calls=%async_computation | async-start | bytes 4194304 | tf_op jit(solution)/shard_map/all_to_all | solution.py:295
  94.3 1.5 copy-start.3
  94.3 1.9 copy-start.4
  101.5 2.8 %copy-start.5 = (bf16[32,8,8,128]{3,2,1,0:T(8,128)(2,1)S(1)}, bf16[32,8,8,128]{3,2,1,0:T(8,128)(2,1)}, u32[]{:S(2)}) copy-start(bf16[32,8,8,128]{3,2,1,0:T(8,128)(2,1)} %copy.116) | copy-start | bytes 1572868
  106.1 2.0 copy-start.1
  108.1 17.1 %slice-start = ((f32[128,1152]{1,0:T(8,128)}), f32[128,8]{1,0:T(8,128)S(1)}, s32[]{:S(2)}) async-start(f32[128,1152]{1,0:T(8,128)} %pad_maximum_fusion.5), calls=%async_computation.3 | async-start | bytes 131072 | tf_op jit(solution)/shard_map/slice | solution.py:309
  108.1 17.3 %copy-start.7 = (f32[128,1152]{1,0:T(8,128)S(1)}, f32[128,1152]{1,0:T(8,128)}, u32[]{:S(2)}) copy-start(f32[128,1152]{1,0:T(8,128)} %pad_maximum_fusion.5) | copy-start | bytes 1769476
  119.5 31.0 %all-to-all-start.1 = ((bf16[8,2,64,1024]{3,2,1,0:T(8,128)(2,1)}), bf16[8,2,64,1024]{3,2,1,0:T(8,128)(2,1)}, u32[]{:S(2)}, u32[]{:S(2)}) async-start(bf16[8,2,64,1024]{3,2,1,0:T(8,128)(2,1)} %bitcast.8), calls=%async_computation.1 | async-start | bytes 4194304 | tf_op jit(solution)/shard_map/all_to_all | solution.py:297
  127.5 4.0 %copy-start.6 = (bf16[224,8,8,128]{3,2,1,0:T(8,128)(2,1)S(1)}, bf16[224,8,8,128]{3,2,1,0:T(8,128)(2,1)}, u32[]{:S(2)}) copy-start(bf16[224,8,8,128]{3,2,1,0:T(8,128)(2,1)} %copy.118) | copy-start | bytes 11010052
  129.5 2.3 %copy-start.2 = (f32[4,8,64,448]{3,2,1,0:T(8,128)S(1)}, f32[4,8,64,448]{3,2,1,0:T(8,128)}, u32[]{:S(2)}) copy-start(f32[4,8,64,448]{3,2,1,0:T(8,128)} %copy-done.1) | copy-start | bytes 11010052
  154.0 1.9 copy-start.17

commit v14 on v12

--- a/solution.py
+++ b/solution.py
@@ -294,8 +294,14 @@
     incoming = lax.all_to_all(outgoing, "seq", split_axis=0, concat_axis=0, tiled=True)
     my_owners = owners[seq_place]
     my_ranks = ranks[seq_place]
-    random_k = incoming[my_owners, my_ranks, 0].reshape(blocks_here, RAND, BLOCK, width_here)
-    random_v = incoming[my_owners, my_ranks, 1].reshape(blocks_here, RAND, BLOCK, width_here)
+    chunk_count = seq_count * capacity
+    slot_chunk = my_owners * capacity + my_ranks
+    pick = (slot_chunk[:, None] == jnp.arange(chunk_count)[None, :]).astype(jnp.bfloat16)
+    chunks = incoming.reshape(chunk_count, 2 * BLOCK * width_here)
+    selected = jnp.dot(pick, chunks, preferred_element_type=jnp.float32).astype(jnp.bfloat16)
+    selected = selected.reshape(blocks_here, RAND, 2, BLOCK, width_here)
+    random_k = selected[:, :, 0]
+    random_v = selected[:, :, 1]
     random_kv = (random_k, random_v)
     near_part = partial_attend(query_view, near_kv[0], near_kv[1], near_valid)
     far_part = partial_attend(

time: 207 us -> 215 us (1.039)
  local copies, waits for them, and re-layouts: 29.6 us -> 35.7 us
  waiting for transfers between devices: 74.2 us -> 69.1 us
  other arithmetic: 18.5 us -> 22.1 us
  matrix products: 11.6 us -> 14 us
    gather x2 -> x0, local copies, waits for them, and re-layouts: 6.89 us -> none  [the longest x1 4.05 us: on_device(): incoming[my_owners, my_ranks, 1]]
    unnamed x37 -> x45, local copies, waits for them, and re-layouts: 8.19 us -> 13.2 us
    reshape x0 -> x1, local copies, waits for them, and re-layouts: none -> 4.83 us  [on_device(): chunks = incoming.reshape(chunk_count, 2 * BLOCK * width_here)]
    dot_general x0 -> x1, matrix products: none -> 3.48 us  [on_device(): jnp.dot(pick, chunks, preferred_element_type=jnp.float32)]
    ppermute x1, waiting for transfers between devices: 2.9 us -> 0.01 us  [on_device(): lax.ppermute(halo_kv[:, tok_here - halo:], 'seq', [(i, (i + 1) % seq_coun...]
  transfers between devices with their start and end apart: 15 -> 15, of which waited for: 15 -> 13; matrix products, arithmetic and copies ran while one was open for 13% -> 15% of each run, Pallas kernels for 0% -> 0%
where the time goes in v14:
time: 215 us; the launch traced here: 214 us
  waiting for transfers between devices  69.1 us (32%)
  blocking collectives  53.1 us (25%)
  local copies, waits for them, and re-layouts  35.7 us (17%)
  other arithmetic  22.1 us (10%)
  starting transfers between devices  17.4 us (8%)
  matrix products  14 us (7%)
  between operations  2.38 us (1%)
    all_to_all x1, blocking collectives, sum_over_head(): gathered = lax.all_to_all(partial, 'head', 0, 0, tiled=True)  53.1 us
    all_to_all x1, waiting for transfers between devices, on_device(): lax.all_to_all(outgoing, 'seq', split_axis=0, concat_axis=0, tiled=True)  27 us
    ppermute x6, waiting for transfers between devices, tree_reduce(): got = lax.ppermute(send, axis, xor_perm(count, bit))  20.9 us
    ppermute x6, waiting for transfers between devices, tree_reduce(): got = lax.ppermute(parts, axis, xor_perm(count, bit))  17.9 us
    unnamed x45, local copies, waits for them, and re-layouts  13.2 us
    all_to_all x1, starting transfers between devices, on_device(): lax.all_to_all(outgoing, 'seq', split_axis=0, concat_axis=0, tiled=True)  5.1 us
    reshape x1, local copies, waits for them, and re-layouts, on_device(): chunks = incoming.reshape(chunk_count, 2 * BLOCK * width_here)  4.83 us
  transfers between devices with their start and end apart: 15, of which 13 were waited for; matrix products, arithmetic and copies ran while one was open for 15% of the time, Pallas kernels for 0%

profile of v14, /device:TPU:2, one launch (start us, length us, event | category | flops | bytes accessed | tf_op | source)
XLA Modules:
  0.0 213.9 jit_solution(8437371323137944584)
XLA Ops:
  1.4 1.1 convert_bitcast_fusion.1
  4.5 0.7 slice_negate_fusion
  5.2 0.6 maximum_multiply_fusion.1
  6.2 1.0 fusion.48
  9.7 1.5 collective-permute-done
  11.4 6.8 %collective-permute-done.1 = bf16[96,1024]{1,0:T(8,128)(2,1)S(1)} collective-permute-done((bf16[96,1024]{1,0:T(8,128)(2,1)S(1)}, bf16[96,1024]{1,0:T(8,128)(2,1)S(1)}, u32[]{:S(2)}, u32[]{:S(2)}) %collective-permute-start.1) | collective-permute-done | bytes 196640 | tf_op jit(solution)/shard_map/ppermute | solution.py:100
  18.3 1.6 collective-permute-start.2
  19.9 3.1 %collective-permute-done.2 = bf16[48,1024]{1,0:T(8,128)(2,1)S(1)} collective-permute-done((bf16[48,1024]{1,0:T(8,128)(2,1)S(1)}, bf16[48,1024]{1,0:T(8,128)(2,1)S(1)}, u32[]{:S(2)}, u32[]{:S(2)}) %collective-permute-start.2) | collective-permute-done | bytes 98336 | tf_op jit(solution)/shard_map/ppermute | solution.py:100
  23.0 1.6 collective-permute-start.3
  25.0 2.7 %collective-permute-done.3 = bf16[48,1024]{1,0:T(8,128)(2,1)S(1)} collective-permute-done((bf16[48,1024]{1,0:T(8,128)(2,1)S(1)}, bf16[48,1024]{1,0:T(8,128)(2,1)S(1)}, u32[]{:S(2)}, u32[]{:S(2)}) %collective-permute-start.3) | collective-permute-done | bytes 98336 | tf_op jit(solution)/shard_map/ppermute | solution.py:104
  28.2 5.4 %collective-permute-done.4 = bf16[96,1024]{1,0:T(8,128)(2,1)S(1)} collective-permute-done((bf16[96,1024]{1,0:T(8,128)(2,1)S(1)}, bf16[96,1024]{1,0:T(8,128)(2,1)S(1)}, u32[]{:S(2)}, u32[]{:S(2)}) %collective-permute-start.4) | collective-permute-done | bytes 196640 | tf_op jit(solution)/shard_map/ppermute | solution.py:104
  33.7 0.8 pad_maximum_fusion.7
  34.7 0.9 copy.155
  35.7 0.6 reshape.390
  36.8 1.1 fusion.129
  37.9 2.4 %collective-permute-start.6 = (bf16[2,128,1024]{2,1,0:T(8,128)(2,1)}, bf16[2,128,1024]{2,1,0:T(8,128)(2,1)}, u32[]{:S(2)}, u32[]{:S(2)}) collective-permute-start(bf16[2,128,1024]{2,1,0:T(8,128)(2,1)} %get-tuple-element.40), channel_id=1, source_target_pairs={{0,4},{4,8},{8,12},{12,16},{16,20},{20,24},{24,28},{1,5},{5,9},{9,... | collective-permute-start | bytes 1572872 | tf_op jit(solution)/shard_map/ppermute | solution.py:233
  40.3 3.2 %collective-permute-start.7 = (bf16[2,128,1024]{2,1,0:T(8,128)(2,1)}, bf16[2,128,1024]{2,1,0:T(8,128)(2,1)}, u32[]{:S(2)}, u32[]{:S(2)}) collective-permute-start(bf16[2,128,1024]{2,1,0:T(8,128)(2,1)} %get-tuple-element.39), channel_id=1, source_target_pairs={{4,0},{8,4},{12,8},{16,12},{20,16},{24,20},{28,24},{5,1},{9,5},{13... | collective-permute-start | bytes 1572872 | tf_op jit(solution)/shard_map/ppermute | solution.py:236
  44.2 1.1 fusion.53
  45.3 0.8 copy.144
  46.1 1.4 convolution_bitcast_fusion
  47.9 0.9 copy.229
  48.7 1.2 concatenate.72
  49.9 3.4 %collective-permute-done.7 = bf16[2,128,1024]{2,1,0:T(8,128)(2,1)} collective-permute-done((bf16[2,128,1024]{2,1,0:T(8,128)(2,1)}, bf16[2,128,1024]{2,1,0:T(8,128)(2,1)}, u32[]{:S(2)}, u32[]{:S(2)}) %collective-permute-start.7) | collective-permute-done | bytes 524320 | tf_op jit(solution)/shard_map/ppermute | solution.py:236
  53.3 0.9 dynamic-slice_bitcast_fusion.2
  54.2 1.8 collective-permute-start.8
  56.1 2.8 %gather_fusion = bf16[16,2,64,1024]{3,2,1,0:T(8,128)(2,1)} fusion(bf16[4,2,64,1024]{3,2,0,1:T(8,128)(2,1)S(1)} %pad_maximum_fusion.2, s32[1024]{0:T(1024)S(1)} %pad_clamp_fusion.1), kind=kCustom, calls=%fused_computation | custom fusion | bytes 8388672 | tf_op jit(solution)/shard_map/gather | solution.py:292
  58.9 0.9 fusion.100
  60.1 1.2 fusion.79
  61.4 0.6 collective-permute-start.9
  62.1 5.1 %collective-permute-done.9 = f32[32,1152]{1,0:T(8,128)S(1)} collective-permute-done((f32[32,1152]{1,0:T(8,128)S(1)}, f32[32,1152]{1,0:T(8,128)S(1)}, u32[]{:S(2)}, u32[]{:S(2)}) %collective-permute-start.9) | collective-permute-done | bytes 147488 | tf_op jit(solution)/shard_map/ppermute | solution.py:100
  67.8 4.3 %collective-permute-done.10 = f32[16,1152]{1,0:T(8,128)S(1)} collective-permute-done((f32[16,1152]{1,0:T(8,128)S(1)}, f32[16,1152]{1,0:T(8,128)S(1)}, u32[]{:S(2)}, u32[]{:S(2)}) %collective-permute-start.10) | collective-permute-done | bytes 73760 | tf_op jit(solution)/shard_map/ppermute | solution.py:100
  72.5 4.3 %collective-permute-done.11 = f32[16,1152]{1,0:T(8,128)S(1)} collective-permute-done((f32[16,1152]{1,0:T(8,128)S(1)}, f32[16,1152]{1,0:T(8,128)S(1)}, u32[]{:S(2)}, u32[]{:S(2)}) %collective-permute-start.11) | collective-permute-done | bytes 73760 | tf_op jit(solution)/shard_map/ppermute | solution.py:104
  76.9 0.6 collective-permute-start.12
  77.6 4.5 %collective-permute-done.12 = f32[32,1152]{1,0:T(8,128)S(1)} collective-permute-done((f32[32,1152]{1,0:T(8,128)S(1)}, f32[32,1152]{1,0:T(8,128)S(1)}, u32[]{:S(2)}, u32[]{:S(2)}) %collective-permute-start.12) | collective-permute-done | bytes 147488 | tf_op jit(solution)/shard_map/ppermute | solution.py:104
  82.3 0.6 fusion.131
  83.0 0.9 collective-permute-done.13
  84.0 0.9 pad_maximum_fusion.6
  84.9 5.1 %all-to-all-start = ((bf16[8,2,2,64,1024]{4,3,2,1,0:T(8,128)(2,1)}), bf16[8,2,2,64,1024]{4,3,2,1,0:T(8,128)(2,1)}, u32[]{:S(2)}, u32[]{:S(2)}) async-start(bf16[8,2,2,64,1024]{4,3,2,1,0:T(8,128)(2,1)} %bitcast.300), calls=%async_computation | async-start | bytes 8388608 | tf_op jit(solution)/shard_map/all_to_all | solution.py:294
  90.3 0.6 fusion.132
  90.9 1.3 compare_and_fusion.1
  92.3 1.3 compare_and_fusion
  93.9 1.0 slice.226
  94.9 1.0 slice.227
  95.9 1.2 maximum_bitcast_fusion
  97.0 1.4 maximum_bitcast_fusion.1
  98.7 1.1 pad_maximum_fusion
  99.8 1.5 fusion.127
  101.3 1.0 copy.165
  102.3 2.7 %copy.166 = bf16[224,8,8,128]{3,2,1,0:T(8,128)(2,1)} copy(bf16[224,8,8,128]{3,1,2,0:T(8,128)(2,1)S(1)} %bitcast.307) | data formatting | bytes 7340032
  105.0 1.8 fusion
  106.9 2.0 copy-done
  108.9 1.5 fusion.5
  110.7 27.0 %all-to-all-done = bf16[8,2,2,64,1024]{4,3,2,1,0:T(8,128)(2,1)} async-done(((bf16[8,2,2,64,1024]{4,3,2,1,0:T(8,128)(2,1)}), bf16[8,2,2,64,1024]{4,3,2,1,0:T(8,128)(2,1)}, u32[]{:S(2)}, u32[]{:S(2)}) %all-to-all-start) | async-done | bytes 4194336 | tf_op jit(solution)/shard_map/all_to_all | solution.py:294
  137.7 4.8 %reshape.385 = bf16[16,131072]{1,0:T(8,128)(2,1)} reshape(bf16[8,2,2,64,1024]{4,3,2,1,0:T(8,128)(2,1)} %all-to-all-done) | data formatting | bytes 8388608 | tf_op jit(solution)/shard_map/reshape | solution.py:300
  142.5 3.5 %convolution_convert_fusion = bf16[12,131072]{1,0:T(8,128)(2,1)S(1)} fusion(bf16[16,131072]{1,0:T(8,128)(2,1)} %reshape.385, s32[12]{0:T(128)S(1)} %fusion.115), kind=kOutput, calls=%fused_computation.4 | convolution fusion | flops 51904704 | bytes 7340080 | tf_op jit(solution)/shard_map/dot_general | solution.py:301
  146.0 2.3 %copy.167 = bf16[2,8,128,1024]{3,2,1,0:T(8,128)(2,1)S(1)} copy(bf16[2,8,128,1024]{3,1,2,0:T(8,128)(2,1)S(1)} %bitcast.291) | data formatting | bytes 8388608
  149.4 1.2 multiply_reduce_fusion
  151.1 0.8 fusion.12
  151.9 1.1 copy-done.1
  153.0 2.1 fusion.32
  155.1 1.2 fusion.42
  156.8 2.5 %convolution_convert_fusion.1 = bf16[256,4096]{1,0:T(8,128)(2,1)S(1)} fusion(bf16[1024,4096]{1,0:T(8,128)(2,1)S(1)} %bitcast.372, bf16[256,1024]{1,0:T(8,128)(2,1)S(1)} %bitcast.349, bf16[256,1024]{1,0:T(8,128)(2,1)S(1)} %bitcast.350, bf16[32,8,8,128]{3,2,1,0:T(8,128)(2,1)S(1)} %bitcast.354, pred[256]{0:T(512)(128)(4,1)S(1)} %broadcast_in_dim.171, ...), kind=kOutput, calls=%fused_computation.6 | convolution fusion | flops 2149056512 | bytes 12059136 | tf_op jit(solution)/shard_map/dot_general | solution.py:140
  159.5 53.1 %all_to_all.10 = bf16[4,1024,256]{1,2,0:T(8,128)(2,1)S(1)} all-to-all(bf16[4,1024,256]{1,2,0:T(8,128)(2,1)S(1)} %bitcast.314), channel_id=1, replica_groups=mesh['seq'=8,'head'=4] {'head'}, dimensions={0} | all-to-all | bytes 4194304 | tf_op jit(solution)/shard_map/all_to_all | solution.py:147
  212.6 1.3 reduce_sum.71
  (147 shorter events, 13.2 us)
Async XLA Ops:
  0.0 2.8 %copy-start.5 = (bf16[256,1024]{1,0:T(8,128)(2,1)S(1)}, bf16[256,1024]{1,0:T(8,128)(2,1)}, u32[]{:S(2)}) copy-start(bf16[256,1024]{1,0:T(8,128)(2,1)} %param.9) | copy-start | bytes 1572868
  2.6 0.7 copy-start.12
  3.3 5.7 %copy-start.7 = (pred[2]{0:T(512)(128)(4,1)}, pred[2]{0:T(512)(128)(4,1)S(1)}, u32[]{:S(2)}) copy-start(pred[2]{0:T(512)(128)(4,1)S(1)} %fusion.114) | copy-start | bytes 10
  5.2 1.0 copy-start.6
  6.2 2.1 copy-start.2
  7.2 2.3 %copy-start.10 = (s32[32,3]{0,1:T(4,128)S(1)}, s32[32,3]{0,1:T(4,128)}, u32[]{:S(2)}) copy-start(s32[32,3]{0,1:T(4,128)} %param.14) | copy-start | bytes 1156
  9.4 1.8 collective-permute-start
  11.2 7.0 %collective-permute-start.1 = (bf16[96,1024]{1,0:T(8,128)(2,1)S(1)}, bf16[96,1024]{1,0:T(8,128)(2,1)S(1)}, u32[]{:S(2)}, u32[]{:S(2)}) collective-permute-start(bf16[96,1024]{1,0:T(8,128)(2,1)S(1)} %dynamic-slice_bitcast_fusion.3), channel_id=1, source_target_pairs={{0,8},{4,12},{8,0},{12,4},{16,24},{20,28},{24,16},{28,20},{1,9},{5... | collective-permute-start | bytes 589832 | tf_op jit(solution)/shard_map/ppermute | solution.py:100
  18.3 4.7 %collective-permute-start.2 = (bf16[48,1024]{1,0:T(8,128)(2,1)S(1)}, bf16[48,1024]{1,0:T(8,128)(2,1)S(1)}, u32[]{:S(2)}, u32[]{:S(2)}) collective-permute-start(bf16[48,1024]{1,0:T(8,128)(2,1)S(1)} %dynamic-slice_bitcast_fusion.6), channel_id=1, source_target_pairs={{0,16},{4,20},{8,24},{12,28},{16,0},{20,4},{24,8},{28,12},{1,17},{... | collective-permute-start | bytes 294920 | tf_op jit(solution)/shard_map/ppermute | solution.py:100
  23.0 4.7 %collective-permute-start.3 = (bf16[48,1024]{1,0:T(8,128)(2,1)S(1)}, bf16[48,1024]{1,0:T(8,128)(2,1)S(1)}, u32[]{:S(2)}, u32[]{:S(2)}) collective-permute-start(bf16[48,1024]{1,0:T(8,128)(2,1)S(1)} %bitcast_add_fusion.2), channel_id=1, source_target_pairs={{0,16},{4,20},{8,24},{12,28},{16,0},{20,4},{24,8},{28,12},{1,17},{... | collective-permute-start | bytes 294920 | tf_op jit(solution)/shard_map/ppermute | solution.py:104
  27.8 5.7 %collective-permute-start.4 = (bf16[96,1024]{1,0:T(8,128)(2,1)S(1)}, bf16[96,1024]{1,0:T(8,128)(2,1)S(1)}, u32[]{:S(2)}, u32[]{:S(2)}) collective-permute-start(bf16[96,1024]{1,0:T(8,128)(2,1)S(1)} %get-tuple-element.65), channel_id=1, source_target_pairs={{0,8},{4,12},{8,0},{12,4},{16,24},{20,28},{24,16},{28,20},{1,9},{5... | collective-permute-start | bytes 589832 | tf_op jit(solution)/shard_map/ppermute | solution.py:104
  34.5 1.9 collective-permute-start.5
  37.9 12.0 %collective-permute-start.6 = (bf16[2,128,1024]{2,1,0:T(8,128)(2,1)}, bf16[2,128,1024]{2,1,0:T(8,128)(2,1)}, u32[]{:S(2)}, u32[]{:S(2)}) collective-permute-start(bf16[2,128,1024]{2,1,0:T(8,128)(2,1)} %get-tuple-element.40), channel_id=1, source_target_pairs={{0,4},{4,8},{8,12},{12,16},{16,20},{20,24},{24,28},{1,5},{5,9},{9,... | collective-permute-start | bytes 1572872 | tf_op jit(solution)/shard_map/ppermute | solution.py:233
  40.3 13.1 %collective-permute-start.7 = (bf16[2,128,1024]{2,1,0:T(8,128)(2,1)}, bf16[2,128,1024]{2,1,0:T(8,128)(2,1)}, u32[]{:S(2)}, u32[]{:S(2)}) collective-permute-start(bf16[2,128,1024]{2,1,0:T(8,128)(2,1)} %get-tuple-element.39), channel_id=1, source_target_pairs={{4,0},{8,4},{12,8},{16,12},{20,16},{24,20},{28,24},{5,1},{9,5},{13... | collective-permute-start | bytes 1572872 | tf_op jit(solution)/shard_map/ppermute | solution.py:236
  47.5 8.4 %copy-start.11 = (s32[16]{0:T(128)S(1)}, s32[16]{0:T(128)}, u32[]{:S(2)}) copy-start(s32[16]{0:T(128)} %reshape.390) | copy-start | bytes 196
  54.2 4.7 %collective-permute-start.8 = (f32[64,1152]{1,0:T(8,128)}, f32[64,1152]{1,0:T(8,128)}, u32[]{:S(2)}, u32[]{:S(2)}) collective-permute-start(f32[64,1152]{1,0:T(8,128)} %get-tuple-element.52), channel_id=1, source_target_pairs={{0,4},{4,0},{8,12},{12,8},{16,20},{20,16},{24,28},{28,24},{1,5},{5... | collective-permute-start | bytes 884744 | tf_op jit(solution)/shard_map/ppermute | solution.py:100
  58.9 3.1 %copy-start.13 = (s32[8]{0:T(128)S(1)}, s32[8]{0:T(128)}, u32[]{:S(2)}) copy-start(s32[8]{0:T(128)} %param.15) | copy-start | bytes 100
  61.3 21.1 %copy-start.9 = (s32[2]{0:T(128)S(1)}, s32[2]{0:T(128)}, u32[]{:S(2)}) copy-start(s32[2]{0:T(128)} %get-tuple-element.31) | copy-start | bytes 28
  61.4 5.8 %collective-permute-start.9 = (f32[32,1152]{1,0:T(8,128)S(1)}, f32[32,1152]{1,0:T(8,128)S(1)}, u32[]{:S(2)}, u32[]{:S(2)}) collective-permute-start(f32[32,1152]{1,0:T(8,128)S(1)} %get-tuple-element.62), channel_id=1, source_target_pairs={{0,8},{4,12},{8,0},{12,4},{16,24},{20,28},{24,16},{28,20},{1,9},{5... | collective-permute-start | bytes 442376 | tf_op jit(solution)/shard_map/ppermute | solution.py:100
  67.7 4.4 %collective-permute-start.10 = (f32[16,1152]{1,0:T(8,128)S(1)}, f32[16,1152]{1,0:T(8,128)S(1)}, u32[]{:S(2)}, u32[]{:S(2)}) collective-permute-start(f32[16,1152]{1,0:T(8,128)S(1)} %get-tuple-element.74), channel_id=1, source_target_pairs={{0,16},{4,20},{8,24},{12,28},{16,0},{20,4},{24,8},{28,12},{1,17},{... | collective-permute-start | bytes 221192 | tf_op jit(solution)/shard_map/ppermute | solution.py:100
  72.5 4.4 %collective-permute-start.11 = (f32[16,1152]{1,0:T(8,128)S(1)}, f32[16,1152]{1,0:T(8,128)S(1)}, u32[]{:S(2)}, u32[]{:S(2)}) collective-permute-start(f32[16,1152]{1,0:T(8,128)S(1)} %concatenate.81), channel_id=1, source_target_pairs={{0,16},{4,20},{8,24},{12,28},{16,0},{20,4},{24,8},{28,12},{1,17},{... | collective-permute-start | bytes 221192 | tf_op jit(solution)/shard_map/ppermute | solution.py:104
  76.9 5.2 %collective-permute-start.12 = (f32[32,1152]{1,0:T(8,128)S(1)}, f32[32,1152]{1,0:T(8,128)S(1)}, u32[]{:S(2)}, u32[]{:S(2)}) collective-permute-start(f32[32,1152]{1,0:T(8,128)S(1)} %get-tuple-element.69), channel_id=1, source_target_pairs={{0,8},{4,12},{8,0},{12,4},{16,24},{20,28},{24,16},{28,20},{1,9},{5... | collective-permute-start | bytes 442376 | tf_op jit(solution)/shard_map/ppermute | solution.py:104
  82.2 1.6 collective-permute-start.13
  84.9 5.4 %copy-start.8 = (pred[2]{0:T(512)(128)(4,1)S(1)}, pred[2]{0:T(512)(128)(4,1)}, u32[]{:S(2)}) copy-start(pred[2]{0:T(512)(128)(4,1)} %copy-done.7) | copy-start | bytes 10
  84.9 52.8 %all-to-all-start = ((bf16[8,2,2,64,1024]{4,3,2,1,0:T(8,128)(2,1)}), bf16[8,2,2,64,1024]{4,3,2,1,0:T(8,128)(2,1)}, u32[]{:S(2)}, u32[]{:S(2)}) async-start(bf16[8,2,2,64,1024]{4,3,2,1,0:T(8,128)(2,1)} %bitcast.300), calls=%async_computation | async-start | bytes 8388608 | tf_op jit(solution)/shard_map/all_to_all | solution.py:294
  106.9 2.0 copy-start
  106.9 3.5 %slice-start = ((f32[128,1152]{1,0:T(8,128)}), f32[128,8]{1,0:T(8,128)S(1)}, s32[]{:S(2)}) async-start(f32[128,1152]{1,0:T(8,128)} %pad_maximum_fusion.6), calls=%async_computation.2 | async-start | bytes 131072 | tf_op jit(solution)/shard_map/slice | solution.py:312
  106.9 3.7 %copy-start.4 = (f32[128,1152]{1,0:T(8,128)S(1)}, f32[128,1152]{1,0:T(8,128)}, u32[]{:S(2)}) copy-start(f32[128,1152]{1,0:T(8,128)} %pad_maximum_fusion.6) | copy-start | bytes 1769476
  149.4 2.5 %copy-start.3 = (bf16[224,8,8,128]{3,2,1,0:T(8,128)(2,1)S(1)}, bf16[224,8,8,128]{3,2,1,0:T(8,128)(2,1)}, u32[]{:S(2)}) copy-start(bf16[224,8,8,128]{3,2,1,0:T(8,128)(2,1)} %copy.166) | copy-start | bytes 11010052
  150.6 2.4 %copy-start.1 = (f32[4,8,64,448]{3,2,1,0:T(8,128)S(1)}, f32[4,8,64,448]{3,2,1,0:T(8,128)}, u32[]{:S(2)}) copy-start(f32[4,8,64,448]{3,2,1,0:T(8,128)} %copy-done) | copy-start | bytes 11010052
  150.6 6.1 %slice-start.1 = ((s8[8388608]{0:T(1024)(128)(4,1)}), s8[4194304]{0:T(1024)(128)(4,1)S(1)}, s32[]{:S(2)}) async-start(s8[8388608]{0:T(1024)(128)(4,1)} %bitcast.371), calls=%async_computation.3 | async-start | bytes 8388608
  153.0 3.7 %slice-start.2 = ((s8[8388608]{0:T(1024)(128)(4,1)}), s8[4194304]{0:T(1024)(128)(4,1)S(1)}, s32[]{:S(2)}) async-start(s8[8388608]{0:T(1024)(128)(4,1)} %bitcast.371), calls=%async_computation.4 | async-start | bytes 8388608

commit v15 on v12

--- a/solution.py
+++ b/solution.py
@@ -272,8 +272,6 @@
         ],
         axis=1,
     )
-    packed, from_left, from_right = lax.optimization_barrier((packed, from_left, from_right))
-    reduced = tree_reduce(packed, softmax_merge, "seq")
     slot_total = blocks_here * RAND
     capacity = (slot_total + seq_count - 1) // seq_count
     flat_ids = random_blocks.reshape(seq_count, slot_total)
@@ -288,8 +286,12 @@
         ranks[:, None, :] == jnp.arange(capacity)[None, :, None]
     )
     send_local = jnp.sum(jnp.where(wanted, local_ids[:, None, :], 0), axis=2)
-    kv_blocks = jnp.stack([key_rot.reshape(blocks_here, BLOCK, width_here), value_view], axis=1)
+    kv_blocks = jnp.transpose(halo_kv.reshape(2, blocks_here, BLOCK, width_here), (1, 0, 2, 3))
     outgoing = kv_blocks[send_local]
+    packed, from_left, from_right, outgoing = lax.optimization_barrier(
+        (packed, from_left, from_right, outgoing)
+    )
+    reduced = tree_reduce(packed, softmax_merge, "seq")
     outgoing, reduced = lax.optimization_barrier((outgoing, reduced))
     incoming = lax.all_to_all(outgoing, "seq", split_axis=0, concat_axis=0, tiled=True)
     my_owners = owners[seq_place]

time: 207 us -> 206 us (level)
  waiting for transfers between devices: 74.2 us -> 67 us
  starting transfers between devices: 17.5 us -> 21.2 us
    ppermute x6, waiting for transfers between devices: 22.1 us -> 16.7 us  [tree_reduce(): got = lax.ppermute(send, axis, xor_perm(count, bit))]
    ppermute x1, waiting for transfers between devices: 4.63 us -> 0.01 us  [on_device(): lax.ppermute(halo_kv[:, :halo], 'seq', [((i + 1) % seq_count, i) for i in...]
    ppermute x6, starting transfers between devices: 4.24 us -> 7.52 us  [tree_reduce(): got = lax.ppermute(send, axis, xor_perm(count, bit))]
    unnamed x37 -> x55, local copies, waits for them, and re-layouts: 8.19 us -> 10.7 us
    all_to_all x1, waiting for transfers between devices: 28.8 us -> 31.3 us  [on_device(): lax.all_to_all(outgoing, 'seq', split_axis=0, concat_axis=0, tiled=True)]
  transfers between devices with their start and end apart: 15 -> 15, of which waited for: 15 -> 13; matrix products, arithmetic and copies ran while one was open for 13% -> 14% of each run, Pallas kernels for 0% -> 0%
where the time goes in v15:
time: 206 us
  waiting for transfers between devices  67 us (33%)
  blocking collectives  53.3 us (26%)
  local copies, waits for them, and re-layouts  30.8 us (15%)
  starting transfers between devices  21.2 us (10%)
  other arithmetic  20.2 us (10%)
  matrix products  10.7 us (5%)
  between operations  2.42 us (1%)
    all_to_all x1, blocking collectives, sum_over_head(): gathered = lax.all_to_all(partial, 'head', 0, 0, tiled=True)  53.3 us
    all_to_all x1, waiting for transfers between devices, on_device(): lax.all_to_all(outgoing, 'seq', split_axis=0, concat_axis=0, tiled=True)  31.3 us
    ppermute x6, waiting for transfers between devices, tree_reduce(): got = lax.ppermute(parts, axis, xor_perm(count, bit))  17 us
    ppermute x6, waiting for transfers between devices, tree_reduce(): got = lax.ppermute(send, axis, xor_perm(count, bit))  16.7 us
    unnamed x55, local copies, waits for them, and re-layouts  10.7 us
    ppermute x6, starting transfers between devices, tree_reduce(): got = lax.ppermute(send, axis, xor_perm(count, bit))  7.52 us
    all_to_all x1, starting transfers between devices, on_device(): lax.all_to_all(outgoing, 'seq', split_axis=0, concat_axis=0, tiled=True)  4.89 us
    ppermute x6, starting transfers between devices, tree_reduce(): got = lax.ppermute(parts, axis, xor_perm(count, bit))  4.46 us
  transfers between devices with their start and end apart: 15, of which 13 were waited for; matrix products, arithmetic and copies ran while one was open for 14% of the time, Pallas kernels for 0%

profile of v15, /device:TPU:2, one launch (start us, length us, event | category | flops | bytes accessed | tf_op | source)
XLA Modules:
  0.0 205.6 jit_solution(1605982890192030318)
XLA Ops:
  1.4 0.7 fusion.118
  2.1 1.2 compare_select_fusion.3
  3.5 1.1 convert_bitcast_fusion
  5.2 0.5 fusion.88
  5.9 0.6 gather_fusion.2
  6.5 0.7 slice_negate_fusion
  7.2 0.6 maximum_multiply_fusion.1
  8.4 1.0 fusion.48
  9.3 0.6 gather_fusion.1
  9.9 0.6 gather_fusion
  11.3 1.2 collective-permute-done
  12.8 6.9 %collective-permute-done.1 = bf16[96,1024]{1,0:T(8,128)(2,1)S(1)} collective-permute-done((bf16[96,1024]{1,0:T(8,128)(2,1)S(1)}, bf16[96,1024]{1,0:T(8,128)(2,1)S(1)}, u32[]{:S(2)}, u32[]{:S(2)}) %collective-permute-start.1) | collective-permute-done | bytes 196640 | tf_op jit(solution)/shard_map/ppermute | solution.py:100
  19.7 1.6 collective-permute-start.2
  21.4 3.0 %collective-permute-done.2 = bf16[48,1024]{1,0:T(8,128)(2,1)S(1)} collective-permute-done((bf16[48,1024]{1,0:T(8,128)(2,1)S(1)}, bf16[48,1024]{1,0:T(8,128)(2,1)S(1)}, u32[]{:S(2)}, u32[]{:S(2)}) %collective-permute-start.2) | collective-permute-done | bytes 98336 | tf_op jit(solution)/shard_map/ppermute | solution.py:100
  24.4 1.6 collective-permute-start.3
  26.0 3.1 %collective-permute-done.3 = bf16[48,1024]{1,0:T(8,128)(2,1)S(1)} collective-permute-done((bf16[48,1024]{1,0:T(8,128)(2,1)S(1)}, bf16[48,1024]{1,0:T(8,128)(2,1)S(1)}, u32[]{:S(2)}, u32[]{:S(2)}) %collective-permute-start.3) | collective-permute-done | bytes 98336 | tf_op jit(solution)/shard_map/ppermute | solution.py:104
  30.2 4.8 %collective-permute-done.4 = bf16[96,1024]{1,0:T(8,128)(2,1)S(1)} collective-permute-done((bf16[96,1024]{1,0:T(8,128)(2,1)S(1)}, bf16[96,1024]{1,0:T(8,128)(2,1)S(1)}, u32[]{:S(2)}, u32[]{:S(2)}) %collective-permute-start.4) | collective-permute-done | bytes 196640 | tf_op jit(solution)/shard_map/ppermute | solution.py:104
  35.5 0.9 copy.107
  36.5 0.5 collective-permute-done.5
  37.5 0.8 copy-done.8
  38.6 1.1 fusion.132
  39.6 1.9 collective-permute-start.7
  41.6 2.4 %collective-permute-start.6 = (bf16[2,128,1024]{2,1,0:T(8,128)(2,1)}, bf16[2,128,1024]{2,1,0:T(8,128)(2,1)}, u32[]{:S(2)}, u32[]{:S(2)}) collective-permute-start(bf16[2,128,1024]{2,1,0:T(8,128)(2,1)} %get-tuple-element.42), channel_id=1, source_target_pairs={{0,4},{4,8},{8,12},{12,16},{16,20},{20,24},{24,28},{1,5},{5,9},{9,... | collective-permute-start | bytes 1572872 | tf_op jit(solution)/shard_map/ppermute | solution.py:233
  44.3 1.4 convolution_bitcast_fusion
  46.0 0.9 copy.180
  47.5 2.8 %gather_fusion.3 = bf16[16,2,64,1024]{3,2,1,0:T(8,128)(2,1)} fusion(bf16[4,2,64,1024]{3,2,0,1:T(8,128)(2,1)S(1)} %bitcast.288, s32[1024]{0:T(1024)S(1)} %pad_clamp_fusion), kind=kCustom, calls=%fused_computation.3 | custom fusion | bytes 8388672 | tf_op jit(solution)/shard_map/gather | solution.py:290
  50.5 1.9 collective-permute-done.6
  52.4 2.8 %collective-permute-start.8 = (f32[64,1152]{1,0:T(8,128)S(1)}, f32[64,1152]{1,0:T(8,128)S(1)}, u32[]{:S(2)}, u32[]{:S(2)}) collective-permute-start(f32[64,1152]{1,0:T(8,128)S(1)} %get-tuple-element.54), channel_id=1, source_target_pairs={{0,4},{4,0},{8,12},{12,8},{16,20},{20,16},{24,28},{28,24},{1,5},{5... | collective-permute-start | bytes 884744 | tf_op jit(solution)/shard_map/ppermute | solution.py:100
  55.2 0.6 fusion.134
  55.8 0.6 fusion.135
  57.1 1.3 compare_and_fusion.1
  58.6 1.3 compare_and_fusion
  60.0 3.2 %collective-permute-done.9 = f32[32,1152]{1,0:T(8,128)S(1)} collective-permute-done((f32[32,1152]{1,0:T(8,128)S(1)}, f32[32,1152]{1,0:T(8,128)S(1)}, u32[]{:S(2)}, u32[]{:S(2)}) %collective-permute-start.9) | collective-permute-done | bytes 147488 | tf_op jit(solution)/shard_map/ppermute | solution.py:100
  63.7 2.9 %collective-permute-start.10 = (f32[16,1152]{1,0:T(8,128)S(1)}, f32[16,1152]{1,0:T(8,128)S(1)}, u32[]{:S(2)}, u32[]{:S(2)}) collective-permute-start(f32[16,1152]{1,0:T(8,128)S(1)} %get-tuple-element.76), channel_id=1, source_target_pairs={{0,16},{4,20},{8,24},{12,28},{16,0},{20,4},{24,8},{28,12},{1,17},{... | collective-permute-start | bytes 221192 | tf_op jit(solution)/shard_map/ppermute | solution.py:100
  66.6 2.3 %collective-permute-done.10 = f32[16,1152]{1,0:T(8,128)S(1)} collective-permute-done((f32[16,1152]{1,0:T(8,128)S(1)}, f32[16,1152]{1,0:T(8,128)S(1)}, u32[]{:S(2)}, u32[]{:S(2)}) %collective-permute-start.10) | collective-permute-done | bytes 73760 | tf_op jit(solution)/shard_map/ppermute | solution.py:100
  69.3 2.0 collective-permute-start.11
  71.4 2.3 %collective-permute-done.11 = f32[16,1152]{1,0:T(8,128)S(1)} collective-permute-done((f32[16,1152]{1,0:T(8,128)S(1)}, f32[16,1152]{1,0:T(8,128)S(1)}, u32[]{:S(2)}, u32[]{:S(2)}) %collective-permute-start.11) | collective-permute-done | bytes 73760 | tf_op jit(solution)/shard_map/ppermute | solution.py:104
  74.2 4.8 %collective-permute-done.12 = f32[32,1152]{1,0:T(8,128)S(1)} collective-permute-done((f32[32,1152]{1,0:T(8,128)S(1)}, f32[32,1152]{1,0:T(8,128)S(1)}, u32[]{:S(2)}, u32[]{:S(2)}) %collective-permute-start.12) | collective-permute-done | bytes 147488 | tf_op jit(solution)/shard_map/ppermute | solution.py:104
  79.3 1.5 collective-permute-done.13
  80.9 0.9 pad_maximum_fusion.5
  81.7 4.9 %all-to-all-start = ((bf16[8,2,2,64,1024]{4,3,2,1,0:T(8,128)(2,1)}), bf16[8,2,2,64,1024]{4,3,2,1,0:T(8,128)(2,1)}, u32[]{:S(2)}, u32[]{:S(2)}) async-start(bf16[8,2,2,64,1024]{4,3,2,1,0:T(8,128)(2,1)} %bitcast.292), calls=%async_computation | async-start | bytes 8388608 | tf_op jit(solution)/shard_map/all_to_all | solution.py:296
  87.8 1.0 slice.225
  88.8 1.0 slice.224
  89.7 1.2 maximum_bitcast_fusion
  90.9 1.4 maximum_bitcast_fusion.1
  92.6 1.1 pad_maximum_fusion
  93.7 1.5 fusion.131
  95.2 1.0 copy.117
  96.2 2.7 %copy.118 = bf16[224,8,8,128]{3,2,1,0:T(8,128)(2,1)} copy(bf16[224,8,8,128]{3,1,2,0:T(8,128)(2,1)S(1)} %bitcast.297) | data formatting | bytes 7340032
  98.9 1.8 fusion
  100.8 1.5 fusion.5
  102.3 0.5 copy-done
  103.1 31.3 %all-to-all-done = bf16[8,2,2,64,1024]{4,3,2,1,0:T(8,128)(2,1)} async-done(((bf16[8,2,2,64,1024]{4,3,2,1,0:T(8,128)(2,1)}), bf16[8,2,2,64,1024]{4,3,2,1,0:T(8,128)(2,1)}, u32[]{:S(2)}, u32[]{:S(2)}) %all-to-all-start) | async-done | bytes 4194336 | tf_op jit(solution)/shard_map/all_to_all | solution.py:296
  134.5 2.8 %gather_fusion.4 = bf16[12,64,1024]{2,1,0:T(8,128)(2,1)S(1)} fusion(bf16[8,2,2,64,1024]{4,3,2,1,0:T(8,128)(2,1)} %all-to-all-done, s32[12]{0:T(128)S(1)} %bitcast.357), kind=kCustom, calls=%fused_computation.4 | custom fusion | bytes 3145872 | tf_op jit(solution)/shard_map/gather | solution.py:299
  137.8 2.8 %gather_fusion.5 = bf16[12,64,1024]{2,1,0:T(8,128)(2,1)S(1)} fusion(bf16[8,2,2,64,1024]{4,3,2,1,0:T(8,128)(2,1)} %all-to-all-done, s32[12]{0:T(128)S(1)} %get-tuple-element.20), kind=kCustom, calls=%fused_computation.5 | custom fusion | bytes 3145872 | tf_op jit(solution)/shard_map/gather | solution.py:300
  141.1 0.6 copy-done.4
  141.7 1.2 multiply_reduce_fusion
  142.9 0.8 fusion.12
  143.7 0.6 copy-done.1
  144.3 2.1 %fusion.32 = f32[4,64,8,128]{3,1,2,0:T(8,128)S(1)} fusion(bf16[4,448,8,128]{3,2,1,0:T(8,128)(2,1)S(1)} %bitcast.316, f32[4,8,64,448]{3,2,1,0:T(8,128)S(1)} %copy-done.1, f32[4,8,64]{2,1,0:T(8,128)S(1)} %get-tuple-element.87, pred[4,8,448]{2,1,0:T(8,128)(4,1)S(1)} %broadcast_in_dim.179, f32[4,64,8]{1,2,0:T(8,128)S(1)} %get-tuple-element.19), kind=kOutput, calls=%fused_computation.34 | convolution fusion | flops 238813184 | bytes 8419328 | tf_op jit(solution)/shard_map/bhqs,bshd->bqhd/dot_general | solution.py:165
  146.4 1.4 fusion.42
  148.3 2.5 %convolution_convert_fusion = bf16[256,4096]{1,0:T(8,128)(2,1)S(1)} fusion(bf16[1024,4096]{1,0:T(8,128)(2,1)S(1)} %bitcast.366, bf16[256,1024]{1,0:T(8,128)(2,1)S(1)} %bitcast.343, bf16[256,1024]{1,0:T(8,128)(2,1)S(1)} %bitcast.342, bf16[32,8,8,128]{3,2,1,0:T(8,128)(2,1)S(1)} %bitcast.347, pred[256]{0:T(512)(128)(4,1)S(1)} %broadcast_in_dim.173, ...), kind=kOutput, calls=%fused_computation.7 | convolution fusion | flops 2149056512 | bytes 12059136 | tf_op jit(solution)/shard_map/dot_general | solution.py:140
  151.0 53.3 %all_to_all.10 = bf16[4,1024,256]{1,2,0:T(8,128)(2,1)S(1)} all-to-all(bf16[4,1024,256]{1,2,0:T(8,128)(2,1)S(1)} %bitcast.307), channel_id=1, replica_groups=mesh['seq'=8,'head'=4] {'head'}, dimensions={0} | all-to-all | bytes 4194304 | tf_op jit(solution)/shard_map/all_to_all | solution.py:147
  204.3 1.3 reduce_sum.71
  (156 shorter events, 12.1 us)
Async XLA Ops:
  0.0 4.9 %copy-start.12 = (bf16[256,1024]{1,0:T(8,128)(2,1)S(1)}, bf16[256,1024]{1,0:T(8,128)(2,1)}, u32[]{:S(2)}) copy-start(bf16[256,1024]{1,0:T(8,128)(2,1)} %param.10) | copy-start | bytes 1572868
  2.1 1.4 copy-start.15
  4.9 1.0 copy-start.2
  7.2 1.0 copy-start.11
  7.2 1.2 copy-start.13
  9.3 1.4 copy-start.6
  10.5 0.7 copy-start.18
  10.8 1.8 collective-permute-start
  12.7 7.0 %collective-permute-start.1 = (bf16[96,1024]{1,0:T(8,128)(2,1)S(1)}, bf16[96,1024]{1,0:T(8,128)(2,1)S(1)}, u32[]{:S(2)}, u32[]{:S(2)}) collective-permute-start(bf16[96,1024]{1,0:T(8,128)(2,1)S(1)} %dynamic-slice_bitcast_fusion.3), channel_id=1, source_target_pairs={{0,8},{4,12},{8,0},{12,4},{16,24},{20,28},{24,16},{28,20},{1,9},{5... | collective-permute-start | bytes 589832 | tf_op jit(solution)/shard_map/ppermute | solution.py:100
  19.7 4.7 %collective-permute-start.2 = (bf16[48,1024]{1,0:T(8,128)(2,1)S(1)}, bf16[48,1024]{1,0:T(8,128)(2,1)S(1)}, u32[]{:S(2)}, u32[]{:S(2)}) collective-permute-start(bf16[48,1024]{1,0:T(8,128)(2,1)S(1)} %dynamic-slice_bitcast_fusion.6), channel_id=1, source_target_pairs={{0,16},{4,20},{8,24},{12,28},{16,0},{20,4},{24,8},{28,12},{1,17},{... | collective-permute-start | bytes 294920 | tf_op jit(solution)/shard_map/ppermute | solution.py:100
  24.4 4.7 %collective-permute-start.3 = (bf16[48,1024]{1,0:T(8,128)(2,1)S(1)}, bf16[48,1024]{1,0:T(8,128)(2,1)S(1)}, u32[]{:S(2)}, u32[]{:S(2)}) collective-permute-start(bf16[48,1024]{1,0:T(8,128)(2,1)S(1)} %bitcast_add_fusion.2), channel_id=1, source_target_pairs={{0,16},{4,20},{8,24},{12,28},{16,0},{20,4},{24,8},{28,12},{1,17},{... | collective-permute-start | bytes 294920 | tf_op jit(solution)/shard_map/ppermute | solution.py:104
  29.2 5.7 %collective-permute-start.4 = (bf16[96,1024]{1,0:T(8,128)(2,1)S(1)}, bf16[96,1024]{1,0:T(8,128)(2,1)S(1)}, u32[]{:S(2)}, u32[]{:S(2)}) collective-permute-start(bf16[96,1024]{1,0:T(8,128)(2,1)S(1)} %get-tuple-element.67), channel_id=1, source_target_pairs={{0,8},{4,12},{8,0},{12,4},{16,24},{20,28},{24,16},{28,20},{1,9},{5... | collective-permute-start | bytes 589832 | tf_op jit(solution)/shard_map/ppermute | solution.py:104
  35.2 1.8 collective-permute-start.5
  37.4 0.9 copy-start.8
  39.6 10.8 %collective-permute-start.7 = (bf16[2,128,1024]{2,1,0:T(8,128)(2,1)}, bf16[2,128,1024]{2,1,0:T(8,128)(2,1)}, u32[]{:S(2)}, u32[]{:S(2)}) collective-permute-start(bf16[2,128,1024]{2,1,0:T(8,128)(2,1)} %get-tuple-element.41), channel_id=1, source_target_pairs={{4,0},{8,4},{12,8},{16,12},{20,16},{24,20},{28,24},{5,1},{9,5},{13... | collective-permute-start | bytes 1572872 | tf_op jit(solution)/shard_map/ppermute | solution.py:236
  41.6 10.8 %collective-permute-start.6 = (bf16[2,128,1024]{2,1,0:T(8,128)(2,1)}, bf16[2,128,1024]{2,1,0:T(8,128)(2,1)}, u32[]{:S(2)}, u32[]{:S(2)}) collective-permute-start(bf16[2,128,1024]{2,1,0:T(8,128)(2,1)} %get-tuple-element.42), channel_id=1, source_target_pairs={{0,4},{4,8},{8,12},{12,16},{16,20},{20,24},{24,28},{1,5},{5,9},{9,... | collective-permute-start | bytes 1572872 | tf_op jit(solution)/shard_map/ppermute | solution.py:233
  47.5 2.8 %copy-start.14 = (f32[16,8,8,128]{3,1,2,0:T(8,128)S(1)}, f32[16,8,8,128]{3,1,2,0:T(8,128)}, u32[]{:S(2)}) copy-start(f32[16,8,8,128]{3,1,2,0:T(8,128)} %copy.180) | copy-start | bytes 1572868
  50.3 4.9 %copy-start.17 = (s32[2]{0:T(128)S(1)}, s32[2]{0:T(128)}, u32[]{:S(2)}) copy-start(s32[2]{0:T(128)} %get-tuple-element.35) | copy-start | bytes 28
  50.3 5.5 %copy-start.16 = (pred[2]{0:T(512)(128)(4,1)S(1)}, pred[2]{0:T(512)(128)(4,1)}, u32[]{:S(2)}) copy-start(pred[2]{0:T(512)(128)(4,1)} %copy-done.15) | copy-start | bytes 10
  52.4 4.0 %collective-permute-start.8 = (f32[64,1152]{1,0:T(8,128)S(1)}, f32[64,1152]{1,0:T(8,128)S(1)}, u32[]{:S(2)}, u32[]{:S(2)}) collective-permute-start(f32[64,1152]{1,0:T(8,128)S(1)} %get-tuple-element.54), channel_id=1, source_target_pairs={{0,4},{4,0},{8,12},{12,8},{16,20},{20,16},{24,28},{28,24},{1,5},{5... | collective-permute-start | bytes 884744 | tf_op jit(solution)/shard_map/ppermute | solution.py:100
  57.0 6.2 %collective-permute-start.9 = (f32[32,1152]{1,0:T(8,128)S(1)}, f32[32,1152]{1,0:T(8,128)S(1)}, u32[]{:S(2)}, u32[]{:S(2)}) collective-permute-start(f32[32,1152]{1,0:T(8,128)S(1)} %get-tuple-element.64), channel_id=1, source_target_pairs={{0,8},{4,12},{8,0},{12,4},{16,24},{20,28},{24,16},{28,20},{1,9},{5... | collective-permute-start | bytes 442376 | tf_op jit(solution)/shard_map/ppermute | solution.py:100
  63.5 15.7 %copy-start.19 = (s32[8]{0:T(128)S(1)}, s32[8]{0:T(128)}, u32[]{:S(2)}) copy-start(s32[8]{0:T(128)} %param.15) | copy-start | bytes 100
  63.7 5.3 %collective-permute-start.10 = (f32[16,1152]{1,0:T(8,128)S(1)}, f32[16,1152]{1,0:T(8,128)S(1)}, u32[]{:S(2)}, u32[]{:S(2)}) collective-permute-start(f32[16,1152]{1,0:T(8,128)S(1)} %get-tuple-element.76), channel_id=1, source_target_pairs={{0,16},{4,20},{8,24},{12,28},{16,0},{20,4},{24,8},{28,12},{1,17},{... | collective-permute-start | bytes 221192 | tf_op jit(solution)/shard_map/ppermute | solution.py:100
  69.3 4.4 %collective-permute-start.11 = (f32[16,1152]{1,0:T(8,128)S(1)}, f32[16,1152]{1,0:T(8,128)S(1)}, u32[]{:S(2)}, u32[]{:S(2)}) collective-permute-start(f32[16,1152]{1,0:T(8,128)S(1)} %concatenate.87), channel_id=1, source_target_pairs={{0,16},{4,20},{8,24},{12,28},{16,0},{20,4},{24,8},{28,12},{1,17},{... | collective-permute-start | bytes 221192 | tf_op jit(solution)/shard_map/ppermute | solution.py:104
  73.8 5.2 %collective-permute-start.12 = (f32[32,1152]{1,0:T(8,128)S(1)}, f32[32,1152]{1,0:T(8,128)S(1)}, u32[]{:S(2)}, u32[]{:S(2)}) collective-permute-start(f32[32,1152]{1,0:T(8,128)S(1)} %get-tuple-element.71), channel_id=1, source_target_pairs={{0,8},{4,12},{8,0},{12,4},{16,24},{20,28},{24,16},{28,20},{1,9},{5... | collective-permute-start | bytes 442376 | tf_op jit(solution)/shard_map/ppermute | solution.py:104
  79.1 1.6 collective-permute-start.13
  81.7 5.1 %copy-start.7 = (bf16[256,1024]{1,0:T(8,128)(2,1)S(1)}, bf16[256,1024]{1,0:T(8,128)(2,1)}, u32[]{:S(2)}) copy-start(bf16[256,1024]{1,0:T(8,128)(2,1)} %copy-done.6) | copy-start | bytes 1572868
  81.7 52.7 %all-to-all-start = ((bf16[8,2,2,64,1024]{4,3,2,1,0:T(8,128)(2,1)}), bf16[8,2,2,64,1024]{4,3,2,1,0:T(8,128)(2,1)}, u32[]{:S(2)}, u32[]{:S(2)}) async-start(bf16[8,2,2,64,1024]{4,3,2,1,0:T(8,128)(2,1)} %bitcast.292), calls=%async_computation | async-start | bytes 8388608 | tf_op jit(solution)/shard_map/all_to_all | solution.py:296
  86.6 1.1 copy-start.9
  87.0 11.9 %copy-start.3 = (bf16[32,8,8,128]{3,2,1,0:T(8,128)(2,1)}, bf16[32,8,8,128]{3,2,1,0:T(8,128)(2,1)S(1)}, u32[]{:S(2)}) copy-start(bf16[32,8,8,128]{3,2,1,0:T(8,128)(2,1)S(1)} %copy.116) | copy-start | bytes 1572868
  100.7 2.0 copy-start
  100.7 2.0 slice-start
  100.8 2.2 %copy-start.10 = (f32[128,1152]{1,0:T(8,128)S(1)}, f32[128,1152]{1,0:T(8,128)}, u32[]{:S(2)}) copy-start(f32[128,1152]{1,0:T(8,128)} %pad_maximum_fusion.5) | copy-start | bytes 1769476
  140.6 1.0 copy-start.4
  140.6 3.0 %copy-start.5 = (bf16[224,8,8,128]{3,2,1,0:T(8,128)(2,1)S(1)}, bf16[224,8,8,128]{3,2,1,0:T(8,128)(2,1)}, u32[]{:S(2)}) copy-start(bf16[224,8,8,128]{3,2,1,0:T(8,128)(2,1)} %copy.118) | copy-start | bytes 11010052
  141.7 2.6 %copy-start.1 = (f32[4,8,64,448]{3,2,1,0:T(8,128)S(1)}, f32[4,8,64,448]{3,2,1,0:T(8,128)}, u32[]{:S(2)}) copy-start(f32[4,8,64,448]{3,2,1,0:T(8,128)} %copy-done) | copy-start | bytes 11010052
  142.9 5.4 %slice-start.1 = ((s8[8388608]{0:T(1024)(128)(4,1)}), s8[4194304]{0:T(1024)(128)(4,1)S(1)}, s32[]{:S(2)}) async-start(s8[8388608]{0:T(1024)(128)(4,1)} %bitcast.365), calls=%async_computation.3 | async-start | bytes 8388608
  144.3 4.0 %slice-start.2 = ((s8[8388608]{0:T(1024)(128)(4,1)}), s8[4194304]{0:T(1024)(128)(4,1)S(1)}, s32[]{:S(2)}) async-start(s8[8388608]{0:T(1024)(128)(4,1)} %bitcast.365), calls=%async_computation.4 | async-start | bytes 8388608

commit v16 on v15

--- a/solution.py
+++ b/solution.py
@@ -291,9 +291,9 @@
     packed, from_left, from_right, outgoing = lax.optimization_barrier(
         (packed, from_left, from_right, outgoing)
     )
+    incoming = lax.all_to_all(outgoing, "seq", split_axis=0, concat_axis=0, tiled=True)
+    packed, incoming = lax.optimization_barrier((packed, incoming))
     reduced = tree_reduce(packed, softmax_merge, "seq")
-    outgoing, reduced = lax.optimization_barrier((outgoing, reduced))
-    incoming = lax.all_to_all(outgoing, "seq", split_axis=0, concat_axis=0, tiled=True)
     my_owners = owners[seq_place]
     my_ranks = ranks[seq_place]
     random_k = incoming[my_owners, my_ranks, 0].reshape(blocks_here, RAND, BLOCK, width_here)

time: 206 us -> 211 us (1.024)
  matrix products: 10.7 us -> 19.1 us
  waiting for transfers between devices: 67 us -> 58.8 us
    ppermute x6, waiting for transfers between devices: 17 us -> 11.6 us  [tree_reduce(): got = lax.ppermute(parts, axis, xor_perm(count, bit))]
    dot_general x2, matrix products: 3.47 us -> 8.51 us  [partial_attend(): jnp.einsum('bhqs,bshd->bqhd', expo.astype(jnp.bfloat16), value_grid, pref...]
    all_to_all x1, starting transfers between devices: 4.89 us -> 8.31 us  [on_device(): lax.all_to_all(outgoing, 'seq', split_axis=0, concat_axis=0, tiled=True)]
    ppermute x6, starting transfers between devices: 7.52 us -> 4.1 us  [tree_reduce(): got = lax.ppermute(send, axis, xor_perm(count, bit))]
    dot_general x2, matrix products: 3.05 us -> 6.36 us  [partial_attend(): jnp.einsum('bqhd,bshd->bhqs', query_grid, key_grid, preferred_element_typ...]
    unnamed x55 -> x39, local copies, waits for them, and re-layouts: 10.7 us -> 10.6 us
  transfers between devices with their start and end apart: 15 -> 15, of which waited for: 13 -> 10; matrix products, arithmetic and copies ran while one was open for 14% -> 26% of each run, Pallas kernels for 0% -> 0%
where the time goes in v16:
time: 211 us; the launch traced here: 209 us
  waiting for transfers between devices  58.8 us (28%)
  blocking collectives  53.5 us (25%)
  local copies, waits for them, and re-layouts  32.6 us (15%)
  other arithmetic  21.6 us (10%)
  starting transfers between devices  21 us (10%)
  matrix products  19.1 us (9%)
  between operations  2.32 us (1%)
    all_to_all x1, blocking collectives, sum_over_head(): gathered = lax.all_to_all(partial, 'head', 0, 0, tiled=True)  53.5 us
    all_to_all x1, waiting for transfers between devices, on_device(): lax.all_to_all(outgoing, 'seq', split_axis=0, concat_axis=0, tiled=True)  30.1 us
    ppermute x6, waiting for transfers between devices, tree_reduce(): got = lax.ppermute(send, axis, xor_perm(count, bit))  15.7 us
    ppermute x6, waiting for transfers between devices, tree_reduce(): got = lax.ppermute(parts, axis, xor_perm(count, bit))  11.6 us
    unnamed x39, local copies, waits for them, and re-layouts  10.6 us
    dot_general x2, matrix products, partial_attend(): jnp.einsum('bhqs,bshd->bqhd', expo.astype(jnp.bfloat16), value_grid, pref...  8.51 us
    all_to_all x1, starting transfers between devices, on_device(): lax.all_to_all(outgoing, 'seq', split_axis=0, concat_axis=0, tiled=True)  8.31 us
    dot_general x2, matrix products, partial_attend(): jnp.einsum('bqhd,bshd->bhqs', query_grid, key_grid, preferred_element_typ...  6.36 us
  transfers between devices with their start and end apart: 15, of which 10 were waited for; matrix products, arithmetic and copies ran while one was open for 26% of the time, Pallas kernels for 0%

profile of v16, /device:TPU:2, one launch (start us, length us, event | category | flops | bytes accessed | tf_op | source)
XLA Modules:
  0.0 209.0 jit_solution(9742877217104123476)
XLA Ops:
  1.4 0.7 fusion.120
  2.1 0.7 compare_select_fusion.3
  2.9 1.1 convert_bitcast_fusion
  4.6 0.5 fusion.90
  5.2 0.8 pad_maximum_fusion.9
  6.0 0.6 gather_fusion.2
  6.5 0.7 slice_negate_fusion
  7.4 0.6 maximum_multiply_fusion.1
  8.1 0.4 copy-done.6
  8.5 1.0 fusion.48
  9.5 0.6 gather_fusion.1
  10.0 0.6 gather_fusion
  12.0 0.7 collective-permute-done
  12.9 6.9 %collective-permute-done.1 = bf16[96,1024]{1,0:T(8,128)(2,1)S(1)} collective-permute-done((bf16[96,1024]{1,0:T(8,128)(2,1)S(1)}, bf16[96,1024]{1,0:T(8,128)(2,1)S(1)}, u32[]{:S(2)}, u32[]{:S(2)}) %collective-permute-start.1) | collective-permute-done | bytes 196640 | tf_op jit(solution)/shard_map/ppermute | solution.py:100
  19.8 1.6 collective-permute-start.2
  21.6 3.0 %collective-permute-done.2 = bf16[48,1024]{1,0:T(8,128)(2,1)S(1)} collective-permute-done((bf16[48,1024]{1,0:T(8,128)(2,1)S(1)}, bf16[48,1024]{1,0:T(8,128)(2,1)S(1)}, u32[]{:S(2)}, u32[]{:S(2)}) %collective-permute-start.2) | collective-permute-done | bytes 98336 | tf_op jit(solution)/shard_map/ppermute | solution.py:100
  24.5 1.6 collective-permute-start.3
  26.1 0.6 fusion.137
  26.7 2.5 %collective-permute-done.3 = bf16[48,1024]{1,0:T(8,128)(2,1)S(1)} collective-permute-done((bf16[48,1024]{1,0:T(8,128)(2,1)S(1)}, bf16[48,1024]{1,0:T(8,128)(2,1)S(1)}, u32[]{:S(2)}, u32[]{:S(2)}) %collective-permute-start.3) | collective-permute-done | bytes 98336 | tf_op jit(solution)/shard_map/ppermute | solution.py:104
  29.3 0.4 collective-permute-start.4
  29.7 5.4 %collective-permute-done.4 = bf16[96,1024]{1,0:T(8,128)(2,1)S(1)} collective-permute-done((bf16[96,1024]{1,0:T(8,128)(2,1)S(1)}, bf16[96,1024]{1,0:T(8,128)(2,1)S(1)}, u32[]{:S(2)}, u32[]{:S(2)}) %collective-permute-start.4) | collective-permute-done | bytes 196640 | tf_op jit(solution)/shard_map/ppermute | solution.py:104
  35.4 0.6 fusion.136
  36.2 0.9 copy.107
  37.1 1.2 compare_and_fusion.1
  39.2 1.1 fusion.134
  40.3 2.3 %collective-permute-start.7 = (bf16[2,128,1024]{2,1,0:T(8,128)(2,1)}, bf16[2,128,1024]{2,1,0:T(8,128)(2,1)}, u32[]{:S(2)}, u32[]{:S(2)}) collective-permute-start(bf16[2,128,1024]{2,1,0:T(8,128)(2,1)} %get-tuple-element.41), channel_id=1, source_target_pairs={{4,0},{8,4},{12,8},{16,12},{20,16},{24,20},{28,24},{5,1},{9,5},{13... | collective-permute-start | bytes 1572872 | tf_op jit(solution)/shard_map/ppermute | solution.py:236
  42.5 2.0 collective-permute-start.6
  44.9 1.4 convolution_bitcast_fusion
  46.7 0.9 copy.182
  47.6 0.5 fusion.53
  48.2 2.8 %gather_fusion.3 = bf16[16,2,64,1024]{3,2,1,0:T(8,128)(2,1)} fusion(bf16[4,2,64,1024]{3,2,0,1:T(8,128)(2,1)S(1)} %bitcast.288, s32[1024]{0:T(1024)S(1)} %pad_clamp_fusion), kind=kCustom, calls=%fused_computation.3 | custom fusion | bytes 8388672 | tf_op jit(solution)/shard_map/gather | solution.py:290
  51.0 0.9 concatenate.78
  51.9 1.4 collective-permute-done.6
  53.4 8.3 %all-to-all-start = ((bf16[8,2,2,64,1024]{4,3,2,1,0:T(8,128)(2,1)}), bf16[8,2,2,64,1024]{4,3,2,1,0:T(8,128)(2,1)}, u32[]{:S(2)}, u32[]{:S(2)}) async-start(bf16[8,2,2,64,1024]{4,3,2,1,0:T(8,128)(2,1)} %bitcast.292), calls=%async_computation | async-start | bytes 8388608 | tf_op jit(solution)/shard_map/all_to_all | solution.py:294
  61.7 1.4 compare_and_fusion
  64.3 1.0 slice.227
  65.2 1.0 slice.226
  66.2 1.2 maximum_bitcast_fusion
  67.4 1.4 maximum_bitcast_fusion.1
  69.1 1.2 pad_maximum_fusion
  70.3 1.5 fusion.133
  71.8 1.0 copy.117
  72.8 2.7 %copy.118 = bf16[224,8,8,128]{3,2,1,0:T(8,128)(2,1)} copy(bf16[224,8,8,128]{3,1,2,0:T(8,128)(2,1)S(1)} %bitcast.297) | data formatting | bytes 7340032
  75.6 3.7 %fusion = (f32[4,8,64]{2,1,0:T(8,128)S(1)}, f32[4,8,64,448]{3,2,1,0:T(8,128)}) fusion(pred[4,8,448]{2,1,0:T(8,128)(4,1)S(1)} %broadcast_in_dim.179, bf16[4,448,8,128]{3,2,1,0:T(8,128)(2,1)S(1)} %bitcast.299, bf16[4,64,8,128]{3,2,1,0:T(8,128)(2,1)S(1)} %bitcast.311), kind=kOutput, calls=%fused_computation.10 | convolution fusion | flops 237631488 | bytes 7886848 | tf_op jit(solution)/shard_map/bqhd,bshd->bhqs/dot_general | solution.py:157
  79.3 30.1 %all-to-all-done = bf16[8,2,2,64,1024]{4,3,2,1,0:T(8,128)(2,1)} async-done(((bf16[8,2,2,64,1024]{4,3,2,1,0:T(8,128)(2,1)}), bf16[8,2,2,64,1024]{4,3,2,1,0:T(8,128)(2,1)}, u32[]{:S(2)}, u32[]{:S(2)}) %all-to-all-start) | async-done | bytes 4194336 | tf_op jit(solution)/shard_map/all_to_all | solution.py:294
  109.5 3.5 %fusion.5 = f32[4,8,64]{2,1,0:T(8,128)S(1)} fusion(f32[4,8,64,448]{3,2,1,0:T(8,128)} %get-tuple-element.88, f32[4,8,64]{2,1,0:T(8,128)S(1)} %get-tuple-element.87, pred[4,8,448]{2,1,0:T(8,128)(4,1)S(1)} %broadcast_in_dim.179), kind=kLoop, calls=%fused_computation.15 | loop fusion | flops 3667968 | bytes 3700736 | tf_op jit(solution)/shard_map/reduce_sum | solution.py:164
  113.0 2.8 %gather_fusion.4 = bf16[12,64,1024]{2,1,0:T(8,128)(2,1)S(1)} fusion(bf16[8,2,2,64,1024]{4,3,2,1,0:T(8,128)(2,1)} %all-to-all-done, s32[12]{0:T(128)S(1)} %bitcast.357), kind=kCustom, calls=%fused_computation.4 | custom fusion | bytes 3145872 | tf_op jit(solution)/shard_map/gather | solution.py:299
  115.9 1.6 copy.119
  118.1 1.6 collective-permute-start.9
  119.6 2.6 %multiply_reduce_fusion = (f32[4,8,64]{2,1,0:T(8,128)S(1)}, f32[4,8,64,192]{3,2,1,0:T(8,128)S(1)}) fusion(bf16[4,192,8,128]{3,2,1,0:T(8,128)(2,1)} %bitcast.310, bf16[4,64,8,128]{3,2,1,0:T(8,128)(2,1)S(1)} %bitcast.312), kind=kOutput, calls=%fused_computation.23 | convolution fusion | flops 101447680 | bytes 3678208 | tf_op jit(solution)/shard_map/bqhd,bshd->bhqs/dot_general | solution.py:157
  122.3 2.1 %collective-permute-done.9 = f32[32,1152]{1,0:T(8,128)S(1)} collective-permute-done((f32[32,1152]{1,0:T(8,128)S(1)}, f32[32,1152]{1,0:T(8,128)S(1)}, u32[]{:S(2)}, u32[]{:S(2)}) %collective-permute-start.9) | collective-permute-done | bytes 147488 | tf_op jit(solution)/shard_map/ppermute | solution.py:100
  124.8 0.7 collective-permute-start.10
  125.6 0.7 fusion.12
  126.3 3.0 %collective-permute-done.10 = f32[16,1152]{1,0:T(8,128)S(1)} collective-permute-done((f32[16,1152]{1,0:T(8,128)S(1)}, f32[16,1152]{1,0:T(8,128)S(1)}, u32[]{:S(2)}, u32[]{:S(2)}) %collective-permute-start.10) | collective-permute-done | bytes 73760 | tf_op jit(solution)/shard_map/ppermute | solution.py:100
  129.6 0.7 collective-permute-start.11
  130.3 3.7 %collective-permute-done.11 = f32[16,1152]{1,0:T(8,128)S(1)} collective-permute-done((f32[16,1152]{1,0:T(8,128)S(1)}, f32[16,1152]{1,0:T(8,128)S(1)}, u32[]{:S(2)}, u32[]{:S(2)}) %collective-permute-start.11) | collective-permute-done | bytes 73760 | tf_op jit(solution)/shard_map/ppermute | solution.py:104
  134.1 1.6 collective-permute-start.12
  135.6 6.0 %fusion.32 = f32[4,64,8,128]{3,1,2,0:T(8,128)} fusion(bf16[4,448,8,128]{3,2,1,0:T(8,128)(2,1)} %bitcast.316, f32[4,8,64,448]{3,2,1,0:T(8,128)} %get-tuple-element.88, f32[4,8,64]{2,1,0:T(8,128)S(1)} %get-tuple-element.87, pred[4,8,448]{2,1,0:T(8,128)(4,1)S(1)} %broadcast_in_dim.179, f32[4,64,8]{1,2,0:T(8,128)S(1)} %get-tuple-element.19), kind=kOutput, calls=%fused_computation.34 | convolution fusion | flops 238813184 | bytes 8419328 | tf_op jit(solution)/shard_map/bhqs,bshd->bqhd/dot_general | solution.py:165
  141.6 4.0 %gather_fusion.5 = bf16[12,64,1024]{2,1,0:T(8,128)(2,1)} fusion(bf16[8,2,2,64,1024]{4,3,2,1,0:T(8,128)(2,1)} %all-to-all-done, s32[12]{0:T(128)S(1)} %get-tuple-element.20), kind=kCustom, calls=%fused_computation.5 | custom fusion | bytes 3145872 | tf_op jit(solution)/shard_map/gather | solution.py:300
  145.6 2.0 copy.120
  147.9 2.5 %fusion.42 = bf16[4,64,8,128]{3,1,2,0:T(8,128)(2,1)S(1)} fusion(f32[4,64,8,128]{3,1,2,0:T(8,128)} %fusion.32, bf16[4,192,8,128]{3,2,1,0:T(8,128)(2,1)S(1)} %bitcast.328, f32[4,8,64,192]{3,2,1,0:T(8,128)S(1)} %get-tuple-element.90, f32[4,8,64]{2,1,0:T(8,128)S(1)} %get-tuple-element.89, f32[4,64,8]{1,2,0:T(8,128)S(1)} %get-tuple-element.17, ...), kind=kOutput, calls=%fused_computation.46 | convolution fusion | flops 102891520 | bytes 4743168 | tf_op jit(solution)/shard_map/bhqs,bshd->bqhd/dot_general | solution.py:165
  151.4 2.5 %convolution_convert_fusion = bf16[256,4096]{1,0:T(8,128)(2,1)S(1)} fusion(bf16[1024,4096]{1,0:T(8,128)(2,1)S(1)} %bitcast.366, bf16[256,1024]{1,0:T(8,128)(2,1)S(1)} %bitcast.343, bf16[256,1024]{1,0:T(8,128)(2,1)S(1)} %bitcast.342, bf16[32,8,8,128]{3,2,1,0:T(8,128)(2,1)S(1)} %bitcast.347, pred[256]{0:T(512)(128)(4,1)S(1)} %broadcast_in_dim.173, ...), kind=kOutput, calls=%fused_computation.7 | convolution fusion | flops 2149056512 | bytes 12059136 | tf_op jit(solution)/shard_map/dot_general | solution.py:140
  154.1 53.5 %all_to_all.10 = bf16[4,1024,256]{1,2,0:T(8,128)(2,1)S(1)} all-to-all(bf16[4,1024,256]{1,2,0:T(8,128)(2,1)S(1)} %bitcast.307), channel_id=1, replica_groups=mesh['seq'=8,'head'=4] {'head'}, dimensions={0} | all-to-all | bytes 4194304 | tf_op jit(solution)/shard_map/all_to_all | solution.py:147
  207.7 1.3 reduce_sum.71
  (138 shorter events, 9.1 us)
Async XLA Ops:
  0.0 4.3 %copy-start.7 = (bf16[256,1024]{1,0:T(8,128)(2,1)S(1)}, bf16[256,1024]{1,0:T(8,128)(2,1)}, u32[]{:S(2)}) copy-start(bf16[256,1024]{1,0:T(8,128)(2,1)} %param.10) | copy-start | bytes 1572868
  4.3 1.7 copy-start
  6.5 0.9 copy-start.9
  7.4 1.0 copy-start.6
  9.5 1.4 copy-start.1
  10.6 0.7 copy-start.10
  10.9 1.8 collective-permute-start
  12.8 7.0 %collective-permute-start.1 = (bf16[96,1024]{1,0:T(8,128)(2,1)S(1)}, bf16[96,1024]{1,0:T(8,128)(2,1)S(1)}, u32[]{:S(2)}, u32[]{:S(2)}) collective-permute-start(bf16[96,1024]{1,0:T(8,128)(2,1)S(1)} %dynamic-slice_bitcast_fusion.3), channel_id=1, source_target_pairs={{0,8},{4,12},{8,0},{12,4},{16,24},{20,28},{24,16},{28,20},{1,9},{5... | collective-permute-start | bytes 589832 | tf_op jit(solution)/shard_map/ppermute | solution.py:100
  19.8 4.7 %collective-permute-start.2 = (bf16[48,1024]{1,0:T(8,128)(2,1)S(1)}, bf16[48,1024]{1,0:T(8,128)(2,1)S(1)}, u32[]{:S(2)}, u32[]{:S(2)}) collective-permute-start(bf16[48,1024]{1,0:T(8,128)(2,1)S(1)} %dynamic-slice_bitcast_fusion.6), channel_id=1, source_target_pairs={{0,16},{4,20},{8,24},{12,28},{16,0},{20,4},{24,8},{28,12},{1,17},{... | collective-permute-start | bytes 294920 | tf_op jit(solution)/shard_map/ppermute | solution.py:100
  24.5 4.7 %collective-permute-start.3 = (bf16[48,1024]{1,0:T(8,128)(2,1)S(1)}, bf16[48,1024]{1,0:T(8,128)(2,1)S(1)}, u32[]{:S(2)}, u32[]{:S(2)}) collective-permute-start(bf16[48,1024]{1,0:T(8,128)(2,1)S(1)} %bitcast_add_fusion.2), channel_id=1, source_target_pairs={{0,16},{4,20},{8,24},{12,28},{16,0},{20,4},{24,8},{28,12},{1,17},{... | collective-permute-start | bytes 294920 | tf_op jit(solution)/shard_map/ppermute | solution.py:104
  29.3 5.7 %collective-permute-start.4 = (bf16[96,1024]{1,0:T(8,128)(2,1)S(1)}, bf16[96,1024]{1,0:T(8,128)(2,1)S(1)}, u32[]{:S(2)}, u32[]{:S(2)}) collective-permute-start(bf16[96,1024]{1,0:T(8,128)(2,1)S(1)} %get-tuple-element.67), channel_id=1, source_target_pairs={{0,8},{4,12},{8,0},{12,4},{16,24},{20,28},{24,16},{28,20},{1,9},{5... | collective-permute-start | bytes 589832 | tf_op jit(solution)/shard_map/ppermute | solution.py:104
  35.3 3.0 %collective-permute-start.5 = (bf16[192,1024]{1,0:T(8,128)(2,1)S(1)}, bf16[192,1024]{1,0:T(8,128)(2,1)S(1)}, u32[]{:S(2)}, u32[]{:S(2)}) collective-permute-start(bf16[192,1024]{1,0:T(8,128)(2,1)S(1)} %get-tuple-element.55), channel_id=1, source_target_pairs={{0,4},{4,0},{8,12},{12,8},{16,20},{20,16},{24,28},{28,24},{1,5},{5... | collective-permute-start | bytes 1179656 | tf_op jit(solution)/shard_map/ppermute | solution.py:104
  38.8 1.5 copy-start.3
  40.3 11.7 %collective-permute-start.7 = (bf16[2,128,1024]{2,1,0:T(8,128)(2,1)}, bf16[2,128,1024]{2,1,0:T(8,128)(2,1)}, u32[]{:S(2)}, u32[]{:S(2)}) collective-permute-start(bf16[2,128,1024]{2,1,0:T(8,128)(2,1)} %get-tuple-element.41), channel_id=1, source_target_pairs={{4,0},{8,4},{12,8},{16,12},{20,16},{24,20},{28,24},{5,1},{9,5},{13... | collective-permute-start | bytes 1572872 | tf_op jit(solution)/shard_map/ppermute | solution.py:236
  42.5 10.8 %collective-permute-start.6 = (bf16[2,128,1024]{2,1,0:T(8,128)(2,1)}, bf16[2,128,1024]{2,1,0:T(8,128)(2,1)}, u32[]{:S(2)}, u32[]{:S(2)}) collective-permute-start(bf16[2,128,1024]{2,1,0:T(8,128)(2,1)} %get-tuple-element.42), channel_id=1, source_target_pairs={{0,4},{4,8},{8,12},{12,16},{16,20},{20,24},{24,28},{1,5},{5,9},{9,... | collective-permute-start | bytes 1572872 | tf_op jit(solution)/shard_map/ppermute | solution.py:233
  48.1 2.9 %copy-start.8 = (f32[16,8,8,128]{3,1,2,0:T(8,128)S(1)}, f32[16,8,8,128]{3,1,2,0:T(8,128)}, u32[]{:S(2)}) copy-start(f32[16,8,8,128]{3,1,2,0:T(8,128)} %copy.182) | copy-start | bytes 1572868
  53.4 10.1 %copy-start.11 = (s32[8]{0:T(128)S(1)}, s32[8]{0:T(128)}, u32[]{:S(2)}) copy-start(s32[8]{0:T(128)} %param.15) | copy-start | bytes 100
  53.4 10.5 %copy-start.2 = (bf16[256,1024]{1,0:T(8,128)(2,1)S(1)}, bf16[256,1024]{1,0:T(8,128)(2,1)}, u32[]{:S(2)}) copy-start(bf16[256,1024]{1,0:T(8,128)(2,1)} %copy-done.1) | copy-start | bytes 1572868
  53.4 56.0 %all-to-all-start = ((bf16[8,2,2,64,1024]{4,3,2,1,0:T(8,128)(2,1)}), bf16[8,2,2,64,1024]{4,3,2,1,0:T(8,128)(2,1)}, u32[]{:S(2)}, u32[]{:S(2)}) async-start(bf16[8,2,2,64,1024]{4,3,2,1,0:T(8,128)(2,1)} %bitcast.292), calls=%async_computation | async-start | bytes 8388608 | tf_op jit(solution)/shard_map/all_to_all | solution.py:294
  61.7 2.5 %copy-start.4 = (bf16[384,1024]{1,0:T(8,128)(2,1)S(1)}, bf16[384,1024]{1,0:T(8,128)(2,1)}, u32[]{:S(2)}) copy-start(bf16[384,1024]{1,0:T(8,128)(2,1)} %copy-done.3) | copy-start | bytes 2359300
  75.5 33.8 %copy-start.5 = (f32[128,1152]{1,0:T(8,128)S(1)}, f32[128,1152]{1,0:T(8,128)}, u32[]{:S(2)}) copy-start(f32[128,1152]{1,0:T(8,128)} %concatenate.78) | copy-start | bytes 1769476
  109.4 8.0 %collective-permute-start.8 = (f32[64,1152]{1,0:T(8,128)S(1)}, f32[64,1152]{1,0:T(8,128)S(1)}, u32[]{:S(2)}, u32[]{:S(2)}) collective-permute-start(f32[64,1152]{1,0:T(8,128)S(1)} %get-tuple-element.54), channel_id=1, source_target_pairs={{0,4},{4,0},{8,12},{12,8},{16,20},{20,16},{24,28},{28,24},{1,5},{5... | collective-permute-start | bytes 884744 | tf_op jit(solution)/shard_map/ppermute | solution.py:100
  118.1 6.3 %collective-permute-start.9 = (f32[32,1152]{1,0:T(8,128)S(1)}, f32[32,1152]{1,0:T(8,128)S(1)}, u32[]{:S(2)}, u32[]{:S(2)}) collective-permute-start(f32[32,1152]{1,0:T(8,128)S(1)} %get-tuple-element.64), channel_id=1, source_target_pairs={{0,8},{4,12},{8,0},{12,4},{16,24},{20,28},{24,16},{28,20},{1,9},{5... | collective-permute-start | bytes 442376 | tf_op jit(solution)/shard_map/ppermute | solution.py:100
  124.8 4.4 %collective-permute-start.10 = (f32[16,1152]{1,0:T(8,128)S(1)}, f32[16,1152]{1,0:T(8,128)S(1)}, u32[]{:S(2)}, u32[]{:S(2)}) collective-permute-start(f32[16,1152]{1,0:T(8,128)S(1)} %get-tuple-element.76), channel_id=1, source_target_pairs={{0,16},{4,20},{8,24},{12,28},{16,0},{20,4},{24,8},{28,12},{1,17},{... | collective-permute-start | bytes 221192 | tf_op jit(solution)/shard_map/ppermute | solution.py:100
  129.6 4.4 %collective-permute-start.11 = (f32[16,1152]{1,0:T(8,128)S(1)}, f32[16,1152]{1,0:T(8,128)S(1)}, u32[]{:S(2)}, u32[]{:S(2)}) collective-permute-start(f32[16,1152]{1,0:T(8,128)S(1)} %concatenate.87), channel_id=1, source_target_pairs={{0,16},{4,20},{8,24},{12,28},{16,0},{20,4},{24,8},{28,12},{1,17},{... | collective-permute-start | bytes 221192 | tf_op jit(solution)/shard_map/ppermute | solution.py:104
  134.1 13.6 %collective-permute-start.12 = (f32[32,1152]{1,0:T(8,128)S(1)}, f32[32,1152]{1,0:T(8,128)S(1)}, u32[]{:S(2)}, u32[]{:S(2)}) collective-permute-start(f32[32,1152]{1,0:T(8,128)S(1)} %get-tuple-element.71), channel_id=1, source_target_pairs={{0,8},{4,12},{8,0},{12,4},{16,24},{20,28},{24,16},{28,20},{1,9},{5... | collective-permute-start | bytes 442376 | tf_op jit(solution)/shard_map/ppermute | solution.py:104
  145.6 5.8 %slice-start = ((s8[8388608]{0:T(1024)(128)(4,1)}), s8[4194304]{0:T(1024)(128)(4,1)S(1)}, s32[]{:S(2)}) async-start(s8[8388608]{0:T(1024)(128)(4,1)} %bitcast.365), calls=%async_computation.2 | async-start | bytes 8388608
  147.8 3.0 %collective-permute-start.13 = (f32[64,1152]{1,0:T(8,128)S(1)}, f32[64,1152]{1,0:T(8,128)S(1)}, u32[]{:S(2)}, u32[]{:S(2)}) collective-permute-start(f32[64,1152]{1,0:T(8,128)S(1)} %get-tuple-element.59), channel_id=1, source_target_pairs={{0,4},{4,0},{8,12},{12,8},{16,20},{20,16},{24,28},{28,24},{1,5},{5... | collective-permute-start | bytes 884744 | tf_op jit(solution)/shard_map/ppermute | solution.py:104
  147.9 3.6 %slice-start.1 = ((s8[8388608]{0:T(1024)(128)(4,1)}), s8[4194304]{0:T(1024)(128)(4,1)S(1)}, s32[]{:S(2)}) async-start(s8[8388608]{0:T(1024)(128)(4,1)} %bitcast.365), calls=%async_computation.3 | async-start | bytes 8388608

commit v17 on v16

--- a/solution.py
+++ b/solution.py
@@ -111,6 +111,25 @@
 
         parts = jax.tree.map(join, parts, got)
     return parts
+
+
+def tree_scatter(parts, merge, axis):
+    count = lax.axis_size(axis)
+    place = lax.axis_index(axis)
+    bit = 1
+    while bit < count:
+        upper = (place // bit) % 2
+        halves = parts.reshape((2, parts.shape[0] // 2) + parts.shape[1:])
+        keep = lax.dynamic_index_in_dim(halves, upper, 0, keepdims=False)
+        send = lax.dynamic_index_in_dim(halves, 1 - upper, 0, keepdims=False)
+        parts = merge(keep, lax.ppermute(send, axis, xor_perm(count, bit)))
+        bit *= 2
+    return parts
+
+
+def bit_reversed(count):
+    width = count.bit_length() - 1
+    return [int(format(i, "0%db" % width)[::-1], 2) if width else 0 for i in range(count)]
 
 
 def add_merge(a, b):
@@ -291,9 +310,24 @@
     packed, from_left, from_right, outgoing = lax.optimization_barrier(
         (packed, from_left, from_right, outgoing)
     )
+    slice_part = tree_scatter(packed, softmax_merge, "seq")
+    slice_rows = (
+        (slice_part[:, :width_here].reshape(-1, heads_here, HEAD_DIM) / slice_part[:, width_here : width_here + heads_here, None])
+        .reshape(-1, width_here)
+        .astype(jnp.bfloat16)
+    )
+    rows_each = slice_rows.shape[0]
+    kv_rows = capacity * 2 * BLOCK
+    outgoing = jnp.concatenate(
+        [
+            outgoing.reshape(seq_count, kv_rows, width_here),
+            jnp.broadcast_to(slice_rows[None], (seq_count, rows_each, width_here)),
+        ],
+        axis=1,
+    )
     incoming = lax.all_to_all(outgoing, "seq", split_axis=0, concat_axis=0, tiled=True)
-    packed, incoming = lax.optimization_barrier((packed, incoming))
-    reduced = tree_reduce(packed, softmax_merge, "seq")
+    global_rows = incoming[:, kv_rows:][jnp.array(bit_reversed(seq_count))]
+    incoming = incoming[:, :kv_rows].reshape(seq_count, capacity, 2, BLOCK, width_here)
     my_owners = owners[seq_place]
     my_ranks = ranks[seq_place]
     random_k = incoming[my_owners, my_ranks, 0].reshape(blocks_here, RAND, BLOCK, width_here)
@@ -304,9 +338,7 @@
         query_view, random_kv[0], random_kv[1], jnp.ones((blocks_here, RAND, heads_here), dtype=bool)
     )
     attended = merge_attend(near_part, far_part)
-    mix_sum = reduced[:, :width_here].reshape(row_total, heads_here, HEAD_DIM)
-    total_sum = reduced[:, width_here : width_here + heads_here]
-    global_out = (mix_sum / total_sum[..., None]).reshape(row_total, width_here).astype(jnp.bfloat16)
+    global_out = global_rows.reshape(row_total, width_here)
     global_out = global_out.reshape(GLOB, BLOCK, width_here)
     block_index = jnp.arange(blocks_here)
     for global_slot in range(GLOB):

time: 211 us -> 210 us (level)
  matrix products: 19.1 us -> 10.7 us
  local copies, waits for them, and re-layouts: 32.6 us -> 39.8 us
    ppermute x0 -> x3, waiting for transfers between devices: none -> 6.56 us  [tree_scatter(): parts = merge(keep, lax.ppermute(send, axis, xor_perm(count, bit)))]
    ppermute x0 -> x3, starting transfers between devices: none -> 6.15 us  [tree_scatter(): parts = merge(keep, lax.ppermute(send, axis, xor_perm(count, bit)))]
    slice x0 -> x2, local copies, waits for them, and re-layouts: none -> 5.62 us  [the longest x1 4.65 us: on_device(): incoming[:, :kv_rows].reshape(seq_count, capacity, 2, BLOCK, width_here)]
    dot_general x2, matrix products: 8.51 us -> 3.47 us  [partial_attend(): jnp.einsum('bhqs,bshd->bqhd', expo.astype(jnp.bfloat16), value_grid, pref...]
    concatenate x0 -> x1, other arithmetic: none -> 4.76 us  [on_device(): jnp.concatenate([outgoing.reshape(seq_count, kv_rows, width_here), jnp.br...]
    ppermute x6 -> x3, waiting for transfers between devices: 15.7 us -> 11.1 us  [tree_reduce(): got = lax.ppermute(send, axis, xor_perm(count, bit))]
    all_to_all x1, starting transfers between devices: 8.31 us -> 4.89 us  [on_device(): lax.all_to_all(outgoing, 'seq', split_axis=0, concat_axis=0, tiled=True)]
    dot_general x2, matrix products: 6.36 us -> 3.05 us  [partial_attend(): jnp.einsum('bqhd,bshd->bhqs', query_grid, key_grid, preferred_element_typ...]
  transfers between devices with their start and end apart: 15 -> 12, of which waited for: 10 -> 10; matrix products, arithmetic and copies ran while one was open for 26% -> 13% of each run, Pallas kernels for 0% -> 0%
where the time goes in v17:
time: 210 us; the launch traced here: 209 us
  waiting for transfers between devices  60.9 us (29%)
  blocking collectives  53.3 us (25%)
  local copies, waits for them, and re-layouts  39.8 us (19%)
  other arithmetic  23 us (11%)
  starting transfers between devices  19.1 us (9%)
  matrix products  10.7 us (5%)
  between operations  2.33 us (1%)
    all_to_all x1, blocking collectives, sum_over_head(): gathered = lax.all_to_all(partial, 'head', 0, 0, tiled=True)  53.3 us
    all_to_all x1, waiting for transfers between devices, on_device(): lax.all_to_all(outgoing, 'seq', split_axis=0, concat_axis=0, tiled=True)  32.8 us
    unnamed x45, local copies, waits for them, and re-layouts  12.5 us
    ppermute x3, waiting for transfers between devices, tree_reduce(): got = lax.ppermute(send, axis, xor_perm(count, bit))  11.1 us
    ppermute x3, waiting for transfers between devices, tree_reduce(): got = lax.ppermute(parts, axis, xor_perm(count, bit))  8.42 us
    ppermute x3, waiting for transfers between devices, tree_scatter(): parts = merge(keep, lax.ppermute(send, axis, xor_perm(count, bit)))  6.56 us
    ppermute x3, starting transfers between devices, tree_scatter(): parts = merge(keep, lax.ppermute(send, axis, xor_perm(count, bit)))  6.15 us
    all_to_all x1, starting transfers between devices, on_device(): lax.all_to_all(outgoing, 'seq', split_axis=0, concat_axis=0, tiled=True)  4.89 us
  transfers between devices with their start and end apart: 12, of which 10 were waited for; matrix products, arithmetic and copies ran while one was open for 13% of the time, Pallas kernels for 0%

profile of v17, /device:TPU:2, one launch (start us, length us, event | category | flops | bytes accessed | tf_op | source)
XLA Modules:
  0.0 209.1 jit_solution(16514631242779598296)
XLA Ops:
  1.4 0.7 fusion.107
  2.1 0.7 compare_select_fusion.3
  2.9 1.1 convert_bitcast_fusion
  4.6 0.5 fusion.79
  5.3 0.6 gather_fusion.2
  5.9 0.7 slice_negate_fusion
  6.6 0.6 maximum_multiply_fusion.1
  7.8 1.0 fusion.48
  8.8 0.6 gather_fusion.1
  9.4 0.6 gather_fusion
  10.8 1.2 collective-permute-done
  12.2 6.9 %collective-permute-done.1 = bf16[96,1024]{1,0:T(8,128)(2,1)S(1)} collective-permute-done((bf16[96,1024]{1,0:T(8,128)(2,1)S(1)}, bf16[96,1024]{1,0:T(8,128)(2,1)S(1)}, u32[]{:S(2)}, u32[]{:S(2)}) %collective-permute-start.1) | collective-permute-done | bytes 196640 | tf_op jit(solution)/shard_map/ppermute | solution.py:100
  19.2 1.6 collective-permute-start.2
  20.8 3.0 %collective-permute-done.2 = bf16[48,1024]{1,0:T(8,128)(2,1)S(1)} collective-permute-done((bf16[48,1024]{1,0:T(8,128)(2,1)S(1)}, bf16[48,1024]{1,0:T(8,128)(2,1)S(1)}, u32[]{:S(2)}, u32[]{:S(2)}) %collective-permute-start.2) | collective-permute-done | bytes 98336 | tf_op jit(solution)/shard_map/ppermute | solution.py:100
  23.9 1.6 collective-permute-start.3
  25.5 3.1 %collective-permute-done.3 = bf16[48,1024]{1,0:T(8,128)(2,1)S(1)} collective-permute-done((bf16[48,1024]{1,0:T(8,128)(2,1)S(1)}, bf16[48,1024]{1,0:T(8,128)(2,1)S(1)}, u32[]{:S(2)}, u32[]{:S(2)}) %collective-permute-start.3) | collective-permute-done | bytes 98336 | tf_op jit(solution)/shard_map/ppermute | solution.py:104
  29.6 4.8 %collective-permute-done.4 = bf16[96,1024]{1,0:T(8,128)(2,1)S(1)} collective-permute-done((bf16[96,1024]{1,0:T(8,128)(2,1)S(1)}, bf16[96,1024]{1,0:T(8,128)(2,1)S(1)}, u32[]{:S(2)}, u32[]{:S(2)}) %collective-permute-start.4) | collective-permute-done | bytes 196640 | tf_op jit(solution)/shard_map/ppermute | solution.py:104
  34.9 0.9 copy.108
  35.9 0.5 collective-permute-done.5
  37.2 1.1 fusion.121
  38.3 1.9 collective-permute-start.7
  40.2 2.4 %collective-permute-start.6 = (bf16[2,128,1024]{2,1,0:T(8,128)(2,1)}, bf16[2,128,1024]{2,1,0:T(8,128)(2,1)}, u32[]{:S(2)}, u32[]{:S(2)}) collective-permute-start(bf16[2,128,1024]{2,1,0:T(8,128)(2,1)} %get-tuple-element.37), channel_id=1, source_target_pairs={{0,4},{4,8},{8,12},{12,16},{16,20},{20,24},{24,28},{1,5},{5,9},{9,... | collective-permute-start | bytes 1572872 | tf_op jit(solution)/shard_map/ppermute | solution.py:252
  43.0 1.4 convolution_bitcast_fusion
  44.7 0.9 copy.181
  45.6 0.5 fusion.53
  46.2 2.8 %gather_fusion.3 = bf16[16,2,64,1024]{3,2,1,0:T(8,128)(2,1)} fusion(bf16[4,2,64,1024]{3,2,0,1:T(8,128)(2,1)S(1)} %bitcast.274, s32[1024]{0:T(1024)S(1)} %pad_clamp_fusion.1), kind=kCustom, calls=%fused_computation.3 | custom fusion | bytes 8388672 | tf_op jit(solution)/shard_map/gather | solution.py:309
  49.1 1.9 collective-permute-done.6
  51.1 2.8 %collective-permute-start.8 = (f32[64,1152]{1,0:T(8,128)S(1)}, f32[64,1152]{1,0:T(8,128)S(1)}, u32[]{:S(2)}, u32[]{:S(2)}) collective-permute-start(f32[64,1152]{1,0:T(8,128)S(1)} %get-tuple-element.47), channel_id=1, source_target_pairs={{0,4},{4,0},{8,12},{12,8},{16,20},{20,16},{24,28},{28,24},{1,5},{5... | collective-permute-start | bytes 884744 | tf_op jit(solution)/shard_map/ppermute | solution.py:125
  53.9 0.6 fusion.123
  54.5 0.6 fusion.124
  55.0 1.2 compare_and_fusion.1
  57.0 1.2 compare_and_fusion
  58.5 4.2 %collective-permute-done.9 = f32[32,1152]{1,0:T(8,128)S(1)} collective-permute-done((f32[32,1152]{1,0:T(8,128)S(1)}, f32[32,1152]{1,0:T(8,128)S(1)}, u32[]{:S(2)}, u32[]{:S(2)}) %collective-permute-start.9) | collective-permute-done | bytes 147488 | tf_op jit(solution)/shard_map/ppermute | solution.py:125
  63.2 3.3 %collective-permute-start.10 = (f32[16,1152]{1,0:T(8,128)S(1)}, f32[16,1152]{1,0:T(8,128)S(1)}, u32[]{:S(2)}, u32[]{:S(2)}) collective-permute-start(f32[16,1152]{1,0:T(8,128)S(1)} %get-tuple-element.61), channel_id=1, source_target_pairs={{0,16},{4,20},{8,24},{12,28},{16,0},{20,4},{24,8},{28,12},{1,17},{... | collective-permute-start | bytes 221192 | tf_op jit(solution)/shard_map/ppermute | solution.py:125
  66.5 2.3 %collective-permute-done.10 = f32[16,1152]{1,0:T(8,128)S(1)} collective-permute-done((f32[16,1152]{1,0:T(8,128)S(1)}, f32[16,1152]{1,0:T(8,128)S(1)}, u32[]{:S(2)}, u32[]{:S(2)}) %collective-permute-start.10) | collective-permute-done | bytes 73760 | tf_op jit(solution)/shard_map/ppermute | solution.py:125
  69.2 4.8 %pad_maximum_fusion.1 = bf16[8,272,1024]{2,1,0:T(8,128)(2,1)} fusion(bf16[8,16,1024]{2,1,0:T(8,128)(2,1)S(1)} %broadcast_in_dim.179, bf16[8,256,1024]{2,1,0:T(8,128)(2,1)} %bitcast.278), kind=kLoop, calls=%fused_computation.9 | loop fusion | flops 8912896 | bytes 8912896 | tf_op jit(solution)/shard_map/concatenate | solution.py:321
  74.0 4.9 %all-to-all-start = ((bf16[8,272,1024]{2,1,0:T(8,128)(2,1)}), bf16[8,272,1024]{2,1,0:T(8,128)(2,1)}, u32[]{:S(2)}, u32[]{:S(2)}) async-start(bf16[8,272,1024]{2,1,0:T(8,128)(2,1)} %pad_maximum_fusion.1), calls=%async_computation | async-start | bytes 8912896 | tf_op jit(solution)/shard_map/all_to_all | solution.py:328
  80.1 1.0 slice.228
  81.0 1.0 slice.227
  82.0 1.2 maximum_bitcast_fusion
  83.2 1.4 maximum_bitcast_fusion.1
  84.9 1.1 pad_maximum_fusion
  85.9 1.5 fusion.120
  87.5 1.0 copy.118
  88.4 2.8 %copy.119 = bf16[224,8,8,128]{3,2,1,0:T(8,128)(2,1)} copy(bf16[224,8,8,128]{3,1,2,0:T(8,128)(2,1)S(1)} %bitcast.283) | data formatting | bytes 7340032
  91.2 1.8 fusion
  93.0 2.1 copy-done
  95.1 1.5 fusion.5
  96.6 32.8 %all-to-all-done = bf16[8,272,1024]{2,1,0:T(8,128)(2,1)} async-done(((bf16[8,272,1024]{2,1,0:T(8,128)(2,1)}), bf16[8,272,1024]{2,1,0:T(8,128)(2,1)}, u32[]{:S(2)}, u32[]{:S(2)}) %all-to-all-start) | async-done | bytes 4456480 | tf_op jit(solution)/shard_map/all_to_all | solution.py:328
  129.4 1.0 slice.222
  130.4 0.6 gather_fusion.4
  131.0 4.6 %slice.231 = bf16[8,256,1024]{2,1,0:T(8,128)(2,1)} slice(bf16[8,272,1024]{2,1,0:T(8,128)(2,1)} %all-to-all-done), slice={[0:8], [0:256], [0:1024]} | slice | bytes 8388608 | tf_op jit(solution)/shard_map/slice | solution.py:330
  135.6 2.8 %gather_fusion.6 = bf16[12,64,1024]{2,1,0:T(8,128)(2,1)S(1)} fusion(bf16[8,2,2,64,1024]{4,3,2,1,0:T(8,128)(2,1)} %bitcast.286, s32[12]{0:T(128)S(1)} %get-tuple-element.16), kind=kCustom, calls=%fused_computation.6 | custom fusion | bytes 3145872 | tf_op jit(solution)/shard_map/gather | solution.py:334
  138.5 4.1 %gather_fusion.5 = bf16[12,64,1024]{2,1,0:T(8,128)(2,1)} fusion(bf16[8,2,2,64,1024]{4,3,2,1,0:T(8,128)(2,1)} %bitcast.287, s32[12]{0:T(128)S(1)} %bitcast.345), kind=kCustom, calls=%fused_computation.5 | custom fusion | bytes 3145872 | tf_op jit(solution)/shard_map/gather | solution.py:333
  142.6 1.8 copy.120
  144.4 0.4 copy.121
  144.9 1.2 multiply_reduce_fusion
  146.1 0.8 fusion.12
  146.9 0.9 copy-done.1
  147.8 2.1 fusion.32
  149.9 1.4 fusion.42
  151.8 2.5 %convolution_convert_fusion = bf16[256,4096]{1,0:T(8,128)(2,1)S(1)} fusion(bf16[1024,4096]{1,0:T(8,128)(2,1)S(1)} %bitcast.352, bf16[256,1024]{1,0:T(8,128)(2,1)S(1)} %bitcast.329, bf16[256,1024]{1,0:T(8,128)(2,1)S(1)} %bitcast.330, bf16[32,8,8,128]{3,2,1,0:T(8,128)(2,1)S(1)} %bitcast.334, pred[256]{0:T(512)(128)(4,1)S(1)} %broadcast_in_dim.185, ...), kind=kOutput, calls=%fused_computation.8 | convolution fusion | flops 2149056512 | bytes 12059136 | tf_op jit(solution)/shard_map/dot_general | solution.py:159
  154.5 53.3 %all_to_all.10 = bf16[4,1024,256]{1,2,0:T(8,128)(2,1)S(1)} all-to-all(bf16[4,1024,256]{1,2,0:T(8,128)(2,1)S(1)} %bitcast.295), channel_id=1, replica_groups=mesh['seq'=8,'head'=4] {'head'}, dimensions={0} | all-to-all | bytes 4194304 | tf_op jit(solution)/shard_map/all_to_all | solution.py:166
  207.8 1.3 reduce_sum.71
  (135 shorter events, 9.6 us)
Async XLA Ops:
  0.0 4.3 %copy-start.9 = (bf16[256,1024]{1,0:T(8,128)(2,1)S(1)}, bf16[256,1024]{1,0:T(8,128)(2,1)}, u32[]{:S(2)}) copy-start(bf16[256,1024]{1,0:T(8,128)(2,1)} %param.11) | copy-start | bytes 1572868
  4.3 1.0 copy-start.2
  6.6 1.0 copy-start.8
  6.6 1.2 copy-start.10
  8.8 1.4 copy-start.4
  9.9 0.7 copy-start.12
  10.2 1.8 collective-permute-start
  12.1 7.0 %collective-permute-start.1 = (bf16[96,1024]{1,0:T(8,128)(2,1)S(1)}, bf16[96,1024]{1,0:T(8,128)(2,1)S(1)}, u32[]{:S(2)}, u32[]{:S(2)}) collective-permute-start(bf16[96,1024]{1,0:T(8,128)(2,1)S(1)} %dynamic-slice_bitcast_fusion.3), channel_id=1, source_target_pairs={{0,8},{4,12},{8,0},{12,4},{16,24},{20,28},{24,16},{28,20},{1,9},{5... | collective-permute-start | bytes 589832 | tf_op jit(solution)/shard_map/ppermute | solution.py:100
  19.2 4.7 %collective-permute-start.2 = (bf16[48,1024]{1,0:T(8,128)(2,1)S(1)}, bf16[48,1024]{1,0:T(8,128)(2,1)S(1)}, u32[]{:S(2)}, u32[]{:S(2)}) collective-permute-start(bf16[48,1024]{1,0:T(8,128)(2,1)S(1)} %dynamic-slice_bitcast_fusion.6), channel_id=1, source_target_pairs={{0,16},{4,20},{8,24},{12,28},{16,0},{20,4},{24,8},{28,12},{1,17},{... | collective-permute-start | bytes 294920 | tf_op jit(solution)/shard_map/ppermute | solution.py:100
  23.9 4.7 %collective-permute-start.3 = (bf16[48,1024]{1,0:T(8,128)(2,1)S(1)}, bf16[48,1024]{1,0:T(8,128)(2,1)S(1)}, u32[]{:S(2)}, u32[]{:S(2)}) collective-permute-start(bf16[48,1024]{1,0:T(8,128)(2,1)S(1)} %bitcast_add_fusion.2), channel_id=1, source_target_pairs={{0,16},{4,20},{8,24},{12,28},{16,0},{20,4},{24,8},{28,12},{1,17},{... | collective-permute-start | bytes 294920 | tf_op jit(solution)/shard_map/ppermute | solution.py:104
  28.7 5.7 %collective-permute-start.4 = (bf16[96,1024]{1,0:T(8,128)(2,1)S(1)}, bf16[96,1024]{1,0:T(8,128)(2,1)S(1)}, u32[]{:S(2)}, u32[]{:S(2)}) collective-permute-start(bf16[96,1024]{1,0:T(8,128)(2,1)S(1)} %get-tuple-element.56), channel_id=1, source_target_pairs={{0,8},{4,12},{8,0},{12,4},{16,24},{20,28},{24,16},{28,20},{1,9},{5... | collective-permute-start | bytes 589832 | tf_op jit(solution)/shard_map/ppermute | solution.py:104
  34.6 1.8 collective-permute-start.5
  36.8 1.5 copy-start.6
  38.3 10.8 %collective-permute-start.7 = (bf16[2,128,1024]{2,1,0:T(8,128)(2,1)}, bf16[2,128,1024]{2,1,0:T(8,128)(2,1)}, u32[]{:S(2)}, u32[]{:S(2)}) collective-permute-start(bf16[2,128,1024]{2,1,0:T(8,128)(2,1)} %get-tuple-element.36), channel_id=1, source_target_pairs={{4,0},{8,4},{12,8},{16,12},{20,16},{24,20},{28,24},{5,1},{9,5},{13... | collective-permute-start | bytes 1572872 | tf_op jit(solution)/shard_map/ppermute | solution.py:255
  40.2 10.8 %collective-permute-start.6 = (bf16[2,128,1024]{2,1,0:T(8,128)(2,1)}, bf16[2,128,1024]{2,1,0:T(8,128)(2,1)}, u32[]{:S(2)}, u32[]{:S(2)}) collective-permute-start(bf16[2,128,1024]{2,1,0:T(8,128)(2,1)} %get-tuple-element.37), channel_id=1, source_target_pairs={{0,4},{4,8},{8,12},{12,16},{16,20},{20,24},{24,28},{1,5},{5,9},{9,... | collective-permute-start | bytes 1572872 | tf_op jit(solution)/shard_map/ppermute | solution.py:252
  46.2 2.8 %copy-start.11 = (f32[16,8,8,128]{3,1,2,0:T(8,128)S(1)}, f32[16,8,8,128]{3,1,2,0:T(8,128)}, u32[]{:S(2)}) copy-start(f32[16,8,8,128]{3,1,2,0:T(8,128)} %copy.181) | copy-start | bytes 1572868
  51.1 5.1 %collective-permute-start.8 = (f32[64,1152]{1,0:T(8,128)S(1)}, f32[64,1152]{1,0:T(8,128)S(1)}, u32[]{:S(2)}, u32[]{:S(2)}) collective-permute-start(f32[64,1152]{1,0:T(8,128)S(1)} %get-tuple-element.47), channel_id=1, source_target_pairs={{0,4},{4,0},{8,12},{12,8},{16,20},{20,16},{24,28},{28,24},{1,5},{5... | collective-permute-start | bytes 884744 | tf_op jit(solution)/shard_map/ppermute | solution.py:125
  56.9 5.8 %collective-permute-start.9 = (f32[32,1152]{1,0:T(8,128)S(1)}, f32[32,1152]{1,0:T(8,128)S(1)}, u32[]{:S(2)}, u32[]{:S(2)}) collective-permute-start(f32[32,1152]{1,0:T(8,128)S(1)} %get-tuple-element.53), channel_id=1, source_target_pairs={{0,8},{4,12},{8,0},{12,4},{16,24},{20,28},{24,16},{28,20},{1,9},{5... | collective-permute-start | bytes 442376 | tf_op jit(solution)/shard_map/ppermute | solution.py:125
  63.2 5.6 %collective-permute-start.10 = (f32[16,1152]{1,0:T(8,128)S(1)}, f32[16,1152]{1,0:T(8,128)S(1)}, u32[]{:S(2)}, u32[]{:S(2)}) collective-permute-start(f32[16,1152]{1,0:T(8,128)S(1)} %get-tuple-element.61), channel_id=1, source_target_pairs={{0,16},{4,20},{8,24},{12,28},{16,0},{20,4},{24,8},{28,12},{1,17},{... | collective-permute-start | bytes 221192 | tf_op jit(solution)/shard_map/ppermute | solution.py:125
  74.0 5.0 %copy-start.14 = (s32[8]{0:T(128)S(1)}, s32[8]{0:T(128)}, u32[]{:S(2)}) copy-start(s32[8]{0:T(128)} %param.16) | copy-start | bytes 100
  74.0 5.3 %copy-start.5 = (bf16[256,1024]{1,0:T(8,128)(2,1)S(1)}, bf16[256,1024]{1,0:T(8,128)(2,1)}, u32[]{:S(2)}) copy-start(bf16[256,1024]{1,0:T(8,128)(2,1)} %copy-done.4) | copy-start | bytes 1572868
  74.0 5.6 %copy-start.13 = (s32[8]{0:T(128)S(1)}, s32[8]{0:T(128)}, u32[]{:S(2)}) copy-start(s32[8]{0:T(128)} %constant.260) | copy-start | bytes 100
  74.0 55.4 %all-to-all-start = ((bf16[8,272,1024]{2,1,0:T(8,128)(2,1)}), bf16[8,272,1024]{2,1,0:T(8,128)(2,1)}, u32[]{:S(2)}, u32[]{:S(2)}) async-start(bf16[8,272,1024]{2,1,0:T(8,128)(2,1)} %pad_maximum_fusion.1), calls=%async_computation | async-start | bytes 8912896 | tf_op jit(solution)/shard_map/all_to_all | solution.py:328
  78.9 1.1 copy-start.7
  93.0 2.1 copy-start
  144.4 2.5 %copy-start.3 = (bf16[224,8,8,128]{3,2,1,0:T(8,128)(2,1)S(1)}, bf16[224,8,8,128]{3,2,1,0:T(8,128)(2,1)}, u32[]{:S(2)}) copy-start(bf16[224,8,8,128]{3,2,1,0:T(8,128)(2,1)} %copy.119) | copy-start | bytes 11010052
  144.9 3.0 %copy-start.1 = (f32[4,8,64,448]{3,2,1,0:T(8,128)S(1)}, f32[4,8,64,448]{3,2,1,0:T(8,128)}, u32[]{:S(2)}) copy-start(f32[4,8,64,448]{3,2,1,0:T(8,128)} %copy-done) | copy-start | bytes 11010052
  146.1 5.7 %slice-start = ((s8[8388608]{0:T(1024)(128)(4,1)}), s8[4194304]{0:T(1024)(128)(4,1)S(1)}, s32[]{:S(2)}) async-start(s8[8388608]{0:T(1024)(128)(4,1)} %bitcast.351), calls=%async_computation.2 | async-start | bytes 8388608
  147.8 4.0 %slice-start.1 = ((s8[8388608]{0:T(1024)(128)(4,1)}), s8[4194304]{0:T(1024)(128)(4,1)S(1)}, s32[]{:S(2)}) async-start(s8[8388608]{0:T(1024)(128)(4,1)} %bitcast.351), calls=%async_computation.3 | async-start | bytes 8388608

commit v18 on v17

--- a/solution.py
+++ b/solution.py
@@ -307,6 +307,15 @@
     send_local = jnp.sum(jnp.where(wanted, local_ids[:, None, :], 0), axis=2)
     kv_blocks = jnp.transpose(halo_kv.reshape(2, blocks_here, BLOCK, width_here), (1, 0, 2, 3))
     outgoing = kv_blocks[send_local]
+    kv_rows = capacity * 2 * BLOCK
+    rows_each = GLOB * BLOCK // seq_count
+    outgoing = jnp.concatenate(
+        [
+            outgoing.reshape(seq_count, kv_rows, width_here),
+            jnp.zeros((seq_count, rows_each, width_here), jnp.bfloat16),
+        ],
+        axis=1,
+    )
     packed, from_left, from_right, outgoing = lax.optimization_barrier(
         (packed, from_left, from_right, outgoing)
     )
@@ -316,22 +325,20 @@
         .reshape(-1, width_here)
         .astype(jnp.bfloat16)
     )
-    rows_each = slice_rows.shape[0]
-    kv_rows = capacity * 2 * BLOCK
-    outgoing = jnp.concatenate(
-        [
-            outgoing.reshape(seq_count, kv_rows, width_here),
-            jnp.broadcast_to(slice_rows[None], (seq_count, rows_each, width_here)),
-        ],
-        axis=1,
+    outgoing = lax.dynamic_update_slice(
+        outgoing, jnp.broadcast_to(slice_rows[None], (seq_count, rows_each, width_here)), (0, kv_rows, 0)
     )
     incoming = lax.all_to_all(outgoing, "seq", split_axis=0, concat_axis=0, tiled=True)
     global_rows = incoming[:, kv_rows:][jnp.array(bit_reversed(seq_count))]
-    incoming = incoming[:, :kv_rows].reshape(seq_count, capacity, 2, BLOCK, width_here)
     my_owners = owners[seq_place]
     my_ranks = ranks[seq_place]
-    random_k = incoming[my_owners, my_ranks, 0].reshape(blocks_here, RAND, BLOCK, width_here)
-    random_v = incoming[my_owners, my_ranks, 1].reshape(blocks_here, RAND, BLOCK, width_here)
+    slot_start = my_ranks * (2 * BLOCK)
+    random_k = jnp.stack(
+        [lax.dynamic_slice(incoming, (my_owners[j], slot_start[j], 0), (1, BLOCK, width_here))[0] for j in range(blocks_here * RAND)]
+    ).reshape(blocks_here, RAND, BLOCK, width_here)
+    random_v = jnp.stack(
+        [lax.dynamic_slice(incoming, (my_owners[j], slot_start[j] + BLOCK, 0), (1, BLOCK, width_here))[0] for j in range(blocks_here * RAND)]
+    ).reshape(blocks_here, RAND, BLOCK, width_here)
     random_kv = (random_k, random_v)
     near_part = partial_attend(query_view, near_kv[0], near_kv[1], near_valid)
     far_part = partial_attend(

time: 210 us -> 253 us (1.20)
  between operations: 2.33 us -> 62.7 us
  waiting for transfers between devices: 60.9 us -> 38.9 us
  local copies, waits for them, and re-layouts: 39.8 us -> 46 us
  other arithmetic: 23 us -> 18.8 us
  matrix products: 10.7 us -> 14.1 us
    all_to_all x1, waiting for transfers between devices: 32.8 us -> 14.1 us  [on_device(): lax.all_to_all(outgoing, 'seq', split_axis=0, concat_axis=0, tiled=True)]
    unnamed x45 -> x60, local copies, waits for them, and re-layouts: 12.5 us -> 22.4 us
    gather x2 -> x0, local copies, waits for them, and re-layouts: 6.92 us -> none  [the longest x1 4.08 us: on_device(): incoming[my_owners, my_ranks, 0]]
    concatenate x0 -> x1, local copies, waits for them, and re-layouts: none -> 4.78 us  [on_device(): jnp.concatenate([outgoing.reshape(seq_count, kv_rows, width_here), jnp.ze...]
    concatenate x2 -> x0, other arithmetic: 4.78 us -> none  [the longest x1 4.76 us: on_device(): jnp.concatenate([outgoing.reshape(seq_count, kv_rows, width_here), jnp.br...]
    ppermute x3, starting transfers between devices: 6.15 us -> 2.39 us  [tree_scatter(): parts = merge(keep, lax.ppermute(send, axis, xor_perm(count, bit)))]
    dot_general x1, matrix products: 2.48 us -> 5.82 us  [head_partials(): lax.dot_general(out_weight, rows, (((0,), (1,)), ((), ())), preferred_ele...]
    slice x1 -> x2, local copies, waits for them, and re-layouts: 4.65 us -> 1.31 us  [the longest x1 0.69 us: on_device(): my_owners[j]]
  transfers between devices with their start and end apart: 12 -> 12, of which waited for: 10 -> 8; matrix products, arithmetic and copies ran while one was open for 13% -> 13% of each run, Pallas kernels for 0% -> 0%
where the time goes in v18:
time: 253 us; the launch traced here: 251 us
  between operations  62.7 us (25%)
  blocking collectives  53.1 us (21%)
  local copies, waits for them, and re-layouts  46 us (18%)
  waiting for transfers between devices  38.9 us (15%)
  other arithmetic  18.8 us (7%)
  starting transfers between devices  17.7 us (7%)
  matrix products  14.1 us (6%)
    all_to_all x1, blocking collectives, sum_over_head(): gathered = lax.all_to_all(partial, 'head', 0, 0, tiled=True)  53.1 us
    unnamed x60, local copies, waits for them, and re-layouts  22.4 us
    all_to_all x1, waiting for transfers between devices, on_device(): lax.all_to_all(outgoing, 'seq', split_axis=0, concat_axis=0, tiled=True)  14.1 us
    ppermute x3, waiting for transfers between devices, tree_reduce(): got = lax.ppermute(send, axis, xor_perm(count, bit))  11.6 us
    ppermute x3, waiting for transfers between devices, tree_reduce(): got = lax.ppermute(parts, axis, xor_perm(count, bit))  8.48 us
    all_to_all x1, starting transfers between devices, on_device(): lax.all_to_all(outgoing, 'seq', split_axis=0, concat_axis=0, tiled=True)  6.05 us
    dot_general x1, matrix products, head_partials(): lax.dot_general(out_weight, rows, (((0,), (1,)), ((), ())), preferred_ele...  5.82 us
  transfers between devices with their start and end apart: 12, of which 8 were waited for; matrix products, arithmetic and copies ran while one was open for 13% of the time, Pallas kernels for 0%

profile of v18, /device:TPU:2, one launch (start us, length us, event | category | flops | bytes accessed | tf_op | source)
XLA Modules:
  0.0 251.4 jit_solution(16114942551784452270)
XLA Ops:
  0.0 0.8 copy.60
  2.3 1.2 convert_bitcast_fusion.1
  6.1 0.7 slice_negate_fusion
  8.0 1.0 fusion.48
  11.3 1.7 collective-permute-done
  13.2 6.9 %collective-permute-done.1 = bf16[96,1024]{1,0:T(8,128)(2,1)S(1)} collective-permute-done((bf16[96,1024]{1,0:T(8,128)(2,1)S(1)}, bf16[96,1024]{1,0:T(8,128)(2,1)S(1)}, u32[]{:S(2)}, u32[]{:S(2)}) %collective-permute-start.1) | collective-permute-done | bytes 196640 | tf_op jit(solution)/shard_map/ppermute | solution.py:100
  20.1 1.6 collective-permute-start.2
  21.7 3.1 %collective-permute-done.2 = bf16[48,1024]{1,0:T(8,128)(2,1)S(1)} collective-permute-done((bf16[48,1024]{1,0:T(8,128)(2,1)S(1)}, bf16[48,1024]{1,0:T(8,128)(2,1)S(1)}, u32[]{:S(2)}, u32[]{:S(2)}) %collective-permute-start.2) | collective-permute-done | bytes 98336 | tf_op jit(solution)/shard_map/ppermute | solution.py:100
  24.8 1.6 collective-permute-start.3
  26.4 3.1 %collective-permute-done.3 = bf16[48,1024]{1,0:T(8,128)(2,1)S(1)} collective-permute-done((bf16[48,1024]{1,0:T(8,128)(2,1)S(1)}, bf16[48,1024]{1,0:T(8,128)(2,1)S(1)}, u32[]{:S(2)}, u32[]{:S(2)}) %collective-permute-start.3) | collective-permute-done | bytes 98336 | tf_op jit(solution)/shard_map/ppermute | solution.py:104
  30.0 5.4 %collective-permute-done.4 = bf16[96,1024]{1,0:T(8,128)(2,1)S(1)} collective-permute-done((bf16[96,1024]{1,0:T(8,128)(2,1)S(1)}, bf16[96,1024]{1,0:T(8,128)(2,1)S(1)}, u32[]{:S(2)}, u32[]{:S(2)}) %collective-permute-start.4) | collective-permute-done | bytes 196640 | tf_op jit(solution)/shard_map/ppermute | solution.py:104
  35.7 0.9 copy.87
  38.2 1.2 fusion.115
  39.3 2.4 collective-permute-start.6
  41.7 3.2 %collective-permute-start.7 = (bf16[2,128,1024]{2,1,0:T(8,128)(2,1)}, bf16[2,128,1024]{2,1,0:T(8,128)(2,1)}, u32[]{:S(2)}, u32[]{:S(2)}) collective-permute-start(bf16[2,128,1024]{2,1,0:T(8,128)(2,1)} %get-tuple-element.58), channel_id=1, source_target_pairs={{4,0},{8,4},{12,8},{16,12},{20,16},{24,20},{28,24},{5,1},{9,5},{13... | collective-permute-start | bytes 1572872 | tf_op jit(solution)/shard_map/ppermute | solution.py:255
  46.3 1.4 convolution_bitcast_fusion
  48.2 2.8 %gather_fusion.3 = bf16[16,2,64,1024]{3,2,1,0:T(8,128)(2,1)} fusion(bf16[4,2,64,1024]{3,2,0,1:T(8,128)(2,1)S(1)} %bitcast.285, s32[1024]{0:T(1024)S(1)} %get-tuple-element.126), kind=kCustom, calls=%fused_computation.3 | custom fusion | bytes 8388672 | tf_op jit(solution)/shard_map/gather | solution.py:309
  50.9 4.8 %concatenate.64 = bf16[8,272,1024]{2,1,0:T(8,128)(2,1)} pad(bf16[8,256,1024]{2,1,0:T(8,128)(2,1)} %bitcast.289, bf16[]{:T(256)} %constant.218.clone.1), padding=0_0x0_16x0_0 | pad | bytes 8650754 | tf_op jit(solution)/shard_map/concatenate | solution.py:312
  55.9 0.7 collective-permute-start.8
  56.7 1.1 collective-permute-done.8
  58.5 0.6 collective-permute-start.9
  59.1 0.7 fusion.120
  61.2 3.5 %collective-permute-done.9 = f32[32,1152]{1,0:T(8,128)S(1)} collective-permute-done((f32[32,1152]{1,0:T(8,128)S(1)}, f32[32,1152]{1,0:T(8,128)S(1)}, u32[]{:S(2)}, u32[]{:S(2)}) %collective-permute-start.9) | collective-permute-done | bytes 147488 | tf_op jit(solution)/shard_map/ppermute | solution.py:125
  65.1 1.1 collective-permute-start.10
  66.2 0.6 fusion.117
  111.1 0.7 broadcast_dynamic-update-slice_fusion
  111.9 6.1 %all-to-all-start = ((bf16[8,272,1024]{2,1,0:T(8,128)(2,1)}), bf16[8,272,1024]{2,1,0:T(8,128)(2,1)}, u32[]{:S(2)}, u32[]{:S(2)}) async-start(bf16[8,272,1024]{2,1,0:T(8,128)(2,1)} %broadcast_dynamic-update-slice_fusion), calls=%async_computation | async-start | bytes 8912896 | tf_op jit(solution)/shard_map/all_to_all | solution.py:331
  118.3 0.6 fusion.118
  119.0 0.7 fusion.119
  119.7 1.3 compare_and_fusion.1
  121.1 1.2 compare_and_fusion
  137.8 1.0 slice.361
  138.8 1.0 slice.362
  139.8 1.2 maximum_bitcast_fusion
  141.0 1.4 maximum_bitcast_fusion.1
  142.6 1.1 pad_maximum_fusion
  143.7 1.5 fusion.114
  145.2 1.0 copy.97
  146.2 2.7 %copy.98 = bf16[224,8,8,128]{3,2,1,0:T(8,128)(2,1)} copy(bf16[224,8,8,128]{3,1,2,0:T(8,128)(2,1)S(1)} %bitcast.294) | data formatting | bytes 7340032
  148.9 1.8 fusion
  150.8 2.1 copy-done
  152.9 1.5 fusion.5
  154.4 14.1 %all-to-all-done = bf16[8,272,1024]{2,1,0:T(8,128)(2,1)} async-done(((bf16[8,272,1024]{2,1,0:T(8,128)(2,1)}), bf16[8,272,1024]{2,1,0:T(8,128)(2,1)}, u32[]{:S(2)}, u32[]{:S(2)}) %all-to-all-start) | async-done | bytes 4456480 | tf_op jit(solution)/shard_map/all_to_all | solution.py:331
  168.5 1.1 dynamic-slice_dynamic-update-slice_fusion.11
  169.5 1.1 dynamic-slice_dynamic-update-slice_fusion.10
  170.6 1.1 dynamic-slice_dynamic-update-slice_fusion.9
  171.7 1.1 dynamic-slice_dynamic-update-slice_fusion.8
  172.8 1.1 dynamic-slice_dynamic-update-slice_fusion.7
  173.8 1.1 dynamic-slice_dynamic-update-slice_fusion.6
  174.9 1.1 dynamic-slice_dynamic-update-slice_fusion.5
  176.0 1.1 dynamic-slice_dynamic-update-slice_fusion.4
  177.0 1.1 dynamic-slice_dynamic-update-slice_fusion.3
  178.1 1.1 dynamic-slice_dynamic-update-slice_fusion.2
  179.2 1.1 dynamic-slice_dynamic-update-slice_fusion.1
  180.3 1.1 dynamic-slice_dynamic-update-slice_fusion
  181.8 1.2 multiply_reduce_fusion
  183.5 0.8 fusion.12
  184.3 1.1 copy-done.1
  185.4 2.1 fusion.32
  187.5 1.4 fusion.42
  189.2 1.0 slice.356
  190.9 5.8 %convolution_convert_fusion = bf16[256,4096]{1,0:T(8,128)(2,1)S(1)} fusion(bf16[1024,4096]{1,0:T(8,128)(2,1)} %param.13, bf16[256,1024]{1,0:T(8,128)(2,1)S(1)} %bitcast.338, bf16[256,1024]{1,0:T(8,128)(2,1)S(1)} %bitcast.339, bf16[32,8,8,128]{3,2,1,0:T(8,128)(2,1)S(1)} %bitcast.343, pred[256]{0:T(512)(128)(4,1)S(1)} %broadcast_in_dim.182, ...), kind=kOutput, calls=%fused_computation.6 | convolution fusion | flops 2149056512 | bytes 12059136 | tf_op jit(solution)/shard_map/dot_general | solution.py:159
  197.0 53.1 %all_to_all.10 = bf16[4,1024,256]{1,2,0:T(8,128)(2,1)S(1)} all-to-all(bf16[4,1024,256]{1,2,0:T(8,128)(2,1)S(1)} %bitcast.304), channel_id=1, replica_groups=mesh['seq'=8,'head'=4] {'head'}, dimensions={0} | all-to-all | bytes 4194304 | tf_op jit(solution)/shard_map/all_to_all | solution.py:166
  250.1 1.3 reduce_sum.71
  (148 shorter events, 15.3 us)
Async XLA Ops:
  2.3 1.4 copy-start.8
  3.7 1.2 copy-start.15
  4.9 5.8 %copy-start.11 = (pred[2]{0:T(512)(128)(4,1)}, pred[2]{0:T(512)(128)(4,1)S(1)}, u32[]{:S(2)}) copy-start(pred[2]{0:T(512)(128)(4,1)S(1)} %fusion.102) | copy-start | bytes 10
  6.8 1.0 copy-start.9
  6.8 1.2 copy-start.10
  8.0 2.1 copy-start.2
  9.0 2.0 copy-start.4
  11.2 1.8 collective-permute-start
  13.1 7.0 %collective-permute-start.1 = (bf16[96,1024]{1,0:T(8,128)(2,1)S(1)}, bf16[96,1024]{1,0:T(8,128)(2,1)S(1)}, u32[]{:S(2)}, u32[]{:S(2)}) collective-permute-start(bf16[96,1024]{1,0:T(8,128)(2,1)S(1)} %dynamic-slice_bitcast_fusion.3), channel_id=1, source_target_pairs={{0,8},{4,12},{8,0},{12,4},{16,24},{20,28},{24,16},{28,20},{1,9},{5... | collective-permute-start | bytes 589832 | tf_op jit(solution)/shard_map/ppermute | solution.py:100
  20.1 4.7 %collective-permute-start.2 = (bf16[48,1024]{1,0:T(8,128)(2,1)S(1)}, bf16[48,1024]{1,0:T(8,128)(2,1)S(1)}, u32[]{:S(2)}, u32[]{:S(2)}) collective-permute-start(bf16[48,1024]{1,0:T(8,128)(2,1)S(1)} %dynamic-slice_bitcast_fusion.6), channel_id=1, source_target_pairs={{0,16},{4,20},{8,24},{12,28},{16,0},{20,4},{24,8},{28,12},{1,17},{... | collective-permute-start | bytes 294920 | tf_op jit(solution)/shard_map/ppermute | solution.py:100
  24.8 4.7 %collective-permute-start.3 = (bf16[48,1024]{1,0:T(8,128)(2,1)S(1)}, bf16[48,1024]{1,0:T(8,128)(2,1)S(1)}, u32[]{:S(2)}, u32[]{:S(2)}) collective-permute-start(bf16[48,1024]{1,0:T(8,128)(2,1)S(1)} %bitcast_add_fusion.2), channel_id=1, source_target_pairs={{0,16},{4,20},{8,24},{12,28},{16,0},{20,4},{24,8},{28,12},{1,17},{... | collective-permute-start | bytes 294920 | tf_op jit(solution)/shard_map/ppermute | solution.py:104
  29.6 5.7 %collective-permute-start.4 = (bf16[96,1024]{1,0:T(8,128)(2,1)S(1)}, bf16[96,1024]{1,0:T(8,128)(2,1)S(1)}, u32[]{:S(2)}, u32[]{:S(2)}) collective-permute-start(bf16[96,1024]{1,0:T(8,128)(2,1)S(1)} %get-tuple-element.78), channel_id=1, source_target_pairs={{0,8},{4,12},{8,0},{12,4},{16,24},{20,28},{24,16},{28,20},{1,9},{5... | collective-permute-start | bytes 589832 | tf_op jit(solution)/shard_map/ppermute | solution.py:104
  35.6 2.2 collective-permute-start.5
  38.2 6.8 %copy-start.6 = (bf16[384,1024]{1,0:T(8,128)(2,1)}, bf16[384,1024]{1,0:T(8,128)(2,1)S(1)}, u32[]{:S(2)}) copy-start(bf16[384,1024]{1,0:T(8,128)(2,1)S(1)} %pad_maximum_fusion.4) | copy-start | bytes 2359300
  39.3 16.5 %collective-permute-start.6 = (bf16[2,128,1024]{2,1,0:T(8,128)(2,1)}, bf16[2,128,1024]{2,1,0:T(8,128)(2,1)}, u32[]{:S(2)}, u32[]{:S(2)}) collective-permute-start(bf16[2,128,1024]{2,1,0:T(8,128)(2,1)} %get-tuple-element.59), channel_id=1, source_target_pairs={{0,4},{4,8},{8,12},{12,16},{16,20},{20,24},{24,28},{1,5},{5,9},{9,... | collective-permute-start | bytes 1572872 | tf_op jit(solution)/shard_map/ppermute | solution.py:252
  41.7 14.1 %collective-permute-start.7 = (bf16[2,128,1024]{2,1,0:T(8,128)(2,1)}, bf16[2,128,1024]{2,1,0:T(8,128)(2,1)}, u32[]{:S(2)}, u32[]{:S(2)}) collective-permute-start(bf16[2,128,1024]{2,1,0:T(8,128)(2,1)} %get-tuple-element.58), channel_id=1, source_target_pairs={{4,0},{8,4},{12,8},{16,12},{20,16},{24,20},{28,24},{5,1},{9,5},{13... | collective-permute-start | bytes 1572872 | tf_op jit(solution)/shard_map/ppermute | solution.py:255
  55.7 0.9 copy-start.17
  55.7 0.9 copy-start.18
  55.9 1.9 collective-permute-start.8
  58.4 52.3 %copy-start.5 = (bf16[256,1024]{1,0:T(8,128)(2,1)S(1)}, bf16[256,1024]{1,0:T(8,128)(2,1)}, u32[]{:S(2)}) copy-start(bf16[256,1024]{1,0:T(8,128)(2,1)} %copy-done.4) | copy-start | bytes 1572868
  58.5 6.2 %collective-permute-start.9 = (f32[32,1152]{1,0:T(8,128)S(1)}, f32[32,1152]{1,0:T(8,128)S(1)}, u32[]{:S(2)}, u32[]{:S(2)}) collective-permute-start(f32[32,1152]{1,0:T(8,128)S(1)} %get-tuple-element.75), channel_id=1, source_target_pairs={{0,8},{4,12},{8,0},{12,4},{16,24},{20,28},{24,16},{28,20},{1,9},{5... | collective-permute-start | bytes 442376 | tf_op jit(solution)/shard_map/ppermute | solution.py:125
  65.1 45.6 %collective-permute-start.10 = (f32[16,1152]{1,0:T(8,128)S(1)}, f32[16,1152]{1,0:T(8,128)S(1)}, u32[]{:S(2)}, u32[]{:S(2)}) collective-permute-start(f32[16,1152]{1,0:T(8,128)S(1)} %get-tuple-element.83), channel_id=1, source_target_pairs={{0,16},{4,20},{8,24},{12,28},{16,0},{20,4},{24,8},{28,12},{1,17},{... | collective-permute-start | bytes 221192 | tf_op jit(solution)/shard_map/ppermute | solution.py:125
  111.9 6.1 %copy-start.16 = (s32[8]{0:T(128)S(1)}, s32[8]{0:T(128)}, u32[]{:S(2)}) copy-start(s32[8]{0:T(128)} %param.16) | copy-start | bytes 100
  111.9 6.5 %copy-start.13 = (s32[2]{0:T(128)S(1)}, s32[2]{0:T(128)}, u32[]{:S(2)}) copy-start(s32[2]{0:T(128)} %get-tuple-element.28) | copy-start | bytes 28
  111.9 7.1 %copy-start.12 = (pred[2]{0:T(512)(128)(4,1)S(1)}, pred[2]{0:T(512)(128)(4,1)}, u32[]{:S(2)}) copy-start(pred[2]{0:T(512)(128)(4,1)} %copy-done.11) | copy-start | bytes 10
  111.9 25.8 %copy-start.14 = (s32[8]{0:T(128)S(1)}, s32[8]{0:T(128)}, u32[]{:S(2)}) copy-start(s32[8]{0:T(128)} %constant.239) | copy-start | bytes 100
  111.9 56.6 %all-to-all-start = ((bf16[8,272,1024]{2,1,0:T(8,128)(2,1)}), bf16[8,272,1024]{2,1,0:T(8,128)(2,1)}, u32[]{:S(2)}, u32[]{:S(2)}) async-start(bf16[8,272,1024]{2,1,0:T(8,128)(2,1)} %broadcast_dynamic-update-slice_fusion), calls=%async_computation | async-start | bytes 8912896 | tf_op jit(solution)/shard_map/all_to_all | solution.py:331
  117.9 19.9 %copy-start.7 = (bf16[384,1024]{1,0:T(8,128)(2,1)S(1)}, bf16[384,1024]{1,0:T(8,128)(2,1)}, u32[]{:S(2)}) copy-start(bf16[384,1024]{1,0:T(8,128)(2,1)} %copy-done.6) | copy-start | bytes 2359300
  150.8 2.1 copy-start
  181.8 2.5 copy-start.3
  183.0 2.4 copy-start.1

commit v19 on v18

--- a/solution.py
+++ b/solution.py
@@ -332,13 +332,9 @@
     global_rows = incoming[:, kv_rows:][jnp.array(bit_reversed(seq_count))]
     my_owners = owners[seq_place]
     my_ranks = ranks[seq_place]
-    slot_start = my_ranks * (2 * BLOCK)
-    random_k = jnp.stack(
-        [lax.dynamic_slice(incoming, (my_owners[j], slot_start[j], 0), (1, BLOCK, width_here))[0] for j in range(blocks_here * RAND)]
-    ).reshape(blocks_here, RAND, BLOCK, width_here)
-    random_v = jnp.stack(
-        [lax.dynamic_slice(incoming, (my_owners[j], slot_start[j] + BLOCK, 0), (1, BLOCK, width_here))[0] for j in range(blocks_here * RAND)]
-    ).reshape(blocks_here, RAND, BLOCK, width_here)
+    incoming = incoming[:, :kv_rows].reshape(seq_count, capacity, 2, BLOCK, width_here)
+    random_k = incoming[my_owners, my_ranks, 0].reshape(blocks_here, RAND, BLOCK, width_here)
+    random_v = incoming[my_owners, my_ranks, 1].reshape(blocks_here, RAND, BLOCK, width_here)
     random_kv = (random_k, random_v)
     near_part = partial_attend(query_view, near_kv[0], near_kv[1], near_valid)
     far_part = partial_attend(

time: 253 us -> 205 us (0.81)
  between operations: 62.7 us -> 2.33 us
  waiting for transfers between devices: 38.9 us -> 60.2 us
  matrix products: 14.1 us -> 10.7 us
  local copies, waits for them, and re-layouts: 46 us -> 43 us
    all_to_all x1, waiting for transfers between devices: 14.1 us -> 32.8 us  [on_device(): lax.all_to_all(outgoing, 'seq', split_axis=0, concat_axis=0, tiled=True)]
    unnamed x60 -> x49, local copies, waits for them, and re-layouts: 22.4 us -> 11.4 us
    gather x0 -> x2, local copies, waits for them, and re-layouts: none -> 5.68 us  [the longest x1 2.84 us: on_device(): incoming[my_owners, my_ranks, 0]]
    dot_general x1, matrix products: 5.82 us -> 2.47 us  [head_partials(): lax.dot_general(out_weight, rows, (((0,), (1,)), ((), ())), preferred_ele...]
    slice x2 -> x1, local copies, waits for them, and re-layouts: 1.31 us -> 4.6 us  [on_device(): incoming[:, :kv_rows].reshape(seq_count, capacity, 2, BLOCK, width_here)]
    ppermute x3, waiting for transfers between devices: 4.65 us -> 7.85 us  [tree_scatter(): parts = merge(keep, lax.ppermute(send, axis, xor_perm(count, bit)))]
  transfers between devices with their start and end apart: 12 -> 12, of which waited for: 8 -> 9; matrix products, arithmetic and copies ran while one was open for 13% -> 16% of each run, Pallas kernels for 0% -> 0%
where the time goes in v19:
time: 205 us; the launch traced here: 204 us
  waiting for transfers between devices  60.2 us (29%)
  blocking collectives  53.1 us (26%)
  local copies, waits for them, and re-layouts  43 us (21%)
  other arithmetic  18.9 us (9%)
  starting transfers between devices  16.1 us (8%)
  matrix products  10.7 us (5%)
  between operations  2.33 us (1%)
    all_to_all x1, blocking collectives, sum_over_head(): gathered = lax.all_to_all(partial, 'head', 0, 0, tiled=True)  53.1 us
    all_to_all x1, waiting for transfers between devices, on_device(): lax.all_to_all(outgoing, 'seq', split_axis=0, concat_axis=0, tiled=True)  32.8 us
    unnamed x49, local copies, waits for them, and re-layouts  11.4 us
    ppermute x3, waiting for transfers between devices, tree_reduce(): got = lax.ppermute(send, axis, xor_perm(count, bit))  11.1 us
    ppermute x3, waiting for transfers between devices, tree_reduce(): got = lax.ppermute(parts, axis, xor_perm(count, bit))  8.42 us
    ppermute x3, waiting for transfers between devices, tree_scatter(): parts = merge(keep, lax.ppermute(send, axis, xor_perm(count, bit)))  7.85 us
    all_to_all x1, starting transfers between devices, on_device(): lax.all_to_all(outgoing, 'seq', split_axis=0, concat_axis=0, tiled=True)  4.88 us
    concatenate x1, local copies, waits for them, and re-layouts, on_device(): jnp.concatenate([outgoing.reshape(seq_count, kv_rows, width_here), jnp.ze...  4.79 us
  transfers between devices with their start and end apart: 12, of which 9 were waited for; matrix products, arithmetic and copies ran while one was open for 16% of the time, Pallas kernels for 0%

profile of v19, /device:TPU:2, one launch (start us, length us, event | category | flops | bytes accessed | tf_op | source)
XLA Modules:
  0.0 204.5 jit_solution(16237186479798729431)
XLA Ops:
  1.4 0.7 fusion.107
  2.1 0.7 compare_select_fusion.3
  2.9 1.1 convert_bitcast_fusion
  4.6 0.5 fusion.79
  5.2 0.8 pad_maximum_fusion.7
  6.0 0.6 gather_fusion.2
  6.5 0.7 slice_negate_fusion
  7.4 0.6 maximum_multiply_fusion.1
  8.5 1.0 fusion.48
  9.5 0.6 gather_fusion.1
  10.0 0.6 gather_fusion
  11.5 1.2 collective-permute-done
  12.9 6.9 %collective-permute-done.1 = bf16[96,1024]{1,0:T(8,128)(2,1)S(1)} collective-permute-done((bf16[96,1024]{1,0:T(8,128)(2,1)S(1)}, bf16[96,1024]{1,0:T(8,128)(2,1)S(1)}, u32[]{:S(2)}, u32[]{:S(2)}) %collective-permute-start.1) | collective-permute-done | bytes 196640 | tf_op jit(solution)/shard_map/ppermute | solution.py:100
  19.8 1.6 collective-permute-start.2
  21.5 3.0 %collective-permute-done.2 = bf16[48,1024]{1,0:T(8,128)(2,1)S(1)} collective-permute-done((bf16[48,1024]{1,0:T(8,128)(2,1)S(1)}, bf16[48,1024]{1,0:T(8,128)(2,1)S(1)}, u32[]{:S(2)}, u32[]{:S(2)}) %collective-permute-start.2) | collective-permute-done | bytes 98336 | tf_op jit(solution)/shard_map/ppermute | solution.py:100
  24.5 1.6 collective-permute-start.3
  26.1 3.1 %collective-permute-done.3 = bf16[48,1024]{1,0:T(8,128)(2,1)S(1)} collective-permute-done((bf16[48,1024]{1,0:T(8,128)(2,1)S(1)}, bf16[48,1024]{1,0:T(8,128)(2,1)S(1)}, u32[]{:S(2)}, u32[]{:S(2)}) %collective-permute-start.3) | collective-permute-done | bytes 98336 | tf_op jit(solution)/shard_map/ppermute | solution.py:104
  30.3 4.8 %collective-permute-done.4 = bf16[96,1024]{1,0:T(8,128)(2,1)S(1)} collective-permute-done((bf16[96,1024]{1,0:T(8,128)(2,1)S(1)}, bf16[96,1024]{1,0:T(8,128)(2,1)S(1)}, u32[]{:S(2)}, u32[]{:S(2)}) %collective-permute-start.4) | collective-permute-done | bytes 196640 | tf_op jit(solution)/shard_map/ppermute | solution.py:104
  35.6 0.9 copy.108
  36.6 0.5 collective-permute-done.5
  37.9 1.1 fusion.121
  39.0 1.9 collective-permute-start.7
  40.9 2.4 %collective-permute-start.6 = (bf16[2,128,1024]{2,1,0:T(8,128)(2,1)}, bf16[2,128,1024]{2,1,0:T(8,128)(2,1)}, u32[]{:S(2)}, u32[]{:S(2)}) collective-permute-start(bf16[2,128,1024]{2,1,0:T(8,128)(2,1)} %get-tuple-element.37), channel_id=1, source_target_pairs={{0,4},{4,8},{8,12},{12,16},{16,20},{20,24},{24,28},{1,5},{5,9},{9,... | collective-permute-start | bytes 1572872 | tf_op jit(solution)/shard_map/ppermute | solution.py:252
  43.7 1.4 convolution_bitcast_fusion
  45.4 0.9 copy.181
  46.3 0.5 fusion.53
  46.9 2.8 %gather_fusion.3 = bf16[16,2,64,1024]{3,2,1,0:T(8,128)(2,1)} fusion(bf16[4,2,64,1024]{3,2,0,1:T(8,128)(2,1)S(1)} %bitcast.273, s32[1024]{0:T(1024)S(1)} %pad_clamp_fusion.1), kind=kCustom, calls=%fused_computation.3 | custom fusion | bytes 8388672 | tf_op jit(solution)/shard_map/gather | solution.py:309
  49.7 4.8 %concatenate.70 = bf16[8,272,1024]{2,1,0:T(8,128)(2,1)} pad(bf16[8,256,1024]{2,1,0:T(8,128)(2,1)} %bitcast.277, bf16[]{:T(256)} %constant.208.clone.1), padding=0_0x0_16x0_0 | pad | bytes 8650754 | tf_op jit(solution)/shard_map/concatenate | solution.py:312
  54.7 2.3 %collective-permute-start.8 = (f32[64,1152]{1,0:T(8,128)S(1)}, f32[64,1152]{1,0:T(8,128)S(1)}, u32[]{:S(2)}, u32[]{:S(2)}) collective-permute-start(f32[64,1152]{1,0:T(8,128)S(1)} %get-tuple-element.47), channel_id=1, source_target_pairs={{0,4},{4,0},{8,12},{12,8},{16,20},{20,16},{24,28},{28,24},{1,5},{5... | collective-permute-start | bytes 884744 | tf_op jit(solution)/shard_map/ppermute | solution.py:125
  57.1 0.6 fusion.123
  57.7 0.6 fusion.124
  58.2 1.2 compare_and_fusion.1
  60.2 1.2 compare_and_fusion
  61.7 4.2 %collective-permute-done.9 = f32[32,1152]{1,0:T(8,128)S(1)} collective-permute-done((f32[32,1152]{1,0:T(8,128)S(1)}, f32[32,1152]{1,0:T(8,128)S(1)}, u32[]{:S(2)}, u32[]{:S(2)}) %collective-permute-start.9) | collective-permute-done | bytes 147488 | tf_op jit(solution)/shard_map/ppermute | solution.py:125
  66.4 0.8 collective-permute-start.10
  67.2 3.6 %collective-permute-done.10 = f32[16,1152]{1,0:T(8,128)S(1)} collective-permute-done((f32[16,1152]{1,0:T(8,128)S(1)}, f32[16,1152]{1,0:T(8,128)S(1)}, u32[]{:S(2)}, u32[]{:S(2)}) %collective-permute-start.10) | collective-permute-done | bytes 73760 | tf_op jit(solution)/shard_map/ppermute | solution.py:125
  71.2 0.8 broadcast_dynamic-update-slice_fusion
  72.0 4.9 %all-to-all-start = ((bf16[8,272,1024]{2,1,0:T(8,128)(2,1)}), bf16[8,272,1024]{2,1,0:T(8,128)(2,1)}, u32[]{:S(2)}, u32[]{:S(2)}) async-start(bf16[8,272,1024]{2,1,0:T(8,128)(2,1)} %broadcast_dynamic-update-slice_fusion), calls=%async_computation | async-start | bytes 8912896 | tf_op jit(solution)/shard_map/all_to_all | solution.py:331
  78.0 1.0 slice.228
  79.0 1.0 slice.227
  80.0 1.2 maximum_bitcast_fusion
  81.1 1.4 maximum_bitcast_fusion.1
  82.8 1.1 pad_maximum_fusion
  83.9 1.5 fusion.120
  85.4 1.0 copy.118
  86.4 2.7 %copy.119 = bf16[224,8,8,128]{3,2,1,0:T(8,128)(2,1)} copy(bf16[224,8,8,128]{3,1,2,0:T(8,128)(2,1)S(1)} %bitcast.282) | data formatting | bytes 7340032
  89.1 1.8 fusion
  91.0 2.1 %copy-done = f32[4,8,64,448]{3,2,1,0:T(8,128)} copy-done((f32[4,8,64,448]{3,2,1,0:T(8,128)}, f32[4,8,64,448]{3,2,1,0:T(8,128)S(1)}, u32[]{:S(2)}) %copy-start) | copy-done | bytes 3670040
  93.1 1.6 fusion.5
  94.6 32.8 %all-to-all-done = bf16[8,272,1024]{2,1,0:T(8,128)(2,1)} async-done(((bf16[8,272,1024]{2,1,0:T(8,128)(2,1)}), bf16[8,272,1024]{2,1,0:T(8,128)(2,1)}, u32[]{:S(2)}, u32[]{:S(2)}) %all-to-all-start) | async-done | bytes 4456480 | tf_op jit(solution)/shard_map/all_to_all | solution.py:331
  127.4 1.0 slice.222
  128.3 0.6 gather_fusion.4
  128.9 4.6 %slice.231 = bf16[8,256,1024]{2,1,0:T(8,128)(2,1)} slice(bf16[8,272,1024]{2,1,0:T(8,128)(2,1)} %all-to-all-done), slice={[0:8], [0:256], [0:1024]} | slice | bytes 8388608 | tf_op jit(solution)/shard_map/slice | solution.py:335
  133.5 2.8 %gather_fusion.6 = bf16[12,64,1024]{2,1,0:T(8,128)(2,1)S(1)} fusion(bf16[8,2,2,64,1024]{4,3,2,1,0:T(8,128)(2,1)} %bitcast.285, s32[12]{0:T(128)S(1)} %get-tuple-element.16), kind=kCustom, calls=%fused_computation.6 | custom fusion | bytes 3145872 | tf_op jit(solution)/shard_map/gather | solution.py:337
  136.4 2.8 %gather_fusion.5 = bf16[12,64,1024]{2,1,0:T(8,128)(2,1)S(1)} fusion(bf16[8,2,2,64,1024]{4,3,2,1,0:T(8,128)(2,1)} %bitcast.286, s32[12]{0:T(128)S(1)} %bitcast.344), kind=kCustom, calls=%fused_computation.5 | custom fusion | bytes 3145872 | tf_op jit(solution)/shard_map/gather | solution.py:336
  140.2 0.6 copy-done.4
  140.7 1.2 multiply_reduce_fusion
  142.0 0.8 fusion.12
  142.8 0.6 copy-done.1
  143.4 2.1 %fusion.32 = f32[4,64,8,128]{3,1,2,0:T(8,128)S(1)} fusion(bf16[4,448,8,128]{3,2,1,0:T(8,128)(2,1)S(1)} %bitcast.303, f32[4,8,64,448]{3,2,1,0:T(8,128)S(1)} %copy-done.1, f32[4,8,64]{2,1,0:T(8,128)S(1)} %get-tuple-element.72, pred[4,8,448]{2,1,0:T(8,128)(4,1)S(1)} %broadcast_in_dim.193, f32[4,64,8]{1,2,0:T(8,128)S(1)} %get-tuple-element.15), kind=kOutput, calls=%fused_computation.35 | convolution fusion | flops 238813184 | bytes 8419328 | tf_op jit(solution)/shard_map/bhqs,bshd->bqhd/dot_general | solution.py:184
  145.5 1.4 fusion.42
  147.4 2.5 %convolution_convert_fusion = bf16[256,4096]{1,0:T(8,128)(2,1)S(1)} fusion(bf16[1024,4096]{1,0:T(8,128)(2,1)S(1)} %bitcast.351, bf16[256,1024]{1,0:T(8,128)(2,1)S(1)} %bitcast.328, bf16[256,1024]{1,0:T(8,128)(2,1)S(1)} %bitcast.329, bf16[32,8,8,128]{3,2,1,0:T(8,128)(2,1)S(1)} %bitcast.333, pred[256]{0:T(512)(128)(4,1)S(1)} %broadcast_in_dim.186, ...), kind=kOutput, calls=%fused_computation.8 | convolution fusion | flops 2149056512 | bytes 12059136 | tf_op jit(solution)/shard_map/dot_general | solution.py:159
  150.1 53.1 %all_to_all.10 = bf16[4,1024,256]{1,2,0:T(8,128)(2,1)S(1)} all-to-all(bf16[4,1024,256]{1,2,0:T(8,128)(2,1)S(1)} %bitcast.294), channel_id=1, replica_groups=mesh['seq'=8,'head'=4] {'head'}, dimensions={0} | all-to-all | bytes 4194304 | tf_op jit(solution)/shard_map/all_to_all | solution.py:166
  203.2 1.3 reduce_sum.71
  (139 shorter events, 10.4 us)
Async XLA Ops:
  0.0 4.3 %copy-start.11 = (bf16[256,1024]{1,0:T(8,128)(2,1)S(1)}, bf16[256,1024]{1,0:T(8,128)(2,1)}, u32[]{:S(2)}) copy-start(bf16[256,1024]{1,0:T(8,128)(2,1)} %param.11) | copy-start | bytes 1572868
  4.3 1.7 copy-start.2
  6.5 0.9 copy-start.13
  7.4 1.0 copy-start.10
  9.5 1.4 copy-start.6
  10.6 0.7 copy-start.14
  10.9 1.8 collective-permute-start
  12.8 7.0 %collective-permute-start.1 = (bf16[96,1024]{1,0:T(8,128)(2,1)S(1)}, bf16[96,1024]{1,0:T(8,128)(2,1)S(1)}, u32[]{:S(2)}, u32[]{:S(2)}) collective-permute-start(bf16[96,1024]{1,0:T(8,128)(2,1)S(1)} %dynamic-slice_bitcast_fusion.3), channel_id=1, source_target_pairs={{0,8},{4,12},{8,0},{12,4},{16,24},{20,28},{24,16},{28,20},{1,9},{5... | collective-permute-start | bytes 589832 | tf_op jit(solution)/shard_map/ppermute | solution.py:100
  19.8 4.7 %collective-permute-start.2 = (bf16[48,1024]{1,0:T(8,128)(2,1)S(1)}, bf16[48,1024]{1,0:T(8,128)(2,1)S(1)}, u32[]{:S(2)}, u32[]{:S(2)}) collective-permute-start(bf16[48,1024]{1,0:T(8,128)(2,1)S(1)} %dynamic-slice_bitcast_fusion.6), channel_id=1, source_target_pairs={{0,16},{4,20},{8,24},{12,28},{16,0},{20,4},{24,8},{28,12},{1,17},{... | collective-permute-start | bytes 294920 | tf_op jit(solution)/shard_map/ppermute | solution.py:100
  24.5 4.7 %collective-permute-start.3 = (bf16[48,1024]{1,0:T(8,128)(2,1)S(1)}, bf16[48,1024]{1,0:T(8,128)(2,1)S(1)}, u32[]{:S(2)}, u32[]{:S(2)}) collective-permute-start(bf16[48,1024]{1,0:T(8,128)(2,1)S(1)} %bitcast_add_fusion.2), channel_id=1, source_target_pairs={{0,16},{4,20},{8,24},{12,28},{16,0},{20,4},{24,8},{28,12},{1,17},{... | collective-permute-start | bytes 294920 | tf_op jit(solution)/shard_map/ppermute | solution.py:104
  29.3 5.7 %collective-permute-start.4 = (bf16[96,1024]{1,0:T(8,128)(2,1)S(1)}, bf16[96,1024]{1,0:T(8,128)(2,1)S(1)}, u32[]{:S(2)}, u32[]{:S(2)}) collective-permute-start(bf16[96,1024]{1,0:T(8,128)(2,1)S(1)} %get-tuple-element.56), channel_id=1, source_target_pairs={{0,8},{4,12},{8,0},{12,4},{16,24},{20,28},{24,16},{28,20},{1,9},{5... | collective-permute-start | bytes 589832 | tf_op jit(solution)/shard_map/ppermute | solution.py:104
  35.3 1.8 collective-permute-start.5
  37.5 1.5 copy-start.8
  39.0 15.7 %collective-permute-start.7 = (bf16[2,128,1024]{2,1,0:T(8,128)(2,1)}, bf16[2,128,1024]{2,1,0:T(8,128)(2,1)}, u32[]{:S(2)}, u32[]{:S(2)}) collective-permute-start(bf16[2,128,1024]{2,1,0:T(8,128)(2,1)} %get-tuple-element.36), channel_id=1, source_target_pairs={{4,0},{8,4},{12,8},{16,12},{20,16},{24,20},{28,24},{5,1},{9,5},{13... | collective-permute-start | bytes 1572872 | tf_op jit(solution)/shard_map/ppermute | solution.py:255
  40.9 13.7 %collective-permute-start.6 = (bf16[2,128,1024]{2,1,0:T(8,128)(2,1)}, bf16[2,128,1024]{2,1,0:T(8,128)(2,1)}, u32[]{:S(2)}, u32[]{:S(2)}) collective-permute-start(bf16[2,128,1024]{2,1,0:T(8,128)(2,1)} %get-tuple-element.37), channel_id=1, source_target_pairs={{0,4},{4,8},{8,12},{12,16},{16,20},{20,24},{24,28},{1,5},{5,9},{9,... | collective-permute-start | bytes 1572872 | tf_op jit(solution)/shard_map/ppermute | solution.py:252
  49.7 4.8 %copy-start.12 = (f32[16,8,8,128]{3,1,2,0:T(8,128)S(1)}, f32[16,8,8,128]{3,1,2,0:T(8,128)}, u32[]{:S(2)}) copy-start(f32[16,8,8,128]{3,1,2,0:T(8,128)} %copy.181) | copy-start | bytes 1572868
  54.7 4.7 %collective-permute-start.8 = (f32[64,1152]{1,0:T(8,128)S(1)}, f32[64,1152]{1,0:T(8,128)S(1)}, u32[]{:S(2)}, u32[]{:S(2)}) collective-permute-start(f32[64,1152]{1,0:T(8,128)S(1)} %get-tuple-element.47), channel_id=1, source_target_pairs={{0,4},{4,0},{8,12},{12,8},{16,20},{20,16},{24,28},{28,24},{1,5},{5... | collective-permute-start | bytes 884744 | tf_op jit(solution)/shard_map/ppermute | solution.py:125
  60.1 5.8 %collective-permute-start.9 = (f32[32,1152]{1,0:T(8,128)S(1)}, f32[32,1152]{1,0:T(8,128)S(1)}, u32[]{:S(2)}, u32[]{:S(2)}) collective-permute-start(f32[32,1152]{1,0:T(8,128)S(1)} %get-tuple-element.53), channel_id=1, source_target_pairs={{0,8},{4,12},{8,0},{12,4},{16,24},{20,28},{24,16},{28,20},{1,9},{5... | collective-permute-start | bytes 442376 | tf_op jit(solution)/shard_map/ppermute | solution.py:125
  66.4 4.4 %collective-permute-start.10 = (f32[16,1152]{1,0:T(8,128)S(1)}, f32[16,1152]{1,0:T(8,128)S(1)}, u32[]{:S(2)}, u32[]{:S(2)}) collective-permute-start(f32[16,1152]{1,0:T(8,128)S(1)} %get-tuple-element.61), channel_id=1, source_target_pairs={{0,16},{4,20},{8,24},{12,28},{16,0},{20,4},{24,8},{28,12},{1,17},{... | collective-permute-start | bytes 221192 | tf_op jit(solution)/shard_map/ppermute | solution.py:125
  71.9 5.0 %copy-start.16 = (s32[8]{0:T(128)S(1)}, s32[8]{0:T(128)}, u32[]{:S(2)}) copy-start(s32[8]{0:T(128)} %param.16) | copy-start | bytes 100
  71.9 5.3 %copy-start.7 = (bf16[256,1024]{1,0:T(8,128)(2,1)S(1)}, bf16[256,1024]{1,0:T(8,128)(2,1)}, u32[]{:S(2)}) copy-start(bf16[256,1024]{1,0:T(8,128)(2,1)} %copy-done.6) | copy-start | bytes 1572868
  71.9 5.6 %copy-start.15 = (s32[8]{0:T(128)S(1)}, s32[8]{0:T(128)}, u32[]{:S(2)}) copy-start(s32[8]{0:T(128)} %constant.263) | copy-start | bytes 100
  72.0 55.4 %all-to-all-start = ((bf16[8,272,1024]{2,1,0:T(8,128)(2,1)}), bf16[8,272,1024]{2,1,0:T(8,128)(2,1)}, u32[]{:S(2)}, u32[]{:S(2)}) async-start(bf16[8,272,1024]{2,1,0:T(8,128)(2,1)} %broadcast_dynamic-update-slice_fusion), calls=%async_computation | async-start | bytes 8912896 | tf_op jit(solution)/shard_map/all_to_all | solution.py:331
  76.8 1.1 copy-start.9
  77.3 11.8 %copy-start.3 = (bf16[32,8,8,128]{3,2,1,0:T(8,128)(2,1)}, bf16[32,8,8,128]{3,2,1,0:T(8,128)(2,1)S(1)}, u32[]{:S(2)}) copy-start(bf16[32,8,8,128]{3,2,1,0:T(8,128)(2,1)S(1)} %copy.117) | copy-start | bytes 1572868
  91.0 2.1 %copy-start = (f32[4,8,64,448]{3,2,1,0:T(8,128)}, f32[4,8,64,448]{3,2,1,0:T(8,128)S(1)}, u32[]{:S(2)}) copy-start(f32[4,8,64,448]{3,2,1,0:T(8,128)S(1)} %get-tuple-element.73) | copy-start | bytes 11010052
  139.7 1.0 copy-start.4
  139.7 3.0 %copy-start.5 = (bf16[224,8,8,128]{3,2,1,0:T(8,128)(2,1)S(1)}, bf16[224,8,8,128]{3,2,1,0:T(8,128)(2,1)}, u32[]{:S(2)}) copy-start(bf16[224,8,8,128]{3,2,1,0:T(8,128)(2,1)} %copy.119) | copy-start | bytes 11010052
  140.7 2.6 %copy-start.1 = (f32[4,8,64,448]{3,2,1,0:T(8,128)S(1)}, f32[4,8,64,448]{3,2,1,0:T(8,128)}, u32[]{:S(2)}) copy-start(f32[4,8,64,448]{3,2,1,0:T(8,128)} %copy-done) | copy-start | bytes 11010052
  142.0 5.4 %slice-start = ((s8[8388608]{0:T(1024)(128)(4,1)}), s8[4194304]{0:T(1024)(128)(4,1)S(1)}, s32[]{:S(2)}) async-start(s8[8388608]{0:T(1024)(128)(4,1)} %bitcast.350), calls=%async_computation.2 | async-start | bytes 8388608
  143.4 4.0 %slice-start.1 = ((s8[8388608]{0:T(1024)(128)(4,1)}), s8[4194304]{0:T(1024)(128)(4,1)S(1)}, s32[]{:S(2)}) async-start(s8[8388608]{0:T(1024)(128)(4,1)} %bitcast.350), calls=%async_computation.3 | async-start | bytes 8388608

commit v20 on v19

--- a/solution.py
+++ b/solution.py
@@ -332,9 +332,13 @@
     global_rows = incoming[:, kv_rows:][jnp.array(bit_reversed(seq_count))]
     my_owners = owners[seq_place]
     my_ranks = ranks[seq_place]
-    incoming = incoming[:, :kv_rows].reshape(seq_count, capacity, 2, BLOCK, width_here)
-    random_k = incoming[my_owners, my_ranks, 0].reshape(blocks_here, RAND, BLOCK, width_here)
-    random_v = incoming[my_owners, my_ranks, 1].reshape(blocks_here, RAND, BLOCK, width_here)
+    sub = math.gcd(BLOCK, rows_each)
+    pieces = incoming.reshape(seq_count, (kv_rows + rows_each) // sub, sub, width_here)
+    first_piece = (my_ranks * (2 * BLOCK) // sub)[:, None] + jnp.arange(BLOCK // sub)[None, :]
+    random_k = pieces[my_owners[:, None], first_piece].reshape(blocks_here, RAND, BLOCK, width_here)
+    random_v = pieces[my_owners[:, None], first_piece + BLOCK // sub].reshape(
+        blocks_here, RAND, BLOCK, width_here
+    )
     random_kv = (random_k, random_v)
     near_part = partial_attend(query_view, near_kv[0], near_kv[1], near_valid)
     far_part = partial_attend(

time: 205 us -> 202 us (0.985)
  local copies, waits for them, and re-layouts: 43 us -> 39.8 us
    slice x1 -> x0, local copies, waits for them, and re-layouts: 4.6 us -> none  [on_device(): incoming[:, :kv_rows].reshape(seq_count, capacity, 2, BLOCK, width_here)]
    unnamed x49 -> x55, local copies, waits for them, and re-layouts: 11.4 us -> 12.3 us
  transfers between devices with their start and end apart: 12 -> 12, of which waited for: 9 -> 8; matrix products, arithmetic and copies ran while one was open for 16% -> 16% of each run, Pallas kernels for 0% -> 0%
where the time goes in v20:
time: 202 us; the launch traced here: 201 us
  waiting for transfers between devices  59.5 us (29%)
  blocking collectives  53.1 us (26%)
  local copies, waits for them, and re-layouts  39.8 us (20%)
  other arithmetic  19.3 us (10%)
  starting transfers between devices  16.5 us (8%)
  matrix products  10.7 us (5%)
  between operations  2.41 us (1%)
    all_to_all x1, blocking collectives, sum_over_head(): gathered = lax.all_to_all(partial, 'head', 0, 0, tiled=True)  53.1 us
    all_to_all x1, waiting for transfers between devices, on_device(): lax.all_to_all(outgoing, 'seq', split_axis=0, concat_axis=0, tiled=True)  32.8 us
    unnamed x55, local copies, waits for them, and re-layouts  12.3 us
    ppermute x3, waiting for transfers between devices, tree_reduce(): got = lax.ppermute(send, axis, xor_perm(count, bit))  10.7 us
    ppermute x3, waiting for transfers between devices, tree_reduce(): got = lax.ppermute(parts, axis, xor_perm(count, bit))  8.17 us
    ppermute x3, waiting for transfers between devices, tree_scatter(): parts = merge(keep, lax.ppermute(send, axis, xor_perm(count, bit)))  7.71 us
    all_to_all x1, starting transfers between devices, on_device(): lax.all_to_all(outgoing, 'seq', split_axis=0, concat_axis=0, tiled=True)  4.87 us
    concatenate x1, local copies, waits for them, and re-layouts, on_device(): jnp.concatenate([outgoing.reshape(seq_count, kv_rows, width_here), jnp.ze...  4.78 us
  transfers between devices with their start and end apart: 12, of which 8 were waited for; matrix products, arithmetic and copies ran while one was open for 16% of the time, Pallas kernels for 0%

profile of v20, /device:TPU:2, one launch (start us, length us, event | category | flops | bytes accessed | tf_op | source)
XLA Modules:
  0.0 201.2 jit_solution(4073982336446291410)
XLA Ops:
  1.4 0.7 fusion.110
  2.1 1.2 compare_select_fusion.4
  3.5 1.1 convert_bitcast_fusion
  5.2 0.5 fusion.79
  5.9 0.6 gather_fusion.2
  6.5 0.7 slice_negate_fusion
  7.2 0.6 maximum_multiply_fusion.1
  8.4 1.0 fusion.48
  9.4 0.6 gather_fusion.1
  10.0 0.6 gather_fusion
  11.5 1.1 collective-permute-done
  12.8 6.9 %collective-permute-done.1 = bf16[96,1024]{1,0:T(8,128)(2,1)S(1)} collective-permute-done((bf16[96,1024]{1,0:T(8,128)(2,1)S(1)}, bf16[96,1024]{1,0:T(8,128)(2,1)S(1)}, u32[]{:S(2)}, u32[]{:S(2)}) %collective-permute-start.1) | collective-permute-done | bytes 196640 | tf_op jit(solution)/shard_map/ppermute | solution.py:100
  19.8 1.6 collective-permute-start.2
  21.8 2.7 %collective-permute-done.2 = bf16[48,1024]{1,0:T(8,128)(2,1)S(1)} collective-permute-done((bf16[48,1024]{1,0:T(8,128)(2,1)S(1)}, bf16[48,1024]{1,0:T(8,128)(2,1)S(1)}, u32[]{:S(2)}, u32[]{:S(2)}) %collective-permute-start.2) | collective-permute-done | bytes 98336 | tf_op jit(solution)/shard_map/ppermute | solution.py:100
  24.5 1.6 collective-permute-start.3
  26.2 3.0 %collective-permute-done.3 = bf16[48,1024]{1,0:T(8,128)(2,1)S(1)} collective-permute-done((bf16[48,1024]{1,0:T(8,128)(2,1)S(1)}, bf16[48,1024]{1,0:T(8,128)(2,1)S(1)}, u32[]{:S(2)}, u32[]{:S(2)}) %collective-permute-start.3) | collective-permute-done | bytes 98336 | tf_op jit(solution)/shard_map/ppermute | solution.py:104
  29.8 5.2 %collective-permute-done.4 = bf16[96,1024]{1,0:T(8,128)(2,1)S(1)} collective-permute-done((bf16[96,1024]{1,0:T(8,128)(2,1)S(1)}, bf16[96,1024]{1,0:T(8,128)(2,1)S(1)}, u32[]{:S(2)}, u32[]{:S(2)}) %collective-permute-start.4) | collective-permute-done | bytes 196640 | tf_op jit(solution)/shard_map/ppermute | solution.py:104
  35.4 0.9 copy.108
  36.3 0.7 fusion.125
  36.9 0.7 fusion.126
  38.2 0.7 copy-done.8
  39.2 1.1 fusion.123
  40.3 2.3 %collective-permute-start.7 = (bf16[2,128,1024]{2,1,0:T(8,128)(2,1)}, bf16[2,128,1024]{2,1,0:T(8,128)(2,1)}, u32[]{:S(2)}, u32[]{:S(2)}) collective-permute-start(bf16[2,128,1024]{2,1,0:T(8,128)(2,1)} %get-tuple-element.34), channel_id=1, source_target_pairs={{4,0},{8,4},{12,8},{16,12},{20,16},{24,20},{28,24},{5,1},{9,5},{13... | collective-permute-start | bytes 1572872 | tf_op jit(solution)/shard_map/ppermute | solution.py:255
  42.6 2.0 %collective-permute-start.6 = (bf16[2,128,1024]{2,1,0:T(8,128)(2,1)}, bf16[2,128,1024]{2,1,0:T(8,128)(2,1)}, u32[]{:S(2)}, u32[]{:S(2)}) collective-permute-start(bf16[2,128,1024]{2,1,0:T(8,128)(2,1)} %get-tuple-element.35), channel_id=1, source_target_pairs={{0,4},{4,8},{8,12},{12,16},{16,20},{20,24},{24,28},{1,5},{5,9},{9,... | collective-permute-start | bytes 1572872 | tf_op jit(solution)/shard_map/ppermute | solution.py:252
  45.0 1.4 convolution_bitcast_fusion
  46.7 0.9 copy.181
  47.6 0.5 fusion.53
  48.2 2.8 %gather_fusion.3 = bf16[16,2,64,1024]{3,2,1,0:T(8,128)(2,1)} fusion(bf16[4,2,64,1024]{3,2,0,1:T(8,128)(2,1)S(1)} %bitcast.270, s32[1024]{0:T(1024)S(1)} %pad_clamp_fusion.1), kind=kCustom, calls=%fused_computation.3 | custom fusion | bytes 8388672 | tf_op jit(solution)/shard_map/gather | solution.py:309
  51.0 4.8 %concatenate.70 = bf16[8,272,1024]{2,1,0:T(8,128)(2,1)} pad(bf16[8,256,1024]{2,1,0:T(8,128)(2,1)} %bitcast.274, bf16[]{:T(256)} %constant.221.clone.1), padding=0_0x0_16x0_0 | pad | bytes 8650754 | tf_op jit(solution)/shard_map/concatenate | solution.py:312
  56.0 2.7 %collective-permute-start.8 = (f32[64,1152]{1,0:T(8,128)S(1)}, f32[64,1152]{1,0:T(8,128)S(1)}, u32[]{:S(2)}, u32[]{:S(2)}) collective-permute-start(f32[64,1152]{1,0:T(8,128)S(1)} %get-tuple-element.45), channel_id=1, source_target_pairs={{0,4},{4,0},{8,12},{12,8},{16,20},{20,16},{24,28},{28,24},{1,5},{5... | collective-permute-start | bytes 884744 | tf_op jit(solution)/shard_map/ppermute | solution.py:125
  58.7 1.4 compare_and_fusion.1
  61.2 5.7 %collective-permute-done.9 = f32[32,1152]{1,0:T(8,128)S(1)} collective-permute-done((f32[32,1152]{1,0:T(8,128)S(1)}, f32[32,1152]{1,0:T(8,128)S(1)}, u32[]{:S(2)}, u32[]{:S(2)}) %collective-permute-start.9) | collective-permute-done | bytes 147488 | tf_op jit(solution)/shard_map/ppermute | solution.py:125
  67.4 0.8 collective-permute-start.10
  68.2 1.2 compare_and_fusion
  69.8 2.0 %collective-permute-done.10 = f32[16,1152]{1,0:T(8,128)S(1)} collective-permute-done((f32[16,1152]{1,0:T(8,128)S(1)}, f32[16,1152]{1,0:T(8,128)S(1)}, u32[]{:S(2)}, u32[]{:S(2)}) %collective-permute-start.10) | collective-permute-done | bytes 73760 | tf_op jit(solution)/shard_map/ppermute | solution.py:125
  72.2 0.7 broadcast_dynamic-update-slice_fusion
  72.9 4.9 %all-to-all-start = ((bf16[8,272,1024]{2,1,0:T(8,128)(2,1)}), bf16[8,272,1024]{2,1,0:T(8,128)(2,1)}, u32[]{:S(2)}, u32[]{:S(2)}) async-start(bf16[8,272,1024]{2,1,0:T(8,128)(2,1)} %broadcast_dynamic-update-slice_fusion), calls=%async_computation | async-start | bytes 8912896 | tf_op jit(solution)/shard_map/all_to_all | solution.py:331
  78.4 0.5 copy-done.9
  79.0 1.0 slice.222
  79.9 1.0 slice.221
  80.9 1.2 maximum_bitcast_fusion
  82.1 1.4 maximum_bitcast_fusion.1
  83.8 1.1 pad_maximum_fusion
  84.8 1.5 fusion.122
  86.4 1.0 copy.118
  87.3 2.7 %copy.119 = bf16[224,8,8,128]{3,2,1,0:T(8,128)(2,1)} copy(bf16[224,8,8,128]{3,1,2,0:T(8,128)(2,1)S(1)} %bitcast.279) | data formatting | bytes 7340032
  90.1 1.8 fusion
  91.9 2.1 %copy-done = f32[4,8,64,448]{3,2,1,0:T(8,128)} copy-done((f32[4,8,64,448]{3,2,1,0:T(8,128)}, f32[4,8,64,448]{3,2,1,0:T(8,128)S(1)}, u32[]{:S(2)}) %copy-start) | copy-done | bytes 3670040
  94.0 1.5 fusion.5
  95.5 32.8 %all-to-all-done = bf16[8,272,1024]{2,1,0:T(8,128)(2,1)} async-done(((bf16[8,272,1024]{2,1,0:T(8,128)(2,1)}), bf16[8,272,1024]{2,1,0:T(8,128)(2,1)}, u32[]{:S(2)}, u32[]{:S(2)}) %all-to-all-start) | async-done | bytes 4456480 | tf_op jit(solution)/shard_map/all_to_all | solution.py:331
  128.3 1.0 slice.216
  129.3 0.6 gather_fusion.4
  129.9 3.0 %gather_fusion.6 = bf16[48,16,1024]{2,1,0:T(8,128)(2,1)S(1)} fusion(bf16[8,17,16,1024]{3,2,1,0:T(8,128)(2,1)} %bitcast.79, s32[48]{0:T(128)S(1)} %reshape.535), kind=kCustom, calls=%fused_computation.6 | custom fusion | bytes 3146112 | tf_op jit(solution)/shard_map/gather | solution.py:339
  133.0 3.0 %gather_fusion.5 = bf16[48,16,1024]{2,1,0:T(8,128)(2,1)S(1)} fusion(bf16[8,17,16,1024]{3,2,1,0:T(8,128)(2,1)} %bitcast.79, s32[48]{0:T(128)S(1)} %reshape.529), kind=kCustom, calls=%fused_computation.5 | custom fusion | bytes 3146112 | tf_op jit(solution)/shard_map/gather | solution.py:338
  136.0 0.4 copy.120
  136.9 0.6 copy-done.4
  137.5 1.2 multiply_reduce_fusion
  138.7 0.8 fusion.12
  139.5 0.6 copy-done.1
  140.1 2.1 %fusion.32 = f32[4,64,8,128]{3,1,2,0:T(8,128)S(1)} fusion(bf16[4,448,8,128]{3,2,1,0:T(8,128)(2,1)S(1)} %bitcast.298, f32[4,8,64,448]{3,2,1,0:T(8,128)S(1)} %copy-done.1, f32[4,8,64]{2,1,0:T(8,128)S(1)} %get-tuple-element.72, pred[4,8,448]{2,1,0:T(8,128)(4,1)S(1)} %broadcast_in_dim.201, f32[4,64,8]{1,2,0:T(8,128)S(1)} %get-tuple-element.15), kind=kOutput, calls=%fused_computation.35 | convolution fusion | flops 238813184 | bytes 8419328 | tf_op jit(solution)/shard_map/bhqs,bshd->bqhd/dot_general | solution.py:184
  142.2 1.4 fusion.42
  144.1 2.5 %convolution_convert_fusion = bf16[256,4096]{1,0:T(8,128)(2,1)S(1)} fusion(bf16[1024,4096]{1,0:T(8,128)(2,1)S(1)} %bitcast.345, bf16[256,1024]{1,0:T(8,128)(2,1)S(1)} %bitcast.323, bf16[256,1024]{1,0:T(8,128)(2,1)S(1)} %bitcast.324, bf16[32,8,8,128]{3,2,1,0:T(8,128)(2,1)S(1)} %bitcast.328, pred[256]{0:T(512)(128)(4,1)S(1)} %broadcast_in_dim.194, ...), kind=kOutput, calls=%fused_computation.8 | convolution fusion | flops 2149056512 | bytes 12059136 | tf_op jit(solution)/shard_map/dot_general | solution.py:159
  146.8 53.1 %all_to_all.10 = bf16[4,1024,256]{1,2,0:T(8,128)(2,1)S(1)} all-to-all(bf16[4,1024,256]{1,2,0:T(8,128)(2,1)S(1)} %bitcast.289), channel_id=1, replica_groups=mesh['seq'=8,'head'=4] {'head'}, dimensions={0} | all-to-all | bytes 4194304 | tf_op jit(solution)/shard_map/all_to_all | solution.py:166
  199.9 1.3 reduce_sum.71
  (147 shorter events, 10.0 us)
Async XLA Ops:
  0.0 4.9 %copy-start.11 = (bf16[256,1024]{1,0:T(8,128)(2,1)S(1)}, bf16[256,1024]{1,0:T(8,128)(2,1)}, u32[]{:S(2)}) copy-start(bf16[256,1024]{1,0:T(8,128)(2,1)} %param.11) | copy-start | bytes 1572868
  2.1 1.4 copy-start.14
  4.9 1.0 copy-start.2
  7.2 1.0 copy-start.10
  7.2 1.2 copy-start.12
  9.4 1.4 copy-start.6
  10.5 0.7 copy-start.17
  10.8 1.8 collective-permute-start
  12.7 7.0 %collective-permute-start.1 = (bf16[96,1024]{1,0:T(8,128)(2,1)S(1)}, bf16[96,1024]{1,0:T(8,128)(2,1)S(1)}, u32[]{:S(2)}, u32[]{:S(2)}) collective-permute-start(bf16[96,1024]{1,0:T(8,128)(2,1)S(1)} %dynamic-slice_bitcast_fusion.3), channel_id=1, source_target_pairs={{0,8},{4,12},{8,0},{12,4},{16,24},{20,28},{24,16},{28,20},{1,9},{5... | collective-permute-start | bytes 589832 | tf_op jit(solution)/shard_map/ppermute | solution.py:100
  19.8 4.7 %collective-permute-start.2 = (bf16[48,1024]{1,0:T(8,128)(2,1)S(1)}, bf16[48,1024]{1,0:T(8,128)(2,1)S(1)}, u32[]{:S(2)}, u32[]{:S(2)}) collective-permute-start(bf16[48,1024]{1,0:T(8,128)(2,1)S(1)} %dynamic-slice_bitcast_fusion.6), channel_id=1, source_target_pairs={{0,16},{4,20},{8,24},{12,28},{16,0},{20,4},{24,8},{28,12},{1,17},{... | collective-permute-start | bytes 294920 | tf_op jit(solution)/shard_map/ppermute | solution.py:100
  24.5 11.8 %copy-start.16 = (s32[2]{0:T(128)S(1)}, s32[2]{0:T(128)}, u32[]{:S(2)}) copy-start(s32[2]{0:T(128)} %get-tuple-element.28) | copy-start | bytes 28
  24.5 12.5 %copy-start.15 = (pred[2]{0:T(512)(128)(4,1)S(1)}, pred[2]{0:T(512)(128)(4,1)}, u32[]{:S(2)}) copy-start(pred[2]{0:T(512)(128)(4,1)} %copy-done.14) | copy-start | bytes 10
  24.5 4.7 %collective-permute-start.3 = (bf16[48,1024]{1,0:T(8,128)(2,1)S(1)}, bf16[48,1024]{1,0:T(8,128)(2,1)S(1)}, u32[]{:S(2)}, u32[]{:S(2)}) collective-permute-start(bf16[48,1024]{1,0:T(8,128)(2,1)S(1)} %bitcast_add_fusion.2), channel_id=1, source_target_pairs={{0,16},{4,20},{8,24},{12,28},{16,0},{20,4},{24,8},{28,12},{1,17},{... | collective-permute-start | bytes 294920 | tf_op jit(solution)/shard_map/ppermute | solution.py:104
  29.3 5.7 %collective-permute-start.4 = (bf16[96,1024]{1,0:T(8,128)(2,1)S(1)}, bf16[96,1024]{1,0:T(8,128)(2,1)S(1)}, u32[]{:S(2)}, u32[]{:S(2)}) collective-permute-start(bf16[96,1024]{1,0:T(8,128)(2,1)S(1)} %get-tuple-element.54), channel_id=1, source_target_pairs={{0,8},{4,12},{8,0},{12,4},{16,24},{20,28},{24,16},{28,20},{1,9},{5... | collective-permute-start | bytes 589832 | tf_op jit(solution)/shard_map/ppermute | solution.py:104
  35.3 2.4 %collective-permute-start.5 = (bf16[192,1024]{1,0:T(8,128)(2,1)S(1)}, bf16[192,1024]{1,0:T(8,128)(2,1)S(1)}, u32[]{:S(2)}, u32[]{:S(2)}) collective-permute-start(bf16[192,1024]{1,0:T(8,128)(2,1)S(1)} %get-tuple-element.46), channel_id=1, source_target_pairs={{0,4},{4,0},{8,12},{12,8},{16,20},{20,16},{24,28},{28,24},{1,5},{5... | collective-permute-start | bytes 1179656 | tf_op jit(solution)/shard_map/ppermute | solution.py:104
  38.0 0.9 copy-start.8
  40.3 15.6 %collective-permute-start.7 = (bf16[2,128,1024]{2,1,0:T(8,128)(2,1)}, bf16[2,128,1024]{2,1,0:T(8,128)(2,1)}, u32[]{:S(2)}, u32[]{:S(2)}) collective-permute-start(bf16[2,128,1024]{2,1,0:T(8,128)(2,1)} %get-tuple-element.34), channel_id=1, source_target_pairs={{4,0},{8,4},{12,8},{16,12},{20,16},{24,20},{28,24},{5,1},{9,5},{13... | collective-permute-start | bytes 1572872 | tf_op jit(solution)/shard_map/ppermute | solution.py:255
  42.6 13.4 %collective-permute-start.6 = (bf16[2,128,1024]{2,1,0:T(8,128)(2,1)}, bf16[2,128,1024]{2,1,0:T(8,128)(2,1)}, u32[]{:S(2)}, u32[]{:S(2)}) collective-permute-start(bf16[2,128,1024]{2,1,0:T(8,128)(2,1)} %get-tuple-element.35), channel_id=1, source_target_pairs={{0,4},{4,8},{8,12},{12,16},{16,20},{20,24},{24,28},{1,5},{5,9},{9,... | collective-permute-start | bytes 1572872 | tf_op jit(solution)/shard_map/ppermute | solution.py:252
  51.0 4.8 %copy-start.13 = (f32[16,8,8,128]{3,1,2,0:T(8,128)S(1)}, f32[16,8,8,128]{3,1,2,0:T(8,128)}, u32[]{:S(2)}) copy-start(f32[16,8,8,128]{3,1,2,0:T(8,128)} %copy.181) | copy-start | bytes 1572868
  56.0 4.4 %collective-permute-start.8 = (f32[64,1152]{1,0:T(8,128)S(1)}, f32[64,1152]{1,0:T(8,128)S(1)}, u32[]{:S(2)}, u32[]{:S(2)}) collective-permute-start(f32[64,1152]{1,0:T(8,128)S(1)} %get-tuple-element.45), channel_id=1, source_target_pairs={{0,4},{4,0},{8,12},{12,8},{16,20},{20,16},{24,28},{28,24},{1,5},{5... | collective-permute-start | bytes 884744 | tf_op jit(solution)/shard_map/ppermute | solution.py:125
  61.1 5.8 %collective-permute-start.9 = (f32[32,1152]{1,0:T(8,128)S(1)}, f32[32,1152]{1,0:T(8,128)S(1)}, u32[]{:S(2)}, u32[]{:S(2)}) collective-permute-start(f32[32,1152]{1,0:T(8,128)S(1)} %get-tuple-element.51), channel_id=1, source_target_pairs={{0,8},{4,12},{8,0},{12,4},{16,24},{20,28},{24,16},{28,20},{1,9},{5... | collective-permute-start | bytes 442376 | tf_op jit(solution)/shard_map/ppermute | solution.py:125
  67.4 4.4 %collective-permute-start.10 = (f32[16,1152]{1,0:T(8,128)S(1)}, f32[16,1152]{1,0:T(8,128)S(1)}, u32[]{:S(2)}, u32[]{:S(2)}) collective-permute-start(f32[16,1152]{1,0:T(8,128)S(1)} %get-tuple-element.59), channel_id=1, source_target_pairs={{0,16},{4,20},{8,24},{12,28},{16,0},{20,4},{24,8},{28,12},{1,17},{... | collective-permute-start | bytes 221192 | tf_op jit(solution)/shard_map/ppermute | solution.py:125
  72.9 5.0 %copy-start.19 = (s32[8]{0:T(128)S(1)}, s32[8]{0:T(128)}, u32[]{:S(2)}) copy-start(s32[8]{0:T(128)} %param.16) | copy-start | bytes 100
  72.9 5.3 %copy-start.7 = (bf16[256,1024]{1,0:T(8,128)(2,1)S(1)}, bf16[256,1024]{1,0:T(8,128)(2,1)}, u32[]{:S(2)}) copy-start(bf16[256,1024]{1,0:T(8,128)(2,1)} %copy-done.6) | copy-start | bytes 1572868
  72.9 5.4 %copy-start.18 = (s32[8]{0:T(128)S(1)}, s32[8]{0:T(128)}, u32[]{:S(2)}) copy-start(s32[8]{0:T(128)} %constant.268) | copy-start | bytes 100
  72.9 55.4 %all-to-all-start = ((bf16[8,272,1024]{2,1,0:T(8,128)(2,1)}), bf16[8,272,1024]{2,1,0:T(8,128)(2,1)}, u32[]{:S(2)}, u32[]{:S(2)}) async-start(bf16[8,272,1024]{2,1,0:T(8,128)(2,1)} %broadcast_dynamic-update-slice_fusion), calls=%async_computation | async-start | bytes 8912896 | tf_op jit(solution)/shard_map/all_to_all | solution.py:331
  77.8 1.1 copy-start.9
  78.3 11.7 %copy-start.3 = (bf16[32,8,8,128]{3,2,1,0:T(8,128)(2,1)}, bf16[32,8,8,128]{3,2,1,0:T(8,128)(2,1)S(1)}, u32[]{:S(2)}) copy-start(bf16[32,8,8,128]{3,2,1,0:T(8,128)(2,1)S(1)} %copy.117) | copy-start | bytes 1572868
  91.9 2.1 %copy-start = (f32[4,8,64,448]{3,2,1,0:T(8,128)}, f32[4,8,64,448]{3,2,1,0:T(8,128)S(1)}, u32[]{:S(2)}) copy-start(f32[4,8,64,448]{3,2,1,0:T(8,128)S(1)} %get-tuple-element.73) | copy-start | bytes 11010052
  136.5 1.0 copy-start.4
  136.5 3.0 %copy-start.5 = (bf16[224,8,8,128]{3,2,1,0:T(8,128)(2,1)S(1)}, bf16[224,8,8,128]{3,2,1,0:T(8,128)(2,1)}, u32[]{:S(2)}) copy-start(bf16[224,8,8,128]{3,2,1,0:T(8,128)(2,1)} %copy.119) | copy-start | bytes 11010052
  137.5 2.6 %copy-start.1 = (f32[4,8,64,448]{3,2,1,0:T(8,128)S(1)}, f32[4,8,64,448]{3,2,1,0:T(8,128)}, u32[]{:S(2)}) copy-start(f32[4,8,64,448]{3,2,1,0:T(8,128)} %copy-done) | copy-start | bytes 11010052
  138.7 5.4 %slice-start = ((s8[8388608]{0:T(1024)(128)(4,1)}), s8[4194304]{0:T(1024)(128)(4,1)S(1)}, s32[]{:S(2)}) async-start(s8[8388608]{0:T(1024)(128)(4,1)} %bitcast.344), calls=%async_computation.2 | async-start | bytes 8388608
  140.1 4.0 %slice-start.1 = ((s8[8388608]{0:T(1024)(128)(4,1)}), s8[4194304]{0:T(1024)(128)(4,1)S(1)}, s32[]{:S(2)}) async-start(s8[8388608]{0:T(1024)(128)(4,1)} %bitcast.344), calls=%async_computation.3 | async-start | bytes 8388608

commit v21 on v20

--- a/solution.py
+++ b/solution.py
@@ -334,11 +334,10 @@
     my_ranks = ranks[seq_place]
     sub = math.gcd(BLOCK, rows_each)
     pieces = incoming.reshape(seq_count, (kv_rows + rows_each) // sub, sub, width_here)
-    first_piece = (my_ranks * (2 * BLOCK) // sub)[:, None] + jnp.arange(BLOCK // sub)[None, :]
-    random_k = pieces[my_owners[:, None], first_piece].reshape(blocks_here, RAND, BLOCK, width_here)
-    random_v = pieces[my_owners[:, None], first_piece + BLOCK // sub].reshape(
-        blocks_here, RAND, BLOCK, width_here
-    )
+    both_pieces = (my_ranks * (2 * BLOCK) // sub)[:, None] + jnp.arange(2 * BLOCK // sub)[None, :]
+    random_both = pieces[my_owners[:, None], both_pieces].reshape(blocks_here, RAND, 2, BLOCK, width_here)
+    random_k = random_both[:, :, 0]
+    random_v = random_both[:, :, 1]
     random_kv = (random_k, random_v)
     near_part = partial_attend(query_view, near_kv[0], near_kv[1], near_valid)
     far_part = partial_attend(

time: 202 us -> 200 us (0.990)
    gather x2 -> x1, local copies, waits for them, and re-layouts: 6.09 us -> 3.29 us  [on_device(): pieces[my_owners[:, None], both_pieces]]
    unnamed x55 -> x51, local copies, waits for them, and re-layouts: 12.3 us -> 11.8 us
  transfers between devices with their start and end apart: 12 -> 12, of which waited for: 8 -> 8; matrix products, arithmetic and copies ran while one was open for 16% -> 17% of each run, Pallas kernels for 0% -> 0%
where the time goes in v21:
time: 200 us
  waiting for transfers between devices  59.8 us (30%)
  blocking collectives  53.1 us (27%)
  local copies, waits for them, and re-layouts  38.1 us (19%)
  other arithmetic  19.1 us (10%)
  starting transfers between devices  16.5 us (8%)
  matrix products  10.7 us (5%)
  between operations  2.4 us (1%)
    all_to_all x1, blocking collectives, sum_over_head(): gathered = lax.all_to_all(partial, 'head', 0, 0, tiled=True)  53.1 us
    all_to_all x1, waiting for transfers between devices, on_device(): lax.all_to_all(outgoing, 'seq', split_axis=0, concat_axis=0, tiled=True)  32.9 us
    unnamed x51, local copies, waits for them, and re-layouts  11.8 us
    ppermute x3, waiting for transfers between devices, tree_reduce(): got = lax.ppermute(send, axis, xor_perm(count, bit))  10.9 us
    ppermute x3, waiting for transfers between devices, tree_reduce(): got = lax.ppermute(parts, axis, xor_perm(count, bit))  8.17 us
    ppermute x3, waiting for transfers between devices, tree_scatter(): parts = merge(keep, lax.ppermute(send, axis, xor_perm(count, bit)))  7.83 us
    all_to_all x1, starting transfers between devices, on_device(): lax.all_to_all(outgoing, 'seq', split_axis=0, concat_axis=0, tiled=True)  4.87 us
    concatenate x1, local copies, waits for them, and re-layouts, on_device(): jnp.concatenate([outgoing.reshape(seq_count, kv_rows, width_here), jnp.ze...  4.78 us
  transfers between devices with their start and end apart: 12, of which 8 were waited for; matrix products, arithmetic and copies ran while one was open for 17% of the time, Pallas kernels for 0%

profile of v21, /device:TPU:2, one launch (start us, length us, event | category | flops | bytes accessed | tf_op | source)
XLA Modules:
  0.0 199.7 jit_solution(10631838520226961341)
XLA Ops:
  1.4 0.7 fusion.107
  2.1 1.2 compare_select_fusion.3
  3.5 1.1 convert_bitcast_fusion
  5.2 0.5 fusion.79
  5.9 0.6 gather_fusion.2
  6.4 0.7 slice_negate_fusion
  7.2 0.6 maximum_multiply_fusion.1
  8.3 1.0 fusion.48
  9.3 0.6 gather_fusion.1
  9.9 0.6 gather_fusion
  11.2 1.4 collective-permute-done
  12.7 6.9 %collective-permute-done.1 = bf16[96,1024]{1,0:T(8,128)(2,1)S(1)} collective-permute-done((bf16[96,1024]{1,0:T(8,128)(2,1)S(1)}, bf16[96,1024]{1,0:T(8,128)(2,1)S(1)}, u32[]{:S(2)}, u32[]{:S(2)}) %collective-permute-start.1) | collective-permute-done | bytes 196640 | tf_op jit(solution)/shard_map/ppermute | solution.py:100
  19.7 1.6 collective-permute-start.2
  21.7 2.7 %collective-permute-done.2 = bf16[48,1024]{1,0:T(8,128)(2,1)S(1)} collective-permute-done((bf16[48,1024]{1,0:T(8,128)(2,1)S(1)}, bf16[48,1024]{1,0:T(8,128)(2,1)S(1)}, u32[]{:S(2)}, u32[]{:S(2)}) %collective-permute-start.2) | collective-permute-done | bytes 98336 | tf_op jit(solution)/shard_map/ppermute | solution.py:100
  24.4 1.6 collective-permute-start.3
  26.1 3.0 %collective-permute-done.3 = bf16[48,1024]{1,0:T(8,128)(2,1)S(1)} collective-permute-done((bf16[48,1024]{1,0:T(8,128)(2,1)S(1)}, bf16[48,1024]{1,0:T(8,128)(2,1)S(1)}, u32[]{:S(2)}, u32[]{:S(2)}) %collective-permute-start.3) | collective-permute-done | bytes 98336 | tf_op jit(solution)/shard_map/ppermute | solution.py:104
  29.7 5.2 %collective-permute-done.4 = bf16[96,1024]{1,0:T(8,128)(2,1)S(1)} collective-permute-done((bf16[96,1024]{1,0:T(8,128)(2,1)S(1)}, bf16[96,1024]{1,0:T(8,128)(2,1)S(1)}, u32[]{:S(2)}, u32[]{:S(2)}) %collective-permute-start.4) | collective-permute-done | bytes 196640 | tf_op jit(solution)/shard_map/ppermute | solution.py:104
  35.3 0.9 copy.125
  36.2 1.3 fusion.123
  37.4 1.4 fusion.124
  39.4 0.7 copy-done.8
  40.5 1.1 fusion.121
  41.5 2.3 %collective-permute-start.7 = (bf16[2,128,1024]{2,1,0:T(8,128)(2,1)}, bf16[2,128,1024]{2,1,0:T(8,128)(2,1)}, u32[]{:S(2)}, u32[]{:S(2)}) collective-permute-start(bf16[2,128,1024]{2,1,0:T(8,128)(2,1)} %get-tuple-element.36), channel_id=1, source_target_pairs={{4,0},{8,4},{12,8},{16,12},{20,16},{24,20},{28,24},{5,1},{9,5},{13... | collective-permute-start | bytes 1572872 | tf_op jit(solution)/shard_map/ppermute | solution.py:255
  43.8 2.0 %collective-permute-start.6 = (bf16[2,128,1024]{2,1,0:T(8,128)(2,1)}, bf16[2,128,1024]{2,1,0:T(8,128)(2,1)}, u32[]{:S(2)}, u32[]{:S(2)}) collective-permute-start(bf16[2,128,1024]{2,1,0:T(8,128)(2,1)} %get-tuple-element.37), channel_id=1, source_target_pairs={{0,4},{4,8},{8,12},{12,16},{16,20},{20,24},{24,28},{1,5},{5,9},{9,... | collective-permute-start | bytes 1572872 | tf_op jit(solution)/shard_map/ppermute | solution.py:252
  46.2 1.4 convolution_bitcast_fusion
  48.0 0.9 copy.198
  48.8 0.5 fusion.53
  49.4 2.8 %gather_fusion.3 = bf16[16,2,64,1024]{3,2,1,0:T(8,128)(2,1)} fusion(bf16[4,2,64,1024]{3,2,0,1:T(8,128)(2,1)S(1)} %bitcast.271, s32[1024]{0:T(1024)S(1)} %pad_clamp_fusion.1), kind=kCustom, calls=%fused_computation.3 | custom fusion | bytes 8388672 | tf_op jit(solution)/shard_map/gather | solution.py:309
  52.3 4.8 %concatenate.67 = bf16[8,272,1024]{2,1,0:T(8,128)(2,1)} pad(bf16[8,256,1024]{2,1,0:T(8,128)(2,1)} %bitcast.275, bf16[]{:T(256)} %constant.219.clone.1), padding=0_0x0_16x0_0 | pad | bytes 8650754 | tf_op jit(solution)/shard_map/concatenate | solution.py:312
  57.3 2.7 %collective-permute-start.8 = (f32[64,1152]{1,0:T(8,128)S(1)}, f32[64,1152]{1,0:T(8,128)S(1)}, u32[]{:S(2)}, u32[]{:S(2)}) collective-permute-start(f32[64,1152]{1,0:T(8,128)S(1)} %get-tuple-element.47), channel_id=1, source_target_pairs={{0,4},{4,0},{8,12},{12,8},{16,20},{20,16},{24,28},{28,24},{1,5},{5... | collective-permute-start | bytes 884744 | tf_op jit(solution)/shard_map/ppermute | solution.py:125
  59.9 1.3 compare_and_fusion.1
  62.4 5.7 %collective-permute-done.9 = f32[32,1152]{1,0:T(8,128)S(1)} collective-permute-done((f32[32,1152]{1,0:T(8,128)S(1)}, f32[32,1152]{1,0:T(8,128)S(1)}, u32[]{:S(2)}, u32[]{:S(2)}) %collective-permute-start.9) | collective-permute-done | bytes 147488 | tf_op jit(solution)/shard_map/ppermute | solution.py:125
  68.5 0.8 collective-permute-start.10
  69.3 1.2 compare_and_fusion
  70.8 2.2 %collective-permute-done.10 = f32[16,1152]{1,0:T(8,128)S(1)} collective-permute-done((f32[16,1152]{1,0:T(8,128)S(1)}, f32[16,1152]{1,0:T(8,128)S(1)}, u32[]{:S(2)}, u32[]{:S(2)}) %collective-permute-start.10) | collective-permute-done | bytes 73760 | tf_op jit(solution)/shard_map/ppermute | solution.py:125
  73.3 0.7 broadcast_dynamic-update-slice_fusion
  74.0 4.9 %all-to-all-start = ((bf16[8,272,1024]{2,1,0:T(8,128)(2,1)}), bf16[8,272,1024]{2,1,0:T(8,128)(2,1)}, u32[]{:S(2)}, u32[]{:S(2)}) async-start(bf16[8,272,1024]{2,1,0:T(8,128)(2,1)} %broadcast_dynamic-update-slice_fusion), calls=%async_computation | async-start | bytes 8912896 | tf_op jit(solution)/shard_map/all_to_all | solution.py:331
  79.6 0.5 copy-done.9
  80.1 1.0 slice.228
  81.1 1.0 slice.227
  82.0 1.2 maximum_bitcast_fusion
  83.2 1.4 maximum_bitcast_fusion.1
  84.9 1.1 pad_maximum_fusion
  86.0 1.5 fusion.119
  87.5 1.0 copy.135
  88.5 2.7 %copy.136 = bf16[224,8,8,128]{3,2,1,0:T(8,128)(2,1)} copy(bf16[224,8,8,128]{3,1,2,0:T(8,128)(2,1)S(1)} %bitcast.280) | data formatting | bytes 7340032
  91.2 1.8 fusion
  93.1 2.1 %copy-done = f32[4,8,64,448]{3,2,1,0:T(8,128)} copy-done((f32[4,8,64,448]{3,2,1,0:T(8,128)}, f32[4,8,64,448]{3,2,1,0:T(8,128)S(1)}, u32[]{:S(2)}) %copy-start) | copy-done | bytes 3670040
  95.1 1.5 fusion.5
  96.6 32.9 %all-to-all-done = bf16[8,272,1024]{2,1,0:T(8,128)(2,1)} async-done(((bf16[8,272,1024]{2,1,0:T(8,128)(2,1)}), bf16[8,272,1024]{2,1,0:T(8,128)(2,1)}, u32[]{:S(2)}, u32[]{:S(2)}) %all-to-all-start) | async-done | bytes 4456480 | tf_op jit(solution)/shard_map/all_to_all | solution.py:331
  129.5 1.0 slice.222
  130.4 0.6 gather_fusion.4
  131.0 3.3 %gather_fusion.5 = bf16[96,16,1024]{2,1,0:T(8,128)(2,1)S(1)} fusion(bf16[8,17,16,1024]{3,2,1,0:T(8,128)(2,1)} %bitcast.79, s32[96]{0:T(128)S(1)} %reshape.506), kind=kCustom, calls=%fused_computation.5 | custom fusion | bytes 6292224 | tf_op jit(solution)/shard_map/gather | solution.py:338
  134.3 0.4 fusion.120
  134.7 0.4 copy.138
  135.2 0.4 copy.137
  135.8 1.2 multiply_reduce_fusion
  137.0 0.8 fusion.12
  137.8 0.8 copy-done.1
  138.6 2.1 %fusion.32 = f32[4,64,8,128]{3,1,2,0:T(8,128)S(1)} fusion(bf16[4,448,8,128]{3,2,1,0:T(8,128)(2,1)S(1)} %bitcast.300, f32[4,8,64,448]{3,2,1,0:T(8,128)S(1)} %copy-done.1, f32[4,8,64]{2,1,0:T(8,128)S(1)} %get-tuple-element.72, pred[4,8,448]{2,1,0:T(8,128)(4,1)S(1)} %broadcast_in_dim.197, f32[4,64,8]{1,2,0:T(8,128)S(1)} %get-tuple-element.15), kind=kOutput, calls=%fused_computation.34 | convolution fusion | flops 238813184 | bytes 8419328 | tf_op jit(solution)/shard_map/bhqs,bshd->bqhd/dot_general | solution.py:184
  140.7 1.4 fusion.42
  142.6 2.5 %convolution_convert_fusion = bf16[256,4096]{1,0:T(8,128)(2,1)S(1)} fusion(bf16[1024,4096]{1,0:T(8,128)(2,1)S(1)} %bitcast.347, bf16[256,1024]{1,0:T(8,128)(2,1)S(1)} %bitcast.325, bf16[256,1024]{1,0:T(8,128)(2,1)S(1)} %bitcast.326, bf16[32,8,8,128]{3,2,1,0:T(8,128)(2,1)S(1)} %bitcast.330, pred[256]{0:T(512)(128)(4,1)S(1)} %broadcast_in_dim.190, ...), kind=kOutput, calls=%fused_computation.7 | convolution fusion | flops 2149056512 | bytes 12059136 | tf_op jit(solution)/shard_map/dot_general | solution.py:159
  145.3 53.1 %all_to_all.10 = bf16[4,1024,256]{1,2,0:T(8,128)(2,1)S(1)} all-to-all(bf16[4,1024,256]{1,2,0:T(8,128)(2,1)S(1)} %bitcast.291), channel_id=1, replica_groups=mesh['seq'=8,'head'=4] {'head'}, dimensions={0} | all-to-all | bytes 4194304 | tf_op jit(solution)/shard_map/all_to_all | solution.py:166
  198.4 1.3 reduce_sum.71
  (142 shorter events, 9.3 us)
Async XLA Ops:
  0.0 4.8 %copy-start.11 = (bf16[256,1024]{1,0:T(8,128)(2,1)S(1)}, bf16[256,1024]{1,0:T(8,128)(2,1)}, u32[]{:S(2)}) copy-start(bf16[256,1024]{1,0:T(8,128)(2,1)} %param.11) | copy-start | bytes 1572868
  2.1 1.4 copy-start.14
  4.6 1.2 copy-start.2
  7.1 1.0 copy-start.10
  7.1 1.2 copy-start.12
  9.3 3.3 %copy-start.6 = (bf16[256,1024]{1,0:T(8,128)(2,1)}, bf16[256,1024]{1,0:T(8,128)(2,1)S(1)}, u32[]{:S(2)}) copy-start(bf16[256,1024]{1,0:T(8,128)(2,1)S(1)} %get-tuple-element.38) | copy-start | bytes 1572868
  9.3 1.6 copy-start.15
  10.8 1.8 collective-permute-start
  12.6 7.0 %collective-permute-start.1 = (bf16[96,1024]{1,0:T(8,128)(2,1)S(1)}, bf16[96,1024]{1,0:T(8,128)(2,1)S(1)}, u32[]{:S(2)}, u32[]{:S(2)}) collective-permute-start(bf16[96,1024]{1,0:T(8,128)(2,1)S(1)} %dynamic-slice_bitcast_fusion.3), channel_id=1, source_target_pairs={{0,8},{4,12},{8,0},{12,4},{16,24},{20,28},{24,16},{28,20},{1,9},{5... | collective-permute-start | bytes 589832 | tf_op jit(solution)/shard_map/ppermute | solution.py:100
  19.7 4.7 %collective-permute-start.2 = (bf16[48,1024]{1,0:T(8,128)(2,1)S(1)}, bf16[48,1024]{1,0:T(8,128)(2,1)S(1)}, u32[]{:S(2)}, u32[]{:S(2)}) collective-permute-start(bf16[48,1024]{1,0:T(8,128)(2,1)S(1)} %dynamic-slice_bitcast_fusion.6), channel_id=1, source_target_pairs={{0,16},{4,20},{8,24},{12,28},{16,0},{20,4},{24,8},{28,12},{1,17},{... | collective-permute-start | bytes 294920 | tf_op jit(solution)/shard_map/ppermute | solution.py:100
  24.4 4.7 %collective-permute-start.3 = (bf16[48,1024]{1,0:T(8,128)(2,1)S(1)}, bf16[48,1024]{1,0:T(8,128)(2,1)S(1)}, u32[]{:S(2)}, u32[]{:S(2)}) collective-permute-start(bf16[48,1024]{1,0:T(8,128)(2,1)S(1)} %bitcast_add_fusion.2), channel_id=1, source_target_pairs={{0,16},{4,20},{8,24},{12,28},{16,0},{20,4},{24,8},{28,12},{1,17},{... | collective-permute-start | bytes 294920 | tf_op jit(solution)/shard_map/ppermute | solution.py:104
  29.2 5.7 %collective-permute-start.4 = (bf16[96,1024]{1,0:T(8,128)(2,1)S(1)}, bf16[96,1024]{1,0:T(8,128)(2,1)S(1)}, u32[]{:S(2)}, u32[]{:S(2)}) collective-permute-start(bf16[96,1024]{1,0:T(8,128)(2,1)S(1)} %get-tuple-element.56), channel_id=1, source_target_pairs={{0,8},{4,12},{8,0},{12,4},{16,24},{20,28},{24,16},{28,20},{1,9},{5... | collective-permute-start | bytes 589832 | tf_op jit(solution)/shard_map/ppermute | solution.py:104
  35.2 3.7 %collective-permute-start.5 = (bf16[192,1024]{1,0:T(8,128)(2,1)S(1)}, bf16[192,1024]{1,0:T(8,128)(2,1)S(1)}, u32[]{:S(2)}, u32[]{:S(2)}) collective-permute-start(bf16[192,1024]{1,0:T(8,128)(2,1)S(1)} %get-tuple-element.48), channel_id=1, source_target_pairs={{0,4},{4,0},{8,12},{12,8},{16,20},{20,16},{24,28},{28,24},{1,5},{5... | collective-permute-start | bytes 1179656 | tf_op jit(solution)/shard_map/ppermute | solution.py:104
  39.3 0.9 copy-start.8
  41.5 15.6 %collective-permute-start.7 = (bf16[2,128,1024]{2,1,0:T(8,128)(2,1)}, bf16[2,128,1024]{2,1,0:T(8,128)(2,1)}, u32[]{:S(2)}, u32[]{:S(2)}) collective-permute-start(bf16[2,128,1024]{2,1,0:T(8,128)(2,1)} %get-tuple-element.36), channel_id=1, source_target_pairs={{4,0},{8,4},{12,8},{16,12},{20,16},{24,20},{28,24},{5,1},{9,5},{13... | collective-permute-start | bytes 1572872 | tf_op jit(solution)/shard_map/ppermute | solution.py:255
  43.8 13.4 %collective-permute-start.6 = (bf16[2,128,1024]{2,1,0:T(8,128)(2,1)}, bf16[2,128,1024]{2,1,0:T(8,128)(2,1)}, u32[]{:S(2)}, u32[]{:S(2)}) collective-permute-start(bf16[2,128,1024]{2,1,0:T(8,128)(2,1)} %get-tuple-element.37), channel_id=1, source_target_pairs={{0,4},{4,8},{8,12},{12,16},{16,20},{20,24},{24,28},{1,5},{5,9},{9,... | collective-permute-start | bytes 1572872 | tf_op jit(solution)/shard_map/ppermute | solution.py:252
  52.3 4.8 %copy-start.13 = (f32[16,8,8,128]{3,1,2,0:T(8,128)S(1)}, f32[16,8,8,128]{3,1,2,0:T(8,128)}, u32[]{:S(2)}) copy-start(f32[16,8,8,128]{3,1,2,0:T(8,128)} %copy.198) | copy-start | bytes 1572868
  57.3 4.3 %collective-permute-start.8 = (f32[64,1152]{1,0:T(8,128)S(1)}, f32[64,1152]{1,0:T(8,128)S(1)}, u32[]{:S(2)}, u32[]{:S(2)}) collective-permute-start(f32[64,1152]{1,0:T(8,128)S(1)} %get-tuple-element.47), channel_id=1, source_target_pairs={{0,4},{4,0},{8,12},{12,8},{16,20},{20,16},{24,28},{28,24},{1,5},{5... | collective-permute-start | bytes 884744 | tf_op jit(solution)/shard_map/ppermute | solution.py:125
  62.2 5.8 %collective-permute-start.9 = (f32[32,1152]{1,0:T(8,128)S(1)}, f32[32,1152]{1,0:T(8,128)S(1)}, u32[]{:S(2)}, u32[]{:S(2)}) collective-permute-start(f32[32,1152]{1,0:T(8,128)S(1)} %get-tuple-element.53), channel_id=1, source_target_pairs={{0,8},{4,12},{8,0},{12,4},{16,24},{20,28},{24,16},{28,20},{1,9},{5... | collective-permute-start | bytes 442376 | tf_op jit(solution)/shard_map/ppermute | solution.py:125
  68.5 4.4 %collective-permute-start.10 = (f32[16,1152]{1,0:T(8,128)S(1)}, f32[16,1152]{1,0:T(8,128)S(1)}, u32[]{:S(2)}, u32[]{:S(2)}) collective-permute-start(f32[16,1152]{1,0:T(8,128)S(1)} %get-tuple-element.61), channel_id=1, source_target_pairs={{0,16},{4,20},{8,24},{12,28},{16,0},{20,4},{24,8},{28,12},{1,17},{... | collective-permute-start | bytes 221192 | tf_op jit(solution)/shard_map/ppermute | solution.py:125
  74.0 5.0 %copy-start.17 = (s32[8]{0:T(128)S(1)}, s32[8]{0:T(128)}, u32[]{:S(2)}) copy-start(s32[8]{0:T(128)} %param.16) | copy-start | bytes 100
  74.0 5.3 %copy-start.7 = (bf16[256,1024]{1,0:T(8,128)(2,1)S(1)}, bf16[256,1024]{1,0:T(8,128)(2,1)}, u32[]{:S(2)}) copy-start(bf16[256,1024]{1,0:T(8,128)(2,1)} %copy-done.6) | copy-start | bytes 1572868
  74.0 5.4 %copy-start.16 = (s32[8]{0:T(128)S(1)}, s32[8]{0:T(128)}, u32[]{:S(2)}) copy-start(s32[8]{0:T(128)} %constant.252) | copy-start | bytes 100
  74.0 55.4 %all-to-all-start = ((bf16[8,272,1024]{2,1,0:T(8,128)(2,1)}), bf16[8,272,1024]{2,1,0:T(8,128)(2,1)}, u32[]{:S(2)}, u32[]{:S(2)}) async-start(bf16[8,272,1024]{2,1,0:T(8,128)(2,1)} %broadcast_dynamic-update-slice_fusion), calls=%async_computation | async-start | bytes 8912896 | tf_op jit(solution)/shard_map/all_to_all | solution.py:331
  78.9 1.1 copy-start.9
  79.5 11.7 %copy-start.3 = (bf16[32,8,8,128]{3,2,1,0:T(8,128)(2,1)}, bf16[32,8,8,128]{3,2,1,0:T(8,128)(2,1)S(1)}, u32[]{:S(2)}) copy-start(bf16[32,8,8,128]{3,2,1,0:T(8,128)(2,1)S(1)} %copy.134) | copy-start | bytes 1572868
  93.0 2.1 %copy-start = (f32[4,8,64,448]{3,2,1,0:T(8,128)}, f32[4,8,64,448]{3,2,1,0:T(8,128)S(1)}, u32[]{:S(2)}) copy-start(f32[4,8,64,448]{3,2,1,0:T(8,128)S(1)} %get-tuple-element.73) | copy-start | bytes 11010052
  134.7 1.0 copy-start.4
  135.2 2.6 %copy-start.5 = (bf16[224,8,8,128]{3,2,1,0:T(8,128)(2,1)S(1)}, bf16[224,8,8,128]{3,2,1,0:T(8,128)(2,1)}, u32[]{:S(2)}) copy-start(bf16[224,8,8,128]{3,2,1,0:T(8,128)(2,1)} %copy.136) | copy-start | bytes 11010052
  135.8 2.9 %copy-start.1 = (f32[4,8,64,448]{3,2,1,0:T(8,128)S(1)}, f32[4,8,64,448]{3,2,1,0:T(8,128)}, u32[]{:S(2)}) copy-start(f32[4,8,64,448]{3,2,1,0:T(8,128)} %copy-done) | copy-start | bytes 11010052
  137.0 5.6 %slice-start = ((s8[8388608]{0:T(1024)(128)(4,1)}), s8[4194304]{0:T(1024)(128)(4,1)S(1)}, s32[]{:S(2)}) async-start(s8[8388608]{0:T(1024)(128)(4,1)} %bitcast.346), calls=%async_computation.2 | async-start | bytes 8388608
  138.6 4.0 %slice-start.1 = ((s8[8388608]{0:T(1024)(128)(4,1)}), s8[4194304]{0:T(1024)(128)(4,1)S(1)}, s32[]{:S(2)}) async-start(s8[8388608]{0:T(1024)(128)(4,1)} %bitcast.346), calls=%async_computation.3 | async-start | bytes 8388608
